TPU v7x, 32 devices: a whole 2x2x4 slice. The times are simulated.
32 devices in a mesh: grp: 2 (over x), limb: 8 (over z, y), coef: 2 (over core).
Axes of the slice: x: 2, y: 2, z: 4, core: 2. Of those that a mesh axis runs over, the one named last changes fastest.
Arguments:
- cipher: bfloat16 [16, 48, 128, 256], P(('grp', 'limb'), None, None, 'coef'), parts along dimension 0, may hold values from -6 to 6
- switch_key: bfloat16 [1, 3, 64, 128, 256], P(None, None, 'limb', None, 'coef'), may hold values from -3 to 3
- raise_table: bfloat16 [3, 48, 16], replicated, may hold values from -1.5 to 1.5
- lower_table: bfloat16 [48, 16], replicated, may hold values from -1.5 to 1.5
- special_inverse: float32 [48], replicated, may hold values from 0.5 to 2
Outputs:
- switched: bfloat16 [1, 16, 48, 128, 256], P(None, ('grp', 'limb'), None, None, 'coef'), parts along dimension 1
There are 2 independent parts, one for each index of `grp`. A program takes and returns all parts, laid end to end along the dimension named above; an argument that names none is the same for every part. Nothing has to cross between parts.
All inputs are finite; a program needn't handle non-finite values.
Results may differ from a plain program's by a relative error of at most 0.018.
Values may be sent and summed in bfloat16 or wider, within the bound.
No kernel may reach another device: no remote copies, remote signals or barrier semaphores. Data moves between devices by JAX's collectives and lax.ppermute only.
A program may use at most 128 MiB of HBM per device.

v0:
```python
import math

import jax
import jax.numpy as jnp
from jax import lax
from jax.experimental import pallas as pl
from jax.experimental.pallas import tpu as pltpu
from jax.sharding import PartitionSpec as P

LIMBS = 48
DIGITS = 3
DIGIT_LIMBS = 16
EXTENDED = 64
CYCLE = 32768
BLK = 16

F32 = jnp.float32
BF16 = jnp.bfloat16
I32 = jnp.int32


def cosine_table(size):
    freq = jnp.arange(size, dtype=jnp.float32)[:, None]
    place = jnp.arange(size, dtype=jnp.float32)[None, :]
    norm = jnp.where(freq == 0, math.sqrt(1.0 / size), math.sqrt(2.0 / size))
    return (norm * jnp.cos(math.pi * (2.0 * place + 1.0) * freq / (2.0 * size))).astype(
        jnp.bfloat16
    )


def _angle(phase):
    ang = (2.0 * math.pi / CYCLE) * phase.astype(F32)
    return jnp.cos(ang), jnp.sin(ang)


def _twiddle(p, q):
    cp, sp = _angle(p)
    cq, sq = _angle(q)
    cp, sp, cq, sq = lax.optimization_barrier((cp, sp, cq, sq))
    return 1.0 + 0.5 * (cp * cq - sp * sq)


def twiddle_tables(me, rows, cols, nc):
    rows_l, cols_l = rows // nc, cols // nc
    m = (2 * jnp.arange(EXTENDED, dtype=I32) + 1)[:, None, None, None]
    fine = jnp.arange(8, dtype=I32)[None, None, :, None]
    coarse = (8 * jnp.arange(rows // 8, dtype=I32))[None, :, None, None]
    bcol = (me * cols_l + jnp.arange(cols_l, dtype=I32))[None, None, None, :]
    w_col = _twiddle(
        (coarse * bcol) % CYCLE * m % CYCLE, (fine * bcol) % CYCLE * m % CYCLE
    ).reshape(EXTENDED, rows, cols_l)
    coarse = (me * rows_l + 8 * jnp.arange(rows_l // 8, dtype=I32))[None, :, None, None]
    ball = jnp.arange(cols, dtype=I32)[None, None, None, :]
    w_row = _twiddle(
        (coarse * ball) % CYCLE * m % CYCLE, (fine * ball) % CYCLE * m % CYCLE
    ).reshape(EXTENDED, rows_l, cols)
    v_row = _twiddle(
        (coarse * cols + ball) * m % CYCLE, (fine * cols) * m % CYCLE
    ).reshape(EXTENDED, rows_l, cols)
    return w_col, w_row, v_row


SMEM_SPEC = pl.BlockSpec(memory_space=pltpu.SMEM)


def _split_store(me_ref, first, second, own_ref, send_ref):
    top = me_ref[0] == 0

    @pl.when(top)
    def _():
        own_ref[...] = first
        send_ref[...] = second

    @pl.when(jnp.logical_not(top))
    def _():
        own_ref[...] = second
        send_ref[...] = first


def _inv_row_kernel(me_ref, y_ref, w_ref, ft_ref, own_ref, send_ref, h_ref):
    ft = ft_ref[...]
    n, rows, _ = y_ref.shape
    for l in range(n):
        h = jnp.dot(ft, y_ref[l], preferred_element_type=F32)
        h_ref[l] = (h / w_ref[l]).astype(BF16)
    half = rows // 2
    _split_store(me_ref, h_ref[:, :half, :], h_ref[:, half:, :], own_ref, send_ref)


def inv_row(me_arr, y, w_col, ft, e0):
    n, rows, cols_l = y.shape
    eb0 = e0 // BLK
    blk = pl.BlockSpec((BLK, rows, cols_l), lambda i: (i, 0, 0))
    out = pl.BlockSpec((BLK, rows // 2, cols_l), lambda i: (i, 0, 0))
    return pl.pallas_call(
        _inv_row_kernel,
        grid=(n // BLK,),
        in_specs=[
            SMEM_SPEC,
            blk,
            pl.BlockSpec((BLK, rows, cols_l), lambda i: (i + eb0, 0, 0)),
            pl.BlockSpec((rows, rows), lambda i: (0, 0)),
        ],
        out_specs=[out, out],
        out_shape=[jax.ShapeDtypeStruct((n, rows // 2, cols_l), BF16)] * 2,
        scratch_shapes=[pltpu.VMEM((BLK, rows, cols_l), BF16)],
    )(me_arr, y, w_col, ft)


def _inv_col_kernel(own_ref, recv_ref, v_ref, fo_ref, fr_ref, out_ref):
    n, rows_l, half = own_ref.shape
    a = own_ref[...].reshape(n * rows_l, half)
    b = recv_ref[...].reshape(n * rows_l, half)
    x = jnp.dot(a, fo_ref[...], preferred_element_type=F32)
    x = x + jnp.dot(b, fr_ref[...], preferred_element_type=F32)
    x = x.reshape(n, rows_l, -1)
    out_ref[...] = (x / v_ref[...]).astype(BF16)


def inv_col(own, recv, v_row, f_own, f_oth, e0):
    n, rows_l, half = own.shape
    cols = 2 * half
    eb0 = e0 // BLK
    blk = pl.BlockSpec((BLK, rows_l, half), lambda i: (i, 0, 0))
    return pl.pallas_call(
        _inv_col_kernel,
        grid=(n // BLK,),
        in_specs=[
            blk,
            blk,
            pl.BlockSpec((BLK, rows_l, cols), lambda i: (i + eb0, 0, 0)),
            pl.BlockSpec((half, cols), lambda i: (0, 0)),
            pl.BlockSpec((half, cols), lambda i: (0, 0)),
        ],
        out_specs=pl.BlockSpec((BLK, rows_l, cols), lambda i: (i, 0, 0)),
        out_shape=jax.ShapeDtypeStruct((n, rows_l, cols), BF16),
    )(own, recv, v_row, f_own, f_oth)


def _fwd_col_kernel(me_ref, x_ref, v_ref, w_ref, ft_ref, own_ref, send_ref):
    n, rows_l, cols = x_ref.shape
    g = (x_ref[...].astype(F32) * v_ref[...]).astype(BF16)
    h = jnp.dot(g.reshape(n * rows_l, cols), ft_ref[...], preferred_element_type=F32)
    h = (h.reshape(n, rows_l, cols) * w_ref[...]).astype(BF16)
    half = cols // 2
    _split_store(me_ref, h[:, :, :half], h[:, :, half:], own_ref, send_ref)


def fwd_col(me_arr, x, v_row, w_row, ft, table_block):
    groups, n, rows_l, cols = x.shape
    half = cols // 2
    xs = pl.BlockSpec((None, BLK, rows_l, cols), lambda j, t: (j, t, 0, 0))
    ts = pl.BlockSpec((BLK, rows_l, cols), lambda j, t: (table_block(j, t), 0, 0))
    os = pl.BlockSpec((None, BLK, rows_l, half), lambda j, t: (j, t, 0, 0))
    return pl.pallas_call(
        _fwd_col_kernel,
        grid=(groups, n // BLK),
        in_specs=[SMEM_SPEC, xs, ts, ts, pl.BlockSpec((cols, cols), lambda j, t: (0, 0))],
        out_specs=[os, os],
        out_shape=[jax.ShapeDtypeStruct((groups, n, rows_l, half), BF16)] * 2,
    )(me_arr, x, v_row, w_row, ft)


def _product_kernel(eb0, fo_ref, fr_ref, cip_ref, key_ref, *rest):
    halves = rest[: 2 * DIGITS]
    out_ref, acc_ref = rest[2 * DIGITS :]
    eb = pl.program_id(0) + eb0
    fo = fo_ref[...]
    fr = fr_ref[...]
    acc_ref[...] = jnp.zeros_like(acc_ref)
    n = acc_ref.shape[0]
    for j in range(DIGITS):
        own_ref, recv_ref = halves[2 * j], halves[2 * j + 1]

        @pl.when(eb == j)
        def _():
            acc_ref[...] += cip_ref[...].astype(F32) * key_ref[j].astype(F32)

        @pl.when(eb != j)
        def _():
            for l in range(n):
                y = jnp.dot(fo, own_ref[l], preferred_element_type=F32)
                y = (y + jnp.dot(fr, recv_ref[l], preferred_element_type=F32)).astype(BF16)
                acc_ref[l] += y.astype(F32) * key_ref[j, l].astype(F32)

    out_ref[...] = acc_ref[...].astype(BF16)


def product(cip, key, own2, recv2, f_own, f_oth, eb0, nblocks):
    _, rows, cols_l = cip.shape
    rows_l = rows // 2

    def lifted_block(j):
        def index(i):
            eb = i + eb0
            tb = jnp.where(eb < j, eb, eb - 1)
            return (j, jnp.clip(tb, 0, DIGITS - 1), 0, 0)

        return pl.BlockSpec((None, BLK, rows_l, cols_l), index)

    half_specs = []
    half_args = []
    for j in range(DIGITS):
        half_specs += [lifted_block(j), lifted_block(j)]
        half_args += [own2, recv2]
    return pl.pallas_call(
        lambda *refs: _product_kernel(eb0, *refs),
        grid=(nblocks,),
        in_specs=[
            pl.BlockSpec((rows, rows_l), lambda i: (0, 0)),
            pl.BlockSpec((rows, rows_l), lambda i: (0, 0)),
            pl.BlockSpec(
                (BLK, rows, cols_l), lambda i: (jnp.minimum(i + eb0, DIGITS - 1), 0, 0)
            ),
            pl.BlockSpec((DIGITS, BLK, rows, cols_l), lambda i: (0, i + eb0, 0, 0)),
        ]
        + half_specs,
        out_specs=pl.BlockSpec((BLK, rows, cols_l), lambda i: (i, 0, 0)),
        out_shape=jax.ShapeDtypeStruct((nblocks * BLK, rows, cols_l), BF16),
        scratch_shapes=[pltpu.VMEM((BLK, rows, cols_l), F32)],
    )(f_own, f_oth, cip, key, *half_args)


def _final_kernel(fo_ref, fr_ref, own_ref, recv_ref, prod_ref, s_ref, out_ref):
    fo = fo_ref[...]
    fr = fr_ref[...]
    for l in range(own_ref.shape[0]):
        y = jnp.dot(fo, own_ref[l], preferred_element_type=F32)
        y = (y + jnp.dot(fr, recv_ref[l], preferred_element_type=F32)).astype(BF16)
        diff = prod_ref[l].astype(F32) - y.astype(F32)
        out_ref[l] = (diff * s_ref[l]).astype(BF16)


def final(own4, recv4, prod, scale, f_own, f_oth):
    n, rows, cols_l = prod.shape
    rows_l = rows // 2
    hs = pl.BlockSpec((BLK, rows_l, cols_l), lambda i: (i, 0, 0))
    return pl.pallas_call(
        _final_kernel,
        grid=(n // BLK,),
        in_specs=[
            pl.BlockSpec((rows, rows_l), lambda i: (0, 0)),
            pl.BlockSpec((rows, rows_l), lambda i: (0, 0)),
            hs,
            hs,
            pl.BlockSpec((BLK, rows, cols_l), lambda i: (i, 0, 0)),
            pl.BlockSpec((BLK, 1, cols_l), lambda i: (i, 0, 0)),
        ],
        out_specs=pl.BlockSpec((BLK, rows, cols_l), lambda i: (i, 0, 0)),
        out_shape=jax.ShapeDtypeStruct((n, rows, cols_l), BF16),
    )(f_own, f_oth, own4, recv4, prod, scale)


def swap(x):
    return lax.ppermute(x, "coef", perm=[(0, 1), (1, 0)])


def body(cipher, switch_key, raise_table, lower_table, special_inverse):
    nc = lax.axis_size("coef")
    me = lax.axis_index("coef")
    me_arr = jnp.reshape(me, (1,)).astype(I32)
    other = 1 - me
    _, limbs, rows, cols_l = cipher.shape
    cols = cols_l * nc
    rows_l = rows // nc

    key = lax.all_gather(switch_key, "limb", axis=2, tiled=True)[0]

    f_rows = cosine_table(rows)
    f_cols = cosine_table(cols)
    ft_rows = f_rows.T
    ft_cols = f_cols.T
    fc_own = lax.dynamic_slice_in_dim(f_cols, me * cols_l, cols_l, axis=0)
    fc_oth = lax.dynamic_slice_in_dim(f_cols, other * cols_l, cols_l, axis=0)
    fr_own = lax.dynamic_slice_in_dim(f_rows, me * rows_l, rows_l, axis=1)
    fr_oth = lax.dynamic_slice_in_dim(f_rows, other * rows_l, rows_l, axis=1)
    w_col, w_row, v_row = twiddle_tables(me, rows, cols, nc)

    ct = cipher[0]
    own1, send1 = inv_row(me_arr, ct, w_col, ft_rows, 0)
    coeffs = inv_col(own1, swap(send1), v_row, fc_own, fc_oth, 0)

    blocks = coeffs.reshape(DIGITS, DIGIT_LIMBS, rows_l * cols)
    raised = lax.dot_general(
        raise_table, blocks, (((2,), (1,)), ((0,), (0,))), preferred_element_type=F32
    )
    raised = raised.astype(BF16).reshape(DIGITS, limbs, rows_l, cols)

    own2, send2 = fwd_col(
        me_arr, raised, v_row, w_row, ft_cols, lambda j, t: jnp.where(t >= j, t + 1, t)
    )
    recv2 = swap(send2)

    prod_special = product(ct, key, own2, recv2, fr_own, fr_oth, DIGITS, 1)
    prod_cipher = product(ct, key, own2, recv2, fr_own, fr_oth, 0, DIGITS)

    own3, send3 = inv_row(me_arr, prod_special, w_col, ft_rows, limbs)
    special = inv_col(own3, swap(send3), v_row, fc_own, fc_oth, limbs)
    lowered = jnp.dot(
        lower_table, special.reshape(DIGIT_LIMBS, rows_l * cols), preferred_element_type=F32
    )
    lowered = lowered.astype(BF16).reshape(1, limbs, rows_l, cols)
    own4, send4 = fwd_col(me_arr, lowered, v_row, w_row, ft_cols, lambda j, t: t)
    scale = jnp.broadcast_to(special_inverse[:, None, None], (limbs, 1, cols_l))
    result = final(own4[0], swap(send4)[0], prod_cipher, scale, fr_own, fr_oth)
    return result[None, None]


def solution(mesh):
    in_specs = (
        P(("grp", "limb"), None, None, "coef"),
        P(None, None, "limb", None, "coef"),
        P(),
        P(),
        P(),
    )
    out_specs = P(None, ("grp", "limb"), None, None, "coef")
    return jax.shard_map(body, mesh=mesh, in_specs=in_specs, out_specs=out_specs, check_vma=False)
```

profile of v0, /device:TPU:0, one launch (start us, length us, event | category | flops | bytes accessed | tf_op | source)
XLA Modules:
  0.0 151.4 jit_solution(3772627966890927370)
XLA Ops:
  6.5 0.0 copy-start
  6.5 0.0 all-gather.2.cloned.1.call-start
  6.5 0.7 all-gather.2.cloned.1.call-update
  7.3 0.1 add_select_fusion.7
  7.4 1.1 fusion.26
  8.5 2.1 %fusion.24 = (f32[64,16,1,128]{3,1,0,2:T(8,128)S(1)}, f32[64,16,1,128]{3,1,0,2:T(8,128)S(1)}) fusion(s32[64]{0:T(128)S(1)} %multiply_add_fusion.1, s32[16,128]{1,0:T(8,128)S(1)} %add_select_fusion.7), kind=kLoop, calls=%fused_computation.57 | loop fusion | flops 1835008 | bytes 1057024 | tf_op jit(solution)/shard_map/sin | solution.py:33
  10.6 0.9 multiply_convert_fusion.2
  11.5 2.9 %add_bitcast_fusion.1.w_ref = f32[64,128,128]{2,1,0:T(8,128)} fusion(f32[64,8,128]{2,1,0:T(8,128)S(1)} %bitcast.72, f32[64,16,128]{2,1,0:T(8,128)S(1)} %bitcast.70, f32[64,8,128]{2,1,0:T(8,128)S(1)} %bitcast.73, f32[64,16,128]{2,1,0:T(8,128)S(1)} %bitcast.71), kind=kLoop, calls=%fused_computation.8 | loop fusion | flops 5242880 | bytes 5767168 | tf_op jit(solution)/shard_map/add | solution.py:40
  14.4 4.8 %shard_map.55 = (bf16[48,64,128]{2,1,0:T(8,128)(2,1)}, bf16[48,64,128]{2,1,0:T(8,128)(2,1)}) custom-call(s32[1]{0:T(128)} %bitcast.me_ref, bf16[48,128,128]{2,1,0:T(8,128)(2,1)} %bitcast.57, f32[64,128,128]{2,1,0:T(8,128)} %add_bitcast_fusion.1.w_ref, bf16[128,128]{1,0:T(8,128)(2,1)} %get-tuple-element.63.ft_ref), custom_call_target="tpu_custom_call" | custom-call | tf_op jit(solution)/shard_map/pallas_call | solution.py:95
  19.3 0.5 collective-permute-start
  19.7 0.1 add_select_fusion.6
  19.8 0.1 iota_add_fusion
  19.9 0.1 fusion.44
  20.0 4.1 %fusion.20 = (f32[64,8,1,256]{3,1,0,2:T(8,128)S(1)}, f32[64,8,1,256]{3,1,0,2:T(8,128)S(1)}, f32[64,8,1,256]{3,1,0,2:T(8,128)S(1)}, f32[64,8,1,256]{3,1,0,2:T(8,128)S(1)}) fusion(s32[64]{0:T(128)S(1)} %multiply_add_fusion.1, s32[8,256]{1,0:T(8,128)S(1)} %add_select_fusion.6, s32[8,256]{1,0:T(8,128)S(1)} %iota_add_fusion), kind=kLoop, calls=%fused_computation.53 | loop fusion | flops 3670016 | bytes 2113792 | tf_op jit(solution)/shard_map/sin | solution.py:33
  24.2 2.6 %multiply_convert_fusion = (bf16[256,256]{1,0:T(8,128)(2,1)}, bf16[256,256]{1,0:T(8,128)(2,1)S(1)}) fusion(f32[256]{0:T(256)S(1)} %get-tuple-element.72, f32[256]{0:T(256)S(1)} %get-tuple-element.71), kind=kLoop, calls=%fused_computation.49 | loop fusion | flops 524288 | bytes 264192 | tf_op jit(solution)/shard_map/convert_element_type | solution.py:26
  26.8 2.1 %fusion.18 = (f32[64,1,8,256]{3,2,0,1:T(8,128)S(1)}, f32[64,1,8,256]{3,2,0,1:T(8,128)S(1)}) fusion(s32[64]{0:T(128)S(1)} %multiply_add_fusion.1, s32[8,256]{1,0:T(8,128)S(1)} %add_select_fusion.5), kind=kLoop, calls=%fused_computation.50 | loop fusion | flops 1835008 | bytes 1057024 | tf_op jit(solution)/shard_map/sin | solution.py:33
  29.0 0.7 constant_dynamic-slice_fusion
  29.6 0.1 copy.6
  29.7 0.1 copy.7
  29.8 3.1 %fusion.2.v_ref = f32[64,64,256]{2,1,0:T(8,128)} fusion(f32[64,64]{1,0:T(8,128)S(1)} %copy.7, f32[64,8,256]{2,1,0:T(8,128)S(1)} %bitcast.68, f32[64,64]{1,0:T(8,128)S(1)} %copy.6, f32[64,8,256]{2,1,0:T(8,128)S(1)} %bitcast.67), kind=kLoop, calls=%fused_computation.5 | loop fusion | flops 5242880 | bytes 5275648 | tf_op jit(solution)/shard_map/add | solution.py:40
  32.9 3.0 %add_bitcast_fusion.w_ref = f32[64,64,256]{2,1,0:T(8,128)} fusion(f32[64,8,256]{2,1,0:T(8,128)S(1)} %bitcast.64, f32[64,8,256]{2,1,0:T(8,128)S(1)} %bitcast.62, f32[64,8,256]{2,1,0:T(8,128)S(1)} %bitcast.65, f32[64,8,256]{2,1,0:T(8,128)S(1)} %bitcast.63), kind=kLoop, calls=%fused_computation.7 | loop fusion | flops 5242880 | bytes 6291456 | tf_op jit(solution)/shard_map/add | solution.py:40
  35.9 0.0 collective-permute-done.recv_ref
  35.9 4.9 %shard_map.56 = bf16[48,64,256]{2,1,0:T(8,128)(2,1)} custom-call(bf16[48,64,128]{2,1,0:T(8,128)(2,1)} %get-tuple-element.29.own_ref, bf16[48,64,128]{2,1,0:T(8,128)(2,1)} %collective-permute-done.recv_ref, f32[64,64,256]{2,1,0:T(8,128)} %fusion.2.v_ref, bf16[128,256]{1,0:T(8,128)(2,1)} %get-tuple-element.46.fo_ref, bf16[128,256]{1,0:T(8,128)(2,1)} %get-tuple-element.45.fr_ref), custom_call_target="tpu_custom_call" | custom-call | tf_op jit(solution)/shard_map/pallas_call | solution.py:125
  40.8 2.8 %reshape.740 = bf16[3,16,16384]{2,1,0:T(8,128)(2,1)S(1)} reshape(bf16[48,64,256]{2,1,0:T(8,128)(2,1)} %shard_map.56) | data formatting | bytes 3145728 | tf_op jit(solution)/shard_map/reshape | solution.py:283
  43.6 0.0 copy-done
  43.6 1.4 convolution_convert_fusion
  45.1 3.7 %copy.8 = bf16[18,8,64,256]{3,2,1,0:T(8,128)(2,1)} copy(bf16[18,8,64,256]{3,1,2,0:T(8,128)(2,1)S(1)} %bitcast.56) | data formatting | bytes 9437184
  48.7 13.8 %shard_map.57 = (bf16[3,48,64,128]{3,2,1,0:T(8,128)(2,1)}, bf16[3,48,64,128]{3,2,1,0:T(8,128)(2,1)}) custom-call(s32[1]{0:T(128)} %bitcast.me_ref, bf16[3,48,64,256]{3,2,1,0:T(8,128)(2,1)} %bitcast.55, f32[64,64,256]{2,1,0:T(8,128)} %fusion.2.v_ref, f32[64,64,256]{2,1,0:T(8,128)} %add_bitcast_fusion.w_ref, bf16[256,256]{1,0:T(8,128)(2,1)} %get-tuple-element.59.ft_ref), custom_call_target="tpu_custom_call" | custom-call | tf_op jit(solution)/shard_map/pallas_call | solution.py:155
  62.5 0.0 collective-permute-start.1
  62.5 0.7 constant_dynamic-slice_fusion.2
  63.3 4.0 %collective-permute-done.1.refs_5_.refs_7_.refs_9_ = bf16[3,48,64,128]{3,2,1,0:T(8,128)(2,1)S(1)} collective-permute-done((bf16[3,48,64,128]{3,2,1,0:T(8,128)(2,1)}, bf16[3,48,64,128]{3,2,1,0:T(8,128)(2,1)S(1)}, u32[]{:S(2)}, u32[]{:S(2)}) %collective-permute-start.1) | collective-permute-done | bytes 2359328 | tf_op jit(solution)/shard_map/ppermute | solution.py:255
  67.3 44.0 %all-gather.2.cloned.1.call-done = bf16[1,3,64,128,128]{4,3,2,1,0:T(8,128)(2,1)} async-done(((bf16[1,3,8,128,128]{4,3,2,1,0:T(8,128)(2,1)}), bf16[1,3,64,128,128]{4,3,2,1,0:T(8,128)(2,1)}) %all-gather.2.cloned.1.call-update) | async-done | bytes 6291472 | tf_op jit(solution)/shard_map/all_gather | solution.py:267
  111.3 3.8 %shard_map.58.y_ref = bf16[16,128,128]{2,1,0:T(8,128)(2,1)} custom-call(bf16[128,64]{1,0:T(8,128)(2,1)} %get-tuple-element.48.refs_0_.fo_ref, bf16[128,64]{1,0:T(8,128)(2,1)} %get-tuple-element.47.refs_1_.fr_ref, bf16[48,128,128]{2,1,0:T(8,128)(2,1)} %bitcast.58, bf16[3,64,128,128]{3,2,1,0:T(8,128)(2,1)} %bitcast.53, ...), custom_call_target="tpu_custom_call" | custom-call | tf_op jit(solution)/shard_map/pallas_call | solution.py:206
  115.1 2.6 %shard_map.59 = (bf16[16,64,128]{2,1,0:T(8,128)(2,1)}, bf16[16,64,128]{2,1,0:T(8,128)(2,1)}) custom-call(s32[1]{0:T(128)} %bitcast.me_ref, bf16[16,128,128]{2,1,0:T(8,128)(2,1)} %shard_map.58.y_ref, f32[64,128,128]{2,1,0:T(8,128)} %add_bitcast_fusion.1.w_ref, bf16[128,128]{1,0:T(8,128)(2,1)} %get-tuple-element.63.ft_ref), custom_call_target="tpu_custom_call" | custom-call | tf_op jit(solution)/shard_map/pallas_call | solution.py:95
  117.7 0.0 collective-permute-start.2
  117.7 1.7 %collective-permute-done.2.recv_ref = bf16[16,64,128]{2,1,0:T(8,128)(2,1)S(1)} collective-permute-done((bf16[16,64,128]{2,1,0:T(8,128)(2,1)}, bf16[16,64,128]{2,1,0:T(8,128)(2,1)S(1)}, u32[]{:S(2)}, u32[]{:S(2)}) %collective-permute-start.2) | collective-permute-done | bytes 262176 | tf_op jit(solution)/shard_map/ppermute | solution.py:255
  119.5 0.7 copy-done.3
  120.2 2.6 %shard_map.60 = bf16[16,64,256]{2,1,0:T(8,128)(2,1)} custom-call(bf16[16,64,128]{2,1,0:T(8,128)(2,1)} %get-tuple-element.41.own_ref, bf16[16,64,128]{2,1,0:T(8,128)(2,1)} %copy-done.3, f32[64,64,256]{2,1,0:T(8,128)} %fusion.2.v_ref, bf16[128,256]{1,0:T(8,128)(2,1)} %get-tuple-element.46.fo_ref, bf16[128,256]{1,0:T(8,128)(2,1)} %get-tuple-element.45.fr_ref), custom_call_target="tpu_custom_call" | custom-call | tf_op jit(solution)/shard_map/pallas_call | solution.py:125
  122.8 1.3 copy.9
  124.2 0.6 convolution_convert_fusion.1
  124.8 1.5 %copy.10 = bf16[6,8,64,256]{3,2,1,0:T(8,128)(2,1)} copy(bf16[6,8,64,256]{3,1,2,0:T(8,128)(2,1)S(1)} %bitcast.61) | data formatting | bytes 3145728
  126.3 5.7 %shard_map.61 = (bf16[1,48,64,128]{3,2,1,0:T(8,128)(2,1)}, bf16[1,48,64,128]{3,2,1,0:T(8,128)(2,1)}) custom-call(s32[1]{0:T(128)} %bitcast.me_ref, bf16[1,48,64,256]{3,2,1,0:T(8,128)(2,1)} %bitcast.60, f32[64,64,256]{2,1,0:T(8,128)} %fusion.2.v_ref, f32[64,64,256]{2,1,0:T(8,128)} %add_bitcast_fusion.w_ref, bf16[256,256]{1,0:T(8,128)(2,1)} %get-tuple-element.59.ft_ref), custom_call_target="tpu_custom_call" | custom-call | tf_op jit(solution)/shard_map/pallas_call | solution.py:155
  132.0 0.1 collective-permute-start.3
  132.1 7.1 %shard_map.62.prod_ref = bf16[48,128,128]{2,1,0:T(8,128)(2,1)} custom-call(bf16[128,64]{1,0:T(8,128)(2,1)} %get-tuple-element.48.refs_0_.fo_ref, bf16[128,64]{1,0:T(8,128)(2,1)} %get-tuple-element.47.refs_1_.fr_ref, bf16[48,128,128]{2,1,0:T(8,128)(2,1)} %bitcast.59, bf16[3,64,128,128]{3,2,1,0:T(8,128)(2,1)} %bitcast.54, ...), custom_call_target="tpu_custom_call" | custom-call | tf_op jit(solution)/shard_map/pallas_call | solution.py:206
  139.2 0.0 collective-permute-done.3
  139.2 0.9 broadcast_in_dim.39.s_ref
  140.1 0.0 copy-done.2
  140.1 4.4 %shard_map.63 = bf16[48,128,128]{2,1,0:T(8,128)(2,1)} custom-call(bf16[128,64]{1,0:T(8,128)(2,1)} %get-tuple-element.48.refs_0_.fo_ref, bf16[128,64]{1,0:T(8,128)(2,1)} %get-tuple-element.47.refs_1_.fr_ref, bf16[48,64,128]{2,1,0:T(8,128)(2,1)} %bitcast.74, bf16[48,64,128]{2,1,0:T(8,128)(2,1)} %bitcast.75, bf16[48,128,128]{2,1,0:T(8,128)(2,1)} %shard_map.62.prod_ref, ...), custom_call_target="tpu_custom_call" | custom-call | tf_op jit(solution)/shard_map/pallas_call | solution.py:238
  (19 shorter events, 0.1 us)
Async XLA Ops:
  6.5 37.1 %copy-start = (bf16[3,48,16]{1,2,0:T(8,128)(2,1)S(1)}, bf16[3,48,16]{1,2,0:T(8,128)(2,1)}, u32[]{:S(2)}) copy-start(bf16[3,48,16]{1,2,0:T(8,128)(2,1)} %param.7) | copy-start | bytes 13828
  6.5 104.8 %all-gather.2.cloned.1.call-start = ((), (), s32[]{:S(2)}) async-start(), calls=%async_computation | async-start | bytes 7077888 | tf_op jit(solution)/shard_map/all_gather | solution.py:267
  19.3 16.7 %collective-permute-start = (bf16[48,64,128]{2,1,0:T(8,128)(2,1)}, bf16[48,64,128]{2,1,0:T(8,128)(2,1)}, u32[]{:S(2)}, u32[]{:S(2)}) collective-permute-start(bf16[48,64,128]{2,1,0:T(8,128)(2,1)} %get-tuple-element.30), channel_id=1, source_target_pairs={{0,1},{1,0},{2,3},{3,2},{4,5},{5,4},{6,7},{7,6},{8,9},{9,8},{10,11... | collective-permute-start | bytes 2359304 | tf_op jit(solution)/shard_map/ppermute | solution.py:255
  62.5 4.7 %collective-permute-start.1 = (bf16[3,48,64,128]{3,2,1,0:T(8,128)(2,1)}, bf16[3,48,64,128]{3,2,1,0:T(8,128)(2,1)S(1)}, u32[]{:S(2)}, u32[]{:S(2)}) collective-permute-start(bf16[3,48,64,128]{3,2,1,0:T(8,128)(2,1)} %get-tuple-element.40), channel_id=1, source_target_pairs={{0,1},{1,0},{2,3},{3,2},{4,5},{5,4},{6,7},{7,6},{8,9},{9,8},{10,11... | collective-permute-start | bytes 7077896 | tf_op jit(solution)/shard_map/ppermute | solution.py:255
  67.3 44.0 %copy-start.1 = (bf16[3,48,64,128]{3,2,1,0:T(8,128)(2,1)}, bf16[3,48,64,128]{3,2,1,0:T(8,128)(2,1)S(1)}, u32[]{:S(2)}) copy-start(bf16[3,48,64,128]{3,2,1,0:T(8,128)(2,1)S(1)} %collective-permute-done.1.refs_5_.refs_7_.refs_9_) | copy-start | bytes 7077892
  117.7 6.4 %copy-start.4 = (bf16[48,16]{0,1:T(8,128)(2,1)S(1)}, bf16[48,16]{0,1:T(8,128)(2,1)}, u32[]{:S(2)}) copy-start(bf16[48,16]{0,1:T(8,128)(2,1)} %param.8) | copy-start | bytes 4612
  117.7 1.7 %collective-permute-start.2 = (bf16[16,64,128]{2,1,0:T(8,128)(2,1)}, bf16[16,64,128]{2,1,0:T(8,128)(2,1)S(1)}, u32[]{:S(2)}, u32[]{:S(2)}) collective-permute-start(bf16[16,64,128]{2,1,0:T(8,128)(2,1)} %get-tuple-element.42), channel_id=1, source_target_pairs={{0,1},{1,0},{2,3},{3,2},{4,5},{5,4},{6,7},{7,6},{8,9},{9,8},{10,11... | collective-permute-start | bytes 786440 | tf_op jit(solution)/shard_map/ppermute | solution.py:255
  119.5 0.7 copy-start.3
  132.0 7.2 %copy-start.5 = (f32[48]{0:T(128)S(1)}, f32[48]{0:T(128)}, u32[]{:S(2)}) copy-start(f32[48]{0:T(128)} %param.9) | copy-start | bytes 580
  132.0 7.2 %collective-permute-start.3 = (bf16[1,48,64,128]{3,2,1,0:T(8,128)(2,1)}, bf16[1,48,64,128]{3,2,1,0:T(8,128)(2,1)S(1)}, u32[]{:S(2)}, u32[]{:S(2)}) collective-permute-start(bf16[1,48,64,128]{3,2,1,0:T(8,128)(2,1)} %get-tuple-element.44), channel_id=1, source_target_pairs={{0,1},{1,0},{2,3},{3,2},{4,5},{5,4},{6,7},{7,6},{8,9},{9,8},{10,11... | collective-permute-start | bytes 2359304 | tf_op jit(solution)/shard_map/ppermute | solution.py:255
  139.2 0.9 copy-start.2
Sparse Core Ops, SparseCore 0:
  9.5 101.7 all-gather.1
where the time goes:
time: 152 us; the launch traced here: 151 us
  waiting for transfers between devices  50.5 us (33%)
  Pallas kernels  49.7 us (33%)
  other arithmetic  22.5 us (15%)
  between operations  13.5 us (9%)
  local copies, waits for them, and re-layouts  12.5 us (8%)
  matrix products  2.02 us (1%)
    all_gather x1, waiting for transfers between devices, body(): key = lax.all_gather(switch_key, 'limb', axis=2, tiled=True)[0]  44 us
    pallas_call x2, Pallas kernels, fwd_col(): pl.pallas_call(_fwd_col_kernel, grid=(groups, n // BLK), in_specs=[SMEM_S...  19.5 us
    pallas_call x2, Pallas kernels, product(): pl.pallas_call(lambda *refs: _product_kernel(eb0, *refs), grid=(nblocks,)...  10.9 us
    sin x5, other arithmetic, _angle(): return (jnp.cos(ang), jnp.sin(ang))  9.59 us
    add x3, other arithmetic, _twiddle(): return 1.0 + 0.5 * (cp * cq - sp * sq)  9.04 us
    pallas_call x2, Pallas kernels, inv_col(): pl.pallas_call(_inv_col_kernel, grid=(n // BLK,), in_specs=[blk, blk, pl....  7.52 us
    pallas_call x2, Pallas kernels, inv_row(): pl.pallas_call(_inv_row_kernel, grid=(n // BLK,), in_specs=[SMEM_SPEC, bl...  7.43 us
    unnamed x15, local copies, waits for them, and re-layouts  7.25 us
  transfers between devices with their start and end apart: 5, of which 3 were waited for; matrix products, arithmetic and copies ran while one was open for 21% of the time, Pallas kernels for 20%

commit v1 on v0

--- a/solution.py
+++ b/solution.py
@@ -251,6 +251,77 @@
     )(f_own, f_oth, own4, recv4, prod, scale)
 
 
+def snake_ring(n):
+    if n % 2:
+        return list(range(n))
+    outer = n // 2
+    return [2 * a for a in range(outer)] + [2 * a + 1 for a in reversed(range(outer))]
+
+
+def ring_setup(shard):
+    n = lax.axis_size("limb")
+    me_l = lax.axis_index("limb")
+    order = snake_ring(n)
+    pos = [0] * n
+    for i, l in enumerate(order):
+        pos[l] = i
+    width = shard.shape[1]
+    full = jnp.zeros((shard.shape[0], n * width) + shard.shape[2:], shard.dtype)
+    full = lax.dynamic_update_slice_in_dim(full, shard, me_l * width, axis=1)
+    return dict(
+        n=n,
+        order=jnp.array(order, I32),
+        p=jnp.array(pos, I32)[me_l],
+        cw=[(order[i], order[(i + 1) % n]) for i in range(n)],
+        ccw=[(order[i], order[(i - 1) % n]) for i in range(n)],
+        width=width,
+        full=full,
+        a=shard,
+        b=shard,
+        s=0,
+    )
+
+
+def ring_steps(st):
+    return st["n"] // 2
+
+
+def ring_step(st):
+    n, width, order, p = st["n"], st["width"], st["order"], st["p"]
+    st["s"] += 1
+    s = st["s"]
+    if 2 * s < n:
+        st["a"] = lax.ppermute(st["a"], "limb", st["cw"])
+        st["b"] = lax.ppermute(st["b"], "limb", st["ccw"])
+        st["full"] = lax.dynamic_update_slice_in_dim(
+            st["full"], st["a"], order[(p - s) % n] * width, axis=1
+        )
+        st["full"] = lax.dynamic_update_slice_in_dim(
+            st["full"], st["b"], order[(p + s) % n] * width, axis=1
+        )
+    else:
+        h = st["a"].shape[2] // 2
+        a = lax.ppermute(st["a"][:, :, :h], "limb", st["cw"])
+        b = lax.ppermute(st["b"][:, :, h:], "limb", st["ccw"])
+        src = order[(p + s) % n] * width
+        st["full"] = lax.dynamic_update_slice_in_dim(
+            st["full"], jnp.concatenate([a, b], axis=2), src, axis=1
+        )
+
+
+def ring_hold(st, x):
+    if st["s"] >= ring_steps(st):
+        return x
+    st["a"], st["b"], x = lax.optimization_barrier((st["a"], st["b"], x))
+    ring_step(st)
+    return x
+
+
+def ring_finish(st):
+    while st["s"] < ring_steps(st):
+        ring_step(st)
+    return st["full"]
+
 def swap(x):
     return lax.ppermute(x, "coef", perm=[(0, 1), (1, 0)])
 
@@ -264,7 +335,9 @@
     cols = cols_l * nc
     rows_l = rows // nc
 
-    key = lax.all_gather(switch_key, "limb", axis=2, tiled=True)[0]
+    ring = ring_setup(switch_key[0])
+    if ring_steps(ring):
+        ring_step(ring)
 
     f_rows = cosine_table(rows)
     f_cols = cosine_table(cols)
@@ -278,6 +351,7 @@
 
     ct = cipher[0]
     own1, send1 = inv_row(me_arr, ct, w_col, ft_rows, 0)
+    own1 = ring_hold(ring, own1)
     coeffs = inv_col(own1, swap(send1), v_row, fc_own, fc_oth, 0)
 
     blocks = coeffs.reshape(DIGITS, DIGIT_LIMBS, rows_l * cols)
@@ -286,10 +360,13 @@
     )
     raised = raised.astype(BF16).reshape(DIGITS, limbs, rows_l, cols)
 
+    raised = ring_hold(ring, raised)
     own2, send2 = fwd_col(
         me_arr, raised, v_row, w_row, ft_cols, lambda j, t: jnp.where(t >= j, t + 1, t)
     )
+    own2, send2 = ring_hold(ring, (own2, send2))
     recv2 = swap(send2)
+    key = ring_finish(ring)
 
     prod_special = product(ct, key, own2, recv2, fr_own, fr_oth, DIGITS, 1)
     prod_cipher = product(ct, key, own2, recv2, fr_own, fr_oth, 0, DIGITS)

time: 152 us -> 134 us (0.88)
  waiting for transfers between devices: 50.5 us -> 11.2 us
  local copies, waits for them, and re-layouts: 12.5 us -> 28.9 us
  starting transfers between devices: 0.61 us -> 9.42 us
  between operations: 13.5 us -> 9.29 us
    all_gather x1 -> x0, waiting for transfers between devices: 44 us -> none  [body(): key = lax.all_gather(switch_key, 'limb', axis=2, tiled=True)[0]]
    ppermute x0 -> x8, waiting for transfers between devices: none -> 9.45 us  [the longest x1 4.59 us: ring_step(): b = lax.ppermute(st['b'][:, :, h:], 'limb', st['ccw'])]
    ppermute x0 -> x8, starting transfers between devices: none -> 9.21 us  [the longest x3 6.42 us: ring_step(): st['a'] = lax.ppermute(st['a'], 'limb', st['cw'])]
    dynamic_update_slice x0 -> x7, local copies, waits for them, and re-layouts: none -> 7.69 us  [the longest x3 3.78 us: ring_step(): lax.dynamic_update_slice_in_dim(st['full'], st['a'], order[(p - s) % n] *...]
    ppermute x4, waiting for transfers between devices: 5.78 us -> 1.75 us  [swap(): return lax.ppermute(x, 'coef', perm=[(0, 1), (1, 0)])]
    unnamed x15 -> x23, local copies, waits for them, and re-layouts: 7.25 us -> 11.2 us
    slice x0 -> x2, local copies, waits for them, and re-layouts: none -> 2.05 us  [the longest x1 1.03 us: ring_step(): b = lax.ppermute(st['b'][:, :, h:], 'limb', st['ccw'])]
    broadcast_in_dim x0 -> x1, local copies, waits for them, and re-layouts: none -> 1.57 us  [ring_setup(): full = jnp.zeros((shard.shape[0], n * width) + shard.shape[2:], shard.dtype)]
  transfers between devices with their start and end apart: 5 -> 12, of which waited for: 3 -> 6; matrix products, arithmetic and copies ran while one was open for 21% -> 33% of each run, Pallas kernels for 20% -> 23%
where the time goes in v1:
time: 134 us; the launch traced here: 133 us
  Pallas kernels  49.5 us (37%)
  local copies, waits for them, and re-layouts  28.9 us (22%)
  other arithmetic  22.6 us (17%)
  waiting for transfers between devices  11.2 us (8%)
  starting transfers between devices  9.42 us (7%)
  between operations  9.29 us (7%)
  matrix products  2.02 us (2%)
    pallas_call x2, Pallas kernels, fwd_col(): pl.pallas_call(_fwd_col_kernel, grid=(groups, n // BLK), in_specs=[SMEM_S...  19.1 us
    unnamed x23, local copies, waits for them, and re-layouts  11.2 us
    pallas_call x2, Pallas kernels, product(): pl.pallas_call(lambda *refs: _product_kernel(eb0, *refs), grid=(nblocks,)...  10.9 us
    sin x5, other arithmetic, _angle(): return (jnp.cos(ang), jnp.sin(ang))  9.6 us
    add x3, other arithmetic, _twiddle(): return 1.0 + 0.5 * (cp * cq - sp * sq)  9.09 us
    pallas_call x2, Pallas kernels, inv_row(): pl.pallas_call(_inv_row_kernel, grid=(n // BLK,), in_specs=[SMEM_SPEC, bl...  7.6 us
    pallas_call x2, Pallas kernels, inv_col(): pl.pallas_call(_inv_col_kernel, grid=(n // BLK,), in_specs=[blk, blk, pl....  7.48 us
    ppermute x3, starting transfers between devices, ring_step(): st['a'] = lax.ppermute(st['a'], 'limb', st['cw'])  6.42 us
  transfers between devices with their start and end apart: 12, of which 6 were waited for; matrix products, arithmetic and copies ran while one was open for 33% of the time, Pallas kernels for 23%

profile of v1, /device:TPU:0, one launch (start us, length us, event | category | flops | bytes accessed | tf_op | source)
XLA Modules:
  0.0 132.9 jit_solution(14875849667695558834)
XLA Ops:
  0.0 3.0 %collective-permute-start = (bf16[3,8,128,128]{3,2,1,0:T(8,128)(2,1)}, bf16[3,8,128,128]{3,2,1,0:T(8,128)(2,1)}, u32[]{:S(2)}, u32[]{:S(2)}) collective-permute-start(bf16[3,8,128,128]{3,2,1,0:T(8,128)(2,1)} %bitcast.89), channel_id=1, source_target_pairs={{0,4},{4,8},{8,12},{12,14},{14,10},{10,6},{6,2},{2,0},{1,5},{5,9},... | collective-permute-start | bytes 2359304 | tf_op jit(solution)/shard_map/ppermute | solution.py:294
  3.2 2.1 %fusion.24 = (f32[64,16,1,128]{3,1,0,2:T(8,128)S(1)}, f32[64,16,1,128]{3,1,0,2:T(8,128)S(1)}) fusion(s32[64]{0:T(128)S(1)} %multiply_add_fusion.1, s32[16,128]{1,0:T(8,128)S(1)} %add_select_fusion.7), kind=kLoop, calls=%fused_computation.58 | loop fusion | flops 1835008 | bytes 1057024 | tf_op jit(solution)/shard_map/sin | solution.py:33
  5.3 1.1 fusion.26
  6.4 0.9 multiply_convert_fusion.2
  7.3 2.9 %add_bitcast_fusion.1.w_ref = f32[64,128,128]{2,1,0:T(8,128)} fusion(f32[64,8,128]{2,1,0:T(8,128)S(1)} %bitcast.85, f32[64,16,128]{2,1,0:T(8,128)S(1)} %bitcast.83, f32[64,8,128]{2,1,0:T(8,128)S(1)} %bitcast.86, f32[64,16,128]{2,1,0:T(8,128)S(1)} %bitcast.84), kind=kLoop, calls=%fused_computation.8 | loop fusion | flops 5242880 | bytes 5767168 | tf_op jit(solution)/shard_map/add | solution.py:40
  10.2 4.8 %shard_map.73 = (bf16[48,64,128]{2,1,0:T(8,128)(2,1)}, bf16[48,64,128]{2,1,0:T(8,128)(2,1)}) custom-call(s32[1]{0:T(128)} %bitcast.me_ref, bf16[48,128,128]{2,1,0:T(8,128)(2,1)} %bitcast.70, f32[64,128,128]{2,1,0:T(8,128)} %add_bitcast_fusion.1.w_ref, bf16[128,128]{1,0:T(8,128)(2,1)} %get-tuple-element.83.ft_ref), custom_call_target="tpu_custom_call" | custom-call | tf_op jit(solution)/shard_map/pallas_call | solution.py:95
  15.3 4.1 %fusion.20 = (f32[64,8,1,256]{3,1,0,2:T(8,128)S(1)}, f32[64,8,1,256]{3,1,0,2:T(8,128)S(1)}, f32[64,8,1,256]{3,1,0,2:T(8,128)S(1)}, f32[64,8,1,256]{3,1,0,2:T(8,128)S(1)}) fusion(s32[64]{0:T(128)S(1)} %multiply_add_fusion.1, s32[8,256]{1,0:T(8,128)S(1)} %add_select_fusion.6, s32[8,256]{1,0:T(8,128)S(1)} %iota_add_fusion), kind=kLoop, calls=%fused_computation.54 | loop fusion | flops 3670016 | bytes 2113792 | tf_op jit(solution)/shard_map/sin | solution.py:33
  19.5 2.6 %multiply_convert_fusion = (bf16[256,256]{1,0:T(8,128)(2,1)}, bf16[256,256]{1,0:T(8,128)(2,1)S(1)}) fusion(f32[256]{0:T(256)S(1)} %get-tuple-element.99, f32[256]{0:T(256)S(1)} %get-tuple-element.98), kind=kLoop, calls=%fused_computation.50 | loop fusion | flops 524288 | bytes 264192 | tf_op jit(solution)/shard_map/convert_element_type | solution.py:26
  22.3 1.8 %collective-permute-start.2 = (bf16[3,8,128,128]{3,2,1,0:T(8,128)(2,1)}, bf16[3,8,128,128]{3,2,1,0:T(8,128)(2,1)}, u32[]{:S(2)}, u32[]{:S(2)}) collective-permute-start(bf16[3,8,128,128]{3,2,1,0:T(8,128)(2,1)} %collective-permute-done), channel_id=1, source_target_pairs={{0,4},{4,8},{8,12},{12,14},{14,10},{10,6},{6,2},{2,0},{1,5},{5,9},... | collective-permute-start | bytes 2359304 | tf_op jit(solution)/shard_map/ppermute | solution.py:294
  24.4 0.7 constant_dynamic-slice_fusion
  25.2 3.1 %fusion.2.v_ref = f32[64,64,256]{2,1,0:T(8,128)} fusion(f32[64,64]{1,0:T(8,128)S(1)} %copy.9, f32[64,8,256]{2,1,0:T(8,128)S(1)} %bitcast.81, f32[64,64]{1,0:T(8,128)S(1)} %copy.8, f32[64,8,256]{2,1,0:T(8,128)S(1)} %bitcast.80), kind=kLoop, calls=%fused_computation.5 | loop fusion | flops 5242880 | bytes 5275648 | tf_op jit(solution)/shard_map/add | solution.py:40
  28.3 4.8 %shard_map.74 = bf16[48,64,256]{2,1,0:T(8,128)(2,1)} custom-call(bf16[48,64,128]{2,1,0:T(8,128)(2,1)} %get-tuple-element.42.own_ref, bf16[48,64,128]{2,1,0:T(8,128)(2,1)} %collective-permute-done.4.recv_ref, f32[64,64,256]{2,1,0:T(8,128)} %fusion.2.v_ref, bf16[128,256]{1,0:T(8,128)(2,1)} %get-tuple-element.66.fo_ref, bf16[128,256]{1,0:T(8,128)(2,1)} %get-tuple-element.65.fr_ref), custom_call_target="tpu_custom_call" | custom-call | tf_op jit(solution)/shard_map/pallas_call | solution.py:125
  33.2 2.6 %reshape.768 = bf16[3,16,16384]{2,1,0:T(8,128)(2,1)S(1)} reshape(bf16[48,64,256]{2,1,0:T(8,128)(2,1)} %shard_map.74) | data formatting | bytes 3145728 | tf_op jit(solution)/shard_map/reshape | solution.py:357
  35.8 1.4 %convolution_convert_fusion = bf16[3,16384,48]{1,2,0:T(8,128)(2,1)S(1)} fusion(bf16[3,16,16384]{2,1,0:T(8,128)(2,1)S(1)} %reshape.768, bf16[3,48,16]{1,2,0:T(8,128)(2,1)S(1)} %copy-done), kind=kOutput, calls=%fused_computation | convolution fusion | flops 77856768 | bytes 6296064 | tf_op jit(solution)/shard_map/dot_general | solution.py:358
  37.2 3.6 %copy.10 = bf16[18,8,64,256]{3,2,1,0:T(8,128)(2,1)} copy(bf16[18,8,64,256]{3,1,2,0:T(8,128)(2,1)S(1)} %bitcast.69) | data formatting | bytes 9437184
  40.7 1.9 %collective-permute-done.2 = bf16[3,8,128,128]{3,2,1,0:T(8,128)(2,1)} collective-permute-done((bf16[3,8,128,128]{3,2,1,0:T(8,128)(2,1)}, bf16[3,8,128,128]{3,2,1,0:T(8,128)(2,1)}, u32[]{:S(2)}, u32[]{:S(2)}) %collective-permute-start.2) | collective-permute-done | bytes 786464 | tf_op jit(solution)/shard_map/ppermute | solution.py:294
  42.6 1.5 %collective-permute-done.3 = bf16[3,8,128,128]{3,2,1,0:T(8,128)(2,1)} collective-permute-done((bf16[3,8,128,128]{3,2,1,0:T(8,128)(2,1)}, bf16[3,8,128,128]{3,2,1,0:T(8,128)(2,1)}, u32[]{:S(2)}, u32[]{:S(2)}) %collective-permute-start.3) | collective-permute-done | bytes 786464 | tf_op jit(solution)/shard_map/ppermute | solution.py:295
  44.1 1.6 %collective-permute-start.5 = (bf16[3,8,128,128]{3,2,1,0:T(8,128)(2,1)}, bf16[3,8,128,128]{3,2,1,0:T(8,128)(2,1)}, u32[]{:S(2)}, u32[]{:S(2)}) collective-permute-start(bf16[3,8,128,128]{3,2,1,0:T(8,128)(2,1)} %collective-permute-done.2), channel_id=1, source_target_pairs={{0,4},{4,8},{8,12},{12,14},{14,10},{10,6},{6,2},{2,0},{1,5},{5,9},... | collective-permute-start | bytes 2359304 | tf_op jit(solution)/shard_map/ppermute | solution.py:294
  46.2 2.1 %fusion.18 = (f32[64,1,8,256]{3,2,0,1:T(8,128)S(1)}, f32[64,1,8,256]{3,2,0,1:T(8,128)S(1)}) fusion(s32[64]{0:T(128)S(1)} %multiply_add_fusion.1, s32[8,256]{1,0:T(8,128)S(1)} %add_select_fusion.5), kind=kLoop, calls=%fused_computation.51 | loop fusion | flops 1835008 | bytes 1057024 | tf_op jit(solution)/shard_map/sin | solution.py:33
  48.3 3.1 %add_bitcast_fusion.w_ref = f32[64,64,256]{2,1,0:T(8,128)} fusion(f32[64,8,256]{2,1,0:T(8,128)S(1)} %bitcast.77, f32[64,8,256]{2,1,0:T(8,128)S(1)} %bitcast.75, f32[64,8,256]{2,1,0:T(8,128)S(1)} %bitcast.78, f32[64,8,256]{2,1,0:T(8,128)S(1)} %bitcast.76), kind=kLoop, calls=%fused_computation.7 | loop fusion | flops 5242880 | bytes 6291456 | tf_op jit(solution)/shard_map/add | solution.py:40
  51.4 13.4 %shard_map.75 = (bf16[3,48,64,128]{3,2,1,0:T(8,128)(2,1)}, bf16[3,48,64,128]{3,2,1,0:T(8,128)(2,1)}) custom-call(s32[1]{0:T(128)} %bitcast.me_ref, bf16[3,48,64,256]{3,2,1,0:T(8,128)(2,1)} %bitcast.68, f32[64,64,256]{2,1,0:T(8,128)} %fusion.2.v_ref, f32[64,64,256]{2,1,0:T(8,128)} %add_bitcast_fusion.w_ref, bf16[256,256]{1,0:T(8,128)(2,1)} %get-tuple-element.79.ft_ref), custom_call_target="tpu_custom_call" | custom-call | tf_op jit(solution)/shard_map/pallas_call | solution.py:155
  70.2 0.7 fusion.46
  75.2 0.7 constant_dynamic-slice_fusion.2
  75.9 1.6 %broadcast_in_dim.40 = bf16[3,64,128,128]{3,2,1,0:T(8,128)(2,1)S(1)} broadcast(bf16[]{:T(256)} %constant.193.clone.1), dimensions={} | broadcast | bytes 6291458 | tf_op jit(solution)/shard_map/broadcast_in_dim | solution.py:269
  77.6 1.3 constant_dynamic-update-slice_fusion.5
  78.9 1.3 constant_dynamic-update-slice_fusion.4
  80.2 1.3 constant_dynamic-update-slice_fusion.3
  81.4 1.0 slice.7
  83.0 1.0 slice.6
  84.0 1.6 %collective-permute-start.7 = (bf16[3,8,64,128]{3,2,1,0:T(8,128)(2,1)S(1)}, bf16[3,8,64,128]{3,2,1,0:T(8,128)(2,1)S(1)}, u32[]{:S(2)}, u32[]{:S(2)}) collective-permute-start(bf16[3,8,64,128]{3,2,1,0:T(8,128)(2,1)S(1)} %slice.6), channel_id=1, source_target_pairs={{0,4},{4,8},{8,12},{12,14},{14,10},{10,6},{6,2},{2,0},{1,5},{5,9},... | collective-permute-start | bytes 1179656 | tf_op jit(solution)/shard_map/ppermute | solution.py:304
  85.6 1.3 constant_dynamic-update-slice_fusion.2
  86.9 1.3 constant_dynamic-update-slice_fusion.1
  88.2 1.3 constant_dynamic-update-slice_fusion
  89.4 4.6 %collective-permute-done.8 = bf16[3,8,64,128]{3,2,1,0:T(8,128)(2,1)S(1)} collective-permute-done((bf16[3,8,64,128]{3,2,1,0:T(8,128)(2,1)S(1)}, bf16[3,8,64,128]{3,2,1,0:T(8,128)(2,1)S(1)}, u32[]{:S(2)}, u32[]{:S(2)}) %collective-permute-start.8) | collective-permute-done | bytes 393248 | tf_op jit(solution)/shard_map/ppermute | solution.py:305
  94.0 1.3 collective-permute-done.7
  95.4 2.6 %copy-done.2 = bf16[3,64,128,128]{3,2,1,0:T(8,128)(2,1)} copy-done((bf16[3,64,128,128]{3,2,1,0:T(8,128)(2,1)}, bf16[3,64,128,128]{3,2,1,0:T(8,128)(2,1)S(1)}, u32[]{:S(2)}) %copy-start.2) | copy-done | bytes 6291480
  98.0 1.4 %copy-done.1 = bf16[3,48,64,128]{3,2,1,0:T(8,128)(2,1)} copy-done((bf16[3,48,64,128]{3,2,1,0:T(8,128)(2,1)}, bf16[3,48,64,128]{3,2,1,0:T(8,128)(2,1)S(1)}, u32[]{:S(2)}) %copy-start.1) | copy-done | bytes 2359320
  99.5 3.8 %shard_map.76.y_ref = bf16[16,128,128]{2,1,0:T(8,128)(2,1)} custom-call(bf16[128,64]{1,0:T(8,128)(2,1)} %get-tuple-element.68.refs_0_.fo_ref, bf16[128,64]{1,0:T(8,128)(2,1)} %get-tuple-element.67.refs_1_.fr_ref, bf16[48,128,128]{2,1,0:T(8,128)(2,1)} %bitcast.71, bf16[3,64,128,128]{3,2,1,0:T(8,128)(2,1)} %copy-done.2, ...), custom_call_target="tpu_custom_call" | custom-call | tf_op jit(solution)/shard_map/pallas_call | solution.py:206
  103.3 2.8 %shard_map.77 = (bf16[16,64,128]{2,1,0:T(8,128)(2,1)}, bf16[16,64,128]{2,1,0:T(8,128)(2,1)}) custom-call(s32[1]{0:T(128)} %bitcast.me_ref, bf16[16,128,128]{2,1,0:T(8,128)(2,1)} %shard_map.76.y_ref, f32[64,128,128]{2,1,0:T(8,128)} %add_bitcast_fusion.1.w_ref, bf16[128,128]{1,0:T(8,128)(2,1)} %get-tuple-element.83.ft_ref), custom_call_target="tpu_custom_call" | custom-call | tf_op jit(solution)/shard_map/pallas_call | solution.py:95
  106.0 1.7 %collective-permute-done.10.recv_ref = bf16[16,64,128]{2,1,0:T(8,128)(2,1)S(1)} collective-permute-done((bf16[16,64,128]{2,1,0:T(8,128)(2,1)}, bf16[16,64,128]{2,1,0:T(8,128)(2,1)S(1)}, u32[]{:S(2)}, u32[]{:S(2)}) %collective-permute-start.10) | collective-permute-done | bytes 262176 | tf_op jit(solution)/shard_map/ppermute | solution.py:326
  107.8 0.7 copy-done.5
  108.5 2.6 %shard_map.78 = bf16[16,64,256]{2,1,0:T(8,128)(2,1)} custom-call(bf16[16,64,128]{2,1,0:T(8,128)(2,1)} %get-tuple-element.61.own_ref, bf16[16,64,128]{2,1,0:T(8,128)(2,1)} %copy-done.5, f32[64,64,256]{2,1,0:T(8,128)} %fusion.2.v_ref, bf16[128,256]{1,0:T(8,128)(2,1)} %get-tuple-element.66.fo_ref, bf16[128,256]{1,0:T(8,128)(2,1)} %get-tuple-element.65.fr_ref), custom_call_target="tpu_custom_call" | custom-call | tf_op jit(solution)/shard_map/pallas_call | solution.py:125
  111.1 1.3 %copy.11 = bf16[2,8,64,256]{3,1,2,0:T(8,128)(2,1)S(1)} copy(bf16[2,8,64,256]{3,2,1,0:T(8,128)(2,1)} %bitcast.82) | data formatting | bytes 1048576
  113.1 1.5 %copy.12 = bf16[6,8,64,256]{3,2,1,0:T(8,128)(2,1)} copy(bf16[6,8,64,256]{3,1,2,0:T(8,128)(2,1)S(1)} %bitcast.74) | data formatting | bytes 3145728
  114.6 5.7 %shard_map.79 = (bf16[1,48,64,128]{3,2,1,0:T(8,128)(2,1)}, bf16[1,48,64,128]{3,2,1,0:T(8,128)(2,1)}) custom-call(s32[1]{0:T(128)} %bitcast.me_ref, bf16[1,48,64,256]{3,2,1,0:T(8,128)(2,1)} %bitcast.73, f32[64,64,256]{2,1,0:T(8,128)} %fusion.2.v_ref, f32[64,64,256]{2,1,0:T(8,128)} %add_bitcast_fusion.w_ref, bf16[256,256]{1,0:T(8,128)(2,1)} %get-tuple-element.79.ft_ref), custom_call_target="tpu_custom_call" | custom-call | tf_op jit(solution)/shard_map/pallas_call | solution.py:155
  120.4 7.1 %shard_map.80.prod_ref = bf16[48,128,128]{2,1,0:T(8,128)(2,1)} custom-call(bf16[128,64]{1,0:T(8,128)(2,1)} %get-tuple-element.68.refs_0_.fo_ref, bf16[128,64]{1,0:T(8,128)(2,1)} %get-tuple-element.67.refs_1_.fr_ref, bf16[48,128,128]{2,1,0:T(8,128)(2,1)} %bitcast.72, bf16[3,64,128,128]{3,2,1,0:T(8,128)(2,1)} %copy-done.2, ...), custom_call_target="tpu_custom_call" | custom-call | tf_op jit(solution)/shard_map/pallas_call | solution.py:206
  127.5 0.9 broadcast_in_dim.43.s_ref
  128.5 4.4 %shard_map.81 = bf16[48,128,128]{2,1,0:T(8,128)(2,1)} custom-call(bf16[128,64]{1,0:T(8,128)(2,1)} %get-tuple-element.68.refs_0_.fo_ref, bf16[128,64]{1,0:T(8,128)(2,1)} %get-tuple-element.67.refs_1_.fr_ref, bf16[48,64,128]{2,1,0:T(8,128)(2,1)} %bitcast.87, bf16[48,64,128]{2,1,0:T(8,128)(2,1)} %bitcast.88, bf16[48,128,128]{2,1,0:T(8,128)(2,1)} %shard_map.80.prod_ref, ...), custom_call_target="tpu_custom_call" | custom-call | tf_op jit(solution)/shard_map/pallas_call | solution.py:238
  (53 shorter events, 3.7 us)
Async XLA Ops:
  0.0 35.7 %copy-start = (bf16[3,48,16]{1,2,0:T(8,128)(2,1)S(1)}, bf16[3,48,16]{1,2,0:T(8,128)(2,1)}, u32[]{:S(2)}) copy-start(bf16[3,48,16]{1,2,0:T(8,128)(2,1)} %param.9) | copy-start | bytes 13828
  0.0 22.1 %collective-permute-start = (bf16[3,8,128,128]{3,2,1,0:T(8,128)(2,1)}, bf16[3,8,128,128]{3,2,1,0:T(8,128)(2,1)}, u32[]{:S(2)}, u32[]{:S(2)}) collective-permute-start(bf16[3,8,128,128]{3,2,1,0:T(8,128)(2,1)} %bitcast.89), channel_id=1, source_target_pairs={{0,4},{4,8},{8,12},{12,14},{14,10},{10,6},{6,2},{2,0},{1,5},{5,9},... | collective-permute-start | bytes 2359304 | tf_op jit(solution)/shard_map/ppermute | solution.py:294
  3.0 19.3 %collective-permute-start.1 = (bf16[3,8,128,128]{3,2,1,0:T(8,128)(2,1)}, bf16[3,8,128,128]{3,2,1,0:T(8,128)(2,1)}, u32[]{:S(2)}, u32[]{:S(2)}) collective-permute-start(bf16[3,8,128,128]{3,2,1,0:T(8,128)(2,1)} %bitcast.90), channel_id=1, source_target_pairs={{0,2},{4,0},{8,4},{12,8},{14,12},{10,14},{6,10},{2,6},{1,3},{5,1},... | collective-permute-start | bytes 2359304 | tf_op jit(solution)/shard_map/ppermute | solution.py:295
  15.1 13.3 %collective-permute-start.4 = (bf16[48,64,128]{2,1,0:T(8,128)(2,1)}, bf16[48,64,128]{2,1,0:T(8,128)(2,1)}, u32[]{:S(2)}, u32[]{:S(2)}) collective-permute-start(bf16[48,64,128]{2,1,0:T(8,128)(2,1)} %get-tuple-element.43), channel_id=1, source_target_pairs={{0,1},{1,0},{2,3},{3,2},{4,5},{5,4},{6,7},{7,6},{8,9},{9,8},{10,11... | collective-permute-start | bytes 2359304 | tf_op jit(solution)/shard_map/ppermute | solution.py:326
  22.3 20.3 %collective-permute-start.2 = (bf16[3,8,128,128]{3,2,1,0:T(8,128)(2,1)}, bf16[3,8,128,128]{3,2,1,0:T(8,128)(2,1)}, u32[]{:S(2)}, u32[]{:S(2)}) collective-permute-start(bf16[3,8,128,128]{3,2,1,0:T(8,128)(2,1)} %collective-permute-done), channel_id=1, source_target_pairs={{0,4},{4,8},{8,12},{12,14},{14,10},{10,6},{6,2},{2,0},{1,5},{5,9},... | collective-permute-start | bytes 2359304 | tf_op jit(solution)/shard_map/ppermute | solution.py:294
  24.2 20.0 %collective-permute-start.3 = (bf16[3,8,128,128]{3,2,1,0:T(8,128)(2,1)}, bf16[3,8,128,128]{3,2,1,0:T(8,128)(2,1)}, u32[]{:S(2)}, u32[]{:S(2)}) collective-permute-start(bf16[3,8,128,128]{3,2,1,0:T(8,128)(2,1)} %collective-permute-done.1), channel_id=1, source_target_pairs={{0,2},{4,0},{8,4},{12,8},{14,12},{10,14},{6,10},{2,6},{1,3},{5,1},... | collective-permute-start | bytes 2359304 | tf_op jit(solution)/shard_map/ppermute | solution.py:295
  44.1 20.7 %collective-permute-start.5 = (bf16[3,8,128,128]{3,2,1,0:T(8,128)(2,1)}, bf16[3,8,128,128]{3,2,1,0:T(8,128)(2,1)}, u32[]{:S(2)}, u32[]{:S(2)}) collective-permute-start(bf16[3,8,128,128]{3,2,1,0:T(8,128)(2,1)} %collective-permute-done.2), channel_id=1, source_target_pairs={{0,4},{4,8},{8,12},{12,14},{14,10},{10,6},{6,2},{2,0},{1,5},{5,9},... | collective-permute-start | bytes 2359304 | tf_op jit(solution)/shard_map/ppermute | solution.py:294
  45.7 19.1 %collective-permute-start.6 = (bf16[3,8,128,128]{3,2,1,0:T(8,128)(2,1)}, bf16[3,8,128,128]{3,2,1,0:T(8,128)(2,1)}, u32[]{:S(2)}, u32[]{:S(2)}) collective-permute-start(bf16[3,8,128,128]{3,2,1,0:T(8,128)(2,1)} %collective-permute-done.3), channel_id=1, source_target_pairs={{0,2},{4,0},{8,4},{12,8},{14,12},{10,14},{6,10},{2,6},{1,3},{5,1},... | collective-permute-start | bytes 2359304 | tf_op jit(solution)/shard_map/ppermute | solution.py:295
  51.4 13.5 %copy-start.9 = (s32[8]{0:T(128)S(1)}, s32[8]{0:T(128)}, u32[]{:S(2)}) copy-start(s32[8]{0:T(128)} %constant.214.clone) | copy-start | bytes 100
  51.4 18.8 %copy-start.6 = (s32[8]{0:T(128)S(1)}, s32[8]{0:T(128)}, u32[]{:S(2)}) copy-start(s32[8]{0:T(128)} %constant.213.clone) | copy-start | bytes 100
  64.8 12.7 %copy-start.4 = (bf16[1,3,8,128,128]{4,3,2,1,0:T(8,128)(2,1)S(1)}, bf16[1,3,8,128,128]{4,3,2,1,0:T(8,128)(2,1)}, u32[]{:S(2)}) copy-start(bf16[1,3,8,128,128]{4,3,2,1,0:T(8,128)(2,1)} %param.8) | copy-start | bytes 2359300
  64.8 30.6 %collective-permute-start.9 = (bf16[3,48,64,128]{3,2,1,0:T(8,128)(2,1)}, bf16[3,48,64,128]{3,2,1,0:T(8,128)(2,1)S(1)}, u32[]{:S(2)}, u32[]{:S(2)}) collective-permute-start(bf16[3,48,64,128]{3,2,1,0:T(8,128)(2,1)} %get-tuple-element.60), channel_id=1, source_target_pairs={{0,1},{1,0},{2,3},{3,2},{4,5},{5,4},{6,7},{7,6},{8,9},{9,8},{10,11... | collective-permute-start | bytes 7077896 | tf_op jit(solution)/shard_map/ppermute | solution.py:326
  82.5 11.5 %collective-permute-start.8 = (bf16[3,8,64,128]{3,2,1,0:T(8,128)(2,1)S(1)}, bf16[3,8,64,128]{3,2,1,0:T(8,128)(2,1)S(1)}, u32[]{:S(2)}, u32[]{:S(2)}) collective-permute-start(bf16[3,8,64,128]{3,2,1,0:T(8,128)(2,1)S(1)} %slice.7), channel_id=1, source_target_pairs={{0,2},{4,0},{8,4},{12,8},{14,12},{10,14},{6,10},{2,6},{1,3},{5,1},... | collective-permute-start | bytes 1179656 | tf_op jit(solution)/shard_map/ppermute | solution.py:305
  84.0 11.3 %collective-permute-start.7 = (bf16[3,8,64,128]{3,2,1,0:T(8,128)(2,1)S(1)}, bf16[3,8,64,128]{3,2,1,0:T(8,128)(2,1)S(1)}, u32[]{:S(2)}, u32[]{:S(2)}) collective-permute-start(bf16[3,8,64,128]{3,2,1,0:T(8,128)(2,1)S(1)} %slice.6), channel_id=1, source_target_pairs={{0,4},{4,8},{8,12},{12,14},{14,10},{10,6},{6,2},{2,0},{1,5},{5,9},... | collective-permute-start | bytes 1179656 | tf_op jit(solution)/shard_map/ppermute | solution.py:304
  95.4 2.6 %copy-start.2 = (bf16[3,64,128,128]{3,2,1,0:T(8,128)(2,1)}, bf16[3,64,128,128]{3,2,1,0:T(8,128)(2,1)S(1)}, u32[]{:S(2)}) copy-start(bf16[3,64,128,128]{3,2,1,0:T(8,128)(2,1)S(1)} %maximum_dynamic-update-slice_fusion.refs_3_) | copy-start | bytes 18874372
  98.0 1.4 %copy-start.1 = (bf16[3,48,64,128]{3,2,1,0:T(8,128)(2,1)}, bf16[3,48,64,128]{3,2,1,0:T(8,128)(2,1)S(1)}, u32[]{:S(2)}) copy-start(bf16[3,48,64,128]{3,2,1,0:T(8,128)(2,1)S(1)} %collective-permute-done.9.refs_5_.refs_7_.refs_9_) | copy-start | bytes 7077892
  106.0 6.4 %copy-start.7 = (bf16[48,16]{0,1:T(8,128)(2,1)S(1)}, bf16[48,16]{0,1:T(8,128)(2,1)}, u32[]{:S(2)}) copy-start(bf16[48,16]{0,1:T(8,128)(2,1)} %param.10) | copy-start | bytes 4612
  106.0 1.7 %collective-permute-start.10 = (bf16[16,64,128]{2,1,0:T(8,128)(2,1)}, bf16[16,64,128]{2,1,0:T(8,128)(2,1)S(1)}, u32[]{:S(2)}, u32[]{:S(2)}) collective-permute-start(bf16[16,64,128]{2,1,0:T(8,128)(2,1)} %get-tuple-element.62), channel_id=1, source_target_pairs={{0,1},{1,0},{2,3},{3,2},{4,5},{5,4},{6,7},{7,6},{8,9},{9,8},{10,11... | collective-permute-start | bytes 786440 | tf_op jit(solution)/shard_map/ppermute | solution.py:326
  107.8 0.7 copy-start.5
  120.3 7.3 %copy-start.8 = (f32[48]{0:T(128)S(1)}, f32[48]{0:T(128)}, u32[]{:S(2)}) copy-start(f32[48]{0:T(128)} %param.11) | copy-start | bytes 580
  120.3 7.2 %collective-permute-start.11 = (bf16[1,48,64,128]{3,2,1,0:T(8,128)(2,1)}, bf16[1,48,64,128]{3,2,1,0:T(8,128)(2,1)S(1)}, u32[]{:S(2)}, u32[]{:S(2)}) collective-permute-start(bf16[1,48,64,128]{3,2,1,0:T(8,128)(2,1)} %get-tuple-element.64), channel_id=1, source_target_pairs={{0,1},{1,0},{2,3},{3,2},{4,5},{5,4},{6,7},{7,6},{8,9},{9,8},{10,11... | collective-permute-start | bytes 2359304 | tf_op jit(solution)/shard_map/ppermute | solution.py:326
  127.5 1.0 copy-start.3

commit v2 on v1

--- a/solution.py
+++ b/solution.py
@@ -1,6 +1,8 @@
 import math
 
 import jax
+import ml_dtypes
+import numpy as np
 import jax.numpy as jnp
 from jax import lax
 from jax.experimental import pallas as pl
@@ -20,11 +22,11 @@
 
 
 def cosine_table(size):
-    freq = jnp.arange(size, dtype=jnp.float32)[:, None]
-    place = jnp.arange(size, dtype=jnp.float32)[None, :]
-    norm = jnp.where(freq == 0, math.sqrt(1.0 / size), math.sqrt(2.0 / size))
-    return (norm * jnp.cos(math.pi * (2.0 * place + 1.0) * freq / (2.0 * size))).astype(
-        jnp.bfloat16
+    freq = np.arange(size, dtype=np.float64)[:, None]
+    place = np.arange(size, dtype=np.float64)[None, :]
+    norm = np.where(freq == 0, math.sqrt(1.0 / size), math.sqrt(2.0 / size))
+    return (norm * np.cos(math.pi * (2.0 * place + 1.0) * freq / (2.0 * size))).astype(
+        ml_dtypes.bfloat16
     )
 
 
@@ -33,30 +35,34 @@
     return jnp.cos(ang), jnp.sin(ang)
 
 
+def _limb_angle(c):
+    shape = (-1,) + (1,) * c.ndim
+    hi = jnp.arange(EXTENDED // 8, dtype=I32).reshape(shape)
+    lo = (2 * jnp.arange(8, dtype=I32) + 1).reshape(shape)
+    ch, sh = _angle((16 * hi * c[None]) % CYCLE)
+    cl, sl = _angle((lo * c[None]) % CYCLE)
+    cos = ch[:, None] * cl[None] - sh[:, None] * sl[None]
+    sin = sh[:, None] * cl[None] + ch[:, None] * sl[None]
+    return cos.reshape((EXTENDED,) + c.shape), sin.reshape((EXTENDED,) + c.shape)
+
+
 def _twiddle(p, q):
-    cp, sp = _angle(p)
-    cq, sq = _angle(q)
+    cp, sp = _limb_angle(p % CYCLE)
+    cq, sq = _limb_angle(q % CYCLE)
     cp, sp, cq, sq = lax.optimization_barrier((cp, sp, cq, sq))
     return 1.0 + 0.5 * (cp * cq - sp * sq)
 
 
 def twiddle_tables(me, rows, cols, nc):
     rows_l, cols_l = rows // nc, cols // nc
-    m = (2 * jnp.arange(EXTENDED, dtype=I32) + 1)[:, None, None, None]
-    fine = jnp.arange(8, dtype=I32)[None, None, :, None]
-    coarse = (8 * jnp.arange(rows // 8, dtype=I32))[None, :, None, None]
-    bcol = (me * cols_l + jnp.arange(cols_l, dtype=I32))[None, None, None, :]
-    w_col = _twiddle(
-        (coarse * bcol) % CYCLE * m % CYCLE, (fine * bcol) % CYCLE * m % CYCLE
-    ).reshape(EXTENDED, rows, cols_l)
-    coarse = (me * rows_l + 8 * jnp.arange(rows_l // 8, dtype=I32))[None, :, None, None]
-    ball = jnp.arange(cols, dtype=I32)[None, None, None, :]
-    w_row = _twiddle(
-        (coarse * ball) % CYCLE * m % CYCLE, (fine * ball) % CYCLE * m % CYCLE
-    ).reshape(EXTENDED, rows_l, cols)
-    v_row = _twiddle(
-        (coarse * cols + ball) * m % CYCLE, (fine * cols) * m % CYCLE
-    ).reshape(EXTENDED, rows_l, cols)
+    fine = jnp.arange(8, dtype=I32)[None, :, None]
+    coarse = (8 * jnp.arange(rows // 8, dtype=I32))[:, None, None]
+    bcol = (me * cols_l + jnp.arange(cols_l, dtype=I32))[None, None, :]
+    w_col = _twiddle(coarse * bcol, fine * bcol).reshape(EXTENDED, rows, cols_l)
+    coarse = (me * rows_l + 8 * jnp.arange(rows_l // 8, dtype=I32))[:, None, None]
+    ball = jnp.arange(cols, dtype=I32)[None, None, :]
+    w_row = _twiddle(coarse * ball, fine * ball).reshape(EXTENDED, rows_l, cols)
+    v_row = _twiddle(coarse * cols + ball, fine * cols).reshape(EXTENDED, rows_l, cols)
     return w_col, w_row, v_row
 
 
@@ -354,11 +360,10 @@
     own1 = ring_hold(ring, own1)
     coeffs = inv_col(own1, swap(send1), v_row, fc_own, fc_oth, 0)
 
-    blocks = coeffs.reshape(DIGITS, DIGIT_LIMBS, rows_l * cols)
+    blocks = coeffs.reshape(DIGITS, DIGIT_LIMBS, rows_l, cols)
     raised = lax.dot_general(
         raise_table, blocks, (((2,), (1,)), ((0,), (0,))), preferred_element_type=F32
-    )
-    raised = raised.astype(BF16).reshape(DIGITS, limbs, rows_l, cols)
+    ).astype(BF16)
 
     raised = ring_hold(ring, raised)
     own2, send2 = fwd_col(
@@ -373,10 +378,10 @@
 
     own3, send3 = inv_row(me_arr, prod_special, w_col, ft_rows, limbs)
     special = inv_col(own3, swap(send3), v_row, fc_own, fc_oth, limbs)
-    lowered = jnp.dot(
-        lower_table, special.reshape(DIGIT_LIMBS, rows_l * cols), preferred_element_type=F32
+    lowered = lax.dot_general(
+        lower_table, special, (((1,), (0,)), ((), ())), preferred_element_type=F32
     )
-    lowered = lowered.astype(BF16).reshape(1, limbs, rows_l, cols)
+    lowered = lowered.astype(BF16)[None]
     own4, send4 = fwd_col(me_arr, lowered, v_row, w_row, ft_cols, lambda j, t: t)
     scale = jnp.broadcast_to(special_inverse[:, None, None], (limbs, 1, cols_l))
     result = final(own4[0], swap(send4)[0], prod_cipher, scale, fr_own, fr_oth)

time: 134 us -> 128 us (0.955)
  other arithmetic: 22.6 us -> 13.4 us
  waiting for transfers between devices: 11.2 us -> 16 us
  local copies, waits for them, and re-layouts: 28.9 us -> 24.5 us
  matrix products: 2.02 us -> 4.53 us
    sin x5 -> x0, other arithmetic: 9.6 us -> none  [_angle(): return (jnp.cos(ang), jnp.sin(ang))]
    dot_general x0 -> x2, local copies, waits for them, and re-layouts: none -> 5.57 us  [the longest x1 3.87 us: body(): lax.dot_general(raise_table, blocks, (((2,), (1,)), ((0,), (0,))), prefer...]
    unnamed x23 -> x32, local copies, waits for them, and re-layouts: 11.2 us -> 5.77 us
    convert_element_type x2 -> x0, other arithmetic: 3.52 us -> none  [cosine_table(): (norm * jnp.cos(math.pi * (2.0 * place + 1.0) * freq / (2.0 * size))).ast...]
    cos x0 -> x4, other arithmetic: none -> 3.32 us  [_angle(): return (jnp.cos(ang), jnp.sin(ang))]
    reshape x1 -> x0, local copies, waits for them, and re-layouts: 2.58 us -> none  [body(): blocks = coeffs.reshape(DIGITS, DIGIT_LIMBS, rows_l * cols)]
    ppermute x3, waiting for transfers between devices: 1.88 us -> 4.3 us  [ring_step(): st['a'] = lax.ppermute(st['a'], 'limb', st['cw'])]
    dynamic_update_slice x3, local copies, waits for them, and re-layouts: 3.78 us -> 1.48 us  [ring_step(): lax.dynamic_update_slice_in_dim(st['full'], st['a'], order[(p - s) % n] *...]
  transfers between devices with their start and end apart: 12 -> 12, of which waited for: 6 -> 6; matrix products, arithmetic and copies ran while one was open for 33% -> 26% of each run, Pallas kernels for 23% -> 24%
where the time goes in v2:
time: 128 us; the launch traced here: 127 us
  Pallas kernels  49.4 us (39%)
  local copies, waits for them, and re-layouts  24.5 us (19%)
  waiting for transfers between devices  16 us (12%)
  other arithmetic  13.4 us (10%)
  starting transfers between devices  9.39 us (7%)
  between operations  9.29 us (7%)
  matrix products  4.53 us (4%)
    pallas_call x2, Pallas kernels, fwd_col(): pl.pallas_call(_fwd_col_kernel, grid=(groups, n // BLK), in_specs=[SMEM_S...  19.1 us
    pallas_call x2, Pallas kernels, product(): pl.pallas_call(lambda *refs: _product_kernel(eb0, *refs), grid=(nblocks,)...  10.9 us
    add x3, other arithmetic, _twiddle(): return 1.0 + 0.5 * (cp * cq - sp * sq)  9.03 us
    pallas_call x2, Pallas kernels, inv_row(): pl.pallas_call(_inv_row_kernel, grid=(n // BLK,), in_specs=[SMEM_SPEC, bl...  7.51 us
    pallas_call x2, Pallas kernels, inv_col(): pl.pallas_call(_inv_col_kernel, grid=(n // BLK,), in_specs=[blk, blk, pl....  7.47 us
    ppermute x1, waiting for transfers between devices, ring_step(): b = lax.ppermute(st['b'][:, :, h:], 'limb', st['ccw'])  6.74 us
    ppermute x3, starting transfers between devices, ring_step(): st['a'] = lax.ppermute(st['a'], 'limb', st['cw'])  6.18 us
    unnamed x32, local copies, waits for them, and re-layouts  5.77 us
  transfers between devices with their start and end apart: 12, of which 6 were waited for; matrix products, arithmetic and copies ran while one was open for 26% of the time, Pallas kernels for 24%

profile of v2, /device:TPU:0, one launch (start us, length us, event | category | flops | bytes accessed | tf_op | source)
XLA Modules:
  0.0 126.5 jit_solution(14482588627171017997)
XLA Ops:
  0.0 3.0 %collective-permute-start = (bf16[3,8,128,128]{3,2,1,0:T(8,128)(2,1)}, bf16[3,8,128,128]{3,2,1,0:T(8,128)(2,1)S(1)}, u32[]{:S(2)}, u32[]{:S(2)}) collective-permute-start(bf16[3,8,128,128]{3,2,1,0:T(8,128)(2,1)} %bitcast.102), channel_id=1, source_target_pairs={{0,4},{4,8},{8,12},{12,14},{14,10},{10,6},{6,2},{2,0},{1,5},{5,9},... | collective-permute-start | bytes 2359304 | tf_op jit(solution)/shard_map/ppermute | solution.py:300
  3.2 0.6 fusion.54
  3.8 0.3 fusion.58
  4.3 2.9 %add_bitcast_fusion.1.w_ref = f32[64,128,128]{2,1,0:T(8,128)} fusion(f32[64,8,128]{2,1,0:T(8,128)S(1)} %bitcast.98, f32[64,16,128]{2,1,0:T(8,128)S(1)} %bitcast.96, f32[64,8,128]{2,1,0:T(8,128)S(1)} %bitcast.99, f32[64,16,128]{2,1,0:T(8,128)S(1)} %bitcast.97), kind=kLoop, calls=%fused_computation.8 | loop fusion | flops 5242880 | bytes 5767168 | tf_op jit(solution)/shard_map/add | solution.py:53
  7.2 4.9 %shard_map.109 = (bf16[48,64,128]{2,1,0:T(8,128)(2,1)}, bf16[48,64,128]{2,1,0:T(8,128)(2,1)}) custom-call(s32[1]{0:T(128)} %bitcast.me_ref, bf16[48,128,128]{2,1,0:T(8,128)(2,1)} %bitcast.85, f32[64,128,128]{2,1,0:T(8,128)} %add_bitcast_fusion.1.w_ref, bf16[128,128]{1,0:T(8,128)(2,1)} %constant.247.clone.ft_ref), custom_call_target="tpu_custom_call" | custom-call | tf_op jit(solution)/shard_map/pallas_call | solution.py:101
  12.5 2.3 %fusion.50 = (f32[8,8,256]{2,1,0:T(8,128)S(1)}, f32[8,8,256]{2,1,0:T(8,128)S(1)}, f32[8,8,256]{2,1,0:T(8,128)S(1)}, f32[8,8,256]{2,1,0:T(8,128)S(1)}, f32[8,8,25...) fusion(s32[8,256]{1,0:T(8,128)S(1)} %add_select_fusion.12, ...), kind=kLoop, calls=%fused_computation.119 | loop fusion | flops 1376256 | bytes 811072 | tf_op jit(solution)/shard_map/cos | solution.py:35
  14.9 0.7 add.605
  15.7 0.7 broadcast_bitcast_fusion
  16.4 4.3 %collective-permute-done = bf16[3,8,128,128]{3,2,1,0:T(8,128)(2,1)S(1)} collective-permute-done((bf16[3,8,128,128]{3,2,1,0:T(8,128)(2,1)}, bf16[3,8,128,128]{3,2,1,0:T(8,128)(2,1)S(1)}, u32[]{:S(2)}, u32[]{:S(2)}) %collective-permute-start) | collective-permute-done | bytes 786464 | tf_op jit(solution)/shard_map/ppermute | solution.py:300
  20.7 1.6 %collective-permute-done.1 = bf16[3,8,128,128]{3,2,1,0:T(8,128)(2,1)} collective-permute-done((bf16[3,8,128,128]{3,2,1,0:T(8,128)(2,1)}, bf16[3,8,128,128]{3,2,1,0:T(8,128)(2,1)}, u32[]{:S(2)}, u32[]{:S(2)}) %collective-permute-start.1) | collective-permute-done | bytes 786464 | tf_op jit(solution)/shard_map/ppermute | solution.py:301
  22.3 1.6 %collective-permute-start.2 = (bf16[3,8,128,128]{3,2,1,0:T(8,128)(2,1)S(1)}, bf16[3,8,128,128]{3,2,1,0:T(8,128)(2,1)}, u32[]{:S(2)}, u32[]{:S(2)}) collective-permute-start(bf16[3,8,128,128]{3,2,1,0:T(8,128)(2,1)S(1)} %collective-permute-done), channel_id=1, source_target_pairs={{0,4},{4,8},{8,12},{12,14},{14,10},{10,6},{6,2},{2,0},{1,5},{5,9},... | collective-permute-start | bytes 2359304 | tf_op jit(solution)/shard_map/ppermute | solution.py:300
  23.9 0.4 collective-permute-start.3
  24.4 0.7 constant_dynamic-slice_fusion
  25.2 3.1 %fusion.3.v_ref = f32[64,64,256]{2,1,0:T(8,128)} fusion(f32[64,64]{1,0:T(8,128)S(1)} %copy.17, f32[64,8,256]{2,1,0:T(8,128)S(1)} %bitcast.94, f32[64,64]{1,0:T(8,128)S(1)} %copy.16, f32[64,8,256]{2,1,0:T(8,128)S(1)} %bitcast.95), kind=kLoop, calls=%fused_computation.5 | loop fusion | flops 5242880 | bytes 5275648 | tf_op jit(solution)/shard_map/add | solution.py:53
  28.3 0.9 copy-done.3
  29.1 4.8 %shard_map.110 = bf16[48,64,256]{2,1,0:T(8,128)(2,1)} custom-call(bf16[48,64,128]{2,1,0:T(8,128)(2,1)} %get-tuple-element.42.own_ref, bf16[48,64,128]{2,1,0:T(8,128)(2,1)} %copy-done.3, f32[64,64,256]{2,1,0:T(8,128)} %fusion.3.v_ref, bf16[128,256]{1,0:T(8,128)(2,1)} %get-tuple-element.74.fo_ref, bf16[128,256]{1,0:T(8,128)(2,1)} %get-tuple-element.73.fr_ref), custom_call_target="tpu_custom_call" | custom-call | tf_op jit(solution)/shard_map/pallas_call | solution.py:131
  34.0 2.9 %fusion.5 = bf16[3,64,256,48]{2,3,1,0:T(8,128)(2,1)S(1)} fusion(bf16[3,16,64,256]{3,2,1,0:T(8,128)(2,1)} %bitcast.88, bf16[3,48,16]{1,2,0:T(8,128)(2,1)S(1)} %copy-done), kind=kOutput, calls=%fused_computation.11 | convolution fusion | flops 75497472 | bytes 6296064 | tf_op jit(solution)/shard_map/dot_general | solution.py:364
  36.9 3.9 %copy.33 = bf16[3,64,256,48]{2,1,3,0:T(8,128)(2,1)} copy(bf16[3,64,256,48]{2,3,1,0:T(8,128)(2,1)S(1)} %fusion.5) | data formatting | bytes 9437184 | tf_op jit(solution)/shard_map/dot_general | solution.py:364
  40.7 1.3 %collective-permute-done.3 = bf16[3,8,128,128]{3,2,1,0:T(8,128)(2,1)} collective-permute-done((bf16[3,8,128,128]{3,2,1,0:T(8,128)(2,1)}, bf16[3,8,128,128]{3,2,1,0:T(8,128)(2,1)}, u32[]{:S(2)}, u32[]{:S(2)}) %collective-permute-start.3) | collective-permute-done | bytes 786464 | tf_op jit(solution)/shard_map/ppermute | solution.py:301
  42.0 1.6 %collective-permute-start.5 = (bf16[3,8,128,128]{3,2,1,0:T(8,128)(2,1)}, bf16[3,8,128,128]{3,2,1,0:T(8,128)(2,1)S(1)}, u32[]{:S(2)}, u32[]{:S(2)}) collective-permute-start(bf16[3,8,128,128]{3,2,1,0:T(8,128)(2,1)} %collective-permute-done.2), channel_id=1, source_target_pairs={{0,4},{4,8},{8,12},{12,14},{14,10},{10,6},{6,2},{2,0},{1,5},{5,9},... | collective-permute-start | bytes 2359304 | tf_op jit(solution)/shard_map/ppermute | solution.py:300
  43.6 0.5 collective-permute-start.6
  44.4 3.0 %add_bitcast_fusion.w_ref = f32[64,64,256]{2,1,0:T(8,128)} fusion(f32[64,8,256]{2,1,0:T(8,128)S(1)} %bitcast.92, f32[64,8,256]{2,1,0:T(8,128)S(1)} %bitcast.90, f32[64,8,256]{2,1,0:T(8,128)S(1)} %bitcast.93, f32[64,8,256]{2,1,0:T(8,128)S(1)} %bitcast.91), kind=kLoop, calls=%fused_computation.7 | loop fusion | flops 5242880 | bytes 6291456 | tf_op jit(solution)/shard_map/add | solution.py:53
  47.4 13.4 %shard_map.111 = (bf16[3,48,64,128]{3,2,1,0:T(8,128)(2,1)}, bf16[3,48,64,128]{3,2,1,0:T(8,128)(2,1)}) custom-call(s32[1]{0:T(128)} %bitcast.me_ref, bf16[3,48,64,256]{3,2,1,0:T(8,128)(2,1)} %bitcast.84, f32[64,64,256]{2,1,0:T(8,128)} %fusion.3.v_ref, f32[64,64,256]{2,1,0:T(8,128)} %add_bitcast_fusion.w_ref, bf16[256,256]{1,0:T(8,128)(2,1)} %constant.248.clone.ft_ref), custom_call_target="tpu_custom_call" | custom-call | tf_op jit(solution)/shard_map/pallas_call | solution.py:161
  61.0 0.6 dynamic_slice.38
  66.2 0.7 fusion.89
  71.2 0.7 constant_dynamic-slice_fusion.2
  71.9 1.6 %broadcast_in_dim.8 = bf16[3,64,128,128]{3,2,1,0:T(8,128)(2,1)S(1)} broadcast(bf16[]{:T(256)} %constant.223.clone.1), dimensions={} | broadcast | bytes 6291458 | tf_op jit(solution)/shard_map/broadcast_in_dim | solution.py:275
  73.8 1.3 constant_dynamic-update-slice_fusion.4
  75.0 1.3 constant_dynamic-update-slice_fusion.3
  76.3 1.0 slice.7
  77.3 0.5 collective-permute-start.8
  77.9 1.6 %collective-permute-start.7 = (bf16[3,8,64,128]{3,2,1,0:T(8,128)(2,1)S(1)}, bf16[3,8,64,128]{3,2,1,0:T(8,128)(2,1)S(1)}, u32[]{:S(2)}, u32[]{:S(2)}) collective-permute-start(bf16[3,8,64,128]{3,2,1,0:T(8,128)(2,1)S(1)} %slice.6), channel_id=1, source_target_pairs={{0,4},{4,8},{8,12},{12,14},{14,10},{10,6},{6,2},{2,0},{1,5},{5,9},... | collective-permute-start | bytes 1179656 | tf_op jit(solution)/shard_map/ppermute | solution.py:310
  79.5 1.3 constant_dynamic-update-slice_fusion.2
  80.9 1.3 constant_dynamic-update-slice_fusion
  82.2 6.7 %collective-permute-done.8 = bf16[3,8,64,128]{3,2,1,0:T(8,128)(2,1)S(1)} collective-permute-done((bf16[3,8,64,128]{3,2,1,0:T(8,128)(2,1)S(1)}, bf16[3,8,64,128]{3,2,1,0:T(8,128)(2,1)S(1)}, u32[]{:S(2)}, u32[]{:S(2)}) %collective-permute-start.8) | collective-permute-done | bytes 393248 | tf_op jit(solution)/shard_map/ppermute | solution.py:311
  89.3 2.7 %copy-done.2 = bf16[3,64,128,128]{3,2,1,0:T(8,128)(2,1)} copy-done((bf16[3,64,128,128]{3,2,1,0:T(8,128)(2,1)}, bf16[3,64,128,128]{3,2,1,0:T(8,128)(2,1)S(1)}, u32[]{:S(2)}) %copy-start.2) | copy-done | bytes 6291480
  92.0 1.5 %copy-done.1 = bf16[3,48,64,128]{3,2,1,0:T(8,128)(2,1)} copy-done((bf16[3,48,64,128]{3,2,1,0:T(8,128)(2,1)}, bf16[3,48,64,128]{3,2,1,0:T(8,128)(2,1)S(1)}, u32[]{:S(2)}) %copy-start.1) | copy-done | bytes 2359320
  93.4 3.8 %shard_map.112.y_ref = bf16[16,128,128]{2,1,0:T(8,128)(2,1)} custom-call(bf16[128,64]{1,0:T(8,128)(2,1)} %get-tuple-element.78.refs_0_.fo_ref, bf16[128,64]{1,0:T(8,128)(2,1)} %get-tuple-element.77.refs_1_.fr_ref, bf16[48,128,128]{2,1,0:T(8,128)(2,1)} %bitcast.86, bf16[3,64,128,128]{3,2,1,0:T(8,128)(2,1)} %copy-done.2, ...), custom_call_target="tpu_custom_call" | custom-call | tf_op jit(solution)/shard_map/pallas_call | solution.py:212
  97.2 2.6 %shard_map.113 = (bf16[16,64,128]{2,1,0:T(8,128)(2,1)}, bf16[16,64,128]{2,1,0:T(8,128)(2,1)}) custom-call(s32[1]{0:T(128)} %bitcast.me_ref, bf16[16,128,128]{2,1,0:T(8,128)(2,1)} %shard_map.112.y_ref, f32[64,128,128]{2,1,0:T(8,128)} %add_bitcast_fusion.1.w_ref, bf16[128,128]{1,0:T(8,128)(2,1)} %constant.247.clone.ft_ref), custom_call_target="tpu_custom_call" | custom-call | tf_op jit(solution)/shard_map/pallas_call | solution.py:101
  99.8 1.7 %collective-permute-done.10.recv_ref = bf16[16,64,128]{2,1,0:T(8,128)(2,1)S(1)} collective-permute-done((bf16[16,64,128]{2,1,0:T(8,128)(2,1)}, bf16[16,64,128]{2,1,0:T(8,128)(2,1)S(1)}, u32[]{:S(2)}, u32[]{:S(2)}) %collective-permute-start.10) | collective-permute-done | bytes 262176 | tf_op jit(solution)/shard_map/ppermute | solution.py:332
  101.5 0.7 copy-done.8
  102.3 2.6 %shard_map.114 = bf16[16,64,256]{2,1,0:T(8,128)(2,1)} custom-call(bf16[16,64,128]{2,1,0:T(8,128)(2,1)} %get-tuple-element.61.own_ref, bf16[16,64,128]{2,1,0:T(8,128)(2,1)} %copy-done.8, f32[64,64,256]{2,1,0:T(8,128)} %fusion.3.v_ref, bf16[128,256]{1,0:T(8,128)(2,1)} %get-tuple-element.74.fo_ref, bf16[128,256]{1,0:T(8,128)(2,1)} %get-tuple-element.73.fr_ref), custom_call_target="tpu_custom_call" | custom-call | tf_op jit(solution)/shard_map/pallas_call | solution.py:131
  104.9 1.7 %fusion.7 = bf16[64,256,48]{1,2,0:T(8,128)(2,1)S(1)} fusion(bf16[16,64,256]{2,1,0:T(8,128)(2,1)} %shard_map.114, bf16[48,16]{0,1:T(8,128)(2,1)S(1)} %copy-done.13), kind=kOutput, calls=%fused_computation.14 | convolution fusion | flops 25165824 | bytes 2098688 | tf_op jit(solution)/shard_map/dot_general | solution.py:381
  106.6 1.7 %copy.34 = bf16[64,256,48]{1,0,2:T(8,128)(2,1)} copy(bf16[64,256,48]{1,2,0:T(8,128)(2,1)S(1)} %fusion.7) | data formatting | bytes 3145728 | tf_op jit(solution)/shard_map/dot_general | solution.py:381
  108.3 5.7 %shard_map.115 = (bf16[1,48,64,128]{3,2,1,0:T(8,128)(2,1)}, bf16[1,48,64,128]{3,2,1,0:T(8,128)(2,1)}) custom-call(s32[1]{0:T(128)} %bitcast.me_ref, bf16[1,48,64,256]{3,2,1,0:T(8,128)(2,1)} %bitcast.89, f32[64,64,256]{2,1,0:T(8,128)} %fusion.3.v_ref, f32[64,64,256]{2,1,0:T(8,128)} %add_bitcast_fusion.w_ref, bf16[256,256]{1,0:T(8,128)(2,1)} %constant.248.clone.ft_ref), custom_call_target="tpu_custom_call" | custom-call | tf_op jit(solution)/shard_map/pallas_call | solution.py:161
  114.1 7.1 %shard_map.116.prod_ref = bf16[48,128,128]{2,1,0:T(8,128)(2,1)} custom-call(bf16[128,64]{1,0:T(8,128)(2,1)} %get-tuple-element.78.refs_0_.fo_ref, bf16[128,64]{1,0:T(8,128)(2,1)} %get-tuple-element.77.refs_1_.fr_ref, bf16[48,128,128]{2,1,0:T(8,128)(2,1)} %bitcast.87, bf16[3,64,128,128]{3,2,1,0:T(8,128)(2,1)} %copy-done.2, ...), custom_call_target="tpu_custom_call" | custom-call | tf_op jit(solution)/shard_map/pallas_call | solution.py:212
  121.2 0.9 broadcast_in_dim.10.s_ref
  122.1 4.4 %shard_map.117 = bf16[48,128,128]{2,1,0:T(8,128)(2,1)} custom-call(bf16[128,64]{1,0:T(8,128)(2,1)} %get-tuple-element.78.refs_0_.fo_ref, bf16[128,64]{1,0:T(8,128)(2,1)} %get-tuple-element.77.refs_1_.fr_ref, bf16[48,64,128]{2,1,0:T(8,128)(2,1)} %bitcast.100, bf16[48,64,128]{2,1,0:T(8,128)(2,1)} %bitcast.101, bf16[48,128,128]{2,1,0:T(8,128)(2,1)} %shard_map.116.prod_ref, ...), custom_call_target="tpu_custom_call" | custom-call | tf_op jit(solution)/shard_map/pallas_call | solution.py:244
  (66 shorter events, 2.3 us)
Async XLA Ops:
  0.0 34.0 %copy-start = (bf16[3,48,16]{1,2,0:T(8,128)(2,1)S(1)}, bf16[3,48,16]{1,2,0:T(8,128)(2,1)}, u32[]{:S(2)}) copy-start(bf16[3,48,16]{1,2,0:T(8,128)(2,1)} %param.13) | copy-start | bytes 13828
  0.0 20.7 %collective-permute-start = (bf16[3,8,128,128]{3,2,1,0:T(8,128)(2,1)}, bf16[3,8,128,128]{3,2,1,0:T(8,128)(2,1)S(1)}, u32[]{:S(2)}, u32[]{:S(2)}) collective-permute-start(bf16[3,8,128,128]{3,2,1,0:T(8,128)(2,1)} %bitcast.102), channel_id=1, source_target_pairs={{0,4},{4,8},{8,12},{12,14},{14,10},{10,6},{6,2},{2,0},{1,5},{5,9},... | collective-permute-start | bytes 2359304 | tf_op jit(solution)/shard_map/ppermute | solution.py:300
  3.0 19.3 %collective-permute-start.1 = (bf16[3,8,128,128]{3,2,1,0:T(8,128)(2,1)}, bf16[3,8,128,128]{3,2,1,0:T(8,128)(2,1)}, u32[]{:S(2)}, u32[]{:S(2)}) collective-permute-start(bf16[3,8,128,128]{3,2,1,0:T(8,128)(2,1)} %bitcast.103), channel_id=1, source_target_pairs={{0,2},{4,0},{8,4},{12,8},{14,12},{10,14},{6,10},{2,6},{1,3},{5,1},... | collective-permute-start | bytes 2359304 | tf_op jit(solution)/shard_map/ppermute | solution.py:301
  3.0 9.3 %copy-start.12 = (s32[8]{0:T(128)}, s32[8]{0:T(128)S(1)}, u32[]{:S(2)}) copy-start(s32[8]{0:T(128)S(1)} %get-tuple-element.135) | copy-start | bytes 100
  7.2 17.1 %copy-start.9 = (bf16[256,256]{1,0:T(8,128)(2,1)S(1)}, bf16[256,256]{1,0:T(8,128)(2,1)}, u32[]{:S(2)}) copy-start(bf16[256,256]{1,0:T(8,128)(2,1)} %constant.245.clone) | copy-start | bytes 393220
  12.2 16.1 %collective-permute-start.4 = (bf16[48,64,128]{2,1,0:T(8,128)(2,1)}, bf16[48,64,128]{2,1,0:T(8,128)(2,1)S(1)}, u32[]{:S(2)}, u32[]{:S(2)}) collective-permute-start(bf16[48,64,128]{2,1,0:T(8,128)(2,1)} %get-tuple-element.43), channel_id=1, source_target_pairs={{0,1},{1,0},{2,3},{3,2},{4,5},{5,4},{6,7},{7,6},{8,9},{9,8},{10,11... | collective-permute-start | bytes 2359304 | tf_op jit(solution)/shard_map/ppermute | solution.py:332
  20.7 13.2 %copy-start.6 = (bf16[3,8,128,128]{3,2,1,0:T(8,128)(2,1)}, bf16[3,8,128,128]{3,2,1,0:T(8,128)(2,1)S(1)}, u32[]{:S(2)}) copy-start(bf16[3,8,128,128]{3,2,1,0:T(8,128)(2,1)S(1)} %collective-permute-done) | copy-start | bytes 2359300
  22.3 18.4 %collective-permute-start.2 = (bf16[3,8,128,128]{3,2,1,0:T(8,128)(2,1)S(1)}, bf16[3,8,128,128]{3,2,1,0:T(8,128)(2,1)}, u32[]{:S(2)}, u32[]{:S(2)}) collective-permute-start(bf16[3,8,128,128]{3,2,1,0:T(8,128)(2,1)S(1)} %collective-permute-done), channel_id=1, source_target_pairs={{0,4},{4,8},{8,12},{12,14},{14,10},{10,6},{6,2},{2,0},{1,5},{5,9},... | collective-permute-start | bytes 2359304 | tf_op jit(solution)/shard_map/ppermute | solution.py:300
  23.9 18.1 %collective-permute-start.3 = (bf16[3,8,128,128]{3,2,1,0:T(8,128)(2,1)}, bf16[3,8,128,128]{3,2,1,0:T(8,128)(2,1)}, u32[]{:S(2)}, u32[]{:S(2)}) collective-permute-start(bf16[3,8,128,128]{3,2,1,0:T(8,128)(2,1)} %collective-permute-done.1), channel_id=1, source_target_pairs={{0,2},{4,0},{8,4},{12,8},{14,12},{10,14},{6,10},{2,6},{1,3},{5,1},... | collective-permute-start | bytes 2359304 | tf_op jit(solution)/shard_map/ppermute | solution.py:301
  28.3 0.9 copy-start.3
  42.0 18.8 %collective-permute-start.5 = (bf16[3,8,128,128]{3,2,1,0:T(8,128)(2,1)}, bf16[3,8,128,128]{3,2,1,0:T(8,128)(2,1)S(1)}, u32[]{:S(2)}, u32[]{:S(2)}) collective-permute-start(bf16[3,8,128,128]{3,2,1,0:T(8,128)(2,1)} %collective-permute-done.2), channel_id=1, source_target_pairs={{0,4},{4,8},{8,12},{12,14},{14,10},{10,6},{6,2},{2,0},{1,5},{5,9},... | collective-permute-start | bytes 2359304 | tf_op jit(solution)/shard_map/ppermute | solution.py:300
  43.6 17.2 %collective-permute-start.6 = (bf16[3,8,128,128]{3,2,1,0:T(8,128)(2,1)}, bf16[3,8,128,128]{3,2,1,0:T(8,128)(2,1)}, u32[]{:S(2)}, u32[]{:S(2)}) collective-permute-start(bf16[3,8,128,128]{3,2,1,0:T(8,128)(2,1)} %collective-permute-done.3), channel_id=1, source_target_pairs={{0,2},{4,0},{8,4},{12,8},{14,12},{10,14},{6,10},{2,6},{1,3},{5,1},... | collective-permute-start | bytes 2359304 | tf_op jit(solution)/shard_map/ppermute | solution.py:301
  47.4 13.5 %copy-start.15 = (s32[8]{0:T(128)S(1)}, s32[8]{0:T(128)}, u32[]{:S(2)}) copy-start(s32[8]{0:T(128)} %constant.244.clone) | copy-start | bytes 100
  47.4 18.8 %copy-start.11 = (s32[8]{0:T(128)S(1)}, s32[8]{0:T(128)}, u32[]{:S(2)}) copy-start(s32[8]{0:T(128)} %constant.243.clone) | copy-start | bytes 100
  47.4 23.8 %copy-start.10 = (bf16[128,128]{1,0:T(8,128)(2,1)S(1)}, bf16[128,128]{1,0:T(8,128)(2,1)}, u32[]{:S(2)}) copy-start(bf16[128,128]{1,0:T(8,128)(2,1)} %constant.246.clone) | copy-start | bytes 98308
  60.9 28.4 %collective-permute-start.9 = (bf16[3,48,64,128]{3,2,1,0:T(8,128)(2,1)}, bf16[3,48,64,128]{3,2,1,0:T(8,128)(2,1)S(1)}, u32[]{:S(2)}, u32[]{:S(2)}) collective-permute-start(bf16[3,48,64,128]{3,2,1,0:T(8,128)(2,1)} %get-tuple-element.60), channel_id=1, source_target_pairs={{0,1},{1,0},{2,3},{3,2},{4,5},{5,4},{6,7},{7,6},{8,9},{9,8},{10,11... | collective-permute-start | bytes 7077896 | tf_op jit(solution)/shard_map/ppermute | solution.py:332
  71.2 2.3 %copy-start.5 = (bf16[1,3,8,128,128]{4,3,2,1,0:T(8,128)(2,1)S(1)}, bf16[1,3,8,128,128]{4,3,2,1,0:T(8,128)(2,1)}, u32[]{:S(2)}) copy-start(bf16[1,3,8,128,128]{4,3,2,1,0:T(8,128)(2,1)} %param.12) | copy-start | bytes 2359300
  71.2 2.4 %copy-start.7 = (bf16[3,8,128,128]{3,2,1,0:T(8,128)(2,1)S(1)}, bf16[3,8,128,128]{3,2,1,0:T(8,128)(2,1)}, u32[]{:S(2)}) copy-start(bf16[3,8,128,128]{3,2,1,0:T(8,128)(2,1)} %copy-done.6) | copy-start | bytes 2359300
  77.3 11.5 %collective-permute-start.8 = (bf16[3,8,64,128]{3,2,1,0:T(8,128)(2,1)S(1)}, bf16[3,8,64,128]{3,2,1,0:T(8,128)(2,1)S(1)}, u32[]{:S(2)}, u32[]{:S(2)}) collective-permute-start(bf16[3,8,64,128]{3,2,1,0:T(8,128)(2,1)S(1)} %slice.7), channel_id=1, source_target_pairs={{0,2},{4,0},{8,4},{12,8},{14,12},{10,14},{6,10},{2,6},{1,3},{5,1},... | collective-permute-start | bytes 1179656 | tf_op jit(solution)/shard_map/ppermute | solution.py:311
  77.9 11.3 %collective-permute-start.7 = (bf16[3,8,64,128]{3,2,1,0:T(8,128)(2,1)S(1)}, bf16[3,8,64,128]{3,2,1,0:T(8,128)(2,1)S(1)}, u32[]{:S(2)}, u32[]{:S(2)}) collective-permute-start(bf16[3,8,64,128]{3,2,1,0:T(8,128)(2,1)S(1)} %slice.6), channel_id=1, source_target_pairs={{0,4},{4,8},{8,12},{12,14},{14,10},{10,6},{6,2},{2,0},{1,5},{5,9},... | collective-permute-start | bytes 1179656 | tf_op jit(solution)/shard_map/ppermute | solution.py:310
  89.3 2.7 %copy-start.2 = (bf16[3,64,128,128]{3,2,1,0:T(8,128)(2,1)}, bf16[3,64,128,128]{3,2,1,0:T(8,128)(2,1)S(1)}, u32[]{:S(2)}) copy-start(bf16[3,64,128,128]{3,2,1,0:T(8,128)(2,1)S(1)} %maximum_dynamic-update-slice_fusion.refs_3_) | copy-start | bytes 18874372
  92.0 1.5 %copy-start.1 = (bf16[3,48,64,128]{3,2,1,0:T(8,128)(2,1)}, bf16[3,48,64,128]{3,2,1,0:T(8,128)(2,1)S(1)}, u32[]{:S(2)}) copy-start(bf16[3,48,64,128]{3,2,1,0:T(8,128)(2,1)S(1)} %collective-permute-done.9.refs_5_.refs_7_.refs_9_) | copy-start | bytes 7077892
  97.2 7.7 %copy-start.13 = (bf16[48,16]{0,1:T(8,128)(2,1)S(1)}, bf16[48,16]{0,1:T(8,128)(2,1)}, u32[]{:S(2)}) copy-start(bf16[48,16]{0,1:T(8,128)(2,1)} %param.14) | copy-start | bytes 4612
  99.8 1.7 %collective-permute-start.10 = (bf16[16,64,128]{2,1,0:T(8,128)(2,1)}, bf16[16,64,128]{2,1,0:T(8,128)(2,1)S(1)}, u32[]{:S(2)}, u32[]{:S(2)}) collective-permute-start(bf16[16,64,128]{2,1,0:T(8,128)(2,1)} %get-tuple-element.62), channel_id=1, source_target_pairs={{0,1},{1,0},{2,3},{3,2},{4,5},{5,4},{6,7},{7,6},{8,9},{9,8},{10,11... | collective-permute-start | bytes 786440 | tf_op jit(solution)/shard_map/ppermute | solution.py:332
  101.5 0.7 copy-start.8
  114.0 7.2 %copy-start.14 = (f32[48]{0:T(128)S(1)}, f32[48]{0:T(128)}, u32[]{:S(2)}) copy-start(f32[48]{0:T(128)} %param.15) | copy-start | bytes 580
  114.0 7.2 %collective-permute-start.11 = (bf16[1,48,64,128]{3,2,1,0:T(8,128)(2,1)}, bf16[1,48,64,128]{3,2,1,0:T(8,128)(2,1)S(1)}, u32[]{:S(2)}, u32[]{:S(2)}) collective-permute-start(bf16[1,48,64,128]{3,2,1,0:T(8,128)(2,1)} %get-tuple-element.64), channel_id=1, source_target_pairs={{0,1},{1,0},{2,3},{3,2},{4,5},{5,4},{6,7},{7,6},{8,9},{9,8},{10,11... | collective-permute-start | bytes 2359304 | tf_op jit(solution)/shard_map/ppermute | solution.py:332
  121.2 0.9 copy-start.4

commit v3 on v2

--- a/solution.py
+++ b/solution.py
@@ -167,64 +167,91 @@
     )(me_arr, x, v_row, w_row, ft)
 
 
-def _product_kernel(eb0, fo_ref, fr_ref, cip_ref, key_ref, *rest):
-    halves = rest[: 2 * DIGITS]
-    out_ref, acc_ref = rest[2 * DIGITS :]
+def _product_kernel(eb0, spb, slot_ref, g_ref, fo_ref, fr_ref, cip_ref, *rest):
+    ring_refs = rest[:spb]
+    side_refs = rest[spb : 2 * spb]
+    halves = rest[2 * spb : 2 * spb + 2 * DIGITS]
+    out_ref, acc_ref = rest[2 * spb + 2 * DIGITS :]
+    width = ring_refs[0].shape[1]
     eb = pl.program_id(0) + eb0
     fo = fo_ref[...]
     fr = fr_ref[...]
     acc_ref[...] = jnp.zeros_like(acc_ref)
     n = acc_ref.shape[0]
-    for j in range(DIGITS):
-        own_ref, recv_ref = halves[2 * j], halves[2 * j + 1]
-
-        @pl.when(eb == j)
-        def _():
-            acc_ref[...] += cip_ref[...].astype(F32) * key_ref[j].astype(F32)
-
-        @pl.when(eb != j)
-        def _():
-            for l in range(n):
-                y = jnp.dot(fo, own_ref[l], preferred_element_type=F32)
-                y = (y + jnp.dot(fr, recv_ref[l], preferred_element_type=F32)).astype(BF16)
-                acc_ref[l] += y.astype(F32) * key_ref[j, l].astype(F32)
+
+    def key(gv, j, l):
+        kd = (j - gv) % DIGITS
+        if kd < 2:
+            return ring_refs[l // width][kd, l % width]
+        return side_refs[l // width][0, l % width]
+
+    for gv in range(2):
+        for j in range(DIGITS):
+            own_ref, recv_ref = halves[2 * j], halves[2 * j + 1]
+
+            @pl.when(jnp.logical_and(g_ref[0] == gv, eb == j))
+            def _():
+                for l in range(n):
+                    acc_ref[l] += cip_ref[l].astype(F32) * key(gv, j, l).astype(F32)
+
+            @pl.when(jnp.logical_and(g_ref[0] == gv, eb != j))
+            def _():
+                for l in range(n):
+                    y = jnp.dot(fo, own_ref[l], preferred_element_type=F32)
+                    y = (y + jnp.dot(fr, recv_ref[l], preferred_element_type=F32)).astype(BF16)
+                    acc_ref[l] += y.astype(F32) * key(gv, j, l).astype(F32)
 
     out_ref[...] = acc_ref[...].astype(BF16)
 
 
-def product(cip, key, own2, recv2, f_own, f_oth, eb0, nblocks):
+def product(cip, ring_key, side_key, slot, g_arr, own2, recv2, f_own, f_oth, eb0, nblocks):
     _, rows, cols_l = cip.shape
     rows_l = rows // 2
+    width = ring_key.shape[1] // slot.shape[0]
+    spb = BLK // width
 
     def lifted_block(j):
-        def index(i):
+        def index(i, slot_ref):
             eb = i + eb0
             tb = jnp.where(eb < j, eb, eb - 1)
             return (j, jnp.clip(tb, 0, DIGITS - 1), 0, 0)
 
         return pl.BlockSpec((None, BLK, rows_l, cols_l), index)
+
+    def key_block(r, depth):
+        return pl.BlockSpec(
+            (depth, width, rows, cols_l),
+            lambda i, slot_ref: (0, slot_ref[(i + eb0) * spb + r], 0, 0),
+        )
 
     half_specs = []
     half_args = []
     for j in range(DIGITS):
         half_specs += [lifted_block(j), lifted_block(j)]
         half_args += [own2, recv2]
-    return pl.pallas_call(
-        lambda *refs: _product_kernel(eb0, *refs),
+    grid_spec = pltpu.PrefetchScalarGridSpec(
+        num_scalar_prefetch=1,
         grid=(nblocks,),
         in_specs=[
-            pl.BlockSpec((rows, rows_l), lambda i: (0, 0)),
-            pl.BlockSpec((rows, rows_l), lambda i: (0, 0)),
+            SMEM_SPEC,
+            pl.BlockSpec((rows, rows_l), lambda i, slot_ref: (0, 0)),
+            pl.BlockSpec((rows, rows_l), lambda i, slot_ref: (0, 0)),
             pl.BlockSpec(
-                (BLK, rows, cols_l), lambda i: (jnp.minimum(i + eb0, DIGITS - 1), 0, 0)
+                (BLK, rows, cols_l),
+                lambda i, slot_ref: (jnp.minimum(i + eb0, DIGITS - 1), 0, 0),
             ),
-            pl.BlockSpec((DIGITS, BLK, rows, cols_l), lambda i: (0, i + eb0, 0, 0)),
         ]
+        + [key_block(r, 2) for r in range(spb)]
+        + [key_block(r, 1) for r in range(spb)]
         + half_specs,
-        out_specs=pl.BlockSpec((BLK, rows, cols_l), lambda i: (i, 0, 0)),
+        out_specs=pl.BlockSpec((BLK, rows, cols_l), lambda i, slot_ref: (i, 0, 0)),
+        scratch_shapes=[pltpu.VMEM((BLK, rows, cols_l), F32)],
+    )
+    return pl.pallas_call(
+        lambda *refs: _product_kernel(eb0, spb, *refs),
+        grid_spec=grid_spec,
         out_shape=jax.ShapeDtypeStruct((nblocks * BLK, rows, cols_l), BF16),
-        scratch_shapes=[pltpu.VMEM((BLK, rows, cols_l), F32)],
-    )(f_own, f_oth, cip, key, *half_args)
+    )(slot, g_arr, f_own, f_oth, cip, *([ring_key] * spb), *([side_key] * spb), *half_args)
 
 
 def _final_kernel(fo_ref, fr_ref, own_ref, recv_ref, prod_ref, s_ref, out_ref):
@@ -267,24 +294,32 @@
 def ring_setup(shard):
     n = lax.axis_size("limb")
     me_l = lax.axis_index("limb")
+    g = lax.axis_index("grp")
     order = snake_ring(n)
     pos = [0] * n
     for i, l in enumerate(order):
         pos[l] = i
-    width = shard.shape[1]
-    full = jnp.zeros((shard.shape[0], n * width) + shard.shape[2:], shard.dtype)
-    full = lax.dynamic_update_slice_in_dim(full, shard, me_l * width, axis=1)
+    pos_arr = jnp.array(pos, I32)
+    p = pos_arr[me_l]
+    d = (pos_arr - p) % n
+    half = (n - 1) // 2
+    slot = jnp.where(d == 0, 0, jnp.where(d <= half, 2 * d, 2 * (n - d) - 1))
+    if n % 2 == 0:
+        slot = jnp.where(d == n // 2, n - 1, slot)
+    piece = lax.dynamic_slice_in_dim(shard, g, 2, axis=0)
     return dict(
         n=n,
-        order=jnp.array(order, I32),
-        p=jnp.array(pos, I32)[me_l],
+        g=g,
+        slot=slot.astype(I32),
         cw=[(order[i], order[(i + 1) % n]) for i in range(n)],
         ccw=[(order[i], order[(i - 1) % n]) for i in range(n)],
-        width=width,
-        full=full,
-        a=shard,
-        b=shard,
+        ring=[piece],
+        side=[lax.dynamic_slice_in_dim(shard, 2 - 2 * g, 1, axis=0)],
+        a=piece,
+        b=piece,
         s=0,
+        fresh=[],
+        pending=[],
     )
 
 
@@ -292,41 +327,52 @@
     return st["n"] // 2
 
 
+def _to_partner(x, g):
+    return lax.ppermute(lax.dynamic_slice_in_dim(x, g, 1, axis=0), "grp", [(0, 1), (1, 0)])
+
+
 def ring_step(st):
-    n, width, order, p = st["n"], st["width"], st["order"], st["p"]
+    n = st["n"]
     st["s"] += 1
-    s = st["s"]
-    if 2 * s < n:
+    if 2 * st["s"] < n:
         st["a"] = lax.ppermute(st["a"], "limb", st["cw"])
         st["b"] = lax.ppermute(st["b"], "limb", st["ccw"])
-        st["full"] = lax.dynamic_update_slice_in_dim(
-            st["full"], st["a"], order[(p - s) % n] * width, axis=1
-        )
-        st["full"] = lax.dynamic_update_slice_in_dim(
-            st["full"], st["b"], order[(p + s) % n] * width, axis=1
-        )
+        st["fresh"] = [st["a"], st["b"]]
     else:
         h = st["a"].shape[2] // 2
         a = lax.ppermute(st["a"][:, :, :h], "limb", st["cw"])
         b = lax.ppermute(st["b"][:, :, h:], "limb", st["ccw"])
-        src = order[(p + s) % n] * width
-        st["full"] = lax.dynamic_update_slice_in_dim(
-            st["full"], jnp.concatenate([a, b], axis=2), src, axis=1
-        )
+        st["fresh"] = [jnp.concatenate([a, b], axis=2)]
+
+
+def _settle(st, x):
+    fresh, pending = st["fresh"], st["pending"]
+    fresh, pending, x = lax.optimization_barrier((fresh, pending, x))
+    st["side"] += pending
+    st["ring"] += fresh
+    if len(fresh) == 2:
+        st["a"], st["b"] = fresh
+    st["pending"] = [_to_partner(jnp.concatenate(fresh, axis=1), st["g"])]
+    st["fresh"] = []
+    return x
 
 
 def ring_hold(st, x):
     if st["s"] >= ring_steps(st):
         return x
-    st["a"], st["b"], x = lax.optimization_barrier((st["a"], st["b"], x))
+    x = _settle(st, x)
     ring_step(st)
     return x
 
 
-def ring_finish(st):
+def ring_finish(st, x):
     while st["s"] < ring_steps(st):
+        x = _settle(st, x)
         ring_step(st)
-    return st["full"]
+    if st["fresh"]:
+        x = _settle(st, x)
+    st["side"] += st["pending"]
+    return jnp.concatenate(st["ring"], axis=1), jnp.concatenate(st["side"], axis=1), x
 
 def swap(x):
     return lax.ppermute(x, "coef", perm=[(0, 1), (1, 0)])
@@ -360,6 +406,7 @@
     own1 = ring_hold(ring, own1)
     coeffs = inv_col(own1, swap(send1), v_row, fc_own, fc_oth, 0)
 
+    coeffs = ring_hold(ring, coeffs)
     blocks = coeffs.reshape(DIGITS, DIGIT_LIMBS, rows_l, cols)
     raised = lax.dot_general(
         raise_table, blocks, (((2,), (1,)), ((0,), (0,))), preferred_element_type=F32
@@ -369,12 +416,17 @@
     own2, send2 = fwd_col(
         me_arr, raised, v_row, w_row, ft_cols, lambda j, t: jnp.where(t >= j, t + 1, t)
     )
-    own2, send2 = ring_hold(ring, (own2, send2))
+    ring_key, side_key, (own2, send2) = ring_finish(ring, (own2, send2))
     recv2 = swap(send2)
-    key = ring_finish(ring)
-
-    prod_special = product(ct, key, own2, recv2, fr_own, fr_oth, DIGITS, 1)
-    prod_cipher = product(ct, key, own2, recv2, fr_own, fr_oth, 0, DIGITS)
+    slot = ring["slot"]
+    g_arr = jnp.reshape(ring["g"], (1,)).astype(I32)
+
+    prod_special = product(
+        ct, ring_key, side_key, slot, g_arr, own2, recv2, fr_own, fr_oth, DIGITS, 1
+    )
+    prod_cipher = product(
+        ct, ring_key, side_key, slot, g_arr, own2, recv2, fr_own, fr_oth, 0, DIGITS
+    )
 
     own3, send3 = inv_row(me_arr, prod_special, w_col, ft_rows, limbs)
     special = inv_col(own3, swap(send3), v_row, fc_own, fc_oth, limbs)

time: 128 us -> 136 us (1.062)
  between operations: 9.29 us -> 0.33 us
  local copies, waits for them, and re-layouts: 24.5 us -> 33.4 us
  other arithmetic: 13.4 us -> 17.8 us
  starting transfers between devices: 9.39 us -> 13.3 us
  Pallas kernels: 49.4 us -> 51.3 us
  matrix products: 4.53 us -> 3.17 us
    unnamed x32 -> x55, local copies, waits for them, and re-layouts: 5.77 us -> 18.7 us
    ppermute x1, waiting for transfers between devices: 6.74 us -> 0.01 us  [ring_step(): b = lax.ppermute(st['b'][:, :, h:], 'limb', st['ccw'])]
    ppermute x0 -> x4, waiting for transfers between devices: none -> 6.59 us  [_to_partner(): lax.ppermute(lax.dynamic_slice_in_dim(x, g, 1, axis=0), 'grp', [(0, 1), (...]
    dynamic_update_slice x7 -> x0, local copies, waits for them, and re-layouts: 5.37 us -> none  [the longest x3 3.78 us: ring_step(): lax.dynamic_update_slice_in_dim(st['full'], st['b'], order[(p + s) % n] *...]
    ppermute x0 -> x4, starting transfers between devices: none -> 3.95 us  [_to_partner(): lax.ppermute(lax.dynamic_slice_in_dim(x, g, 1, axis=0), 'grp', [(0, 1), (...]
    mul x4, local copies, waits for them, and re-layouts: 0.83 us -> 4.14 us  [_twiddle(): return 1.0 + 0.5 * (cp * cq - sp * sq)]
    pallas_call x2, Pallas kernels: 10.9 us -> 12.9 us  [product(): pl.pallas_call(lambda *refs: _product_kernel(eb0, spb, *refs), grid_spec=...]
    concatenate x0 -> x4, other arithmetic: none -> 1.77 us  [the longest x3 0.94 us: _settle(): st['pending'] = [_to_partner(jnp.concatenate(fresh, axis=1), st['g'])]]
  transfers between devices with their start and end apart: 12 -> 16, of which waited for: 6 -> 6; matrix products, arithmetic and copies ran while one was open for 26% -> 32% of each run, Pallas kernels for 24% -> 23%
where the time goes in v3:
time: 136 us; the launch traced here: 135 us
  Pallas kernels  51.3 us (38%)
  local copies, waits for them, and re-layouts  33.4 us (25%)
  other arithmetic  17.8 us (13%)
  waiting for transfers between devices  15.4 us (11%)
  starting transfers between devices  13.3 us (10%)
  matrix products  3.17 us (2%)
    pallas_call x2, Pallas kernels, fwd_col(): pl.pallas_call(_fwd_col_kernel, grid=(groups, n // BLK), in_specs=[SMEM_S...  19.1 us
    unnamed x55, local copies, waits for them, and re-layouts  18.7 us
    pallas_call x2, Pallas kernels, product(): pl.pallas_call(lambda *refs: _product_kernel(eb0, spb, *refs), grid_spec=...  12.9 us
    add x3, other arithmetic, _twiddle(): return 1.0 + 0.5 * (cp * cq - sp * sq)  10.3 us
    pallas_call x2, Pallas kernels, inv_col(): pl.pallas_call(_inv_col_kernel, grid=(n // BLK,), in_specs=[blk, blk, pl....  7.52 us
    pallas_call x2, Pallas kernels, inv_row(): pl.pallas_call(_inv_row_kernel, grid=(n // BLK,), in_specs=[SMEM_SPEC, bl...  7.41 us
    ppermute x4, waiting for transfers between devices, _to_partner(): lax.ppermute(lax.dynamic_slice_in_dim(x, g, 1, axis=0), 'grp', [(0, 1), (...  6.59 us
    ppermute x3, starting transfers between devices, ring_step(): st['a'] = lax.ppermute(st['a'], 'limb', st['cw'])  6.24 us
  transfers between devices with their start and end apart: 16, of which 6 were waited for; matrix products, arithmetic and copies ran while one was open for 32% of the time, Pallas kernels for 23%

profile of v3, /device:TPU:0, one launch (start us, length us, event | category | flops | bytes accessed | tf_op | source)
XLA Modules:
  0.0 134.6 jit_solution(15179954438613317239)
XLA Ops:
  0.0 2.1 %constant_dynamic-update-slice_fusion.7 = (bf16[2,64,128,128]{3,2,1,0:T(8,128)(2,1)}, bf16[2,8,128,128]{3,2,1,0:T(8,128)(2,1)S(1)}) fusion(bf16[1,3,8,128,128]{4,3,2,1,0:T(8,128)(2,1)} %param.11, s32[]{:T(128)S(6)} %select_n.312), kind=kLoop, calls=%fused_computation.142 | loop fusion | bytes 1572868
  2.1 3.0 %collective-permute-start = (bf16[2,8,128,128]{3,2,1,0:T(8,128)(2,1)S(1)}, bf16[2,8,128,128]{3,2,1,0:T(8,128)(2,1)S(1)}, u32[]{:S(2)}, u32[]{:S(2)}) collective-permute-start(bf16[2,8,128,128]{3,2,1,0:T(8,128)(2,1)S(1)} %get-tuple-element.76), channel_id=1, source_target_pairs={{0,4},{4,8},{8,12},{12,14},{14,10},{10,6},{6,2},{2,0},{1,5},{5,9},... | collective-permute-start | bytes 1572872 | tf_op jit(solution)/shard_map/ppermute | solution.py:338
  6.4 2.9 %add_bitcast_fusion.1.w_ref = f32[64,128,128]{2,1,0:T(8,128)} fusion(f32[64,8,128]{2,1,0:T(8,128)S(1)} %bitcast.89, f32[64,16,128]{2,1,0:T(8,128)S(1)} %bitcast.87, f32[64,8,128]{2,1,0:T(8,128)S(1)} %bitcast.90, f32[64,16,128]{2,1,0:T(8,128)S(1)} %bitcast.88), kind=kLoop, calls=%fused_computation.8 | loop fusion | flops 5242880 | bytes 5767168 | tf_op jit(solution)/shard_map/add | solution.py:53
  9.3 4.8 %shard_map.100 = (bf16[48,64,128]{2,1,0:T(8,128)(2,1)}, bf16[48,64,128]{2,1,0:T(8,128)(2,1)}) custom-call(s32[1]{0:T(128)} %bitcast.me_ref, bf16[48,128,128]{2,1,0:T(8,128)(2,1)} %bitcast.76, f32[64,128,128]{2,1,0:T(8,128)} %add_bitcast_fusion.1.w_ref, bf16[128,128]{1,0:T(8,128)(2,1)} %constant.210.clone.ft_ref), custom_call_target="tpu_custom_call" | custom-call | tf_op jit(solution)/shard_map/pallas_call | solution.py:101
  14.5 2.4 %fusion.53 = (f32[8,8,256]{2,1,0:T(8,128)S(1)}, f32[8,8,256]{2,1,0:T(8,128)S(1)}, f32[8,8,256]{2,1,0:T(8,128)S(1)}, f32[8,8,256]{2,1,0:T(8,128)S(1)}, f32[8,8,25...) fusion(s32[8,256]{1,0:T(8,128)S(1)} %add_select_fusion.12, ...), kind=kLoop, calls=%fused_computation.130 | loop fusion | flops 1376256 | bytes 811072 | tf_op jit(solution)/shard_map/cos | solution.py:35
  18.5 1.6 %collective-permute-start.2 = (bf16[2,8,128,128]{3,2,1,0:T(8,128)(2,1)S(1)}, bf16[2,8,128,128]{3,2,1,0:T(8,128)(2,1)S(1)}, u32[]{:S(2)}, u32[]{:S(2)}) collective-permute-start(bf16[2,8,128,128]{3,2,1,0:T(8,128)(2,1)S(1)} %collective-permute-done), channel_id=1, source_target_pairs={{0,4},{4,8},{8,12},{12,14},{14,10},{10,6},{6,2},{2,0},{1,5},{5,9},... | collective-permute-start | bytes 1572872 | tf_op jit(solution)/shard_map/ppermute | solution.py:338
  20.6 0.8 fusion.9
  21.4 1.5 %collective-permute-start.4 = (bf16[1,16,128,128]{3,2,1,0:T(8,128)(2,1)}, bf16[1,16,128,128]{3,2,1,0:T(8,128)(2,1)}, u32[]{:S(2)}, u32[]{:S(2)}) collective-permute-start(bf16[1,16,128,128]{3,2,1,0:T(8,128)(2,1)} %fusion.9), channel_id=1, source_target_pairs={{0,16},{16,0},{1,17},{17,1},{2,18},{18,2},{3,19},{19,3},{4,20},{20... | collective-permute-start | bytes 1572872 | tf_op jit(solution)/shard_map/ppermute | solution.py:331
  23.5 1.5 %copy.16 = f32[64,64]{1,0:T(8,128)} copy(f32[64,64]{0,1:T(8,128)} %broadcast_bitcast_fusion) | data formatting | bytes 32768 | tf_op jit(solution)/shard_map/mul | solution.py:53
  25.0 1.5 %copy.15 = f32[64,64]{1,0:T(8,128)} copy(f32[64,64]{0,1:T(8,128)} %broadcast_bitcast_fusion.1) | data formatting | bytes 32768 | tf_op jit(solution)/shard_map/mul | solution.py:53
  26.4 1.5 %constant_dynamic-slice_fusion.1 = (bf16[128,256]{1,0:T(8,128)(2,1)}, bf16[128,256]{1,0:T(8,128)(2,1)}) fusion(bf16[256,256]{1,0:T(8,128)(2,1)} %constant.208.clone, s32[]{:T(128)S(6)} %select_n.327, s32[]{:T(128)S(6)} %select_n.326), kind=kLoop, calls=%fused_computation.206 | loop fusion | bytes 262152 | tf_op jit(solution)/shard_map/dynamic_slice | solution.py:399
  27.9 4.1 %fusion.3.v_ref = f32[64,64,256]{2,1,0:T(8,128)} fusion(f32[64,64]{1,0:T(8,128)} %copy.16, f32[64,8,256]{2,1,0:T(8,128)S(1)} %bitcast.85, f32[64,64]{1,0:T(8,128)} %copy.15, f32[64,8,256]{2,1,0:T(8,128)S(1)} %bitcast.86), kind=kLoop, calls=%fused_computation.5 | loop fusion | flops 5242880 | bytes 5275648 | tf_op jit(solution)/shard_map/add | solution.py:53
  32.1 4.9 %shard_map.101 = bf16[48,64,256]{2,1,0:T(8,128)(2,1)} custom-call(bf16[48,64,128]{2,1,0:T(8,128)(2,1)} %get-tuple-element.47.own_ref, bf16[48,64,128]{2,1,0:T(8,128)(2,1)} %collective-permute-done.5.recv_ref, f32[64,64,256]{2,1,0:T(8,128)} %fusion.3.v_ref, bf16[128,256]{1,0:T(8,128)(2,1)} %get-tuple-element.86.fo_ref, bf16[128,256]{1,0:T(8,128)(2,1)} %get-tuple-element.85.fr_ref), custom_call_target="tpu_custom_call" | custom-call | tf_op jit(solution)/shard_map/pallas_call | solution.py:131
  37.1 1.6 %collective-permute-start.6 = (bf16[2,8,128,128]{3,2,1,0:T(8,128)(2,1)S(1)}, bf16[2,8,128,128]{3,2,1,0:T(8,128)(2,1)S(1)}, u32[]{:S(2)}, u32[]{:S(2)}) collective-permute-start(bf16[2,8,128,128]{3,2,1,0:T(8,128)(2,1)S(1)} %collective-permute-done.2), channel_id=1, source_target_pairs={{0,4},{4,8},{8,12},{12,14},{14,10},{10,6},{6,2},{2,0},{1,5},{5,9},... | collective-permute-start | bytes 1572872 | tf_op jit(solution)/shard_map/ppermute | solution.py:338
  40.0 1.5 %fusion.5 = bf16[3,64,256,48]{2,3,1,0:T(8,128)(2,1)S(1)} fusion(bf16[3,16,64,256]{3,2,1,0:T(8,128)(2,1)S(1)} %bitcast.79, bf16[3,48,16]{1,2,0:T(8,128)(2,1)S(1)} %copy-done), kind=kOutput, calls=%fused_computation.11 | convolution fusion | flops 75497472 | bytes 6296064 | tf_op jit(solution)/shard_map/dot_general | solution.py:411
  41.5 3.9 %copy.32 = bf16[3,64,256,48]{2,1,3,0:T(8,128)(2,1)} copy(bf16[3,64,256,48]{2,3,1,0:T(8,128)(2,1)S(1)} %fusion.5) | data formatting | bytes 9437184 | tf_op jit(solution)/shard_map/dot_general | solution.py:411
  45.4 5.0 %collective-permute-done.6 = bf16[2,8,128,128]{3,2,1,0:T(8,128)(2,1)S(1)} collective-permute-done((bf16[2,8,128,128]{3,2,1,0:T(8,128)(2,1)S(1)}, bf16[2,8,128,128]{3,2,1,0:T(8,128)(2,1)S(1)}, u32[]{:S(2)}, u32[]{:S(2)}) %collective-permute-start.6) | collective-permute-done | bytes 524320 | tf_op jit(solution)/shard_map/ppermute | solution.py:338
  50.4 1.3 collective-permute-done.7
  53.0 1.6 %collective-permute-start.10 = (bf16[2,8,64,128]{3,2,1,0:T(8,128)(2,1)S(1)}, bf16[2,8,64,128]{3,2,1,0:T(8,128)(2,1)S(1)}, u32[]{:S(2)}, u32[]{:S(2)}) collective-permute-start(bf16[2,8,64,128]{3,2,1,0:T(8,128)(2,1)S(1)} %slice.7), channel_id=1, source_target_pairs={{0,2},{4,0},{8,4},{12,8},{14,12},{10,14},{6,10},{2,6},{1,3},{5,1},... | collective-permute-start | bytes 786440 | tf_op jit(solution)/shard_map/ppermute | solution.py:344
  55.1 3.3 %add_bitcast_fusion.w_ref = f32[64,64,256]{2,1,0:T(8,128)} fusion(f32[64,8,256]{2,1,0:T(8,128)S(1)} %bitcast.83, f32[64,8,256]{2,1,0:T(8,128)S(1)} %bitcast.81, f32[64,8,256]{2,1,0:T(8,128)S(1)} %bitcast.84, f32[64,8,256]{2,1,0:T(8,128)S(1)} %bitcast.82), kind=kLoop, calls=%fused_computation.7 | loop fusion | flops 5242880 | bytes 6291456 | tf_op jit(solution)/shard_map/add | solution.py:53
  58.4 13.4 %shard_map.102 = (bf16[3,48,64,128]{3,2,1,0:T(8,128)(2,1)}, bf16[3,48,64,128]{3,2,1,0:T(8,128)(2,1)}) custom-call(s32[1]{0:T(128)} %bitcast.me_ref, bf16[3,48,64,256]{3,2,1,0:T(8,128)(2,1)} %bitcast.75, f32[64,64,256]{2,1,0:T(8,128)} %fusion.3.v_ref, f32[64,64,256]{2,1,0:T(8,128)} %add_bitcast_fusion.w_ref, bf16[256,256]{1,0:T(8,128)(2,1)} %constant.211.clone.ft_ref), custom_call_target="tpu_custom_call" | custom-call | tf_op jit(solution)/shard_map/pallas_call | solution.py:161
  71.8 0.8 pad_maximum_fusion
  72.7 0.8 copy-done.13
  74.8 1.0 bitcast_dynamic-update-slice_fusion
  75.9 1.2 compare_select_fusion.6.refs_0_
  77.1 1.9 %constant_dynamic-update-slice_fusion.6 = bf16[2,64,128,128]{3,2,1,0:T(8,128)(2,1)} fusion(bf16[2,64,128,128]{3,2,1,0:T(8,128)(2,1)} %get-tuple-element.75, bf16[2,8,128,128]{3,2,1,0:T(8,128)(2,1)} %copy-done.6), kind=kLoop, calls=%fused_computation.141 | loop fusion | bytes 1048576
  79.0 1.9 %constant_dynamic-update-slice_fusion.5 = bf16[2,64,128,128]{3,2,1,0:T(8,128)(2,1)} fusion(bf16[2,64,128,128]{3,2,1,0:T(8,128)(2,1)} %constant_dynamic-update-slice_fusion.6, bf16[2,8,128,128]{3,2,1,0:T(8,128)(2,1)} %copy-done.7), kind=kLoop, calls=%fused_computation.140 | loop fusion | bytes 1048576
  81.0 2.0 %constant_dynamic-update-slice_fusion.4 = bf16[2,64,128,128]{3,2,1,0:T(8,128)(2,1)} fusion(bf16[2,64,128,128]{3,2,1,0:T(8,128)(2,1)} %constant_dynamic-update-slice_fusion.5, bf16[2,8,128,128]{3,2,1,0:T(8,128)(2,1)} %copy-done.8), kind=kLoop, calls=%fused_computation.139 | loop fusion | bytes 1048576
  83.0 2.0 %constant_dynamic-update-slice_fusion.3 = bf16[2,64,128,128]{3,2,1,0:T(8,128)(2,1)} fusion(bf16[2,64,128,128]{3,2,1,0:T(8,128)(2,1)} %constant_dynamic-update-slice_fusion.4, bf16[2,8,128,128]{3,2,1,0:T(8,128)(2,1)} %copy-done.9), kind=kLoop, calls=%fused_computation.138 | loop fusion | bytes 1048576
  85.0 1.1 constant_dynamic-update-slice_fusion.11
  86.1 0.9 constant_dynamic-update-slice_fusion.2
  87.0 0.9 constant_dynamic-update-slice_fusion.1
  87.9 1.4 %collective-permute-start.12 = (bf16[1,8,128,128]{3,2,1,0:T(8,128)(2,1)S(1)}, bf16[1,8,128,128]{3,2,1,0:T(8,128)(2,1)S(1)}, u32[]{:S(2)}, u32[]{:S(2)}) collective-permute-start(bf16[1,8,128,128]{3,2,1,0:T(8,128)(2,1)S(1)} %constant_dynamic-slice_fusion), channel_id=1, source_target_pairs={{0,16},{16,0},{1,17},{17,1},{2,18},{18,2},{3,19},{19,3},{4,20},{20... | collective-permute-start | bytes 786440 | tf_op jit(solution)/shard_map/ppermute | solution.py:331
  89.4 0.9 constant_dynamic-update-slice_fusion.refs_5_.refs_6_
  90.4 6.3 %collective-permute-done.12 = bf16[1,8,128,128]{3,2,1,0:T(8,128)(2,1)S(1)} collective-permute-done((bf16[1,8,128,128]{3,2,1,0:T(8,128)(2,1)S(1)}, bf16[1,8,128,128]{3,2,1,0:T(8,128)(2,1)S(1)}, u32[]{:S(2)}, u32[]{:S(2)}) %collective-permute-start.12) | collective-permute-done | bytes 262176 | tf_op jit(solution)/shard_map/ppermute | solution.py:331
  96.8 1.3 copy-done.3
  98.1 1.4 %copy-done.2 = bf16[3,48,64,128]{3,2,1,0:T(8,128)(2,1)} copy-done((bf16[3,48,64,128]{3,2,1,0:T(8,128)(2,1)}, bf16[3,48,64,128]{3,2,1,0:T(8,128)(2,1)S(1)}, u32[]{:S(2)}) %copy-start.2) | copy-done | bytes 2359320
  99.5 4.8 %shard_map.103.y_ref = bf16[16,128,128]{2,1,0:T(8,128)(2,1)} custom-call(s32[8]{0:T(128)} %compare_select_fusion.6.refs_0_, s32[1]{0:T(128)} %bitcast.2.refs_1_, bf16[128,64]{1,0:T(8,128)(2,1)} %get-tuple-element.90.refs_2_.fo_ref, bf16[128,64]{1,0:T(8,128)(2,1)} %get-tuple-element.89.refs_3_.fr_ref, bf16[48,128,128]{2,1,0:T(8,128)(2,1)} %bitcast.77, ...), custom_call_target="tpu_custom_call" | custom-call | tf_op jit(solution)/shard_map/pallas_call | solution.py:250
  104.3 2.6 %shard_map.104 = (bf16[16,64,128]{2,1,0:T(8,128)(2,1)}, bf16[16,64,128]{2,1,0:T(8,128)(2,1)}) custom-call(s32[1]{0:T(128)} %bitcast.me_ref, bf16[16,128,128]{2,1,0:T(8,128)(2,1)} %shard_map.103.y_ref, f32[64,128,128]{2,1,0:T(8,128)} %add_bitcast_fusion.1.w_ref, bf16[128,128]{1,0:T(8,128)(2,1)} %constant.210.clone.ft_ref), custom_call_target="tpu_custom_call" | custom-call | tf_op jit(solution)/shard_map/pallas_call | solution.py:101
  106.9 1.7 %collective-permute-done.14.recv_ref = bf16[16,64,128]{2,1,0:T(8,128)(2,1)S(1)} collective-permute-done((bf16[16,64,128]{2,1,0:T(8,128)(2,1)}, bf16[16,64,128]{2,1,0:T(8,128)(2,1)S(1)}, u32[]{:S(2)}, u32[]{:S(2)}) %collective-permute-start.14) | collective-permute-done | bytes 262176 | tf_op jit(solution)/shard_map/ppermute | solution.py:378
  108.7 0.7 copy-done.17
  109.4 2.6 %shard_map.105 = bf16[16,64,256]{2,1,0:T(8,128)(2,1)} custom-call(bf16[16,64,128]{2,1,0:T(8,128)(2,1)} %get-tuple-element.71.own_ref, bf16[16,64,128]{2,1,0:T(8,128)(2,1)} %copy-done.17, f32[64,64,256]{2,1,0:T(8,128)} %fusion.3.v_ref, bf16[128,256]{1,0:T(8,128)(2,1)} %get-tuple-element.86.fo_ref, bf16[128,256]{1,0:T(8,128)(2,1)} %get-tuple-element.85.fr_ref), custom_call_target="tpu_custom_call" | custom-call | tf_op jit(solution)/shard_map/pallas_call | solution.py:131
  112.0 1.7 %fusion.10 = bf16[64,256,48]{1,2,0:T(8,128)(2,1)S(1)} fusion(bf16[16,64,256]{2,1,0:T(8,128)(2,1)} %shard_map.105, bf16[48,16]{0,1:T(8,128)(2,1)S(1)} %copy-done.19), kind=kOutput, calls=%fused_computation.23 | convolution fusion | flops 25165824 | bytes 2098688 | tf_op jit(solution)/shard_map/dot_general | solution.py:433
  113.7 1.7 %copy.33 = bf16[64,256,48]{1,0,2:T(8,128)(2,1)} copy(bf16[64,256,48]{1,2,0:T(8,128)(2,1)S(1)} %fusion.10) | data formatting | bytes 3145728 | tf_op jit(solution)/shard_map/dot_general | solution.py:433
  115.4 5.7 %shard_map.106 = (bf16[1,48,64,128]{3,2,1,0:T(8,128)(2,1)}, bf16[1,48,64,128]{3,2,1,0:T(8,128)(2,1)}) custom-call(s32[1]{0:T(128)} %bitcast.me_ref, bf16[1,48,64,256]{3,2,1,0:T(8,128)(2,1)} %bitcast.80, f32[64,64,256]{2,1,0:T(8,128)} %fusion.3.v_ref, f32[64,64,256]{2,1,0:T(8,128)} %add_bitcast_fusion.w_ref, bf16[256,256]{1,0:T(8,128)(2,1)} %constant.211.clone.ft_ref), custom_call_target="tpu_custom_call" | custom-call | tf_op jit(solution)/shard_map/pallas_call | solution.py:161
  121.2 8.0 %shard_map.107.prod_ref = bf16[48,128,128]{2,1,0:T(8,128)(2,1)} custom-call(s32[8]{0:T(128)} %compare_select_fusion.6.refs_0_, s32[1]{0:T(128)} %bitcast.2.refs_1_, bf16[128,64]{1,0:T(8,128)(2,1)} %get-tuple-element.90.refs_2_.fo_ref, bf16[128,64]{1,0:T(8,128)(2,1)} %get-tuple-element.89.refs_3_.fr_ref, bf16[48,128,128]{2,1,0:T(8,128)(2,1)} %bitcast.78, ...), custom_call_target="tpu_custom_call" | custom-call | tf_op jit(solution)/shard_map/pallas_call | solution.py:250
  129.3 0.9 broadcast_in_dim.10.s_ref
  130.2 4.4 %shard_map.108 = bf16[48,128,128]{2,1,0:T(8,128)(2,1)} custom-call(bf16[128,64]{1,0:T(8,128)(2,1)} %get-tuple-element.90.refs_2_.fo_ref, bf16[128,64]{1,0:T(8,128)(2,1)} %get-tuple-element.89.refs_3_.fr_ref, bf16[48,64,128]{2,1,0:T(8,128)(2,1)} %bitcast.91, bf16[48,64,128]{2,1,0:T(8,128)(2,1)} %bitcast.92, bf16[48,128,128]{2,1,0:T(8,128)(2,1)} %shard_map.107.prod_ref, ...), custom_call_target="tpu_custom_call" | custom-call | tf_op jit(solution)/shard_map/pallas_call | solution.py:271
  (95 shorter events, 9.0 us)
Async XLA Ops:
  0.0 39.9 %copy-start = (bf16[3,48,16]{1,2,0:T(8,128)(2,1)S(1)}, bf16[3,48,16]{1,2,0:T(8,128)(2,1)}, u32[]{:S(2)}) copy-start(bf16[3,48,16]{1,2,0:T(8,128)(2,1)} %param.12) | copy-start | bytes 13828
  2.1 15.7 %collective-permute-start = (bf16[2,8,128,128]{3,2,1,0:T(8,128)(2,1)S(1)}, bf16[2,8,128,128]{3,2,1,0:T(8,128)(2,1)S(1)}, u32[]{:S(2)}, u32[]{:S(2)}) collective-permute-start(bf16[2,8,128,128]{3,2,1,0:T(8,128)(2,1)S(1)} %get-tuple-element.76), channel_id=1, source_target_pairs={{0,4},{4,8},{8,12},{12,14},{14,10},{10,6},{6,2},{2,0},{1,5},{5,9},... | collective-permute-start | bytes 1572872 | tf_op jit(solution)/shard_map/ppermute | solution.py:338
  5.1 13.4 %collective-permute-start.1 = (bf16[2,8,128,128]{3,2,1,0:T(8,128)(2,1)S(1)}, bf16[2,8,128,128]{3,2,1,0:T(8,128)(2,1)S(1)}, u32[]{:S(2)}, u32[]{:S(2)}) collective-permute-start(bf16[2,8,128,128]{3,2,1,0:T(8,128)(2,1)S(1)} %get-tuple-element.76), channel_id=1, source_target_pairs={{0,2},{4,0},{8,4},{12,8},{14,12},{10,14},{6,10},{2,6},{1,3},{5,1},... | collective-permute-start | bytes 1572872 | tf_op jit(solution)/shard_map/ppermute | solution.py:339
  14.1 18.0 %collective-permute-start.5 = (bf16[48,64,128]{2,1,0:T(8,128)(2,1)}, bf16[48,64,128]{2,1,0:T(8,128)(2,1)}, u32[]{:S(2)}, u32[]{:S(2)}) collective-permute-start(bf16[48,64,128]{2,1,0:T(8,128)(2,1)} %get-tuple-element.48), channel_id=1, source_target_pairs={{0,1},{1,0},{2,3},{3,2},{4,5},{5,4},{6,7},{7,6},{8,9},{9,8},{10,11... | collective-permute-start | bytes 2359304 | tf_op jit(solution)/shard_map/ppermute | solution.py:378
  17.8 19.1 %copy-start.6 = (bf16[2,8,128,128]{3,2,1,0:T(8,128)(2,1)}, bf16[2,8,128,128]{3,2,1,0:T(8,128)(2,1)S(1)}, u32[]{:S(2)}) copy-start(bf16[2,8,128,128]{3,2,1,0:T(8,128)(2,1)S(1)} %collective-permute-done) | copy-start | bytes 1572868
  18.5 18.5 %copy-start.7 = (bf16[2,8,128,128]{3,2,1,0:T(8,128)(2,1)}, bf16[2,8,128,128]{3,2,1,0:T(8,128)(2,1)S(1)}, u32[]{:S(2)}) copy-start(bf16[2,8,128,128]{3,2,1,0:T(8,128)(2,1)S(1)} %collective-permute-done.1) | copy-start | bytes 1572868
  18.5 18.5 %collective-permute-start.2 = (bf16[2,8,128,128]{3,2,1,0:T(8,128)(2,1)S(1)}, bf16[2,8,128,128]{3,2,1,0:T(8,128)(2,1)S(1)}, u32[]{:S(2)}, u32[]{:S(2)}) collective-permute-start(bf16[2,8,128,128]{3,2,1,0:T(8,128)(2,1)S(1)} %collective-permute-done), channel_id=1, source_target_pairs={{0,4},{4,8},{8,12},{12,14},{14,10},{10,6},{6,2},{2,0},{1,5},{5,9},... | collective-permute-start | bytes 1572872 | tf_op jit(solution)/shard_map/ppermute | solution.py:338
  20.1 16.9 %collective-permute-start.3 = (bf16[2,8,128,128]{3,2,1,0:T(8,128)(2,1)S(1)}, bf16[2,8,128,128]{3,2,1,0:T(8,128)(2,1)S(1)}, u32[]{:S(2)}, u32[]{:S(2)}) collective-permute-start(bf16[2,8,128,128]{3,2,1,0:T(8,128)(2,1)S(1)} %collective-permute-done.1), channel_id=1, source_target_pairs={{0,2},{4,0},{8,4},{12,8},{14,12},{10,14},{6,10},{2,6},{1,3},{5,1},... | collective-permute-start | bytes 1572872 | tf_op jit(solution)/shard_map/ppermute | solution.py:339
  21.4 15.6 %collective-permute-start.4 = (bf16[1,16,128,128]{3,2,1,0:T(8,128)(2,1)}, bf16[1,16,128,128]{3,2,1,0:T(8,128)(2,1)}, u32[]{:S(2)}, u32[]{:S(2)}) collective-permute-start(bf16[1,16,128,128]{3,2,1,0:T(8,128)(2,1)} %fusion.9), channel_id=1, source_target_pairs={{0,16},{16,0},{1,17},{17,1},{2,18},{18,2},{3,19},{19,3},{4,20},{20... | collective-permute-start | bytes 1572872 | tf_op jit(solution)/shard_map/ppermute | solution.py:331
  32.1 7.7 %copy-start.15 = (f32[8,8,256]{2,1,0:T(8,128)S(1)}, f32[8,8,256]{2,1,0:T(8,128)}, u32[]{:S(2)}) copy-start(f32[8,8,256]{2,1,0:T(8,128)} %get-tuple-element.129) | copy-start | bytes 196612
  32.1 7.7 %copy-start.16 = (f32[8,8,256]{2,1,0:T(8,128)S(1)}, f32[8,8,256]{2,1,0:T(8,128)}, u32[]{:S(2)}) copy-start(f32[8,8,256]{2,1,0:T(8,128)} %get-tuple-element.130) | copy-start | bytes 196612
  37.0 3.0 %copy-start.4 = (bf16[48,64,256]{2,1,0:T(8,128)(2,1)S(1)}, bf16[48,64,256]{2,1,0:T(8,128)(2,1)}, u32[]{:S(2)}) copy-start(bf16[48,64,256]{2,1,0:T(8,128)(2,1)} %shard_map.101) | copy-start | bytes 4718596
  37.0 4.5 %copy-start.8 = (bf16[2,8,128,128]{3,2,1,0:T(8,128)(2,1)}, bf16[2,8,128,128]{3,2,1,0:T(8,128)(2,1)S(1)}, u32[]{:S(2)}) copy-start(bf16[2,8,128,128]{3,2,1,0:T(8,128)(2,1)S(1)} %collective-permute-done.2) | copy-start | bytes 1572868
  37.0 4.5 %copy-start.9 = (bf16[2,8,128,128]{3,2,1,0:T(8,128)(2,1)}, bf16[2,8,128,128]{3,2,1,0:T(8,128)(2,1)S(1)}, u32[]{:S(2)}) copy-start(bf16[2,8,128,128]{3,2,1,0:T(8,128)(2,1)S(1)} %collective-permute-done.3) | copy-start | bytes 1572868
  37.1 13.4 %collective-permute-start.6 = (bf16[2,8,128,128]{3,2,1,0:T(8,128)(2,1)S(1)}, bf16[2,8,128,128]{3,2,1,0:T(8,128)(2,1)S(1)}, u32[]{:S(2)}, u32[]{:S(2)}) collective-permute-start(bf16[2,8,128,128]{3,2,1,0:T(8,128)(2,1)S(1)} %collective-permute-done.2), channel_id=1, source_target_pairs={{0,4},{4,8},{8,12},{12,14},{14,10},{10,6},{6,2},{2,0},{1,5},{5,9},... | collective-permute-start | bytes 1572872 | tf_op jit(solution)/shard_map/ppermute | solution.py:338
  38.7 13.0 %collective-permute-start.7 = (bf16[2,8,128,128]{3,2,1,0:T(8,128)(2,1)S(1)}, bf16[2,8,128,128]{3,2,1,0:T(8,128)(2,1)S(1)}, u32[]{:S(2)}, u32[]{:S(2)}) collective-permute-start(bf16[2,8,128,128]{3,2,1,0:T(8,128)(2,1)S(1)} %collective-permute-done.3), channel_id=1, source_target_pairs={{0,2},{4,0},{8,4},{12,8},{14,12},{10,14},{6,10},{2,6},{1,3},{5,1},... | collective-permute-start | bytes 1572872 | tf_op jit(solution)/shard_map/ppermute | solution.py:339
  39.2 12.8 %collective-permute-start.8 = (bf16[1,16,128,128]{3,2,1,0:T(8,128)(2,1)S(1)}, bf16[1,16,128,128]{3,2,1,0:T(8,128)(2,1)S(1)}, u32[]{:S(2)}, u32[]{:S(2)}) collective-permute-start(bf16[1,16,128,128]{3,2,1,0:T(8,128)(2,1)S(1)} %fusion.8), channel_id=1, source_target_pairs={{0,16},{16,0},{1,17},{17,1},{2,18},{18,2},{3,19},{19,3},{4,20},{20... | collective-permute-start | bytes 1572872 | tf_op jit(solution)/shard_map/ppermute | solution.py:331
  52.0 0.8 copy-start.11
  52.1 20.6 %collective-permute-start.11 = (bf16[1,16,128,128]{3,2,1,0:T(8,128)(2,1)S(1)}, bf16[1,16,128,128]{3,2,1,0:T(8,128)(2,1)S(1)}, u32[]{:S(2)}, u32[]{:S(2)}) collective-permute-start(bf16[1,16,128,128]{3,2,1,0:T(8,128)(2,1)S(1)} %fusion.7), channel_id=1, source_target_pairs={{0,16},{16,0},{1,17},{17,1},{2,18},{18,2},{3,19},{19,3},{4,20},{20... | collective-permute-start | bytes 1572872 | tf_op jit(solution)/shard_map/ppermute | solution.py:331
  53.0 18.8 %collective-permute-start.10 = (bf16[2,8,64,128]{3,2,1,0:T(8,128)(2,1)S(1)}, bf16[2,8,64,128]{3,2,1,0:T(8,128)(2,1)S(1)}, u32[]{:S(2)}, u32[]{:S(2)}) collective-permute-start(bf16[2,8,64,128]{3,2,1,0:T(8,128)(2,1)S(1)} %slice.7), channel_id=1, source_target_pairs={{0,2},{4,0},{8,4},{12,8},{14,12},{10,14},{6,10},{2,6},{1,3},{5,1},... | collective-permute-start | bytes 786440 | tf_op jit(solution)/shard_map/ppermute | solution.py:344
  54.6 17.2 %collective-permute-start.9 = (bf16[2,8,64,128]{3,2,1,0:T(8,128)(2,1)S(1)}, bf16[2,8,64,128]{3,2,1,0:T(8,128)(2,1)S(1)}, u32[]{:S(2)}, u32[]{:S(2)}) collective-permute-start(bf16[2,8,64,128]{3,2,1,0:T(8,128)(2,1)S(1)} %slice.6), channel_id=1, source_target_pairs={{0,4},{4,8},{8,12},{12,14},{14,10},{10,6},{6,2},{2,0},{1,5},{5,9},... | collective-permute-start | bytes 786440 | tf_op jit(solution)/shard_map/ppermute | solution.py:343
  58.4 15.1 %copy-start.21 = (s32[8]{0:T(128)S(1)}, s32[8]{0:T(128)}, u32[]{:S(2)}) copy-start(s32[8]{0:T(128)} %constant.207.clone) | copy-start | bytes 100
  58.4 15.7 %copy-start.18 = (bf16[128,128]{1,0:T(8,128)(2,1)S(1)}, bf16[128,128]{1,0:T(8,128)(2,1)}, u32[]{:S(2)}) copy-start(bf16[128,128]{1,0:T(8,128)(2,1)} %constant.209.clone) | copy-start | bytes 98308
  72.7 0.8 copy-start.13
  73.5 23.3 %collective-permute-start.13 = (bf16[3,48,64,128]{3,2,1,0:T(8,128)(2,1)}, bf16[3,48,64,128]{3,2,1,0:T(8,128)(2,1)S(1)}, u32[]{:S(2)}, u32[]{:S(2)}) collective-permute-start(bf16[3,48,64,128]{3,2,1,0:T(8,128)(2,1)} %get-tuple-element.70), channel_id=1, source_target_pairs={{0,1},{1,0},{2,3},{3,2},{4,5},{5,4},{6,7},{7,6},{8,9},{9,8},{10,11... | collective-permute-start | bytes 7077896 | tf_op jit(solution)/shard_map/ppermute | solution.py:378
  74.1 13.8 %copy-start.5 = (bf16[2,8,128,128]{3,2,1,0:T(8,128)(2,1)S(1)}, bf16[2,8,128,128]{3,2,1,0:T(8,128)(2,1)}, u32[]{:S(2)}) copy-start(bf16[2,8,128,128]{3,2,1,0:T(8,128)(2,1)} %pad_maximum_fusion) | copy-start | bytes 1572868
  74.8 14.5 %copy-start.12 = (bf16[1,16,128,128]{3,2,1,0:T(8,128)(2,1)S(1)}, bf16[1,16,128,128]{3,2,1,0:T(8,128)(2,1)}, u32[]{:S(2)}) copy-start(bf16[1,16,128,128]{3,2,1,0:T(8,128)(2,1)} %copy-done.11) | copy-start | bytes 1572868
  81.0 9.4 %copy-start.14 = (bf16[1,16,128,128]{3,2,1,0:T(8,128)(2,1)S(1)}, bf16[1,16,128,128]{3,2,1,0:T(8,128)(2,1)}, u32[]{:S(2)}) copy-start(bf16[1,16,128,128]{3,2,1,0:T(8,128)(2,1)} %copy-done.13) | copy-start | bytes 1572868
  87.9 8.8 %collective-permute-start.12 = (bf16[1,8,128,128]{3,2,1,0:T(8,128)(2,1)S(1)}, bf16[1,8,128,128]{3,2,1,0:T(8,128)(2,1)S(1)}, u32[]{:S(2)}, u32[]{:S(2)}) collective-permute-start(bf16[1,8,128,128]{3,2,1,0:T(8,128)(2,1)S(1)} %constant_dynamic-slice_fusion), channel_id=1, source_target_pairs={{0,16},{16,0},{1,17},{17,1},{2,18},{18,2},{3,19},{19,3},{4,20},{20... | collective-permute-start | bytes 786440 | tf_op jit(solution)/shard_map/ppermute | solution.py:331
  96.8 1.3 %copy-start.3 = (bf16[1,64,128,128]{3,2,1,0:T(8,128)(2,1)}, bf16[1,64,128,128]{3,2,1,0:T(8,128)(2,1)S(1)}, u32[]{:S(2)}) copy-start(bf16[1,64,128,128]{3,2,1,0:T(8,128)(2,1)S(1)} %constant_dynamic-update-slice_fusion.8.refs_7_.refs_8_) | copy-start | bytes 6291460
  98.1 1.4 %copy-start.2 = (bf16[3,48,64,128]{3,2,1,0:T(8,128)(2,1)}, bf16[3,48,64,128]{3,2,1,0:T(8,128)(2,1)S(1)}, u32[]{:S(2)}) copy-start(bf16[3,48,64,128]{3,2,1,0:T(8,128)(2,1)S(1)} %collective-permute-done.13.refs_10_.refs_12_.refs_14_) | copy-start | bytes 7077892
  104.3 7.7 %copy-start.19 = (bf16[48,16]{0,1:T(8,128)(2,1)S(1)}, bf16[48,16]{0,1:T(8,128)(2,1)}, u32[]{:S(2)}) copy-start(bf16[48,16]{0,1:T(8,128)(2,1)} %param.13) | copy-start | bytes 4612
  106.9 1.7 %collective-permute-start.14 = (bf16[16,64,128]{2,1,0:T(8,128)(2,1)}, bf16[16,64,128]{2,1,0:T(8,128)(2,1)S(1)}, u32[]{:S(2)}, u32[]{:S(2)}) collective-permute-start(bf16[16,64,128]{2,1,0:T(8,128)(2,1)} %get-tuple-element.72), channel_id=1, source_target_pairs={{0,1},{1,0},{2,3},{3,2},{4,5},{5,4},{6,7},{7,6},{8,9},{9,8},{10,11... | collective-permute-start | bytes 786440 | tf_op jit(solution)/shard_map/ppermute | solution.py:378
  108.7 0.7 copy-start.17
  121.1 8.2 %copy-start.20 = (f32[48]{0:T(128)S(1)}, f32[48]{0:T(128)}, u32[]{:S(2)}) copy-start(f32[48]{0:T(128)} %param.14) | copy-start | bytes 580
  121.1 8.1 %collective-permute-start.15 = (bf16[1,48,64,128]{3,2,1,0:T(8,128)(2,1)}, bf16[1,48,64,128]{3,2,1,0:T(8,128)(2,1)S(1)}, u32[]{:S(2)}, u32[]{:S(2)}) collective-permute-start(bf16[1,48,64,128]{3,2,1,0:T(8,128)(2,1)} %get-tuple-element.74), channel_id=1, source_target_pairs={{0,1},{1,0},{2,3},{3,2},{4,5},{5,4},{6,7},{7,6},{8,9},{9,8},{10,11... | collective-permute-start | bytes 2359304 | tf_op jit(solution)/shard_map/ppermute | solution.py:378
  121.2 13.4 %copy-start.1 = (bf16[3,48,16]{1,2,0:T(8,128)(2,1)S(1)}, bf16[3,48,16]{1,2,0:T(8,128)(2,1)}, u32[]{:S(2)}) copy-start(bf16[3,48,16]{1,2,0:T(8,128)(2,1)} %param.12) | copy-start | bytes 13828
  129.2 0.9 copy-start.10

commit v4 on v3

--- a/solution.py
+++ b/solution.py
@@ -167,13 +167,24 @@
     )(me_arr, x, v_row, w_row, ft)
 
 
-def _product_kernel(eb0, spb, slot_ref, g_ref, fo_ref, fr_ref, cip_ref, *rest):
-    ring_refs = rest[:spb]
-    side_refs = rest[spb : 2 * spb]
-    halves = rest[2 * spb : 2 * spb + 2 * DIGITS]
-    out_ref, acc_ref = rest[2 * spb + 2 * DIGITS :]
-    width = ring_refs[0].shape[1]
+def _product_kernel(eb0, spb, ring_map, side_map, slot_ref, g_ref, fo_ref, fr_ref, cip_ref, *rest):
+    nr, ns = len(ring_map), len(set(i for i, _ in side_map))
+    ring_refs = rest[:nr]
+    side_refs = rest[nr : nr + ns]
+    halves = rest[nr + ns : nr + ns + 2 * DIGITS]
+    out_ref, acc_ref, kring, kside = rest[nr + ns + 2 * DIGITS :]
+    width = kring.shape[2]
     eb = pl.program_id(0) + eb0
+    for r in range(spb):
+        where = slot_ref[eb * spb + r]
+        for k in range(nr):
+            ai, off = side_map[k]
+
+            @pl.when(where == k)
+            def _():
+                pltpu.sync_copy(ring_refs[k], kring.at[r])
+                pltpu.sync_copy(side_refs[ai].at[:, pl.ds(off * width, width)], kside.at[r])
+
     fo = fo_ref[...]
     fr = fr_ref[...]
     acc_ref[...] = jnp.zeros_like(acc_ref)
@@ -182,8 +193,8 @@
     def key(gv, j, l):
         kd = (j - gv) % DIGITS
         if kd < 2:
-            return ring_refs[l // width][kd, l % width]
-        return side_refs[l // width][0, l % width]
+            return kring[l // width, kd, l % width]
+        return kside[l // width, 0, l % width]
 
     for gv in range(2):
         for j in range(DIGITS):
@@ -204,11 +215,15 @@
     out_ref[...] = acc_ref[...].astype(BF16)
 
 
-def product(cip, ring_key, side_key, slot, g_arr, own2, recv2, f_own, f_oth, eb0, nblocks):
+def product(cip, ring_pieces, side_pieces, slot, g_arr, own2, recv2, f_own, f_oth, eb0, nblocks):
     _, rows, cols_l = cip.shape
     rows_l = rows // 2
-    width = ring_key.shape[1] // slot.shape[0]
+    width = ring_pieces[0].shape[1]
     spb = BLK // width
+    side_map = []
+    for i, piece in enumerate(side_pieces):
+        side_map += [(i, off) for off in range(piece.shape[1] // width)]
+    ring_map = list(range(len(ring_pieces)))
 
     def lifted_block(j):
         def index(i, slot_ref):
@@ -218,12 +233,7 @@
 
         return pl.BlockSpec((None, BLK, rows_l, cols_l), index)
 
-    def key_block(r, depth):
-        return pl.BlockSpec(
-            (depth, width, rows, cols_l),
-            lambda i, slot_ref: (0, slot_ref[(i + eb0) * spb + r], 0, 0),
-        )
-
+    any_spec = pl.BlockSpec(memory_space=pl.ANY)
     half_specs = []
     half_args = []
     for j in range(DIGITS):
@@ -241,17 +251,20 @@
                 lambda i, slot_ref: (jnp.minimum(i + eb0, DIGITS - 1), 0, 0),
             ),
         ]
-        + [key_block(r, 2) for r in range(spb)]
-        + [key_block(r, 1) for r in range(spb)]
+        + [any_spec] * (len(ring_pieces) + len(side_pieces))
         + half_specs,
         out_specs=pl.BlockSpec((BLK, rows, cols_l), lambda i, slot_ref: (i, 0, 0)),
-        scratch_shapes=[pltpu.VMEM((BLK, rows, cols_l), F32)],
+        scratch_shapes=[
+            pltpu.VMEM((BLK, rows, cols_l), F32),
+            pltpu.VMEM((spb, 2, width, rows, cols_l), BF16),
+            pltpu.VMEM((spb, 1, width, rows, cols_l), BF16),
+        ],
     )
     return pl.pallas_call(
-        lambda *refs: _product_kernel(eb0, spb, *refs),
+        lambda *refs: _product_kernel(eb0, spb, ring_map, side_map, *refs),
         grid_spec=grid_spec,
         out_shape=jax.ShapeDtypeStruct((nblocks * BLK, rows, cols_l), BF16),
-    )(slot, g_arr, f_own, f_oth, cip, *([ring_key] * spb), *([side_key] * spb), *half_args)
+    )(slot, g_arr, f_own, f_oth, cip, *ring_pieces, *side_pieces, *half_args)
 
 
 def _final_kernel(fo_ref, fr_ref, own_ref, recv_ref, prod_ref, s_ref, out_ref):
@@ -372,7 +385,7 @@
     if st["fresh"]:
         x = _settle(st, x)
     st["side"] += st["pending"]
-    return jnp.concatenate(st["ring"], axis=1), jnp.concatenate(st["side"], axis=1), x
+    return st["ring"], st["side"], x
 
 def swap(x):
     return lax.ppermute(x, "coef", perm=[(0, 1), (1, 0)])

time: 136 us -> 139 us (1.022)
  Pallas kernels: 51.3 us -> 66.4 us
  local copies, waits for them, and re-layouts: 33.4 us -> 20.7 us
  waiting for transfers between devices: 15.4 us -> 12.9 us
  other arithmetic: 17.8 us -> 20.2 us
    pallas_call x2, Pallas kernels: 12.9 us -> 28 us  [product(): pl.pallas_call(lambda *refs: _product_kernel(eb0, spb, ring_map, side_map...]
    unnamed x55 -> x46, local copies, waits for them, and re-layouts: 18.7 us -> 4.41 us
    ppermute x3, waiting for transfers between devices: 5.03 us -> 0.01 us  [ring_step(): st['a'] = lax.ppermute(st['a'], 'limb', st['cw'])]
    ppermute x4, waiting for transfers between devices: 6.59 us -> 11.1 us  [_to_partner(): lax.ppermute(lax.dynamic_slice_in_dim(x, g, 1, axis=0), 'grp', [(0, 1), (...]
    ppermute x3, waiting for transfers between devices: 1.99 us -> 0.01 us  [ring_step(): st['b'] = lax.ppermute(st['b'], 'limb', st['ccw'])]
    add x6, other arithmetic: 0.69 us -> 2.62 us  [_limb_angle(): sin = sh[:, None] * cl[None] + ch[:, None] * sl[None]]
    dynamic_slice x1, local copies, waits for them, and re-layouts: 0.02 us -> 1.67 us  [_to_partner(): lax.dynamic_slice_in_dim(x, g, 1, axis=0)]
  transfers between devices with their start and end apart: 16 -> 16, of which waited for: 6 -> 3; matrix products, arithmetic and copies ran while one was open for 32% -> 26% of each run, Pallas kernels for 23% -> 31%
where the time goes in v4:
time: 139 us; the launch traced here: 137 us
  Pallas kernels  66.4 us (48%)
  local copies, waits for them, and re-layouts  20.7 us (15%)
  other arithmetic  20.2 us (15%)
  starting transfers between devices  13.5 us (10%)
  waiting for transfers between devices  12.9 us (9%)
  matrix products  3.18 us (2%)
    pallas_call x2, Pallas kernels, product(): pl.pallas_call(lambda *refs: _product_kernel(eb0, spb, ring_map, side_map...  28 us
    pallas_call x2, Pallas kernels, fwd_col(): pl.pallas_call(_fwd_col_kernel, grid=(groups, n // BLK), in_specs=[SMEM_S...  19.1 us
    ppermute x4, waiting for transfers between devices, _to_partner(): lax.ppermute(lax.dynamic_slice_in_dim(x, g, 1, axis=0), 'grp', [(0, 1), (...  11.1 us
    add x3, other arithmetic, _twiddle(): return 1.0 + 0.5 * (cp * cq - sp * sq)  11 us
    pallas_call x2, Pallas kernels, inv_col(): pl.pallas_call(_inv_col_kernel, grid=(n // BLK,), in_specs=[blk, blk, pl....  7.5 us
    pallas_call x2, Pallas kernels, inv_row(): pl.pallas_call(_inv_row_kernel, grid=(n // BLK,), in_specs=[SMEM_SPEC, bl...  7.41 us
    ppermute x3, starting transfers between devices, ring_step(): st['a'] = lax.ppermute(st['a'], 'limb', st['cw'])  6.78 us
    unnamed x46, local copies, waits for them, and re-layouts  4.41 us
  transfers between devices with their start and end apart: 16, of which 3 were waited for; matrix products, arithmetic and copies ran while one was open for 26% of the time, Pallas kernels for 31%

profile of v4, /device:TPU:0, one launch (start us, length us, event | category | flops | bytes accessed | tf_op | source)
XLA Modules:
  0.0 137.2 jit_solution(1678257318710959468)
XLA Ops:
  0.0 1.1 copy-done
  1.2 3.1 %collective-permute-start = (bf16[2,8,128,128]{3,2,1,0:T(8,128)(2,1)S(1)}, bf16[2,8,128,128]{3,2,1,0:T(8,128)(2,1)S(1)}, u32[]{:S(2)}, u32[]{:S(2)}) collective-permute-start(bf16[2,8,128,128]{3,2,1,0:T(8,128)(2,1)S(1)} %dynamic-slice_bitcast_fusion.refs_5_), channel_id=1, source_target_pairs={{0,4},{4,8},{8,12},{12,14},{14,10},{10,6},{6,2},{2,0},{1,5},{5,9},... | collective-permute-start | bytes 1572872 | tf_op jit(solution)/shard_map/ppermute | solution.py:351
  4.4 0.6 fusion.57
  5.5 2.9 %add_bitcast_fusion.1.w_ref = f32[64,128,128]{2,1,0:T(8,128)} fusion(f32[64,8,128]{2,1,0:T(8,128)S(1)} %bitcast.88, f32[64,16,128]{2,1,0:T(8,128)S(1)} %bitcast.86, f32[64,8,128]{2,1,0:T(8,128)S(1)} %bitcast.89, f32[64,16,128]{2,1,0:T(8,128)S(1)} %bitcast.87), kind=kLoop, calls=%fused_computation.8 | loop fusion | flops 5242880 | bytes 5767168 | tf_op jit(solution)/shard_map/add | solution.py:53
  8.4 4.8 %shard_map.100 = (bf16[48,64,128]{2,1,0:T(8,128)(2,1)}, bf16[48,64,128]{2,1,0:T(8,128)(2,1)}) custom-call(s32[1]{0:T(128)} %bitcast.me_ref, bf16[48,128,128]{2,1,0:T(8,128)(2,1)} %bitcast.75, f32[64,128,128]{2,1,0:T(8,128)} %add_bitcast_fusion.1.w_ref, bf16[128,128]{1,0:T(8,128)(2,1)} %constant.210.clone.ft_ref), custom_call_target="tpu_custom_call" | custom-call | tf_op jit(solution)/shard_map/pallas_call | solution.py:101
  13.6 2.4 %fusion.53 = (f32[8,8,256]{2,1,0:T(8,128)S(1)}, f32[8,8,256]{2,1,0:T(8,128)S(1)}, f32[8,8,256]{2,1,0:T(8,128)S(1)}, f32[8,8,256]{2,1,0:T(8,128)S(1)}, f32[8,8,25...) fusion(s32[8,256]{1,0:T(8,128)S(1)} %add_select_fusion.12, ...), kind=kLoop, calls=%fused_computation.130 | loop fusion | flops 1376256 | bytes 811072 | tf_op jit(solution)/shard_map/cos | solution.py:35
  16.3 1.1 multiply_add_fusion.2
  17.4 0.6 broadcast_bitcast_fusion.1
  18.0 2.1 %collective-permute-start.2 = (bf16[2,8,128,128]{3,2,1,0:T(8,128)(2,1)S(1)}, bf16[2,8,128,128]{3,2,1,0:T(8,128)(2,1)S(1)}, u32[]{:S(2)}, u32[]{:S(2)}) collective-permute-start(bf16[2,8,128,128]{3,2,1,0:T(8,128)(2,1)S(1)} %collective-permute-done.refs_6_), channel_id=1, source_target_pairs={{0,4},{4,8},{8,12},{12,14},{14,10},{10,6},{6,2},{2,0},{1,5},{5,9},... | collective-permute-start | bytes 1572872 | tf_op jit(solution)/shard_map/ppermute | solution.py:351
  20.1 0.8 fusion.9
  21.0 1.9 %collective-permute-start.4 = (bf16[1,16,128,128]{3,2,1,0:T(8,128)(2,1)}, bf16[1,16,128,128]{3,2,1,0:T(8,128)(2,1)S(1)}, u32[]{:S(2)}, u32[]{:S(2)}) collective-permute-start(bf16[1,16,128,128]{3,2,1,0:T(8,128)(2,1)} %fusion.9), channel_id=1, source_target_pairs={{0,16},{16,0},{1,17},{17,1},{2,18},{18,2},{3,19},{19,3},{4,20},{20... | collective-permute-start | bytes 1572872 | tf_op jit(solution)/shard_map/ppermute | solution.py:344
  22.9 0.6 broadcast_bitcast_fusion
  23.5 1.5 %copy.15 = f32[64,64]{1,0:T(8,128)} copy(f32[64,64]{0,1:T(8,128)} %broadcast_bitcast_fusion.1) | data formatting | bytes 32768 | tf_op jit(solution)/shard_map/mul | solution.py:53
  25.0 1.4 %copy.16 = f32[64,64]{1,0:T(8,128)} copy(f32[64,64]{0,1:T(8,128)} %broadcast_bitcast_fusion) | data formatting | bytes 32768 | tf_op jit(solution)/shard_map/mul | solution.py:53
  26.4 1.5 %constant_dynamic-slice_fusion.1 = (bf16[128,256]{1,0:T(8,128)(2,1)}, bf16[128,256]{1,0:T(8,128)(2,1)}) fusion(bf16[256,256]{1,0:T(8,128)(2,1)} %constant.208.clone, s32[]{:T(128)S(6)} %select_n.327, s32[]{:T(128)S(6)} %select_n.326), kind=kLoop, calls=%fused_computation.194 | loop fusion | bytes 262152 | tf_op jit(solution)/shard_map/dynamic_slice | solution.py:412
  27.9 4.7 %fusion.3.v_ref = f32[64,64,256]{2,1,0:T(8,128)} fusion(f32[64,64]{1,0:T(8,128)} %copy.16, f32[64,8,256]{2,1,0:T(8,128)} %bitcast.84, f32[64,64]{1,0:T(8,128)} %copy.15, f32[64,8,256]{2,1,0:T(8,128)} %bitcast.85), kind=kLoop, calls=%fused_computation.5 | loop fusion | flops 5242880 | bytes 5275648 | tf_op jit(solution)/shard_map/add | solution.py:53
  32.7 4.9 %shard_map.101 = bf16[48,64,256]{2,1,0:T(8,128)(2,1)} custom-call(bf16[48,64,128]{2,1,0:T(8,128)(2,1)} %get-tuple-element.47.own_ref, bf16[48,64,128]{2,1,0:T(8,128)(2,1)} %collective-permute-done.5.recv_ref, f32[64,64,256]{2,1,0:T(8,128)} %fusion.3.v_ref, bf16[128,256]{1,0:T(8,128)(2,1)} %get-tuple-element.84.fo_ref, bf16[128,256]{1,0:T(8,128)(2,1)} %get-tuple-element.83.fr_ref), custom_call_target="tpu_custom_call" | custom-call | tf_op jit(solution)/shard_map/pallas_call | solution.py:131
  37.6 1.6 %collective-permute-start.6 = (bf16[2,8,128,128]{3,2,1,0:T(8,128)(2,1)S(1)}, bf16[2,8,128,128]{3,2,1,0:T(8,128)(2,1)S(1)}, u32[]{:S(2)}, u32[]{:S(2)}) collective-permute-start(bf16[2,8,128,128]{3,2,1,0:T(8,128)(2,1)S(1)} %collective-permute-done.2.refs_8_), channel_id=1, source_target_pairs={{0,4},{4,8},{8,12},{12,14},{14,10},{10,6},{6,2},{2,0},{1,5},{5,9},... | collective-permute-start | bytes 1572872 | tf_op jit(solution)/shard_map/ppermute | solution.py:351
  40.0 1.1 multiply_add_fusion.1
  41.1 1.5 %fusion.5 = bf16[3,64,256,48]{2,3,1,0:T(8,128)(2,1)S(1)} fusion(bf16[3,16,64,256]{3,2,1,0:T(8,128)(2,1)S(1)} %bitcast.78, bf16[3,48,16]{1,2,0:T(8,128)(2,1)S(1)} %copy-done.19), kind=kOutput, calls=%fused_computation.11 | convolution fusion | flops 75497472 | bytes 6296064 | tf_op jit(solution)/shard_map/dot_general | solution.py:424
  42.7 4.0 %copy.32 = bf16[3,64,256,48]{2,1,3,0:T(8,128)(2,1)} copy(bf16[3,64,256,48]{2,3,1,0:T(8,128)(2,1)S(1)} %fusion.5) | data formatting | bytes 9437184 | tf_op jit(solution)/shard_map/dot_general | solution.py:424
  46.7 6.0 %collective-permute-done.8.refs_15_ = bf16[1,16,128,128]{3,2,1,0:T(8,128)(2,1)S(1)} collective-permute-done((bf16[1,16,128,128]{3,2,1,0:T(8,128)(2,1)S(1)}, bf16[1,16,128,128]{3,2,1,0:T(8,128)(2,1)S(1)}, u32[]{:S(2)}, u32[]{:S(2)}) %collective-permute-start.8) | collective-permute-done | bytes 524320 | tf_op jit(solution)/shard_map/ppermute | solution.py:344
  53.8 1.5 %collective-permute-start.10 = (bf16[2,8,64,128]{3,2,1,0:T(8,128)(2,1)S(1)}, bf16[2,8,64,128]{3,2,1,0:T(8,128)(2,1)S(1)}, u32[]{:S(2)}, u32[]{:S(2)}) collective-permute-start(bf16[2,8,64,128]{3,2,1,0:T(8,128)(2,1)S(1)} %slice.7), channel_id=1, source_target_pairs={{0,2},{4,0},{8,4},{12,8},{14,12},{10,14},{6,10},{2,6},{1,3},{5,1},... | collective-permute-start | bytes 786440 | tf_op jit(solution)/shard_map/ppermute | solution.py:357
  55.2 0.6 collective-permute-start.9
  55.8 3.3 %add_bitcast_fusion.w_ref = f32[64,64,256]{2,1,0:T(8,128)} fusion(f32[64,8,256]{2,1,0:T(8,128)S(1)} %bitcast.82, f32[64,8,256]{2,1,0:T(8,128)S(1)} %bitcast.80, f32[64,8,256]{2,1,0:T(8,128)S(1)} %bitcast.83, f32[64,8,256]{2,1,0:T(8,128)S(1)} %bitcast.81), kind=kLoop, calls=%fused_computation.7 | loop fusion | flops 5242880 | bytes 6291456 | tf_op jit(solution)/shard_map/add | solution.py:53
  59.1 13.4 %shard_map.102 = (bf16[3,48,64,128]{3,2,1,0:T(8,128)(2,1)}, bf16[3,48,64,128]{3,2,1,0:T(8,128)(2,1)}) custom-call(s32[1]{0:T(128)} %bitcast.me_ref, bf16[3,48,64,256]{3,2,1,0:T(8,128)(2,1)} %bitcast.74, f32[64,64,256]{2,1,0:T(8,128)} %fusion.3.v_ref, f32[64,64,256]{2,1,0:T(8,128)} %add_bitcast_fusion.w_ref, bf16[256,256]{1,0:T(8,128)(2,1)} %constant.211.clone.ft_ref), custom_call_target="tpu_custom_call" | custom-call | tf_op jit(solution)/shard_map/pallas_call | solution.py:161
  72.6 0.8 pad_maximum_fusion.refs_12_
  73.4 0.8 copy-done.12
  74.2 0.7 dynamic-slice_bitcast_fusion.1.refs_13_
  74.9 1.7 %constant_dynamic-slice_fusion = bf16[1,8,128,128]{3,2,1,0:T(8,128)(2,1)} fusion(bf16[2,8,128,128]{3,2,1,0:T(8,128)(2,1)} %pad_maximum_fusion.refs_12_, s32[]{:T(128)S(6)} %select_n.319), kind=kLoop, calls=%fused_computation.193 | loop fusion | bytes 524292 | tf_op jit(solution)/shard_map/dynamic_slice | solution.py:344
  76.6 1.4 %collective-permute-start.12 = (bf16[1,8,128,128]{3,2,1,0:T(8,128)(2,1)}, bf16[1,8,128,128]{3,2,1,0:T(8,128)(2,1)S(1)}, u32[]{:S(2)}, u32[]{:S(2)}) collective-permute-start(bf16[1,8,128,128]{3,2,1,0:T(8,128)(2,1)} %constant_dynamic-slice_fusion), channel_id=1, source_target_pairs={{0,16},{16,0},{1,17},{17,1},{2,18},{18,2},{3,19},{19,3},{4,20},{20... | collective-permute-start | bytes 786440 | tf_op jit(solution)/shard_map/ppermute | solution.py:344
  78.0 0.7 constant_dynamic-slice_fusion.3
  78.7 0.6 dynamic_slice.39
  79.3 1.1 compare_select_fusion.6.refs_0_
  80.5 5.1 %collective-permute-done.12.refs_17_ = bf16[1,8,128,128]{3,2,1,0:T(8,128)(2,1)S(1)} collective-permute-done((bf16[1,8,128,128]{3,2,1,0:T(8,128)(2,1)}, bf16[1,8,128,128]{3,2,1,0:T(8,128)(2,1)S(1)}, u32[]{:S(2)}, u32[]{:S(2)}) %collective-permute-start.12) | collective-permute-done | bytes 262176 | tf_op jit(solution)/shard_map/ppermute | solution.py:344
  85.5 0.7 copy-done.13
  86.2 0.8 copy-done.1
  87.0 8.5 %shard_map.103.y_ref = bf16[16,128,128]{2,1,0:T(8,128)(2,1)} custom-call(s32[8]{0:T(128)} %compare_select_fusion.6.refs_0_, s32[1]{0:T(128)} %bitcast.2.refs_1_, bf16[128,64]{1,0:T(8,128)(2,1)} %get-tuple-element.88.refs_2_.fo_ref, bf16[128,64]{1,0:T(8,128)(2,1)} %get-tuple-element.87.refs_3_.fr_ref, bf16[48,128,128]{2,1,0:T(8,128)(2,1)} %bitcast.76, ...), custom_call_target="tpu_custom_call" | custom-call | tf_op jit(solution)/shard_map/pallas_call | solution.py:263
  95.5 2.6 %shard_map.104 = (bf16[16,64,128]{2,1,0:T(8,128)(2,1)}, bf16[16,64,128]{2,1,0:T(8,128)(2,1)}) custom-call(s32[1]{0:T(128)} %bitcast.me_ref, bf16[16,128,128]{2,1,0:T(8,128)(2,1)} %shard_map.103.y_ref, f32[64,128,128]{2,1,0:T(8,128)} %add_bitcast_fusion.1.w_ref, bf16[128,128]{1,0:T(8,128)(2,1)} %constant.210.clone.ft_ref), custom_call_target="tpu_custom_call" | custom-call | tf_op jit(solution)/shard_map/pallas_call | solution.py:101
  98.1 1.7 %collective-permute-done.14.recv_ref = bf16[16,64,128]{2,1,0:T(8,128)(2,1)S(1)} collective-permute-done((bf16[16,64,128]{2,1,0:T(8,128)(2,1)}, bf16[16,64,128]{2,1,0:T(8,128)(2,1)S(1)}, u32[]{:S(2)}, u32[]{:S(2)}) %collective-permute-start.14) | collective-permute-done | bytes 262176 | tf_op jit(solution)/shard_map/ppermute | solution.py:391
  99.9 0.7 copy-done.17
  100.6 2.6 %shard_map.105 = bf16[16,64,256]{2,1,0:T(8,128)(2,1)} custom-call(bf16[16,64,128]{2,1,0:T(8,128)(2,1)} %get-tuple-element.71.own_ref, bf16[16,64,128]{2,1,0:T(8,128)(2,1)} %copy-done.17, f32[64,64,256]{2,1,0:T(8,128)} %fusion.3.v_ref, bf16[128,256]{1,0:T(8,128)(2,1)} %get-tuple-element.84.fo_ref, bf16[128,256]{1,0:T(8,128)(2,1)} %get-tuple-element.83.fr_ref), custom_call_target="tpu_custom_call" | custom-call | tf_op jit(solution)/shard_map/pallas_call | solution.py:131
  103.2 1.6 %fusion.10 = bf16[64,256,48]{1,2,0:T(8,128)(2,1)S(1)} fusion(bf16[16,64,256]{2,1,0:T(8,128)(2,1)} %shard_map.105, bf16[48,16]{0,1:T(8,128)(2,1)S(1)} %copy-done.20), kind=kOutput, calls=%fused_computation.23 | convolution fusion | flops 25165824 | bytes 2098688 | tf_op jit(solution)/shard_map/dot_general | solution.py:446
  104.9 1.7 %copy.33 = bf16[64,256,48]{1,0,2:T(8,128)(2,1)} copy(bf16[64,256,48]{1,2,0:T(8,128)(2,1)S(1)} %fusion.10) | data formatting | bytes 3145728 | tf_op jit(solution)/shard_map/dot_general | solution.py:446
  106.6 5.7 %shard_map.106 = (bf16[1,48,64,128]{3,2,1,0:T(8,128)(2,1)}, bf16[1,48,64,128]{3,2,1,0:T(8,128)(2,1)}) custom-call(s32[1]{0:T(128)} %bitcast.me_ref, bf16[1,48,64,256]{3,2,1,0:T(8,128)(2,1)} %bitcast.79, f32[64,64,256]{2,1,0:T(8,128)} %fusion.3.v_ref, f32[64,64,256]{2,1,0:T(8,128)} %add_bitcast_fusion.w_ref, bf16[256,256]{1,0:T(8,128)(2,1)} %constant.211.clone.ft_ref), custom_call_target="tpu_custom_call" | custom-call | tf_op jit(solution)/shard_map/pallas_call | solution.py:161
  112.4 19.4 %shard_map.107.prod_ref = bf16[48,128,128]{2,1,0:T(8,128)(2,1)} custom-call(s32[8]{0:T(128)} %compare_select_fusion.6.refs_0_, s32[1]{0:T(128)} %bitcast.2.refs_1_, bf16[128,64]{1,0:T(8,128)(2,1)} %get-tuple-element.88.refs_2_.fo_ref, bf16[128,64]{1,0:T(8,128)(2,1)} %get-tuple-element.87.refs_3_.fr_ref, bf16[48,128,128]{2,1,0:T(8,128)(2,1)} %bitcast.77, ...), custom_call_target="tpu_custom_call" | custom-call | tf_op jit(solution)/shard_map/pallas_call | solution.py:263
  131.9 0.9 broadcast_in_dim.10.s_ref
  132.8 4.4 %shard_map.108 = bf16[48,128,128]{2,1,0:T(8,128)(2,1)} custom-call(bf16[128,64]{1,0:T(8,128)(2,1)} %get-tuple-element.88.refs_2_.fo_ref, bf16[128,64]{1,0:T(8,128)(2,1)} %get-tuple-element.87.refs_3_.fr_ref, bf16[48,64,128]{2,1,0:T(8,128)(2,1)} %bitcast.90, bf16[48,64,128]{2,1,0:T(8,128)(2,1)} %bitcast.91, bf16[48,128,128]{2,1,0:T(8,128)(2,1)} %shard_map.107.prod_ref, ...), custom_call_target="tpu_custom_call" | custom-call | tf_op jit(solution)/shard_map/pallas_call | solution.py:284
  (86 shorter events, 3.2 us)
Async XLA Ops:
  0.0 1.1 copy-start
  1.2 12.1 %copy-start.9 = (bf16[2,8,128,128]{3,2,1,0:T(8,128)(2,1)}, bf16[2,8,128,128]{3,2,1,0:T(8,128)(2,1)S(1)}, u32[]{:S(2)}) copy-start(bf16[2,8,128,128]{3,2,1,0:T(8,128)(2,1)S(1)} %dynamic-slice_bitcast_fusion.refs_5_) | copy-start | bytes 1572868
  1.2 16.8 %collective-permute-start = (bf16[2,8,128,128]{3,2,1,0:T(8,128)(2,1)S(1)}, bf16[2,8,128,128]{3,2,1,0:T(8,128)(2,1)S(1)}, u32[]{:S(2)}, u32[]{:S(2)}) collective-permute-start(bf16[2,8,128,128]{3,2,1,0:T(8,128)(2,1)S(1)} %dynamic-slice_bitcast_fusion.refs_5_), channel_id=1, source_target_pairs={{0,4},{4,8},{8,12},{12,14},{14,10},{10,6},{6,2},{2,0},{1,5},{5,9},... | collective-permute-start | bytes 1572872 | tf_op jit(solution)/shard_map/ppermute | solution.py:351
  4.3 13.8 %collective-permute-start.1 = (bf16[2,8,128,128]{3,2,1,0:T(8,128)(2,1)S(1)}, bf16[2,8,128,128]{3,2,1,0:T(8,128)(2,1)S(1)}, u32[]{:S(2)}, u32[]{:S(2)}) collective-permute-start(bf16[2,8,128,128]{3,2,1,0:T(8,128)(2,1)S(1)} %dynamic-slice_bitcast_fusion.refs_5_), channel_id=1, source_target_pairs={{0,2},{4,0},{8,4},{12,8},{14,12},{10,14},{6,10},{2,6},{1,3},{5,1},... | collective-permute-start | bytes 1572872 | tf_op jit(solution)/shard_map/ppermute | solution.py:352
  13.2 19.4 %collective-permute-start.5 = (bf16[48,64,128]{2,1,0:T(8,128)(2,1)}, bf16[48,64,128]{2,1,0:T(8,128)(2,1)}, u32[]{:S(2)}, u32[]{:S(2)}) collective-permute-start(bf16[48,64,128]{2,1,0:T(8,128)(2,1)} %get-tuple-element.48), channel_id=1, source_target_pairs={{0,1},{1,0},{2,3},{3,2},{4,5},{5,4},{6,7},{7,6},{8,9},{9,8},{10,11... | collective-permute-start | bytes 2359304 | tf_op jit(solution)/shard_map/ppermute | solution.py:391
  18.0 19.5 %copy-start.5 = (bf16[2,8,128,128]{3,2,1,0:T(8,128)(2,1)}, bf16[2,8,128,128]{3,2,1,0:T(8,128)(2,1)S(1)}, u32[]{:S(2)}) copy-start(bf16[2,8,128,128]{3,2,1,0:T(8,128)(2,1)S(1)} %collective-permute-done.refs_6_) | copy-start | bytes 1572868
  18.0 19.5 %copy-start.6 = (bf16[2,8,128,128]{3,2,1,0:T(8,128)(2,1)}, bf16[2,8,128,128]{3,2,1,0:T(8,128)(2,1)S(1)}, u32[]{:S(2)}) copy-start(bf16[2,8,128,128]{3,2,1,0:T(8,128)(2,1)S(1)} %collective-permute-done.1.refs_7_) | copy-start | bytes 1572868
  18.0 19.5 %collective-permute-start.2 = (bf16[2,8,128,128]{3,2,1,0:T(8,128)(2,1)S(1)}, bf16[2,8,128,128]{3,2,1,0:T(8,128)(2,1)S(1)}, u32[]{:S(2)}, u32[]{:S(2)}) collective-permute-start(bf16[2,8,128,128]{3,2,1,0:T(8,128)(2,1)S(1)} %collective-permute-done.refs_6_), channel_id=1, source_target_pairs={{0,4},{4,8},{8,12},{12,14},{14,10},{10,6},{6,2},{2,0},{1,5},{5,9},... | collective-permute-start | bytes 1572872 | tf_op jit(solution)/shard_map/ppermute | solution.py:351
  20.1 17.5 %collective-permute-start.3 = (bf16[2,8,128,128]{3,2,1,0:T(8,128)(2,1)S(1)}, bf16[2,8,128,128]{3,2,1,0:T(8,128)(2,1)S(1)}, u32[]{:S(2)}, u32[]{:S(2)}) collective-permute-start(bf16[2,8,128,128]{3,2,1,0:T(8,128)(2,1)S(1)} %collective-permute-done.1.refs_7_), channel_id=1, source_target_pairs={{0,2},{4,0},{8,4},{12,8},{14,12},{10,14},{6,10},{2,6},{1,3},{5,1},... | collective-permute-start | bytes 1572872 | tf_op jit(solution)/shard_map/ppermute | solution.py:352
  21.0 16.6 %collective-permute-start.4 = (bf16[1,16,128,128]{3,2,1,0:T(8,128)(2,1)}, bf16[1,16,128,128]{3,2,1,0:T(8,128)(2,1)S(1)}, u32[]{:S(2)}, u32[]{:S(2)}) collective-permute-start(bf16[1,16,128,128]{3,2,1,0:T(8,128)(2,1)} %fusion.9), channel_id=1, source_target_pairs={{0,16},{16,0},{1,17},{17,1},{2,18},{18,2},{3,19},{19,3},{4,20},{20... | collective-permute-start | bytes 1572872 | tf_op jit(solution)/shard_map/ppermute | solution.py:344
  32.7 8.4 %copy-start.19 = (bf16[3,48,16]{1,2,0:T(8,128)(2,1)S(1)}, bf16[3,48,16]{1,2,0:T(8,128)(2,1)}, u32[]{:S(2)}) copy-start(bf16[3,48,16]{1,2,0:T(8,128)(2,1)} %param.12) | copy-start | bytes 13828
  37.6 3.5 %copy-start.2 = (bf16[48,64,256]{2,1,0:T(8,128)(2,1)S(1)}, bf16[48,64,256]{2,1,0:T(8,128)(2,1)}, u32[]{:S(2)}) copy-start(bf16[48,64,256]{2,1,0:T(8,128)(2,1)} %shard_map.101) | copy-start | bytes 4718596
  37.6 5.0 %copy-start.10 = (bf16[1,16,128,128]{3,2,1,0:T(8,128)(2,1)}, bf16[1,16,128,128]{3,2,1,0:T(8,128)(2,1)S(1)}, u32[]{:S(2)}) copy-start(bf16[1,16,128,128]{3,2,1,0:T(8,128)(2,1)S(1)} %collective-permute-done.4.refs_14_) | copy-start | bytes 1572868
  37.6 5.0 %copy-start.7 = (bf16[2,8,128,128]{3,2,1,0:T(8,128)(2,1)}, bf16[2,8,128,128]{3,2,1,0:T(8,128)(2,1)S(1)}, u32[]{:S(2)}) copy-start(bf16[2,8,128,128]{3,2,1,0:T(8,128)(2,1)S(1)} %collective-permute-done.2.refs_8_) | copy-start | bytes 1572868
  37.6 5.0 %copy-start.8 = (bf16[2,8,128,128]{3,2,1,0:T(8,128)(2,1)}, bf16[2,8,128,128]{3,2,1,0:T(8,128)(2,1)S(1)}, u32[]{:S(2)}) copy-start(bf16[2,8,128,128]{3,2,1,0:T(8,128)(2,1)S(1)} %collective-permute-done.3.refs_9_) | copy-start | bytes 1572868
  37.6 15.1 %collective-permute-start.6 = (bf16[2,8,128,128]{3,2,1,0:T(8,128)(2,1)S(1)}, bf16[2,8,128,128]{3,2,1,0:T(8,128)(2,1)S(1)}, u32[]{:S(2)}, u32[]{:S(2)}) collective-permute-start(bf16[2,8,128,128]{3,2,1,0:T(8,128)(2,1)S(1)} %collective-permute-done.2.refs_8_), channel_id=1, source_target_pairs={{0,4},{4,8},{8,12},{12,14},{14,10},{10,6},{6,2},{2,0},{1,5},{5,9},... | collective-permute-start | bytes 1572872 | tf_op jit(solution)/shard_map/ppermute | solution.py:351
  39.3 13.4 %collective-permute-start.7 = (bf16[2,8,128,128]{3,2,1,0:T(8,128)(2,1)S(1)}, bf16[2,8,128,128]{3,2,1,0:T(8,128)(2,1)S(1)}, u32[]{:S(2)}, u32[]{:S(2)}) collective-permute-start(bf16[2,8,128,128]{3,2,1,0:T(8,128)(2,1)S(1)} %collective-permute-done.3.refs_9_), channel_id=1, source_target_pairs={{0,2},{4,0},{8,4},{12,8},{14,12},{10,14},{6,10},{2,6},{1,3},{5,1},... | collective-permute-start | bytes 1572872 | tf_op jit(solution)/shard_map/ppermute | solution.py:352
  39.8 12.9 %collective-permute-start.8 = (bf16[1,16,128,128]{3,2,1,0:T(8,128)(2,1)S(1)}, bf16[1,16,128,128]{3,2,1,0:T(8,128)(2,1)S(1)}, u32[]{:S(2)}, u32[]{:S(2)}) collective-permute-start(bf16[1,16,128,128]{3,2,1,0:T(8,128)(2,1)S(1)} %fusion.8), channel_id=1, source_target_pairs={{0,16},{16,0},{1,17},{17,1},{2,18},{18,2},{3,19},{19,3},{4,20},{20... | collective-permute-start | bytes 1572872 | tf_op jit(solution)/shard_map/ppermute | solution.py:344
  42.7 10.7 %copy-start.15 = (f32[8,8,256]{2,1,0:T(8,128)S(1)}, f32[8,8,256]{2,1,0:T(8,128)}, u32[]{:S(2)}) copy-start(f32[8,8,256]{2,1,0:T(8,128)} %get-tuple-element.123) | copy-start | bytes 196612
  42.7 10.7 %copy-start.16 = (f32[8,8,256]{2,1,0:T(8,128)S(1)}, f32[8,8,256]{2,1,0:T(8,128)}, u32[]{:S(2)}) copy-start(f32[8,8,256]{2,1,0:T(8,128)} %get-tuple-element.124) | copy-start | bytes 196612
  52.7 2.5 %copy-start.11 = (bf16[1,16,128,128]{3,2,1,0:T(8,128)(2,1)}, bf16[1,16,128,128]{3,2,1,0:T(8,128)(2,1)S(1)}, u32[]{:S(2)}) copy-start(bf16[1,16,128,128]{3,2,1,0:T(8,128)(2,1)S(1)} %collective-permute-done.8.refs_15_) | copy-start | bytes 1572868
  52.7 0.8 copy-start.3
  52.8 1.0 copy-start.4
  52.8 20.6 %collective-permute-start.11 = (bf16[1,16,128,128]{3,2,1,0:T(8,128)(2,1)S(1)}, bf16[1,16,128,128]{3,2,1,0:T(8,128)(2,1)S(1)}, u32[]{:S(2)}, u32[]{:S(2)}) collective-permute-start(bf16[1,16,128,128]{3,2,1,0:T(8,128)(2,1)S(1)} %fusion.7), channel_id=1, source_target_pairs={{0,16},{16,0},{1,17},{17,1},{2,18},{18,2},{3,19},{19,3},{4,20},{20... | collective-permute-start | bytes 1572872 | tf_op jit(solution)/shard_map/ppermute | solution.py:344
  53.8 18.8 %collective-permute-start.10 = (bf16[2,8,64,128]{3,2,1,0:T(8,128)(2,1)S(1)}, bf16[2,8,64,128]{3,2,1,0:T(8,128)(2,1)S(1)}, u32[]{:S(2)}, u32[]{:S(2)}) collective-permute-start(bf16[2,8,64,128]{3,2,1,0:T(8,128)(2,1)S(1)} %slice.7), channel_id=1, source_target_pairs={{0,2},{4,0},{8,4},{12,8},{14,12},{10,14},{6,10},{2,6},{1,3},{5,1},... | collective-permute-start | bytes 786440 | tf_op jit(solution)/shard_map/ppermute | solution.py:357
  55.2 17.3 %collective-permute-start.9 = (bf16[2,8,64,128]{3,2,1,0:T(8,128)(2,1)S(1)}, bf16[2,8,64,128]{3,2,1,0:T(8,128)(2,1)S(1)}, u32[]{:S(2)}, u32[]{:S(2)}) collective-permute-start(bf16[2,8,64,128]{3,2,1,0:T(8,128)(2,1)S(1)} %slice.6), channel_id=1, source_target_pairs={{0,4},{4,8},{8,12},{12,14},{14,10},{10,6},{6,2},{2,0},{1,5},{5,9},... | collective-permute-start | bytes 786440 | tf_op jit(solution)/shard_map/ppermute | solution.py:356
  59.1 18.9 %copy-start.18 = (bf16[128,128]{1,0:T(8,128)(2,1)S(1)}, bf16[128,128]{1,0:T(8,128)(2,1)}, u32[]{:S(2)}) copy-start(bf16[128,128]{1,0:T(8,128)(2,1)} %constant.209.clone) | copy-start | bytes 98308
  59.1 19.6 %copy-start.22 = (s32[8]{0:T(128)S(1)}, s32[8]{0:T(128)}, u32[]{:S(2)}) copy-start(s32[8]{0:T(128)} %constant.207.clone) | copy-start | bytes 100
  73.4 0.8 copy-start.12
  74.2 11.3 %collective-permute-start.13 = (bf16[3,48,64,128]{3,2,1,0:T(8,128)(2,1)}, bf16[3,48,64,128]{3,2,1,0:T(8,128)(2,1)S(1)}, u32[]{:S(2)}, u32[]{:S(2)}) collective-permute-start(bf16[3,48,64,128]{3,2,1,0:T(8,128)(2,1)} %get-tuple-element.70), channel_id=1, source_target_pairs={{0,1},{1,0},{2,3},{3,2},{4,5},{5,4},{6,7},{7,6},{8,9},{9,8},{10,11... | collective-permute-start | bytes 7077896 | tf_op jit(solution)/shard_map/ppermute | solution.py:391
  76.6 8.9 %collective-permute-start.12 = (bf16[1,8,128,128]{3,2,1,0:T(8,128)(2,1)}, bf16[1,8,128,128]{3,2,1,0:T(8,128)(2,1)S(1)}, u32[]{:S(2)}, u32[]{:S(2)}) collective-permute-start(bf16[1,8,128,128]{3,2,1,0:T(8,128)(2,1)} %constant_dynamic-slice_fusion), channel_id=1, source_target_pairs={{0,16},{16,0},{1,17},{17,1},{2,18},{18,2},{3,19},{19,3},{4,20},{20... | collective-permute-start | bytes 786440 | tf_op jit(solution)/shard_map/ppermute | solution.py:344
  85.5 0.7 copy-start.13
  85.5 1.5 %copy-start.1 = (bf16[3,48,64,128]{3,2,1,0:T(8,128)(2,1)}, bf16[3,48,64,128]{3,2,1,0:T(8,128)(2,1)S(1)}, u32[]{:S(2)}) copy-start(bf16[3,48,64,128]{3,2,1,0:T(8,128)(2,1)S(1)} %collective-permute-done.13.refs_19_.refs_21_.refs_23_) | copy-start | bytes 7077892
  95.5 7.7 %copy-start.20 = (bf16[48,16]{0,1:T(8,128)(2,1)S(1)}, bf16[48,16]{0,1:T(8,128)(2,1)}, u32[]{:S(2)}) copy-start(bf16[48,16]{0,1:T(8,128)(2,1)} %param.13) | copy-start | bytes 4612
  98.1 1.7 %collective-permute-start.14 = (bf16[16,64,128]{2,1,0:T(8,128)(2,1)}, bf16[16,64,128]{2,1,0:T(8,128)(2,1)S(1)}, u32[]{:S(2)}, u32[]{:S(2)}) collective-permute-start(bf16[16,64,128]{2,1,0:T(8,128)(2,1)} %get-tuple-element.72), channel_id=1, source_target_pairs={{0,1},{1,0},{2,3},{3,2},{4,5},{5,4},{6,7},{7,6},{8,9},{9,8},{10,11... | collective-permute-start | bytes 786440 | tf_op jit(solution)/shard_map/ppermute | solution.py:391
  99.9 0.7 copy-start.17
  112.3 19.6 %copy-start.21 = (f32[48]{0:T(128)S(1)}, f32[48]{0:T(128)}, u32[]{:S(2)}) copy-start(f32[48]{0:T(128)} %param.14) | copy-start | bytes 580
  112.3 19.6 %collective-permute-start.15 = (bf16[1,48,64,128]{3,2,1,0:T(8,128)(2,1)}, bf16[1,48,64,128]{3,2,1,0:T(8,128)(2,1)S(1)}, u32[]{:S(2)}, u32[]{:S(2)}) collective-permute-start(bf16[1,48,64,128]{3,2,1,0:T(8,128)(2,1)} %get-tuple-element.74), channel_id=1, source_target_pairs={{0,1},{1,0},{2,3},{3,2},{4,5},{5,4},{6,7},{7,6},{8,9},{9,8},{10,11... | collective-permute-start | bytes 2359304 | tf_op jit(solution)/shard_map/ppermute | solution.py:391
  131.8 0.9 copy-start.14

commit v5 on v3

--- a/solution.py
+++ b/solution.py
@@ -167,91 +167,67 @@
     )(me_arr, x, v_row, w_row, ft)
 
 
-def _product_kernel(eb0, spb, slot_ref, g_ref, fo_ref, fr_ref, cip_ref, *rest):
-    ring_refs = rest[:spb]
-    side_refs = rest[spb : 2 * spb]
-    halves = rest[2 * spb : 2 * spb + 2 * DIGITS]
-    out_ref, acc_ref = rest[2 * spb + 2 * DIGITS :]
-    width = ring_refs[0].shape[1]
+def _product_kernel(eb0, g_ref, fo_ref, fr_ref, cip_ref, key_ref, *rest):
+    halves = rest[: 2 * DIGITS]
+    out_ref, acc_ref = rest[2 * DIGITS :]
     eb = pl.program_id(0) + eb0
     fo = fo_ref[...]
     fr = fr_ref[...]
     acc_ref[...] = jnp.zeros_like(acc_ref)
     n = acc_ref.shape[0]
-
-    def key(gv, j, l):
-        kd = (j - gv) % DIGITS
-        if kd < 2:
-            return ring_refs[l // width][kd, l % width]
-        return side_refs[l // width][0, l % width]
-
     for gv in range(2):
         for j in range(DIGITS):
             own_ref, recv_ref = halves[2 * j], halves[2 * j + 1]
+            kd = (j - gv) % DIGITS
 
             @pl.when(jnp.logical_and(g_ref[0] == gv, eb == j))
             def _():
-                for l in range(n):
-                    acc_ref[l] += cip_ref[l].astype(F32) * key(gv, j, l).astype(F32)
+                acc_ref[...] += cip_ref[...].astype(F32) * key_ref[kd].astype(F32)
 
             @pl.when(jnp.logical_and(g_ref[0] == gv, eb != j))
             def _():
                 for l in range(n):
                     y = jnp.dot(fo, own_ref[l], preferred_element_type=F32)
                     y = (y + jnp.dot(fr, recv_ref[l], preferred_element_type=F32)).astype(BF16)
-                    acc_ref[l] += y.astype(F32) * key(gv, j, l).astype(F32)
+                    acc_ref[l] += y.astype(F32) * key_ref[kd, l].astype(F32)
 
     out_ref[...] = acc_ref[...].astype(BF16)
 
 
-def product(cip, ring_key, side_key, slot, g_arr, own2, recv2, f_own, f_oth, eb0, nblocks):
+def product(cip, key, g_arr, own2, recv2, f_own, f_oth, eb0, nblocks):
     _, rows, cols_l = cip.shape
     rows_l = rows // 2
-    width = ring_key.shape[1] // slot.shape[0]
-    spb = BLK // width
 
     def lifted_block(j):
-        def index(i, slot_ref):
+        def index(i):
             eb = i + eb0
             tb = jnp.where(eb < j, eb, eb - 1)
             return (j, jnp.clip(tb, 0, DIGITS - 1), 0, 0)
 
         return pl.BlockSpec((None, BLK, rows_l, cols_l), index)
-
-    def key_block(r, depth):
-        return pl.BlockSpec(
-            (depth, width, rows, cols_l),
-            lambda i, slot_ref: (0, slot_ref[(i + eb0) * spb + r], 0, 0),
-        )
 
     half_specs = []
     half_args = []
     for j in range(DIGITS):
         half_specs += [lifted_block(j), lifted_block(j)]
         half_args += [own2, recv2]
-    grid_spec = pltpu.PrefetchScalarGridSpec(
-        num_scalar_prefetch=1,
+    return pl.pallas_call(
+        lambda *refs: _product_kernel(eb0, *refs),
         grid=(nblocks,),
         in_specs=[
             SMEM_SPEC,
-            pl.BlockSpec((rows, rows_l), lambda i, slot_ref: (0, 0)),
-            pl.BlockSpec((rows, rows_l), lambda i, slot_ref: (0, 0)),
+            pl.BlockSpec((rows, rows_l), lambda i: (0, 0)),
+            pl.BlockSpec((rows, rows_l), lambda i: (0, 0)),
             pl.BlockSpec(
-                (BLK, rows, cols_l),
-                lambda i, slot_ref: (jnp.minimum(i + eb0, DIGITS - 1), 0, 0),
+                (BLK, rows, cols_l), lambda i: (jnp.minimum(i + eb0, DIGITS - 1), 0, 0)
             ),
+            pl.BlockSpec((DIGITS, BLK, rows, cols_l), lambda i: (0, i + eb0, 0, 0)),
         ]
-        + [key_block(r, 2) for r in range(spb)]
-        + [key_block(r, 1) for r in range(spb)]
         + half_specs,
-        out_specs=pl.BlockSpec((BLK, rows, cols_l), lambda i, slot_ref: (i, 0, 0)),
+        out_specs=pl.BlockSpec((BLK, rows, cols_l), lambda i: (i, 0, 0)),
+        out_shape=jax.ShapeDtypeStruct((nblocks * BLK, rows, cols_l), BF16),
         scratch_shapes=[pltpu.VMEM((BLK, rows, cols_l), F32)],
-    )
-    return pl.pallas_call(
-        lambda *refs: _product_kernel(eb0, spb, *refs),
-        grid_spec=grid_spec,
-        out_shape=jax.ShapeDtypeStruct((nblocks * BLK, rows, cols_l), BF16),
-    )(slot, g_arr, f_own, f_oth, cip, *([ring_key] * spb), *([side_key] * spb), *half_args)
+    )(g_arr, f_own, f_oth, cip, key, *half_args)
 
 
 def _final_kernel(fo_ref, fr_ref, own_ref, recv_ref, prod_ref, s_ref, out_ref):
@@ -299,22 +275,22 @@
     pos = [0] * n
     for i, l in enumerate(order):
         pos[l] = i
-    pos_arr = jnp.array(pos, I32)
-    p = pos_arr[me_l]
-    d = (pos_arr - p) % n
-    half = (n - 1) // 2
-    slot = jnp.where(d == 0, 0, jnp.where(d <= half, 2 * d, 2 * (n - d) - 1))
-    if n % 2 == 0:
-        slot = jnp.where(d == n // 2, n - 1, slot)
+    p = jnp.array(pos, I32)[me_l]
     piece = lax.dynamic_slice_in_dim(shard, g, 2, axis=0)
+    width = shard.shape[1]
+    full = jnp.zeros((DIGITS, n * width) + shard.shape[2:], shard.dtype)
+    full = lax.dynamic_update_slice(full, piece, (0, me_l * width, 0, 0))
+    own_side = lax.dynamic_slice_in_dim(shard, 2 - 2 * g, 1, axis=0)
+    full = lax.dynamic_update_slice(full, own_side, (2, me_l * width, 0, 0))
+    order_arr = jnp.array(order, I32)
     return dict(
+        full=full,
+        width=width,
+        src=[order_arr[(p - k) % n] * width for k in range(n)],
         n=n,
         g=g,
-        slot=slot.astype(I32),
         cw=[(order[i], order[(i + 1) % n]) for i in range(n)],
         ccw=[(order[i], order[(i - 1) % n]) for i in range(n)],
-        ring=[piece],
-        side=[lax.dynamic_slice_in_dim(shard, 2 - 2 * g, 1, axis=0)],
         a=piece,
         b=piece,
         s=0,
@@ -347,14 +323,28 @@
 
 def _settle(st, x):
     fresh, pending = st["fresh"], st["pending"]
-    fresh, pending, x = lax.optimization_barrier((fresh, pending, x))
-    st["side"] += pending
-    st["ring"] += fresh
+    fresh, pending, st["full"], x = lax.optimization_barrier((fresh, pending, st["full"], x))
+    _place(st, st["s"], fresh, 0)
+    _place(st, st["s"] - 1, pending, 2)
     if len(fresh) == 2:
         st["a"], st["b"] = fresh
     st["pending"] = [_to_partner(jnp.concatenate(fresh, axis=1), st["g"])]
     st["fresh"] = []
     return x
+
+
+def _place(st, s, pieces, digit):
+    if s < 1 or not pieces:
+        return
+    n, w = st["n"], st["width"]
+    if len(pieces) == 2:
+        parts = [(pieces[0], s), (pieces[1], -s)]
+    elif pieces[0].shape[1] == 2 * w:
+        parts = [(pieces[0][:, :w], s), (pieces[0][:, w:], -s)]
+    else:
+        parts = [(pieces[0], s)]
+    for part, k in parts:
+        st["full"] = lax.dynamic_update_slice(st["full"], part, (digit, st["src"][k % n], 0, 0))
 
 
 def ring_hold(st, x):
@@ -371,8 +361,8 @@
         ring_step(st)
     if st["fresh"]:
         x = _settle(st, x)
-    st["side"] += st["pending"]
-    return jnp.concatenate(st["ring"], axis=1), jnp.concatenate(st["side"], axis=1), x
+    _place(st, st["s"], st["pending"], 2)
+    return st["full"], x
 
 def swap(x):
     return lax.ppermute(x, "coef", perm=[(0, 1), (1, 0)])
@@ -416,17 +406,12 @@
     own2, send2 = fwd_col(
         me_arr, raised, v_row, w_row, ft_cols, lambda j, t: jnp.where(t >= j, t + 1, t)
     )
-    ring_key, side_key, (own2, send2) = ring_finish(ring, (own2, send2))
+    key, (own2, send2) = ring_finish(ring, (own2, send2))
     recv2 = swap(send2)
-    slot = ring["slot"]
     g_arr = jnp.reshape(ring["g"], (1,)).astype(I32)
 
-    prod_special = product(
-        ct, ring_key, side_key, slot, g_arr, own2, recv2, fr_own, fr_oth, DIGITS, 1
-    )
-    prod_cipher = product(
-        ct, ring_key, side_key, slot, g_arr, own2, recv2, fr_own, fr_oth, 0, DIGITS
-    )
+    prod_special = product(ct, key, g_arr, own2, recv2, fr_own, fr_oth, DIGITS, 1)
+    prod_cipher = product(ct, key, g_arr, own2, recv2, fr_own, fr_oth, 0, DIGITS)
 
     own3, send3 = inv_row(me_arr, prod_special, w_col, ft_rows, limbs)
     special = inv_col(own3, swap(send3), v_row, fc_own, fc_oth, limbs)

time: 136 us -> 140 us (1.029)
  between operations: 0.33 us -> 8.56 us
  waiting for transfers between devices: 15.4 us -> 7.32 us
  local copies, waits for them, and re-layouts: 33.4 us -> 36.6 us
  starting transfers between devices: 13.3 us -> 15.1 us
  other arithmetic: 17.8 us -> 16.3 us
    dynamic_update_slice x0 -> x16, local copies, waits for them, and re-layouts: none -> 16.4 us  [the longest x14 13.4 us: _place(): lax.dynamic_update_slice(st['full'], part, (digit, st['src'][k % n], 0, 0))]
    unnamed x55 -> x24, local copies, waits for them, and re-layouts: 18.7 us -> 3.01 us
    ppermute x3, waiting for transfers between devices: 5.03 us -> 0.01 us  [ring_step(): st['a'] = lax.ppermute(st['a'], 'limb', st['cw'])]
    broadcast_in_dim x0 -> x1, local copies, waits for them, and re-layouts: none -> 4.26 us  [ring_setup(): full = jnp.zeros((DIGITS, n * width) + shard.shape[2:], shard.dtype)]
    ppermute x4, waiting for transfers between devices: 6.59 us -> 4.39 us  [_to_partner(): lax.ppermute(lax.dynamic_slice_in_dim(x, g, 1, axis=0), 'grp', [(0, 1), (...]
    ppermute x4, starting transfers between devices: 3.95 us -> 5.74 us  [_to_partner(): lax.ppermute(lax.dynamic_slice_in_dim(x, g, 1, axis=0), 'grp', [(0, 1), (...]
    pallas_call x2, Pallas kernels: 12.9 us -> 11.4 us  [product(): pl.pallas_call(lambda *refs: _product_kernel(eb0, *refs), grid=(nblocks,)...]
  transfers between devices with their start and end apart: 16 -> 16, of which waited for: 6 -> 6; matrix products, arithmetic and copies ran while one was open for 32% -> 32% of each run, Pallas kernels for 23% -> 22%
where the time goes in v5:
time: 140 us; the launch traced here: 138 us
  Pallas kernels  50 us (36%)
  local copies, waits for them, and re-layouts  36.6 us (26%)
  other arithmetic  16.3 us (12%)
  starting transfers between devices  15.1 us (11%)
  between operations  8.56 us (6%)
  waiting for transfers between devices  7.32 us (5%)
  matrix products  4.52 us (3%)
    pallas_call x2, Pallas kernels, fwd_col(): pl.pallas_call(_fwd_col_kernel, grid=(groups, n // BLK), in_specs=[SMEM_S...  19.1 us
    dynamic_update_slice x14, local copies, waits for them, and re-layouts, _place(): lax.dynamic_update_slice(st['full'], part, (digit, st['src'][k % n], 0, 0))  13.4 us
    pallas_call x2, Pallas kernels, product(): pl.pallas_call(lambda *refs: _product_kernel(eb0, *refs), grid=(nblocks,)...  11.4 us
    add x3, other arithmetic, _twiddle(): return 1.0 + 0.5 * (cp * cq - sp * sq)  10.6 us
    pallas_call x2, Pallas kernels, inv_row(): pl.pallas_call(_inv_row_kernel, grid=(n // BLK,), in_specs=[SMEM_SPEC, bl...  7.62 us
    pallas_call x2, Pallas kernels, inv_col(): pl.pallas_call(_inv_col_kernel, grid=(n // BLK,), in_specs=[blk, blk, pl....  7.47 us
    ppermute x3, starting transfers between devices, ring_step(): st['a'] = lax.ppermute(st['a'], 'limb', st['cw'])  6.87 us
    ppermute x4, starting transfers between devices, _to_partner(): lax.ppermute(lax.dynamic_slice_in_dim(x, g, 1, axis=0), 'grp', [(0, 1), (...  5.74 us
  transfers between devices with their start and end apart: 16, of which 6 were waited for; matrix products, arithmetic and copies ran while one was open for 32% of the time, Pallas kernels for 22%

profile of v5, /device:TPU:0, one launch (start us, length us, event | category | flops | bytes accessed | tf_op | source)
XLA Modules:
  0.0 138.5 jit_solution(15178490175862060243)
XLA Ops:
  0.0 4.3 %broadcast_in_dim.8 = bf16[3,64,128,128]{3,2,1,0:T(8,128)(2,1)} broadcast(bf16[]{:T(256)} %constant.238.clone.1), dimensions={} | broadcast | bytes 6291458 | tf_op jit(solution)/shard_map/broadcast_in_dim | solution.py:281
  4.3 1.3 constant_dynamic-update-slice_fusion.8
  5.6 3.1 %collective-permute-start = (bf16[2,8,128,128]{3,2,1,0:T(8,128)(2,1)}, bf16[2,8,128,128]{3,2,1,0:T(8,128)(2,1)S(1)}, u32[]{:S(2)}, u32[]{:S(2)}) collective-permute-start(bf16[2,8,128,128]{3,2,1,0:T(8,128)(2,1)} %get-tuple-element.84), channel_id=1, source_target_pairs={{0,4},{4,8},{8,12},{12,14},{14,10},{10,6},{6,2},{2,0},{1,5},{5,9},... | collective-permute-start | bytes 1572872 | tf_op jit(solution)/shard_map/ppermute | solution.py:314
  10.0 2.8 %add_bitcast_fusion.1.w_ref = f32[64,128,128]{2,1,0:T(8,128)} fusion(f32[64,8,128]{2,1,0:T(8,128)S(1)} %bitcast.102, f32[64,16,128]{2,1,0:T(8,128)S(1)} %bitcast.100, f32[64,8,128]{2,1,0:T(8,128)S(1)} %bitcast.103, f32[64,16,128]{2,1,0:T(8,128)S(1)} %bitcast.101), kind=kLoop, calls=%fused_computation.8 | loop fusion | flops 5242880 | bytes 5767168 | tf_op jit(solution)/shard_map/add | solution.py:53
  12.8 4.8 %shard_map.109 = (bf16[48,64,128]{2,1,0:T(8,128)(2,1)}, bf16[48,64,128]{2,1,0:T(8,128)(2,1)}) custom-call(s32[1]{0:T(128)} %bitcast.me_ref, bf16[48,128,128]{2,1,0:T(8,128)(2,1)} %bitcast.89, f32[64,128,128]{2,1,0:T(8,128)} %add_bitcast_fusion.1.w_ref, bf16[128,128]{1,0:T(8,128)(2,1)} %constant.263.clone.ft_ref), custom_call_target="tpu_custom_call" | custom-call | tf_op jit(solution)/shard_map/pallas_call | solution.py:101
  18.2 1.6 %fusion.53 = (f32[8,8,256]{2,1,0:T(8,128)S(1)}, f32[8,8,256]{2,1,0:T(8,128)S(1)}, f32[8,8,256]{2,1,0:T(8,128)S(1)}, f32[8,8,256]{2,1,0:T(8,128)S(1)}, f32[8,8,25...) fusion(s32[8,256]{1,0:T(8,128)S(1)} %add_select_fusion.12, ...), kind=kLoop, calls=%fused_computation.136 | loop fusion | flops 1376256 | bytes 811072 | tf_op jit(solution)/shard_map/cos | solution.py:35
  19.8 1.1 multiply_add_fusion.2
  22.4 1.7 %bitcast_dynamic-update-slice_fusion = bf16[3,64,128,128]{3,2,1,0:T(8,128)(2,1)} fusion(bf16[3,64,128,128]{3,2,1,0:T(8,128)(2,1)} %get-tuple-element.83, s32[]{:T(128)S(6)} %select_n.374, bf16[1,3,8,128,128]{4,3,2,1,0:T(8,128)(2,1)} %param.12, s32[]{:T(128)S(6)} %select_n.375), kind=kLoop, calls=%fused_computation.34 | loop fusion | bytes 524296 | tf_op jit(solution)/shard_map/dynamic_update_slice | solution.py:284
  24.1 3.1 %add_bitcast_fusion.w_ref = f32[64,64,256]{2,1,0:T(8,128)} fusion(f32[64,8,256]{2,1,0:T(8,128)S(1)} %bitcast.96, f32[64,8,256]{2,1,0:T(8,128)S(1)} %bitcast.94, f32[64,8,256]{2,1,0:T(8,128)S(1)} %bitcast.97, f32[64,8,256]{2,1,0:T(8,128)S(1)} %bitcast.95), kind=kLoop, calls=%fused_computation.7 | loop fusion | flops 5242880 | bytes 6291456 | tf_op jit(solution)/shard_map/add | solution.py:53
  27.8 1.2 dynamic_slice.65
  37.5 0.8 copy.17
  38.4 0.8 copy.16
  39.2 2.1 %collective-permute-start.2 = (bf16[2,8,128,128]{3,2,1,0:T(8,128)(2,1)S(1)}, bf16[2,8,128,128]{3,2,1,0:T(8,128)(2,1)S(1)}, u32[]{:S(2)}, u32[]{:S(2)}) collective-permute-start(bf16[2,8,128,128]{3,2,1,0:T(8,128)(2,1)S(1)} %collective-permute-done), channel_id=1, source_target_pairs={{0,4},{4,8},{8,12},{12,14},{14,10},{10,6},{6,2},{2,0},{1,5},{5,9},... | collective-permute-start | bytes 1572872 | tf_op jit(solution)/shard_map/ppermute | solution.py:314
  41.4 2.0 %collective-permute-start.4 = (bf16[1,16,128,128]{3,2,1,0:T(8,128)(2,1)S(1)}, bf16[1,16,128,128]{3,2,1,0:T(8,128)(2,1)S(1)}, u32[]{:S(2)}, u32[]{:S(2)}) collective-permute-start(bf16[1,16,128,128]{3,2,1,0:T(8,128)(2,1)S(1)} %fusion.9), channel_id=1, source_target_pairs={{0,16},{16,0},{1,17},{17,1},{2,18},{18,2},{3,19},{19,3},{4,20},{20... | collective-permute-start | bytes 1572872 | tf_op jit(solution)/shard_map/ppermute | solution.py:307
  43.3 4.7 %fusion.3.v_ref = f32[64,64,256]{2,1,0:T(8,128)} fusion(f32[64,64]{1,0:T(8,128)S(1)} %copy.17, f32[64,8,256]{2,1,0:T(8,128)} %bitcast.98, f32[64,64]{1,0:T(8,128)S(1)} %copy.16, f32[64,8,256]{2,1,0:T(8,128)} %bitcast.99), kind=kLoop, calls=%fused_computation.5 | loop fusion | flops 5242880 | bytes 5275648 | tf_op jit(solution)/shard_map/add | solution.py:53
  48.0 0.9 constant_dynamic-update-slice_fusion.6
  48.9 0.9 constant_dynamic-update-slice_fusion.5
  49.8 4.8 %shard_map.110 = bf16[48,64,256]{2,1,0:T(8,128)(2,1)} custom-call(bf16[48,64,128]{2,1,0:T(8,128)(2,1)} %get-tuple-element.52.own_ref, bf16[48,64,128]{2,1,0:T(8,128)(2,1)} %collective-permute-done.5.recv_ref, f32[64,64,256]{2,1,0:T(8,128)} %fusion.3.v_ref, bf16[128,256]{1,0:T(8,128)(2,1)} %get-tuple-element.94.fo_ref, bf16[128,256]{1,0:T(8,128)(2,1)} %get-tuple-element.93.fr_ref), custom_call_target="tpu_custom_call" | custom-call | tf_op jit(solution)/shard_map/pallas_call | solution.py:131
  55.5 1.7 %collective-permute-start.6 = (bf16[2,8,128,128]{3,2,1,0:T(8,128)(2,1)S(1)}, bf16[2,8,128,128]{3,2,1,0:T(8,128)(2,1)S(1)}, u32[]{:S(2)}, u32[]{:S(2)}) collective-permute-start(bf16[2,8,128,128]{3,2,1,0:T(8,128)(2,1)S(1)} %collective-permute-done.2), channel_id=1, source_target_pairs={{0,4},{4,8},{8,12},{12,14},{14,10},{10,6},{6,2},{2,0},{1,5},{5,9},... | collective-permute-start | bytes 1572872 | tf_op jit(solution)/shard_map/ppermute | solution.py:314
  57.5 1.7 %collective-permute-start.8 = (bf16[1,16,128,128]{3,2,1,0:T(8,128)(2,1)S(1)}, bf16[1,16,128,128]{3,2,1,0:T(8,128)(2,1)S(1)}, u32[]{:S(2)}, u32[]{:S(2)}) collective-permute-start(bf16[1,16,128,128]{3,2,1,0:T(8,128)(2,1)S(1)} %fusion.8), channel_id=1, source_target_pairs={{0,16},{16,0},{1,17},{17,1},{2,18},{18,2},{3,19},{19,3},{4,20},{20... | collective-permute-start | bytes 1572872 | tf_op jit(solution)/shard_map/ppermute | solution.py:307
  59.2 0.9 constant_dynamic-update-slice_fusion.4
  60.1 2.9 %fusion.5 = bf16[3,64,256,48]{2,3,1,0:T(8,128)(2,1)S(1)} fusion(bf16[3,16,64,256]{3,2,1,0:T(8,128)(2,1)} %bitcast.92, bf16[3,48,16]{1,2,0:T(8,128)(2,1)S(1)} %copy-done), kind=kOutput, calls=%fused_computation.11 | convolution fusion | flops 75497472 | bytes 6296064 | tf_op jit(solution)/shard_map/dot_general | solution.py:401
  63.0 0.9 constant_dynamic-update-slice_fusion.3
  63.9 3.9 %copy.33 = bf16[3,64,256,48]{2,1,3,0:T(8,128)(2,1)} copy(bf16[3,64,256,48]{2,3,1,0:T(8,128)(2,1)S(1)} %fusion.5) | data formatting | bytes 9437184 | tf_op jit(solution)/shard_map/dot_general | solution.py:401
  68.6 0.7 slice_dynamic-update-slice_fusion.4
  70.4 1.4 collective-permute-start.10
  72.4 1.4 %collective-permute-start.11 = (bf16[1,16,128,128]{3,2,1,0:T(8,128)(2,1)S(1)}, bf16[1,16,128,128]{3,2,1,0:T(8,128)(2,1)S(1)}, u32[]{:S(2)}, u32[]{:S(2)}) collective-permute-start(bf16[1,16,128,128]{3,2,1,0:T(8,128)(2,1)S(1)} %fusion.7), channel_id=1, source_target_pairs={{0,16},{16,0},{1,17},{17,1},{2,18},{18,2},{3,19},{19,3},{4,20},{20... | collective-permute-start | bytes 1572872 | tf_op jit(solution)/shard_map/ppermute | solution.py:307
  73.8 0.9 constant_dynamic-update-slice_fusion.2
  74.7 0.9 constant_dynamic-update-slice_fusion.1
  76.4 13.4 %shard_map.111 = (bf16[3,48,64,128]{3,2,1,0:T(8,128)(2,1)}, bf16[3,48,64,128]{3,2,1,0:T(8,128)(2,1)}) custom-call(s32[1]{0:T(128)} %bitcast.me_ref, bf16[3,48,64,256]{3,2,1,0:T(8,128)(2,1)} %bitcast.88, f32[64,64,256]{2,1,0:T(8,128)} %fusion.3.v_ref, f32[64,64,256]{2,1,0:T(8,128)} %add_bitcast_fusion.w_ref, bf16[256,256]{1,0:T(8,128)(2,1)} %constant.264.clone.ft_ref), custom_call_target="tpu_custom_call" | custom-call | tf_op jit(solution)/shard_map/pallas_call | solution.py:161
  90.5 1.0 pad_maximum_fusion
  91.5 0.8 copy-done.5
  94.3 0.9 constant_dynamic-update-slice_fusion
  95.2 1.7 %slice_dynamic-update-slice_fusion.1 = bf16[3,64,128,128]{3,2,1,0:T(8,128)(2,1)} fusion(bf16[3,64,128,128]{3,2,1,0:T(8,128)(2,1)} %constant_dynamic-update-slice_fusion, s32[]{:T(128)S(6)} %select_n.406, bf16[1,16,128,128]{3,2,1,0:T(8,128)(2,1)} %copy-done.5), kind=kLoop, calls=%fused_computation.36 | loop fusion | bytes 524292 | tf_op jit(solution)/shard_map/dynamic_update_slice | solution.py:347
  96.9 1.7 %slice_dynamic-update-slice_fusion = bf16[3,64,128,128]{3,2,1,0:T(8,128)(2,1)} fusion(bf16[3,64,128,128]{3,2,1,0:T(8,128)(2,1)} %slice_dynamic-update-slice_fusion.1, s32[]{:T(128)S(6)} %select_n.409, bf16[1,16,128,128]{3,2,1,0:T(8,128)(2,1)} %copy-done.5), kind=kLoop, calls=%fused_computation.35 | loop fusion | bytes 524292 | tf_op jit(solution)/shard_map/dynamic_update_slice | solution.py:347
  98.6 3.8 %collective-permute-done.12 = bf16[1,8,128,128]{3,2,1,0:T(8,128)(2,1)S(1)} collective-permute-done((bf16[1,8,128,128]{3,2,1,0:T(8,128)(2,1)S(1)}, bf16[1,8,128,128]{3,2,1,0:T(8,128)(2,1)S(1)}, u32[]{:S(2)}, u32[]{:S(2)}) %collective-permute-start.12) | collective-permute-done | bytes 262176 | tf_op jit(solution)/shard_map/ppermute | solution.py:307
  102.4 0.7 constant_dynamic-update-slice_fusion.7.refs_4_
  103.2 1.5 %copy-done.2 = bf16[3,48,64,128]{3,2,1,0:T(8,128)(2,1)} copy-done((bf16[3,48,64,128]{3,2,1,0:T(8,128)(2,1)}, bf16[3,48,64,128]{3,2,1,0:T(8,128)(2,1)S(1)}, u32[]{:S(2)}) %copy-start.2) | copy-done | bytes 2359320
  104.6 4.2 %shard_map.112.y_ref = bf16[16,128,128]{2,1,0:T(8,128)(2,1)} custom-call(s32[1]{0:T(128)} %bitcast.1.refs_0_, bf16[128,64]{1,0:T(8,128)(2,1)} %get-tuple-element.98.refs_1_.fo_ref, bf16[128,64]{1,0:T(8,128)(2,1)} %get-tuple-element.97.refs_2_.fr_ref, bf16[48,128,128]{2,1,0:T(8,128)(2,1)} %bitcast.90, ...), custom_call_target="tpu_custom_call" | custom-call | tf_op jit(solution)/shard_map/pallas_call | solution.py:214
  108.8 2.8 %shard_map.113 = (bf16[16,64,128]{2,1,0:T(8,128)(2,1)}, bf16[16,64,128]{2,1,0:T(8,128)(2,1)}) custom-call(s32[1]{0:T(128)} %bitcast.me_ref, bf16[16,128,128]{2,1,0:T(8,128)(2,1)} %shard_map.112.y_ref, f32[64,128,128]{2,1,0:T(8,128)} %add_bitcast_fusion.1.w_ref, bf16[128,128]{1,0:T(8,128)(2,1)} %constant.263.clone.ft_ref), custom_call_target="tpu_custom_call" | custom-call | tf_op jit(solution)/shard_map/pallas_call | solution.py:101
  111.6 1.7 %collective-permute-done.14.recv_ref = bf16[16,64,128]{2,1,0:T(8,128)(2,1)S(1)} collective-permute-done((bf16[16,64,128]{2,1,0:T(8,128)(2,1)}, bf16[16,64,128]{2,1,0:T(8,128)(2,1)S(1)}, u32[]{:S(2)}, u32[]{:S(2)}) %collective-permute-start.14) | collective-permute-done | bytes 262176 | tf_op jit(solution)/shard_map/ppermute | solution.py:368
  114.1 2.6 %shard_map.114 = bf16[16,64,256]{2,1,0:T(8,128)(2,1)} custom-call(bf16[16,64,128]{2,1,0:T(8,128)(2,1)} %get-tuple-element.79.own_ref, bf16[16,64,128]{2,1,0:T(8,128)(2,1)} %copy-done.6, f32[64,64,256]{2,1,0:T(8,128)} %fusion.3.v_ref, bf16[128,256]{1,0:T(8,128)(2,1)} %get-tuple-element.94.fo_ref, bf16[128,256]{1,0:T(8,128)(2,1)} %get-tuple-element.93.fr_ref), custom_call_target="tpu_custom_call" | custom-call | tf_op jit(solution)/shard_map/pallas_call | solution.py:131
  116.7 1.6 %fusion.10 = bf16[64,256,48]{1,2,0:T(8,128)(2,1)S(1)} fusion(bf16[16,64,256]{2,1,0:T(8,128)(2,1)} %shard_map.114, bf16[48,16]{0,1:T(8,128)(2,1)S(1)} %copy-done.10), kind=kOutput, calls=%fused_computation.23 | convolution fusion | flops 25165824 | bytes 2098688 | tf_op jit(solution)/shard_map/dot_general | solution.py:418
  118.4 1.7 %copy.34 = bf16[64,256,48]{1,0,2:T(8,128)(2,1)} copy(bf16[64,256,48]{1,2,0:T(8,128)(2,1)S(1)} %fusion.10) | data formatting | bytes 3145728 | tf_op jit(solution)/shard_map/dot_general | solution.py:418
  120.0 5.7 %shard_map.115 = (bf16[1,48,64,128]{3,2,1,0:T(8,128)(2,1)}, bf16[1,48,64,128]{3,2,1,0:T(8,128)(2,1)}) custom-call(s32[1]{0:T(128)} %bitcast.me_ref, bf16[1,48,64,256]{3,2,1,0:T(8,128)(2,1)} %bitcast.93, f32[64,64,256]{2,1,0:T(8,128)} %fusion.3.v_ref, f32[64,64,256]{2,1,0:T(8,128)} %add_bitcast_fusion.w_ref, bf16[256,256]{1,0:T(8,128)(2,1)} %constant.264.clone.ft_ref), custom_call_target="tpu_custom_call" | custom-call | tf_op jit(solution)/shard_map/pallas_call | solution.py:161
  125.9 7.3 %shard_map.116.prod_ref = bf16[48,128,128]{2,1,0:T(8,128)(2,1)} custom-call(s32[1]{0:T(128)} %bitcast.1.refs_0_, bf16[128,64]{1,0:T(8,128)(2,1)} %get-tuple-element.98.refs_1_.fo_ref, bf16[128,64]{1,0:T(8,128)(2,1)} %get-tuple-element.97.refs_2_.fr_ref, bf16[48,128,128]{2,1,0:T(8,128)(2,1)} %bitcast.91, ...), custom_call_target="tpu_custom_call" | custom-call | tf_op jit(solution)/shard_map/pallas_call | solution.py:214
  133.2 0.9 broadcast_in_dim.10.s_ref
  134.0 4.4 %shard_map.117 = bf16[48,128,128]{2,1,0:T(8,128)(2,1)} custom-call(bf16[128,64]{1,0:T(8,128)(2,1)} %get-tuple-element.98.refs_1_.fo_ref, bf16[128,64]{1,0:T(8,128)(2,1)} %get-tuple-element.97.refs_2_.fr_ref, bf16[48,64,128]{2,1,0:T(8,128)(2,1)} %bitcast.104, bf16[48,64,128]{2,1,0:T(8,128)(2,1)} %bitcast.105, bf16[48,128,128]{2,1,0:T(8,128)(2,1)} %shard_map.116.prod_ref, ...), custom_call_target="tpu_custom_call" | custom-call | tf_op jit(solution)/shard_map/pallas_call | solution.py:247
  (79 shorter events, 12.1 us)
Async XLA Ops:
  0.0 60.1 %copy-start = (bf16[3,48,16]{1,2,0:T(8,128)(2,1)S(1)}, bf16[3,48,16]{1,2,0:T(8,128)(2,1)}, u32[]{:S(2)}) copy-start(bf16[3,48,16]{1,2,0:T(8,128)(2,1)} %param.13) | copy-start | bytes 13828
  0.0 4.3 %copy-start.4 = (bf16[1,3,8,128,128]{4,3,2,1,0:T(8,128)(2,1)S(1)}, bf16[1,3,8,128,128]{4,3,2,1,0:T(8,128)(2,1)}, u32[]{:S(2)}) copy-start(bf16[1,3,8,128,128]{4,3,2,1,0:T(8,128)(2,1)} %param.12) | copy-start | bytes 2359300
  5.6 33.6 %collective-permute-start = (bf16[2,8,128,128]{3,2,1,0:T(8,128)(2,1)}, bf16[2,8,128,128]{3,2,1,0:T(8,128)(2,1)S(1)}, u32[]{:S(2)}, u32[]{:S(2)}) collective-permute-start(bf16[2,8,128,128]{3,2,1,0:T(8,128)(2,1)} %get-tuple-element.84), channel_id=1, source_target_pairs={{0,4},{4,8},{8,12},{12,14},{14,10},{10,6},{6,2},{2,0},{1,5},{5,9},... | collective-permute-start | bytes 1572872 | tf_op jit(solution)/shard_map/ppermute | solution.py:314
  8.7 30.5 %collective-permute-start.1 = (bf16[2,8,128,128]{3,2,1,0:T(8,128)(2,1)}, bf16[2,8,128,128]{3,2,1,0:T(8,128)(2,1)S(1)}, u32[]{:S(2)}, u32[]{:S(2)}) collective-permute-start(bf16[2,8,128,128]{3,2,1,0:T(8,128)(2,1)} %get-tuple-element.84), channel_id=1, source_target_pairs={{0,2},{4,0},{8,4},{12,8},{14,12},{10,14},{6,10},{2,6},{1,3},{5,1},... | collective-permute-start | bytes 1572872 | tf_op jit(solution)/shard_map/ppermute | solution.py:315
  17.6 32.2 %collective-permute-start.5 = (bf16[48,64,128]{2,1,0:T(8,128)(2,1)}, bf16[48,64,128]{2,1,0:T(8,128)(2,1)}, u32[]{:S(2)}, u32[]{:S(2)}) collective-permute-start(bf16[48,64,128]{2,1,0:T(8,128)(2,1)} %get-tuple-element.53), channel_id=1, source_target_pairs={{0,1},{1,0},{2,3},{3,2},{4,5},{5,4},{6,7},{7,6},{8,9},{9,8},{10,11... | collective-permute-start | bytes 2359304 | tf_op jit(solution)/shard_map/ppermute | solution.py:368
  22.1 5.1 %copy-start.7 = (bf16[256,256]{1,0:T(8,128)(2,1)S(1)}, bf16[256,256]{1,0:T(8,128)(2,1)}, u32[]{:S(2)}) copy-start(bf16[256,256]{1,0:T(8,128)(2,1)} %constant.261.clone) | copy-start | bytes 393220
  22.1 11.0 %copy-start.9 = (s32[8]{0:T(128)S(1)}, s32[8]{0:T(128)}, u32[]{:S(2)}) copy-start(s32[8]{0:T(128)} %constant.260.clone) | copy-start | bytes 100
  39.2 15.4 %collective-permute-start.2 = (bf16[2,8,128,128]{3,2,1,0:T(8,128)(2,1)S(1)}, bf16[2,8,128,128]{3,2,1,0:T(8,128)(2,1)S(1)}, u32[]{:S(2)}, u32[]{:S(2)}) collective-permute-start(bf16[2,8,128,128]{3,2,1,0:T(8,128)(2,1)S(1)} %collective-permute-done), channel_id=1, source_target_pairs={{0,4},{4,8},{8,12},{12,14},{14,10},{10,6},{6,2},{2,0},{1,5},{5,9},... | collective-permute-start | bytes 1572872 | tf_op jit(solution)/shard_map/ppermute | solution.py:314
  41.3 14.0 %collective-permute-start.3 = (bf16[2,8,128,128]{3,2,1,0:T(8,128)(2,1)S(1)}, bf16[2,8,128,128]{3,2,1,0:T(8,128)(2,1)S(1)}, u32[]{:S(2)}, u32[]{:S(2)}) collective-permute-start(bf16[2,8,128,128]{3,2,1,0:T(8,128)(2,1)S(1)} %collective-permute-done.1), channel_id=1, source_target_pairs={{0,2},{4,0},{8,4},{12,8},{14,12},{10,14},{6,10},{2,6},{1,3},{5,1},... | collective-permute-start | bytes 1572872 | tf_op jit(solution)/shard_map/ppermute | solution.py:315
  41.4 14.1 %collective-permute-start.4 = (bf16[1,16,128,128]{3,2,1,0:T(8,128)(2,1)S(1)}, bf16[1,16,128,128]{3,2,1,0:T(8,128)(2,1)S(1)}, u32[]{:S(2)}, u32[]{:S(2)}) collective-permute-start(bf16[1,16,128,128]{3,2,1,0:T(8,128)(2,1)S(1)} %fusion.9), channel_id=1, source_target_pairs={{0,16},{16,0},{1,17},{17,1},{2,18},{18,2},{3,19},{19,3},{4,20},{20... | collective-permute-start | bytes 1572872 | tf_op jit(solution)/shard_map/ppermute | solution.py:307
  55.5 13.9 %collective-permute-start.6 = (bf16[2,8,128,128]{3,2,1,0:T(8,128)(2,1)S(1)}, bf16[2,8,128,128]{3,2,1,0:T(8,128)(2,1)S(1)}, u32[]{:S(2)}, u32[]{:S(2)}) collective-permute-start(bf16[2,8,128,128]{3,2,1,0:T(8,128)(2,1)S(1)} %collective-permute-done.2), channel_id=1, source_target_pairs={{0,4},{4,8},{8,12},{12,14},{14,10},{10,6},{6,2},{2,0},{1,5},{5,9},... | collective-permute-start | bytes 1572872 | tf_op jit(solution)/shard_map/ppermute | solution.py:314
  57.2 12.6 %collective-permute-start.7 = (bf16[2,8,128,128]{3,2,1,0:T(8,128)(2,1)S(1)}, bf16[2,8,128,128]{3,2,1,0:T(8,128)(2,1)S(1)}, u32[]{:S(2)}, u32[]{:S(2)}) collective-permute-start(bf16[2,8,128,128]{3,2,1,0:T(8,128)(2,1)S(1)} %collective-permute-done.3), channel_id=1, source_target_pairs={{0,2},{4,0},{8,4},{12,8},{14,12},{10,14},{6,10},{2,6},{1,3},{5,1},... | collective-permute-start | bytes 1572872 | tf_op jit(solution)/shard_map/ppermute | solution.py:315
  57.5 12.7 %collective-permute-start.8 = (bf16[1,16,128,128]{3,2,1,0:T(8,128)(2,1)S(1)}, bf16[1,16,128,128]{3,2,1,0:T(8,128)(2,1)S(1)}, u32[]{:S(2)}, u32[]{:S(2)}) collective-permute-start(bf16[1,16,128,128]{3,2,1,0:T(8,128)(2,1)S(1)} %fusion.8), channel_id=1, source_target_pairs={{0,16},{16,0},{1,17},{17,1},{2,18},{18,2},{3,19},{19,3},{4,20},{20... | collective-permute-start | bytes 1572872 | tf_op jit(solution)/shard_map/ppermute | solution.py:307
  70.4 20.2 %collective-permute-start.10 = (bf16[2,8,64,128]{3,2,1,0:T(8,128)(2,1)S(1)}, bf16[2,8,64,128]{3,2,1,0:T(8,128)(2,1)S(1)}, u32[]{:S(2)}, u32[]{:S(2)}) collective-permute-start(bf16[2,8,64,128]{3,2,1,0:T(8,128)(2,1)S(1)} %slice.27), channel_id=1, source_target_pairs={{0,2},{4,0},{8,4},{12,8},{14,12},{10,14},{6,10},{2,6},{1,3},{5,1},... | collective-permute-start | bytes 786440 | tf_op jit(solution)/shard_map/ppermute | solution.py:320
  71.7 18.8 %collective-permute-start.9 = (bf16[2,8,64,128]{3,2,1,0:T(8,128)(2,1)S(1)}, bf16[2,8,64,128]{3,2,1,0:T(8,128)(2,1)}, u32[]{:S(2)}, u32[]{:S(2)}) collective-permute-start(bf16[2,8,64,128]{3,2,1,0:T(8,128)(2,1)S(1)} %slice.26), channel_id=1, source_target_pairs={{0,4},{4,8},{8,12},{12,14},{14,10},{10,6},{6,2},{2,0},{1,5},{5,9},... | collective-permute-start | bytes 786440 | tf_op jit(solution)/shard_map/ppermute | solution.py:319
  72.4 19.1 %collective-permute-start.11 = (bf16[1,16,128,128]{3,2,1,0:T(8,128)(2,1)S(1)}, bf16[1,16,128,128]{3,2,1,0:T(8,128)(2,1)S(1)}, u32[]{:S(2)}, u32[]{:S(2)}) collective-permute-start(bf16[1,16,128,128]{3,2,1,0:T(8,128)(2,1)S(1)} %fusion.7), channel_id=1, source_target_pairs={{0,16},{16,0},{1,17},{17,1},{2,18},{18,2},{3,19},{19,3},{4,20},{20... | collective-permute-start | bytes 1572872 | tf_op jit(solution)/shard_map/ppermute | solution.py:307
  76.4 16.5 %copy-start.8 = (bf16[128,128]{1,0:T(8,128)(2,1)S(1)}, bf16[128,128]{1,0:T(8,128)(2,1)}, u32[]{:S(2)}) copy-start(bf16[128,128]{1,0:T(8,128)(2,1)} %constant.262.clone) | copy-start | bytes 98308
  91.5 0.8 copy-start.5
  92.3 10.8 %collective-permute-start.13 = (bf16[3,48,64,128]{3,2,1,0:T(8,128)(2,1)}, bf16[3,48,64,128]{3,2,1,0:T(8,128)(2,1)S(1)}, u32[]{:S(2)}, u32[]{:S(2)}) collective-permute-start(bf16[3,48,64,128]{3,2,1,0:T(8,128)(2,1)} %get-tuple-element.78), channel_id=1, source_target_pairs={{0,1},{1,0},{2,3},{3,2},{4,5},{5,4},{6,7},{7,6},{8,9},{9,8},{10,11... | collective-permute-start | bytes 7077896 | tf_op jit(solution)/shard_map/ppermute | solution.py:368
  93.6 8.8 %collective-permute-start.12 = (bf16[1,8,128,128]{3,2,1,0:T(8,128)(2,1)S(1)}, bf16[1,8,128,128]{3,2,1,0:T(8,128)(2,1)S(1)}, u32[]{:S(2)}, u32[]{:S(2)}) collective-permute-start(bf16[1,8,128,128]{3,2,1,0:T(8,128)(2,1)S(1)} %constant_dynamic-slice_fusion), channel_id=1, source_target_pairs={{0,16},{16,0},{1,17},{17,1},{2,18},{18,2},{3,19},{19,3},{4,20},{20... | collective-permute-start | bytes 786440 | tf_op jit(solution)/shard_map/ppermute | solution.py:307
  103.1 1.5 %copy-start.2 = (bf16[3,48,64,128]{3,2,1,0:T(8,128)(2,1)}, bf16[3,48,64,128]{3,2,1,0:T(8,128)(2,1)S(1)}, u32[]{:S(2)}) copy-start(bf16[3,48,64,128]{3,2,1,0:T(8,128)(2,1)S(1)} %collective-permute-done.13.refs_6_.refs_8_.refs_10_) | copy-start | bytes 7077892
  108.8 7.9 %copy-start.10 = (bf16[48,16]{0,1:T(8,128)(2,1)S(1)}, bf16[48,16]{0,1:T(8,128)(2,1)}, u32[]{:S(2)}) copy-start(bf16[48,16]{0,1:T(8,128)(2,1)} %param.14) | copy-start | bytes 4612
  111.6 1.7 %collective-permute-start.14 = (bf16[16,64,128]{2,1,0:T(8,128)(2,1)}, bf16[16,64,128]{2,1,0:T(8,128)(2,1)S(1)}, u32[]{:S(2)}, u32[]{:S(2)}) collective-permute-start(bf16[16,64,128]{2,1,0:T(8,128)(2,1)} %get-tuple-element.80), channel_id=1, source_target_pairs={{0,1},{1,0},{2,3},{3,2},{4,5},{5,4},{6,7},{7,6},{8,9},{9,8},{10,11... | collective-permute-start | bytes 786440 | tf_op jit(solution)/shard_map/ppermute | solution.py:368
  113.3 0.7 copy-start.6
  125.7 7.4 %copy-start.11 = (f32[48]{0:T(128)S(1)}, f32[48]{0:T(128)}, u32[]{:S(2)}) copy-start(f32[48]{0:T(128)} %param.15) | copy-start | bytes 580
  125.7 7.4 %collective-permute-start.15 = (bf16[1,48,64,128]{3,2,1,0:T(8,128)(2,1)}, bf16[1,48,64,128]{3,2,1,0:T(8,128)(2,1)S(1)}, u32[]{:S(2)}, u32[]{:S(2)}) collective-permute-start(bf16[1,48,64,128]{3,2,1,0:T(8,128)(2,1)} %get-tuple-element.82), channel_id=1, source_target_pairs={{0,1},{1,0},{2,3},{3,2},{4,5},{5,4},{6,7},{7,6},{8,9},{9,8},{10,11... | collective-permute-start | bytes 2359304 | tf_op jit(solution)/shard_map/ppermute | solution.py:368
  125.9 12.6 %copy-start.1 = (bf16[3,48,16]{1,2,0:T(8,128)(2,1)S(1)}, bf16[3,48,16]{1,2,0:T(8,128)(2,1)}, u32[]{:S(2)}) copy-start(bf16[3,48,16]{1,2,0:T(8,128)(2,1)} %param.13) | copy-start | bytes 13828
  133.1 0.9 copy-start.3

commit v6 on v5

--- a/solution.py
+++ b/solution.py
@@ -53,17 +53,22 @@
     return 1.0 + 0.5 * (cp * cq - sp * sq)
 
 
-def twiddle_tables(me, rows, cols, nc):
-    rows_l, cols_l = rows // nc, cols // nc
+def col_table(me, rows, cols, nc):
+    cols_l = cols // nc
     fine = jnp.arange(8, dtype=I32)[None, :, None]
     coarse = (8 * jnp.arange(rows // 8, dtype=I32))[:, None, None]
     bcol = (me * cols_l + jnp.arange(cols_l, dtype=I32))[None, None, :]
-    w_col = _twiddle(coarse * bcol, fine * bcol).reshape(EXTENDED, rows, cols_l)
+    return _twiddle(coarse * bcol, fine * bcol).reshape(EXTENDED, rows, cols_l)
+
+
+def row_tables(me, rows, cols, nc):
+    rows_l = rows // nc
+    fine = jnp.arange(8, dtype=I32)[None, :, None]
     coarse = (me * rows_l + 8 * jnp.arange(rows_l // 8, dtype=I32))[:, None, None]
     ball = jnp.arange(cols, dtype=I32)[None, None, :]
     w_row = _twiddle(coarse * ball, fine * ball).reshape(EXTENDED, rows_l, cols)
     v_row = _twiddle(coarse * cols + ball, fine * cols).reshape(EXTENDED, rows_l, cols)
-    return w_col, w_row, v_row
+    return w_row, v_row
 
 
 SMEM_SPEC = pl.BlockSpec(memory_space=pltpu.SMEM)
@@ -389,11 +394,12 @@
     fc_oth = lax.dynamic_slice_in_dim(f_cols, other * cols_l, cols_l, axis=0)
     fr_own = lax.dynamic_slice_in_dim(f_rows, me * rows_l, rows_l, axis=1)
     fr_oth = lax.dynamic_slice_in_dim(f_rows, other * rows_l, rows_l, axis=1)
-    w_col, w_row, v_row = twiddle_tables(me, rows, cols, nc)
+    w_col = col_table(me, rows, cols, nc)
 
     ct = cipher[0]
     own1, send1 = inv_row(me_arr, ct, w_col, ft_rows, 0)
-    own1 = ring_hold(ring, own1)
+    own1, me_late = ring_hold(ring, (own1, me))
+    w_row, v_row = row_tables(me_late, rows, cols, nc)
     coeffs = inv_col(own1, swap(send1), v_row, fc_own, fc_oth, 0)
 
     coeffs = ring_hold(ring, coeffs)

time: 140 us -> 138 us (0.986)
  local copies, waits for them, and re-layouts: 36.6 us -> 38.5 us
    dynamic_update_slice x14, local copies, waits for them, and re-layouts: 13.4 us -> 15.4 us  [_place(): lax.dynamic_update_slice(st['full'], part, (digit, st['src'][k % n], 0, 0))]
    mul x4, local copies, waits for them, and re-layouts: 2.88 us -> 4.8 us  [_twiddle(): return 1.0 + 0.5 * (cp * cq - sp * sq)]
    unnamed x24 -> x28, local copies, waits for them, and re-layouts: 3.01 us -> 2.22 us
  transfers between devices with their start and end apart: 16 -> 16, of which waited for: 6 -> 4; matrix products, arithmetic and copies ran while one was open for 32% -> 34% of each run, Pallas kernels for 22% -> 22%
where the time goes in v6:
time: 138 us; the launch traced here: 137 us
  Pallas kernels  50 us (36%)
  local copies, waits for them, and re-layouts  38.5 us (28%)
  other arithmetic  15.5 us (11%)
  starting transfers between devices  13.8 us (10%)
  between operations  8.79 us (6%)
  waiting for transfers between devices  5.98 us (4%)
  matrix products  4.5 us (3%)
    pallas_call x2, Pallas kernels, fwd_col(): pl.pallas_call(_fwd_col_kernel, grid=(groups, n // BLK), in_specs=[SMEM_S...  19 us
    dynamic_update_slice x14, local copies, waits for them, and re-layouts, _place(): lax.dynamic_update_slice(st['full'], part, (digit, st['src'][k % n], 0, 0))  15.4 us
    pallas_call x2, Pallas kernels, product(): pl.pallas_call(lambda *refs: _product_kernel(eb0, *refs), grid=(nblocks,)...  11.4 us
    add x3, other arithmetic, _twiddle(): return 1.0 + 0.5 * (cp * cq - sp * sq)  10.1 us
    pallas_call x2, Pallas kernels, inv_row(): pl.pallas_call(_inv_row_kernel, grid=(n // BLK,), in_specs=[SMEM_SPEC, bl...  7.65 us
    pallas_call x2, Pallas kernels, inv_col(): pl.pallas_call(_inv_col_kernel, grid=(n // BLK,), in_specs=[blk, blk, pl....  7.47 us
    ppermute x3, starting transfers between devices, ring_step(): st['a'] = lax.ppermute(st['a'], 'limb', st['cw'])  6.75 us
    mul x4, local copies, waits for them, and re-layouts, _twiddle(): return 1.0 + 0.5 * (cp * cq - sp * sq)  4.8 us
  transfers between devices with their start and end apart: 16, of which 4 were waited for; matrix products, arithmetic and copies ran while one was open for 34% of the time, Pallas kernels for 22%

profile of v6, /device:TPU:0, one launch (start us, length us, event | category | flops | bytes accessed | tf_op | source)
XLA Modules:
  0.0 137.0 jit_solution(14831205086437456515)
XLA Ops:
  0.0 4.3 %broadcast_in_dim.8 = bf16[3,64,128,128]{3,2,1,0:T(8,128)(2,1)} broadcast(bf16[]{:T(256)} %constant.238.clone.1), dimensions={} | broadcast | bytes 6291458 | tf_op jit(solution)/shard_map/broadcast_in_dim | solution.py:286
  4.3 1.1 constant_dynamic-update-slice_fusion.8
  5.4 3.0 %collective-permute-start = (bf16[2,8,128,128]{3,2,1,0:T(8,128)(2,1)S(1)}, bf16[2,8,128,128]{3,2,1,0:T(8,128)(2,1)S(1)}, u32[]{:S(2)}, u32[]{:S(2)}) collective-permute-start(bf16[2,8,128,128]{3,2,1,0:T(8,128)(2,1)S(1)} %get-tuple-element.86), channel_id=1, source_target_pairs={{0,4},{4,8},{8,12},{12,14},{14,10},{10,6},{6,2},{2,0},{1,5},{5,9},... | collective-permute-start | bytes 1572872 | tf_op jit(solution)/shard_map/ppermute | solution.py:319
  9.7 2.9 %add_bitcast_fusion.1.w_ref = f32[64,128,128]{2,1,0:T(8,128)} fusion(f32[64,8,128]{2,1,0:T(8,128)S(1)} %bitcast.102, f32[64,16,128]{2,1,0:T(8,128)S(1)} %bitcast.98, f32[64,8,128]{2,1,0:T(8,128)S(1)} %bitcast.103, f32[64,16,128]{2,1,0:T(8,128)S(1)} %bitcast.99), kind=kLoop, calls=%fused_computation.8 | loop fusion | flops 5242880 | bytes 5767168 | tf_op jit(solution)/shard_map/add | solution.py:53
  12.6 4.8 %shard_map.109 = (bf16[48,64,128]{2,1,0:T(8,128)(2,1)}, bf16[48,64,128]{2,1,0:T(8,128)(2,1)}) custom-call(s32[1]{0:T(128)} %bitcast.me_ref, bf16[48,128,128]{2,1,0:T(8,128)(2,1)} %bitcast.89, f32[64,128,128]{2,1,0:T(8,128)} %add_bitcast_fusion.1.w_ref, bf16[128,128]{1,0:T(8,128)(2,1)} %constant.263.clone.ft_ref), custom_call_target="tpu_custom_call" | custom-call | tf_op jit(solution)/shard_map/pallas_call | solution.py:106
  29.0 2.1 %collective-permute-start.2 = (bf16[2,8,128,128]{3,2,1,0:T(8,128)(2,1)S(1)}, bf16[2,8,128,128]{3,2,1,0:T(8,128)(2,1)S(1)}, u32[]{:S(2)}, u32[]{:S(2)}) collective-permute-start(bf16[2,8,128,128]{3,2,1,0:T(8,128)(2,1)S(1)} %collective-permute-done), channel_id=1, source_target_pairs={{0,4},{4,8},{8,12},{12,14},{14,10},{10,6},{6,2},{2,0},{1,5},{5,9},... | collective-permute-start | bytes 1572872 | tf_op jit(solution)/shard_map/ppermute | solution.py:319
  31.1 0.9 fusion.9
  31.9 1.9 %collective-permute-start.4 = (bf16[1,16,128,128]{3,2,1,0:T(8,128)(2,1)}, bf16[1,16,128,128]{3,2,1,0:T(8,128)(2,1)}, u32[]{:S(2)}, u32[]{:S(2)}) collective-permute-start(bf16[1,16,128,128]{3,2,1,0:T(8,128)(2,1)} %fusion.9), channel_id=1, source_target_pairs={{0,16},{16,0},{1,17},{17,1},{2,18},{18,2},{3,19},{19,3},{4,20},{20... | collective-permute-start | bytes 1572872 | tf_op jit(solution)/shard_map/ppermute | solution.py:312
  34.0 2.3 %fusion.53 = (f32[8,8,256]{2,1,0:T(8,128)S(1)}, f32[8,8,256]{2,1,0:T(8,128)S(1)}, f32[8,8,256]{2,1,0:T(8,128)S(1)}, f32[8,8,256]{2,1,0:T(8,128)S(1)}, f32[8,8,25...) fusion(s32[8,256]{1,0:T(8,128)S(1)} %add_select_fusion.12, ...), kind=kLoop, calls=%fused_computation.136 | loop fusion | flops 1376256 | bytes 811072 | tf_op jit(solution)/shard_map/cos | solution.py:35
  36.5 1.3 broadcast_bitcast_fusion
  37.8 1.5 %copy.17 = f32[64,64]{1,0:T(8,128)} copy(f32[64,64]{0,1:T(8,128)} %broadcast_bitcast_fusion) | data formatting | bytes 32768 | tf_op jit(solution)/shard_map/mul | solution.py:53
  39.9 1.4 %copy.16 = f32[64,64]{1,0:T(8,128)} copy(f32[64,64]{0,1:T(8,128)} %broadcast_bitcast_fusion.1) | data formatting | bytes 32768 | tf_op jit(solution)/shard_map/mul | solution.py:53
  41.3 4.1 %fusion.3.v_ref = f32[64,64,256]{2,1,0:T(8,128)} fusion(f32[64,64]{1,0:T(8,128)} %copy.17, f32[64,8,256]{2,1,0:T(8,128)S(1)} %bitcast.100, f32[64,64]{1,0:T(8,128)} %copy.16, f32[64,8,256]{2,1,0:T(8,128)S(1)} %bitcast.101), kind=kLoop, calls=%fused_computation.5 | loop fusion | flops 5242880 | bytes 5275648 | tf_op jit(solution)/shard_map/add | solution.py:53
  45.7 0.9 constant_dynamic-update-slice_fusion.6
  46.7 0.9 constant_dynamic-update-slice_fusion.5
  47.6 3.1 %add_bitcast_fusion.w_ref = f32[64,64,256]{2,1,0:T(8,128)} fusion(f32[64,8,256]{2,1,0:T(8,128)S(1)} %bitcast.96, f32[64,8,256]{2,1,0:T(8,128)S(1)} %bitcast.94, f32[64,8,256]{2,1,0:T(8,128)S(1)} %bitcast.97, f32[64,8,256]{2,1,0:T(8,128)S(1)} %bitcast.95), kind=kLoop, calls=%fused_computation.7 | loop fusion | flops 5242880 | bytes 6291456 | tf_op jit(solution)/shard_map/add | solution.py:53
  50.7 4.8 %shard_map.110 = bf16[48,64,256]{2,1,0:T(8,128)(2,1)} custom-call(bf16[48,64,128]{2,1,0:T(8,128)(2,1)} %get-tuple-element.53.own_ref, bf16[48,64,128]{2,1,0:T(8,128)(2,1)} %collective-permute-done.5.recv_ref, f32[64,64,256]{2,1,0:T(8,128)} %fusion.3.v_ref, bf16[128,256]{1,0:T(8,128)(2,1)} %get-tuple-element.96.fo_ref, bf16[128,256]{1,0:T(8,128)(2,1)} %get-tuple-element.95.fr_ref), custom_call_target="tpu_custom_call" | custom-call | tf_op jit(solution)/shard_map/pallas_call | solution.py:136
  55.5 1.6 %collective-permute-start.6 = (bf16[2,8,128,128]{3,2,1,0:T(8,128)(2,1)S(1)}, bf16[2,8,128,128]{3,2,1,0:T(8,128)(2,1)S(1)}, u32[]{:S(2)}, u32[]{:S(2)}) collective-permute-start(bf16[2,8,128,128]{3,2,1,0:T(8,128)(2,1)S(1)} %collective-permute-done.2), channel_id=1, source_target_pairs={{0,4},{4,8},{8,12},{12,14},{14,10},{10,6},{6,2},{2,0},{1,5},{5,9},... | collective-permute-start | bytes 1572872 | tf_op jit(solution)/shard_map/ppermute | solution.py:319
  58.0 0.9 constant_dynamic-update-slice_fusion.4
  58.9 2.9 %fusion.5 = bf16[3,64,256,48]{2,3,1,0:T(8,128)(2,1)S(1)} fusion(bf16[3,16,64,256]{3,2,1,0:T(8,128)(2,1)} %bitcast.92, bf16[3,48,16]{1,2,0:T(8,128)(2,1)S(1)} %copy-done), kind=kOutput, calls=%fused_computation.11 | convolution fusion | flops 75497472 | bytes 6296064 | tf_op jit(solution)/shard_map/dot_general | solution.py:407
  61.8 0.9 constant_dynamic-update-slice_fusion.3
  62.7 3.9 %copy.33 = bf16[3,64,256,48]{2,1,3,0:T(8,128)(2,1)} copy(bf16[3,64,256,48]{2,3,1,0:T(8,128)(2,1)S(1)} %fusion.5) | data formatting | bytes 9437184 | tf_op jit(solution)/shard_map/dot_general | solution.py:407
  66.6 1.7 %slice_dynamic-update-slice_fusion.5 = bf16[3,64,128,128]{3,2,1,0:T(8,128)(2,1)} fusion(bf16[3,64,128,128]{3,2,1,0:T(8,128)(2,1)} %constant_dynamic-update-slice_fusion.3, s32[]{:T(128)S(6)} %select_n.386, bf16[1,16,128,128]{3,2,1,0:T(8,128)(2,1)} %collective-permute-done.4), kind=kLoop, calls=%fused_computation.40 | loop fusion | bytes 524292 | tf_op jit(solution)/shard_map/dynamic_update_slice | solution.py:352
  68.3 1.7 %slice_dynamic-update-slice_fusion.4 = bf16[3,64,128,128]{3,2,1,0:T(8,128)(2,1)} fusion(bf16[3,64,128,128]{3,2,1,0:T(8,128)(2,1)} %slice_dynamic-update-slice_fusion.5, s32[]{:T(128)S(6)} %select_n.389, bf16[1,16,128,128]{3,2,1,0:T(8,128)(2,1)} %collective-permute-done.4), kind=kLoop, calls=%fused_computation.39 | loop fusion | bytes 524292 | tf_op jit(solution)/shard_map/dynamic_update_slice | solution.py:352
  70.8 1.6 %collective-permute-start.10 = (bf16[2,8,64,128]{3,2,1,0:T(8,128)(2,1)S(1)}, bf16[2,8,64,128]{3,2,1,0:T(8,128)(2,1)S(1)}, u32[]{:S(2)}, u32[]{:S(2)}) collective-permute-start(bf16[2,8,64,128]{3,2,1,0:T(8,128)(2,1)S(1)} %slice.27), channel_id=1, source_target_pairs={{0,2},{4,0},{8,4},{12,8},{14,12},{10,14},{6,10},{2,6},{1,3},{5,1},... | collective-permute-start | bytes 786440 | tf_op jit(solution)/shard_map/ppermute | solution.py:325
  72.8 1.2 collective-permute-start.11
  74.0 0.9 constant_dynamic-update-slice_fusion.2
  74.9 0.9 constant_dynamic-update-slice_fusion.1
  75.8 0.7 slice_dynamic-update-slice_fusion.3
  76.6 13.4 %shard_map.111 = (bf16[3,48,64,128]{3,2,1,0:T(8,128)(2,1)}, bf16[3,48,64,128]{3,2,1,0:T(8,128)(2,1)}) custom-call(s32[1]{0:T(128)} %bitcast.me_ref, bf16[3,48,64,256]{3,2,1,0:T(8,128)(2,1)} %bitcast.88, f32[64,64,256]{2,1,0:T(8,128)} %fusion.3.v_ref, f32[64,64,256]{2,1,0:T(8,128)} %add_bitcast_fusion.w_ref, bf16[256,256]{1,0:T(8,128)(2,1)} %constant.264.clone.ft_ref), custom_call_target="tpu_custom_call" | custom-call | tf_op jit(solution)/shard_map/pallas_call | solution.py:166
  90.0 0.7 slice_dynamic-update-slice_fusion.2
  92.3 0.9 collective-permute-start.12
  93.2 0.9 constant_dynamic-update-slice_fusion
  94.1 1.7 %slice_dynamic-update-slice_fusion.1 = bf16[3,64,128,128]{3,2,1,0:T(8,128)(2,1)} fusion(bf16[3,64,128,128]{3,2,1,0:T(8,128)(2,1)} %constant_dynamic-update-slice_fusion, s32[]{:T(128)S(6)} %select_n.406, bf16[1,16,128,128]{3,2,1,0:T(8,128)(2,1)} %collective-permute-done.11), kind=kLoop, calls=%fused_computation.36 | loop fusion | bytes 524292 | tf_op jit(solution)/shard_map/dynamic_update_slice | solution.py:352
  95.8 1.7 %slice_dynamic-update-slice_fusion = bf16[3,64,128,128]{3,2,1,0:T(8,128)(2,1)} fusion(bf16[3,64,128,128]{3,2,1,0:T(8,128)(2,1)} %slice_dynamic-update-slice_fusion.1, s32[]{:T(128)S(6)} %select_n.409, bf16[1,16,128,128]{3,2,1,0:T(8,128)(2,1)} %collective-permute-done.11), kind=kLoop, calls=%fused_computation.35 | loop fusion | bytes 524292 | tf_op jit(solution)/shard_map/dynamic_update_slice | solution.py:352
  97.5 3.6 %collective-permute-done.12 = bf16[1,8,128,128]{3,2,1,0:T(8,128)(2,1)S(1)} collective-permute-done((bf16[1,8,128,128]{3,2,1,0:T(8,128)(2,1)S(1)}, bf16[1,8,128,128]{3,2,1,0:T(8,128)(2,1)S(1)}, u32[]{:S(2)}, u32[]{:S(2)}) %collective-permute-start.12) | collective-permute-done | bytes 262176 | tf_op jit(solution)/shard_map/ppermute | solution.py:312
  101.1 0.8 constant_dynamic-update-slice_fusion.7.refs_4_
  101.8 1.5 %copy-done.2 = bf16[3,48,64,128]{3,2,1,0:T(8,128)(2,1)} copy-done((bf16[3,48,64,128]{3,2,1,0:T(8,128)(2,1)}, bf16[3,48,64,128]{3,2,1,0:T(8,128)(2,1)S(1)}, u32[]{:S(2)}) %copy-start.2) | copy-done | bytes 2359320
  103.3 4.2 %shard_map.112.y_ref = bf16[16,128,128]{2,1,0:T(8,128)(2,1)} custom-call(s32[1]{0:T(128)} %bitcast.1.refs_0_, bf16[128,64]{1,0:T(8,128)(2,1)} %get-tuple-element.100.refs_1_.fo_ref, bf16[128,64]{1,0:T(8,128)(2,1)} %get-tuple-element.99.refs_2_.fr_ref, bf16[48,128,128]{2,1,0:T(8,128)(2,1)} %bitcast.90, ...), custom_call_target="tpu_custom_call" | custom-call | tf_op jit(solution)/shard_map/pallas_call | solution.py:219
  107.4 2.8 %shard_map.113 = (bf16[16,64,128]{2,1,0:T(8,128)(2,1)}, bf16[16,64,128]{2,1,0:T(8,128)(2,1)}) custom-call(s32[1]{0:T(128)} %bitcast.me_ref, bf16[16,128,128]{2,1,0:T(8,128)(2,1)} %shard_map.112.y_ref, f32[64,128,128]{2,1,0:T(8,128)} %add_bitcast_fusion.1.w_ref, bf16[128,128]{1,0:T(8,128)(2,1)} %constant.263.clone.ft_ref), custom_call_target="tpu_custom_call" | custom-call | tf_op jit(solution)/shard_map/pallas_call | solution.py:106
  110.2 1.7 %collective-permute-done.14.recv_ref = bf16[16,64,128]{2,1,0:T(8,128)(2,1)S(1)} collective-permute-done((bf16[16,64,128]{2,1,0:T(8,128)(2,1)}, bf16[16,64,128]{2,1,0:T(8,128)(2,1)S(1)}, u32[]{:S(2)}, u32[]{:S(2)}) %collective-permute-start.14) | collective-permute-done | bytes 262176 | tf_op jit(solution)/shard_map/ppermute | solution.py:373
  112.7 2.6 %shard_map.114 = bf16[16,64,256]{2,1,0:T(8,128)(2,1)} custom-call(bf16[16,64,128]{2,1,0:T(8,128)(2,1)} %get-tuple-element.81.own_ref, bf16[16,64,128]{2,1,0:T(8,128)(2,1)} %copy-done.7, f32[64,64,256]{2,1,0:T(8,128)} %fusion.3.v_ref, bf16[128,256]{1,0:T(8,128)(2,1)} %get-tuple-element.96.fo_ref, bf16[128,256]{1,0:T(8,128)(2,1)} %get-tuple-element.95.fr_ref), custom_call_target="tpu_custom_call" | custom-call | tf_op jit(solution)/shard_map/pallas_call | solution.py:136
  115.3 1.6 %fusion.10 = bf16[64,256,48]{1,2,0:T(8,128)(2,1)S(1)} fusion(bf16[16,64,256]{2,1,0:T(8,128)(2,1)} %shard_map.114, bf16[48,16]{0,1:T(8,128)(2,1)S(1)} %copy-done.11), kind=kOutput, calls=%fused_computation.23 | convolution fusion | flops 25165824 | bytes 2098688 | tf_op jit(solution)/shard_map/dot_general | solution.py:424
  117.0 1.7 %copy.34 = bf16[64,256,48]{1,0,2:T(8,128)(2,1)} copy(bf16[64,256,48]{1,2,0:T(8,128)(2,1)S(1)} %fusion.10) | data formatting | bytes 3145728 | tf_op jit(solution)/shard_map/dot_general | solution.py:424
  118.7 5.7 %shard_map.115 = (bf16[1,48,64,128]{3,2,1,0:T(8,128)(2,1)}, bf16[1,48,64,128]{3,2,1,0:T(8,128)(2,1)}) custom-call(s32[1]{0:T(128)} %bitcast.me_ref, bf16[1,48,64,256]{3,2,1,0:T(8,128)(2,1)} %bitcast.93, f32[64,64,256]{2,1,0:T(8,128)} %fusion.3.v_ref, f32[64,64,256]{2,1,0:T(8,128)} %add_bitcast_fusion.w_ref, bf16[256,256]{1,0:T(8,128)(2,1)} %constant.264.clone.ft_ref), custom_call_target="tpu_custom_call" | custom-call | tf_op jit(solution)/shard_map/pallas_call | solution.py:166
  124.5 7.2 %shard_map.116.prod_ref = bf16[48,128,128]{2,1,0:T(8,128)(2,1)} custom-call(s32[1]{0:T(128)} %bitcast.1.refs_0_, bf16[128,64]{1,0:T(8,128)(2,1)} %get-tuple-element.100.refs_1_.fo_ref, bf16[128,64]{1,0:T(8,128)(2,1)} %get-tuple-element.99.refs_2_.fr_ref, bf16[48,128,128]{2,1,0:T(8,128)(2,1)} %bitcast.91, ...), custom_call_target="tpu_custom_call" | custom-call | tf_op jit(solution)/shard_map/pallas_call | solution.py:219
  131.7 0.9 broadcast_in_dim.10.s_ref
  132.6 4.4 %shard_map.117 = bf16[48,128,128]{2,1,0:T(8,128)(2,1)} custom-call(bf16[128,64]{1,0:T(8,128)(2,1)} %get-tuple-element.100.refs_1_.fo_ref, bf16[128,64]{1,0:T(8,128)(2,1)} %get-tuple-element.99.refs_2_.fr_ref, bf16[48,64,128]{2,1,0:T(8,128)(2,1)} %bitcast.104, bf16[48,64,128]{2,1,0:T(8,128)(2,1)} %bitcast.105, bf16[48,128,128]{2,1,0:T(8,128)(2,1)} %shard_map.116.prod_ref, ...), custom_call_target="tpu_custom_call" | custom-call | tf_op jit(solution)/shard_map/pallas_call | solution.py:252
  (84 shorter events, 9.9 us)
Async XLA Ops:
  0.0 58.9 %copy-start = (bf16[3,48,16]{1,2,0:T(8,128)(2,1)S(1)}, bf16[3,48,16]{1,2,0:T(8,128)(2,1)}, u32[]{:S(2)}) copy-start(bf16[3,48,16]{1,2,0:T(8,128)(2,1)} %param.13) | copy-start | bytes 13828
  0.0 4.3 %copy-start.4 = (bf16[1,3,8,128,128]{4,3,2,1,0:T(8,128)(2,1)S(1)}, bf16[1,3,8,128,128]{4,3,2,1,0:T(8,128)(2,1)}, u32[]{:S(2)}) copy-start(bf16[1,3,8,128,128]{4,3,2,1,0:T(8,128)(2,1)} %param.12) | copy-start | bytes 2359300
  5.4 23.6 %collective-permute-start = (bf16[2,8,128,128]{3,2,1,0:T(8,128)(2,1)S(1)}, bf16[2,8,128,128]{3,2,1,0:T(8,128)(2,1)S(1)}, u32[]{:S(2)}, u32[]{:S(2)}) collective-permute-start(bf16[2,8,128,128]{3,2,1,0:T(8,128)(2,1)S(1)} %get-tuple-element.86), channel_id=1, source_target_pairs={{0,4},{4,8},{8,12},{12,14},{14,10},{10,6},{6,2},{2,0},{1,5},{5,9},... | collective-permute-start | bytes 1572872 | tf_op jit(solution)/shard_map/ppermute | solution.py:319
  8.4 20.5 %collective-permute-start.1 = (bf16[2,8,128,128]{3,2,1,0:T(8,128)(2,1)S(1)}, bf16[2,8,128,128]{3,2,1,0:T(8,128)(2,1)S(1)}, u32[]{:S(2)}, u32[]{:S(2)}) collective-permute-start(bf16[2,8,128,128]{3,2,1,0:T(8,128)(2,1)S(1)} %get-tuple-element.86), channel_id=1, source_target_pairs={{0,2},{4,0},{8,4},{12,8},{14,12},{10,14},{6,10},{2,6},{1,3},{5,1},... | collective-permute-start | bytes 1572872 | tf_op jit(solution)/shard_map/ppermute | solution.py:320
  9.7 7.9 %copy-start.13 = (s32[8]{0:T(128)S(1)}, s32[8]{0:T(128)}, u32[]{:S(2)}) copy-start(s32[8]{0:T(128)} %constant.259.clone) | copy-start | bytes 100
  9.7 12.6 %copy-start.10 = (s32[8]{0:T(128)S(1)}, s32[8]{0:T(128)}, u32[]{:S(2)}) copy-start(s32[8]{0:T(128)} %constant.260.clone) | copy-start | bytes 100
  9.7 17.8 %copy-start.8 = (bf16[256,256]{1,0:T(8,128)(2,1)S(1)}, bf16[256,256]{1,0:T(8,128)(2,1)}, u32[]{:S(2)}) copy-start(bf16[256,256]{1,0:T(8,128)(2,1)} %constant.261.clone) | copy-start | bytes 393220
  17.5 33.2 %collective-permute-start.5 = (bf16[48,64,128]{2,1,0:T(8,128)(2,1)}, bf16[48,64,128]{2,1,0:T(8,128)(2,1)}, u32[]{:S(2)}, u32[]{:S(2)}) collective-permute-start(bf16[48,64,128]{2,1,0:T(8,128)(2,1)} %get-tuple-element.54), channel_id=1, source_target_pairs={{0,1},{1,0},{2,3},{3,2},{4,5},{5,4},{6,7},{7,6},{8,9},{9,8},{10,11... | collective-permute-start | bytes 2359304 | tf_op jit(solution)/shard_map/ppermute | solution.py:373
  29.0 26.5 %collective-permute-start.2 = (bf16[2,8,128,128]{3,2,1,0:T(8,128)(2,1)S(1)}, bf16[2,8,128,128]{3,2,1,0:T(8,128)(2,1)S(1)}, u32[]{:S(2)}, u32[]{:S(2)}) collective-permute-start(bf16[2,8,128,128]{3,2,1,0:T(8,128)(2,1)S(1)} %collective-permute-done), channel_id=1, source_target_pairs={{0,4},{4,8},{8,12},{12,14},{14,10},{10,6},{6,2},{2,0},{1,5},{5,9},... | collective-permute-start | bytes 1572872 | tf_op jit(solution)/shard_map/ppermute | solution.py:319
  31.1 24.4 %collective-permute-start.3 = (bf16[2,8,128,128]{3,2,1,0:T(8,128)(2,1)S(1)}, bf16[2,8,128,128]{3,2,1,0:T(8,128)(2,1)S(1)}, u32[]{:S(2)}, u32[]{:S(2)}) collective-permute-start(bf16[2,8,128,128]{3,2,1,0:T(8,128)(2,1)S(1)} %collective-permute-done.1), channel_id=1, source_target_pairs={{0,2},{4,0},{8,4},{12,8},{14,12},{10,14},{6,10},{2,6},{1,3},{5,1},... | collective-permute-start | bytes 1572872 | tf_op jit(solution)/shard_map/ppermute | solution.py:320
  31.9 23.6 %collective-permute-start.4 = (bf16[1,16,128,128]{3,2,1,0:T(8,128)(2,1)}, bf16[1,16,128,128]{3,2,1,0:T(8,128)(2,1)}, u32[]{:S(2)}, u32[]{:S(2)}) collective-permute-start(bf16[1,16,128,128]{3,2,1,0:T(8,128)(2,1)} %fusion.9), channel_id=1, source_target_pairs={{0,16},{16,0},{1,17},{17,1},{2,18},{18,2},{3,19},{19,3},{4,20},{20... | collective-permute-start | bytes 1572872 | tf_op jit(solution)/shard_map/ppermute | solution.py:312
  41.3 4.1 %copy-start.5 = (f32[8,8,256]{2,1,0:T(8,128)S(1)}, f32[8,8,256]{2,1,0:T(8,128)}, u32[]{:S(2)}) copy-start(f32[8,8,256]{2,1,0:T(8,128)} %get-tuple-element.139) | copy-start | bytes 196612
  41.3 4.1 %copy-start.6 = (f32[8,8,256]{2,1,0:T(8,128)S(1)}, f32[8,8,256]{2,1,0:T(8,128)}, u32[]{:S(2)}) copy-start(f32[8,8,256]{2,1,0:T(8,128)} %get-tuple-element.140) | copy-start | bytes 196612
  55.5 14.5 %collective-permute-start.6 = (bf16[2,8,128,128]{3,2,1,0:T(8,128)(2,1)S(1)}, bf16[2,8,128,128]{3,2,1,0:T(8,128)(2,1)S(1)}, u32[]{:S(2)}, u32[]{:S(2)}) collective-permute-start(bf16[2,8,128,128]{3,2,1,0:T(8,128)(2,1)S(1)} %collective-permute-done.2), channel_id=1, source_target_pairs={{0,4},{4,8},{8,12},{12,14},{14,10},{10,6},{6,2},{2,0},{1,5},{5,9},... | collective-permute-start | bytes 1572872 | tf_op jit(solution)/shard_map/ppermute | solution.py:319
  57.2 13.2 %collective-permute-start.7 = (bf16[2,8,128,128]{3,2,1,0:T(8,128)(2,1)S(1)}, bf16[2,8,128,128]{3,2,1,0:T(8,128)(2,1)S(1)}, u32[]{:S(2)}, u32[]{:S(2)}) collective-permute-start(bf16[2,8,128,128]{3,2,1,0:T(8,128)(2,1)S(1)} %collective-permute-done.3), channel_id=1, source_target_pairs={{0,2},{4,0},{8,4},{12,8},{14,12},{10,14},{6,10},{2,6},{1,3},{5,1},... | collective-permute-start | bytes 1572872 | tf_op jit(solution)/shard_map/ppermute | solution.py:320
  57.7 13.0 %collective-permute-start.8 = (bf16[1,16,128,128]{3,2,1,0:T(8,128)(2,1)S(1)}, bf16[1,16,128,128]{3,2,1,0:T(8,128)(2,1)S(1)}, u32[]{:S(2)}, u32[]{:S(2)}) collective-permute-start(bf16[1,16,128,128]{3,2,1,0:T(8,128)(2,1)S(1)} %fusion.8), channel_id=1, source_target_pairs={{0,16},{16,0},{1,17},{17,1},{2,18},{18,2},{3,19},{19,3},{4,20},{20... | collective-permute-start | bytes 1572872 | tf_op jit(solution)/shard_map/ppermute | solution.py:312
  70.8 19.9 %collective-permute-start.10 = (bf16[2,8,64,128]{3,2,1,0:T(8,128)(2,1)S(1)}, bf16[2,8,64,128]{3,2,1,0:T(8,128)(2,1)S(1)}, u32[]{:S(2)}, u32[]{:S(2)}) collective-permute-start(bf16[2,8,64,128]{3,2,1,0:T(8,128)(2,1)S(1)} %slice.27), channel_id=1, source_target_pairs={{0,2},{4,0},{8,4},{12,8},{14,12},{10,14},{6,10},{2,6},{1,3},{5,1},... | collective-permute-start | bytes 786440 | tf_op jit(solution)/shard_map/ppermute | solution.py:325
  72.4 18.3 %collective-permute-start.9 = (bf16[2,8,64,128]{3,2,1,0:T(8,128)(2,1)S(1)}, bf16[2,8,64,128]{3,2,1,0:T(8,128)(2,1)S(1)}, u32[]{:S(2)}, u32[]{:S(2)}) collective-permute-start(bf16[2,8,64,128]{3,2,1,0:T(8,128)(2,1)S(1)} %slice.26), channel_id=1, source_target_pairs={{0,4},{4,8},{8,12},{12,14},{14,10},{10,6},{6,2},{2,0},{1,5},{5,9},... | collective-permute-start | bytes 786440 | tf_op jit(solution)/shard_map/ppermute | solution.py:324
  72.8 17.9 %collective-permute-start.11 = (bf16[1,16,128,128]{3,2,1,0:T(8,128)(2,1)S(1)}, bf16[1,16,128,128]{3,2,1,0:T(8,128)(2,1)}, u32[]{:S(2)}, u32[]{:S(2)}) collective-permute-start(bf16[1,16,128,128]{3,2,1,0:T(8,128)(2,1)S(1)} %fusion.7), channel_id=1, source_target_pairs={{0,16},{16,0},{1,17},{17,1},{2,18},{18,2},{3,19},{19,3},{4,20},{20... | collective-permute-start | bytes 1572872 | tf_op jit(solution)/shard_map/ppermute | solution.py:312
  76.6 15.0 %copy-start.9 = (bf16[128,128]{1,0:T(8,128)(2,1)S(1)}, bf16[128,128]{1,0:T(8,128)(2,1)}, u32[]{:S(2)}) copy-start(bf16[128,128]{1,0:T(8,128)(2,1)} %constant.262.clone) | copy-start | bytes 98308
  90.8 11.1 %collective-permute-start.13 = (bf16[3,48,64,128]{3,2,1,0:T(8,128)(2,1)}, bf16[3,48,64,128]{3,2,1,0:T(8,128)(2,1)S(1)}, u32[]{:S(2)}, u32[]{:S(2)}) collective-permute-start(bf16[3,48,64,128]{3,2,1,0:T(8,128)(2,1)} %get-tuple-element.80), channel_id=1, source_target_pairs={{0,1},{1,0},{2,3},{3,2},{4,5},{5,4},{6,7},{7,6},{8,9},{9,8},{10,11... | collective-permute-start | bytes 7077896 | tf_op jit(solution)/shard_map/ppermute | solution.py:373
  92.3 8.8 %collective-permute-start.12 = (bf16[1,8,128,128]{3,2,1,0:T(8,128)(2,1)S(1)}, bf16[1,8,128,128]{3,2,1,0:T(8,128)(2,1)S(1)}, u32[]{:S(2)}, u32[]{:S(2)}) collective-permute-start(bf16[1,8,128,128]{3,2,1,0:T(8,128)(2,1)S(1)} %constant_dynamic-slice_fusion), channel_id=1, source_target_pairs={{0,16},{16,0},{1,17},{17,1},{2,18},{18,2},{3,19},{19,3},{4,20},{20... | collective-permute-start | bytes 786440 | tf_op jit(solution)/shard_map/ppermute | solution.py:312
  101.8 1.5 %copy-start.2 = (bf16[3,48,64,128]{3,2,1,0:T(8,128)(2,1)}, bf16[3,48,64,128]{3,2,1,0:T(8,128)(2,1)S(1)}, u32[]{:S(2)}) copy-start(bf16[3,48,64,128]{3,2,1,0:T(8,128)(2,1)S(1)} %collective-permute-done.13.refs_6_.refs_8_.refs_10_) | copy-start | bytes 7077892
  107.4 7.9 %copy-start.11 = (bf16[48,16]{0,1:T(8,128)(2,1)S(1)}, bf16[48,16]{0,1:T(8,128)(2,1)}, u32[]{:S(2)}) copy-start(bf16[48,16]{0,1:T(8,128)(2,1)} %param.14) | copy-start | bytes 4612
  110.2 1.7 %collective-permute-start.14 = (bf16[16,64,128]{2,1,0:T(8,128)(2,1)}, bf16[16,64,128]{2,1,0:T(8,128)(2,1)S(1)}, u32[]{:S(2)}, u32[]{:S(2)}) collective-permute-start(bf16[16,64,128]{2,1,0:T(8,128)(2,1)} %get-tuple-element.82), channel_id=1, source_target_pairs={{0,1},{1,0},{2,3},{3,2},{4,5},{5,4},{6,7},{7,6},{8,9},{9,8},{10,11... | collective-permute-start | bytes 786440 | tf_op jit(solution)/shard_map/ppermute | solution.py:373
  112.0 0.7 copy-start.7
  124.3 7.4 %copy-start.12 = (f32[48]{0:T(128)S(1)}, f32[48]{0:T(128)}, u32[]{:S(2)}) copy-start(f32[48]{0:T(128)} %param.15) | copy-start | bytes 580
  124.3 7.4 %collective-permute-start.15 = (bf16[1,48,64,128]{3,2,1,0:T(8,128)(2,1)}, bf16[1,48,64,128]{3,2,1,0:T(8,128)(2,1)S(1)}, u32[]{:S(2)}, u32[]{:S(2)}) collective-permute-start(bf16[1,48,64,128]{3,2,1,0:T(8,128)(2,1)} %get-tuple-element.84), channel_id=1, source_target_pairs={{0,1},{1,0},{2,3},{3,2},{4,5},{5,4},{6,7},{7,6},{8,9},{9,8},{10,11... | collective-permute-start | bytes 2359304 | tf_op jit(solution)/shard_map/ppermute | solution.py:373
  124.5 12.5 %copy-start.1 = (bf16[3,48,16]{1,2,0:T(8,128)(2,1)S(1)}, bf16[3,48,16]{1,2,0:T(8,128)(2,1)}, u32[]{:S(2)}) copy-start(bf16[3,48,16]{1,2,0:T(8,128)(2,1)} %param.13) | copy-start | bytes 13828
  131.7 0.9 copy-start.3

commit v7 on v2

--- a/solution.py
+++ b/solution.py
@@ -143,7 +143,7 @@
     )(own, recv, v_row, f_own, f_oth)
 
 
-def _fwd_col_kernel(me_ref, x_ref, v_ref, w_ref, ft_ref, own_ref, send_ref):
+def _fwd_col_kernel(sj_ref, st_ref, se_ref, me_ref, x_ref, v_ref, w_ref, ft_ref, own_ref, send_ref):
     n, rows_l, cols = x_ref.shape
     g = (x_ref[...].astype(F32) * v_ref[...]).astype(BF16)
     h = jnp.dot(g.reshape(n * rows_l, cols), ft_ref[...], preferred_element_type=F32)
@@ -152,19 +152,30 @@
     _split_store(me_ref, h[:, :, :half], h[:, :, half:], own_ref, send_ref)
 
 
-def fwd_col(me_arr, x, v_row, w_row, ft, table_block):
+def fwd_col(me_arr, x, v_row, w_row, ft, steps):
     groups, n, rows_l, cols = x.shape
     half = cols // 2
-    xs = pl.BlockSpec((None, BLK, rows_l, cols), lambda j, t: (j, t, 0, 0))
-    ts = pl.BlockSpec((BLK, rows_l, cols), lambda j, t: (table_block(j, t), 0, 0))
-    os = pl.BlockSpec((None, BLK, rows_l, half), lambda j, t: (j, t, 0, 0))
+    sj, st, se = (jnp.array([step[k] for step in steps], I32) for k in range(3))
+    xs = pl.BlockSpec((None, BLK, rows_l, cols), lambda i, a, b, c: (a[i], b[i], 0, 0))
+    ts = pl.BlockSpec((BLK, rows_l, cols), lambda i, a, b, c: (c[i], 0, 0))
+    os = pl.BlockSpec((None, BLK, rows_l, half), lambda i, a, b, c: (a[i], b[i], 0, 0))
+    grid_spec = pltpu.PrefetchScalarGridSpec(
+        num_scalar_prefetch=3,
+        grid=(len(steps),),
+        in_specs=[
+            SMEM_SPEC,
+            xs,
+            ts,
+            ts,
+            pl.BlockSpec((cols, cols), lambda i, a, b, c: (0, 0)),
+        ],
+        out_specs=[os, os],
+    )
     return pl.pallas_call(
         _fwd_col_kernel,
-        grid=(groups, n // BLK),
-        in_specs=[SMEM_SPEC, xs, ts, ts, pl.BlockSpec((cols, cols), lambda j, t: (0, 0))],
-        out_specs=[os, os],
+        grid_spec=grid_spec,
         out_shape=[jax.ShapeDtypeStruct((groups, n, rows_l, half), BF16)] * 2,
-    )(me_arr, x, v_row, w_row, ft)
+    )(sj, st, se, me_arr, x, v_row, w_row, ft)
 
 
 def _product_kernel(eb0, fo_ref, fr_ref, cip_ref, key_ref, *rest):
@@ -230,11 +241,13 @@
 def _final_kernel(fo_ref, fr_ref, own_ref, recv_ref, prod_ref, s_ref, out_ref):
     fo = fo_ref[...]
     fr = fr_ref[...]
-    for l in range(own_ref.shape[0]):
+    n = own_ref.shape[0]
+    base = pl.program_id(0) * n
+    for l in range(n):
         y = jnp.dot(fo, own_ref[l], preferred_element_type=F32)
         y = (y + jnp.dot(fr, recv_ref[l], preferred_element_type=F32)).astype(BF16)
         diff = prod_ref[l].astype(F32) - y.astype(F32)
-        out_ref[l] = (diff * s_ref[l]).astype(BF16)
+        out_ref[l] = (diff * s_ref[base + l]).astype(BF16)
 
 
 def final(own4, recv4, prod, scale, f_own, f_oth):
@@ -250,7 +263,7 @@
             hs,
             hs,
             pl.BlockSpec((BLK, rows, cols_l), lambda i: (i, 0, 0)),
-            pl.BlockSpec((BLK, 1, cols_l), lambda i: (i, 0, 0)),
+            SMEM_SPEC,
         ],
         out_specs=pl.BlockSpec((BLK, rows, cols_l), lambda i: (i, 0, 0)),
         out_shape=jax.ShapeDtypeStruct((n, rows, cols_l), BF16),
@@ -366,9 +379,12 @@
     ).astype(BF16)
 
     raised = ring_hold(ring, raised)
-    own2, send2 = fwd_col(
-        me_arr, raised, v_row, w_row, ft_cols, lambda j, t: jnp.where(t >= j, t + 1, t)
-    )
+    digit_steps = []
+    for eb in range(EXTENDED // BLK):
+        for j in range(DIGITS):
+            if j != eb:
+                digit_steps.append((j, eb if eb < j else eb - 1, eb))
+    own2, send2 = fwd_col(me_arr, raised, v_row, w_row, ft_cols, digit_steps)
     own2, send2 = ring_hold(ring, (own2, send2))
     recv2 = swap(send2)
     key = ring_finish(ring)
@@ -382,8 +398,10 @@
         lower_table, special, (((1,), (0,)), ((), ())), preferred_element_type=F32
     )
     lowered = lowered.astype(BF16)[None]
-    own4, send4 = fwd_col(me_arr, lowered, v_row, w_row, ft_cols, lambda j, t: t)
-    scale = jnp.broadcast_to(special_inverse[:, None, None], (limbs, 1, cols_l))
+    own4, send4 = fwd_col(
+        me_arr, lowered, v_row, w_row, ft_cols, [(0, t, t) for t in range(limbs // BLK)]
+    )
+    scale = special_inverse
     result = final(own4[0], swap(send4)[0], prod_cipher, scale, fr_own, fr_oth)
     return result[None, None]
 

time: 128 us -> 129 us (level)
    unnamed x32 -> x30, local copies, waits for them, and re-layouts: 5.77 us -> 6.68 us
  transfers between devices with their start and end apart: 12 -> 12, of which waited for: 6 -> 7; matrix products, arithmetic and copies ran while one was open for 26% -> 25% of each run, Pallas kernels for 24% -> 23%
where the time goes in v7:
time: 129 us; the launch traced here: 128 us
  Pallas kernels  49.5 us (38%)
  local copies, waits for them, and re-layouts  25.5 us (20%)
  waiting for transfers between devices  16.5 us (13%)
  other arithmetic  13.4 us (10%)
  between operations  9.46 us (7%)
  starting transfers between devices  9.29 us (7%)
  matrix products  4.53 us (4%)
    pallas_call x2, Pallas kernels, fwd_col(): pl.pallas_call(_fwd_col_kernel, grid_spec=grid_spec, out_shape=[jax.Shape...  19.2 us
    pallas_call x2, Pallas kernels, product(): pl.pallas_call(lambda *refs: _product_kernel(eb0, *refs), grid=(nblocks,)...  10.9 us
    add x3, other arithmetic, _twiddle(): return 1.0 + 0.5 * (cp * cq - sp * sq)  9.03 us
    pallas_call x2, Pallas kernels, inv_row(): pl.pallas_call(_inv_row_kernel, grid=(n // BLK,), in_specs=[SMEM_SPEC, bl...  7.51 us
    pallas_call x2, Pallas kernels, inv_col(): pl.pallas_call(_inv_col_kernel, grid=(n // BLK,), in_specs=[blk, blk, pl....  7.47 us
    ppermute x1, waiting for transfers between devices, ring_step(): b = lax.ppermute(st['b'][:, :, h:], 'limb', st['ccw'])  6.77 us
    unnamed x30, local copies, waits for them, and re-layouts  6.68 us
    ppermute x3, starting transfers between devices, ring_step(): st['a'] = lax.ppermute(st['a'], 'limb', st['cw'])  6.18 us
  transfers between devices with their start and end apart: 12, of which 7 were waited for; matrix products, arithmetic and copies ran while one was open for 25% of the time, Pallas kernels for 23%

profile of v7, /device:TPU:0, one launch (start us, length us, event | category | flops | bytes accessed | tf_op | source)
XLA Modules:
  0.0 128.1 jit_solution(5094379238610863907)
XLA Ops:
  0.0 3.0 %collective-permute-start = (bf16[3,8,128,128]{3,2,1,0:T(8,128)(2,1)}, bf16[3,8,128,128]{3,2,1,0:T(8,128)(2,1)S(1)}, u32[]{:S(2)}, u32[]{:S(2)}) collective-permute-start(bf16[3,8,128,128]{3,2,1,0:T(8,128)(2,1)} %bitcast.102), channel_id=1, source_target_pairs={{0,4},{4,8},{8,12},{12,14},{14,10},{10,6},{6,2},{2,0},{1,5},{5,9},... | collective-permute-start | bytes 2359304 | tf_op jit(solution)/shard_map/ppermute | solution.py:313
  3.2 0.6 fusion.54
  4.3 2.9 %add_bitcast_fusion.1.w_ref = f32[64,128,128]{2,1,0:T(8,128)} fusion(f32[64,8,128]{2,1,0:T(8,128)S(1)} %bitcast.98, f32[64,16,128]{2,1,0:T(8,128)S(1)} %bitcast.96, f32[64,8,128]{2,1,0:T(8,128)S(1)} %bitcast.99, f32[64,16,128]{2,1,0:T(8,128)S(1)} %bitcast.97), kind=kLoop, calls=%fused_computation.8 | loop fusion | flops 5242880 | bytes 5767168 | tf_op jit(solution)/shard_map/add | solution.py:53
  7.2 4.9 %shard_map.163 = (bf16[48,64,128]{2,1,0:T(8,128)(2,1)}, bf16[48,64,128]{2,1,0:T(8,128)(2,1)}) custom-call(s32[1]{0:T(128)} %bitcast.me_ref, bf16[48,128,128]{2,1,0:T(8,128)(2,1)} %bitcast.85, f32[64,128,128]{2,1,0:T(8,128)} %add_bitcast_fusion.1.w_ref, bf16[128,128]{1,0:T(8,128)(2,1)} %constant.257.clone.ft_ref), custom_call_target="tpu_custom_call" | custom-call | tf_op jit(solution)/shard_map/pallas_call | solution.py:101
  12.5 2.2 %fusion.50 = (f32[8,8,256]{2,1,0:T(8,128)S(1)}, f32[8,8,256]{2,1,0:T(8,128)S(1)}, f32[8,8,256]{2,1,0:T(8,128)S(1)}, f32[8,8,256]{2,1,0:T(8,128)S(1)}, f32[8,8,25...) fusion(s32[8,256]{1,0:T(8,128)S(1)} %add_select_fusion.12, ...), kind=kLoop, calls=%fused_computation.119 | loop fusion | flops 1376256 | bytes 811072 | tf_op jit(solution)/shard_map/cos | solution.py:35
  14.9 0.7 add.605
  15.7 0.7 broadcast_bitcast_fusion
  16.4 4.4 %collective-permute-done = bf16[3,8,128,128]{3,2,1,0:T(8,128)(2,1)S(1)} collective-permute-done((bf16[3,8,128,128]{3,2,1,0:T(8,128)(2,1)}, bf16[3,8,128,128]{3,2,1,0:T(8,128)(2,1)S(1)}, u32[]{:S(2)}, u32[]{:S(2)}) %collective-permute-start) | collective-permute-done | bytes 786464 | tf_op jit(solution)/shard_map/ppermute | solution.py:313
  20.7 1.6 %collective-permute-done.1 = bf16[3,8,128,128]{3,2,1,0:T(8,128)(2,1)} collective-permute-done((bf16[3,8,128,128]{3,2,1,0:T(8,128)(2,1)}, bf16[3,8,128,128]{3,2,1,0:T(8,128)(2,1)}, u32[]{:S(2)}, u32[]{:S(2)}) %collective-permute-start.1) | collective-permute-done | bytes 786464 | tf_op jit(solution)/shard_map/ppermute | solution.py:314
  22.3 1.6 %collective-permute-start.2 = (bf16[3,8,128,128]{3,2,1,0:T(8,128)(2,1)S(1)}, bf16[3,8,128,128]{3,2,1,0:T(8,128)(2,1)}, u32[]{:S(2)}, u32[]{:S(2)}) collective-permute-start(bf16[3,8,128,128]{3,2,1,0:T(8,128)(2,1)S(1)} %collective-permute-done), channel_id=1, source_target_pairs={{0,4},{4,8},{8,12},{12,14},{14,10},{10,6},{6,2},{2,0},{1,5},{5,9},... | collective-permute-start | bytes 2359304 | tf_op jit(solution)/shard_map/ppermute | solution.py:313
  24.4 0.6 constant_dynamic-slice_fusion
  25.2 3.1 %fusion.3.v_ref = f32[64,64,256]{2,1,0:T(8,128)} fusion(f32[64,64]{1,0:T(8,128)S(1)} %copy.23, f32[64,8,256]{2,1,0:T(8,128)S(1)} %bitcast.94, f32[64,64]{1,0:T(8,128)S(1)} %copy.22, f32[64,8,256]{2,1,0:T(8,128)S(1)} %bitcast.95), kind=kLoop, calls=%fused_computation.5 | loop fusion | flops 5242880 | bytes 5275648 | tf_op jit(solution)/shard_map/add | solution.py:53
  28.3 0.9 copy-done.3
  29.1 4.8 %shard_map.164 = bf16[48,64,256]{2,1,0:T(8,128)(2,1)} custom-call(bf16[48,64,128]{2,1,0:T(8,128)(2,1)} %get-tuple-element.42.own_ref, bf16[48,64,128]{2,1,0:T(8,128)(2,1)} %copy-done.3, f32[64,64,256]{2,1,0:T(8,128)} %fusion.3.v_ref, bf16[128,256]{1,0:T(8,128)(2,1)} %get-tuple-element.74.fo_ref, bf16[128,256]{1,0:T(8,128)(2,1)} %get-tuple-element.73.fr_ref), custom_call_target="tpu_custom_call" | custom-call | tf_op jit(solution)/shard_map/pallas_call | solution.py:131
  34.0 2.9 %fusion.5 = bf16[3,64,256,48]{2,3,1,0:T(8,128)(2,1)S(1)} fusion(bf16[3,16,64,256]{3,2,1,0:T(8,128)(2,1)} %bitcast.88, bf16[3,48,16]{1,2,0:T(8,128)(2,1)S(1)} %copy-done), kind=kOutput, calls=%fused_computation.11 | convolution fusion | flops 75497472 | bytes 6296064 | tf_op jit(solution)/shard_map/dot_general | solution.py:377
  36.9 3.9 %copy.39 = bf16[3,64,256,48]{2,1,3,0:T(8,128)(2,1)} copy(bf16[3,64,256,48]{2,3,1,0:T(8,128)(2,1)S(1)} %fusion.5) | data formatting | bytes 9437184 | tf_op jit(solution)/shard_map/dot_general | solution.py:377
  40.7 1.3 %collective-permute-done.3 = bf16[3,8,128,128]{3,2,1,0:T(8,128)(2,1)} collective-permute-done((bf16[3,8,128,128]{3,2,1,0:T(8,128)(2,1)}, bf16[3,8,128,128]{3,2,1,0:T(8,128)(2,1)}, u32[]{:S(2)}, u32[]{:S(2)}) %collective-permute-start.3) | collective-permute-done | bytes 786464 | tf_op jit(solution)/shard_map/ppermute | solution.py:314
  42.0 1.6 %collective-permute-start.5 = (bf16[3,8,128,128]{3,2,1,0:T(8,128)(2,1)}, bf16[3,8,128,128]{3,2,1,0:T(8,128)(2,1)S(1)}, u32[]{:S(2)}, u32[]{:S(2)}) collective-permute-start(bf16[3,8,128,128]{3,2,1,0:T(8,128)(2,1)} %collective-permute-done.2), channel_id=1, source_target_pairs={{0,4},{4,8},{8,12},{12,14},{14,10},{10,6},{6,2},{2,0},{1,5},{5,9},... | collective-permute-start | bytes 2359304 | tf_op jit(solution)/shard_map/ppermute | solution.py:313
  43.6 0.5 collective-permute-start.6
  44.4 3.0 %add_bitcast_fusion.w_ref = f32[64,64,256]{2,1,0:T(8,128)} fusion(f32[64,8,256]{2,1,0:T(8,128)S(1)} %bitcast.92, f32[64,8,256]{2,1,0:T(8,128)S(1)} %bitcast.90, f32[64,8,256]{2,1,0:T(8,128)S(1)} %bitcast.93, f32[64,8,256]{2,1,0:T(8,128)S(1)} %bitcast.91), kind=kLoop, calls=%fused_computation.7 | loop fusion | flops 5242880 | bytes 6291456 | tf_op jit(solution)/shard_map/add | solution.py:53
  47.4 12.8 %shard_map.165 = (bf16[3,48,64,128]{3,2,1,0:T(8,128)(2,1)}, bf16[3,48,64,128]{3,2,1,0:T(8,128)(2,1)}) custom-call(s32[9]{0:T(128)} %constant.258.clone.sj_ref, s32[9]{0:T(128)} %constant.259.clone.st_ref, s32[9]{0:T(128)} %constant.260.clone.se_ref, s32[1]{0:T(128)} %bitcast.me_ref, bf16[3,48,64,256]{3,2,1,0:T(8,128)(2,1)} %bitcast.84, ...), custom_call_target="tpu_custom_call" | custom-call | tf_op jit(solution)/shard_map/pallas_call | solution.py:174
  60.6 0.6 dynamic_slice.38
  65.8 0.7 fusion.89
  71.0 0.7 constant_dynamic-slice_fusion.2
  71.7 1.6 %broadcast_in_dim.6 = bf16[3,64,128,128]{3,2,1,0:T(8,128)(2,1)S(1)} broadcast(bf16[]{:T(256)} %constant.233.clone.1), dimensions={} | broadcast | bytes 6291458 | tf_op jit(solution)/shard_map/broadcast_in_dim | solution.py:288
  73.6 1.3 constant_dynamic-update-slice_fusion.4
  74.8 1.3 constant_dynamic-update-slice_fusion.3
  76.1 1.0 slice.7
  77.1 0.5 collective-permute-start.8
  77.7 1.6 %collective-permute-start.7 = (bf16[3,8,64,128]{3,2,1,0:T(8,128)(2,1)S(1)}, bf16[3,8,64,128]{3,2,1,0:T(8,128)(2,1)S(1)}, u32[]{:S(2)}, u32[]{:S(2)}) collective-permute-start(bf16[3,8,64,128]{3,2,1,0:T(8,128)(2,1)S(1)} %slice.6), channel_id=1, source_target_pairs={{0,4},{4,8},{8,12},{12,14},{14,10},{10,6},{6,2},{2,0},{1,5},{5,9},... | collective-permute-start | bytes 1179656 | tf_op jit(solution)/shard_map/ppermute | solution.py:323
  79.3 1.3 constant_dynamic-update-slice_fusion.2
  80.7 1.3 constant_dynamic-update-slice_fusion
  81.9 6.8 %collective-permute-done.8 = bf16[3,8,64,128]{3,2,1,0:T(8,128)(2,1)S(1)} collective-permute-done((bf16[3,8,64,128]{3,2,1,0:T(8,128)(2,1)S(1)}, bf16[3,8,64,128]{3,2,1,0:T(8,128)(2,1)S(1)}, u32[]{:S(2)}, u32[]{:S(2)}) %collective-permute-start.8) | collective-permute-done | bytes 393248 | tf_op jit(solution)/shard_map/ppermute | solution.py:324
  89.1 2.7 %copy-done.2 = bf16[3,64,128,128]{3,2,1,0:T(8,128)(2,1)} copy-done((bf16[3,64,128,128]{3,2,1,0:T(8,128)(2,1)}, bf16[3,64,128,128]{3,2,1,0:T(8,128)(2,1)S(1)}, u32[]{:S(2)}) %copy-start.2) | copy-done | bytes 6291480
  91.8 1.4 %copy-done.1 = bf16[3,48,64,128]{3,2,1,0:T(8,128)(2,1)} copy-done((bf16[3,48,64,128]{3,2,1,0:T(8,128)(2,1)}, bf16[3,48,64,128]{3,2,1,0:T(8,128)(2,1)S(1)}, u32[]{:S(2)}) %copy-start.1) | copy-done | bytes 2359320
  93.2 3.8 %shard_map.166.y_ref = bf16[16,128,128]{2,1,0:T(8,128)(2,1)} custom-call(bf16[128,64]{1,0:T(8,128)(2,1)} %get-tuple-element.78.refs_0_.fo_ref, bf16[128,64]{1,0:T(8,128)(2,1)} %get-tuple-element.77.refs_1_.fr_ref, bf16[48,128,128]{2,1,0:T(8,128)(2,1)} %bitcast.86, bf16[3,64,128,128]{3,2,1,0:T(8,128)(2,1)} %copy-done.2, ...), custom_call_target="tpu_custom_call" | custom-call | tf_op jit(solution)/shard_map/pallas_call | solution.py:223
  97.0 2.6 %shard_map.167 = (bf16[16,64,128]{2,1,0:T(8,128)(2,1)}, bf16[16,64,128]{2,1,0:T(8,128)(2,1)}) custom-call(s32[1]{0:T(128)} %bitcast.me_ref, bf16[16,128,128]{2,1,0:T(8,128)(2,1)} %shard_map.166.y_ref, f32[64,128,128]{2,1,0:T(8,128)} %add_bitcast_fusion.1.w_ref, bf16[128,128]{1,0:T(8,128)(2,1)} %constant.257.clone.ft_ref), custom_call_target="tpu_custom_call" | custom-call | tf_op jit(solution)/shard_map/pallas_call | solution.py:101
  99.6 1.7 %collective-permute-done.10.recv_ref = bf16[16,64,128]{2,1,0:T(8,128)(2,1)S(1)} collective-permute-done((bf16[16,64,128]{2,1,0:T(8,128)(2,1)}, bf16[16,64,128]{2,1,0:T(8,128)(2,1)S(1)}, u32[]{:S(2)}, u32[]{:S(2)}) %collective-permute-start.10) | collective-permute-done | bytes 262176 | tf_op jit(solution)/shard_map/ppermute | solution.py:345
  101.3 0.7 copy-done.8
  102.0 2.6 %shard_map.168 = bf16[16,64,256]{2,1,0:T(8,128)(2,1)} custom-call(bf16[16,64,128]{2,1,0:T(8,128)(2,1)} %get-tuple-element.61.own_ref, bf16[16,64,128]{2,1,0:T(8,128)(2,1)} %copy-done.8, f32[64,64,256]{2,1,0:T(8,128)} %fusion.3.v_ref, bf16[128,256]{1,0:T(8,128)(2,1)} %get-tuple-element.74.fo_ref, bf16[128,256]{1,0:T(8,128)(2,1)} %get-tuple-element.73.fr_ref), custom_call_target="tpu_custom_call" | custom-call | tf_op jit(solution)/shard_map/pallas_call | solution.py:131
  104.7 1.7 %fusion.7 = bf16[64,256,48]{1,2,0:T(8,128)(2,1)S(1)} fusion(bf16[16,64,256]{2,1,0:T(8,128)(2,1)} %shard_map.168, bf16[48,16]{0,1:T(8,128)(2,1)S(1)} %copy-done.13), kind=kOutput, calls=%fused_computation.14 | convolution fusion | flops 25165824 | bytes 2098688 | tf_op jit(solution)/shard_map/dot_general | solution.py:397
  106.3 1.7 %copy.40 = bf16[64,256,48]{1,0,2:T(8,128)(2,1)} copy(bf16[64,256,48]{1,2,0:T(8,128)(2,1)S(1)} %fusion.7) | data formatting | bytes 3145728 | tf_op jit(solution)/shard_map/dot_general | solution.py:397
  108.0 0.6 call_exported.1.st_ref.se_ref
  108.6 0.5 call_exported.0.sj_ref
  109.1 6.4 %shard_map.169 = (bf16[1,48,64,128]{3,2,1,0:T(8,128)(2,1)}, bf16[1,48,64,128]{3,2,1,0:T(8,128)(2,1)}) custom-call(s32[3]{0:T(128)} %call_exported.0.sj_ref, s32[3]{0:T(128)} %call_exported.1.st_ref.se_ref, s32[3]{0:T(128)} %call_exported.1.st_ref.se_ref, s32[1]{0:T(128)} %bitcast.me_ref, bf16[1,48,64,256]{3,2,1,0:T(8,128)(2,1)} %bitcast.89, ...), custom_call_target="tpu_custom_call" | custom-call | tf_op jit(solution)/shard_map/pallas_call | solution.py:174
  115.6 7.1 %shard_map.170.prod_ref = bf16[48,128,128]{2,1,0:T(8,128)(2,1)} custom-call(bf16[128,64]{1,0:T(8,128)(2,1)} %get-tuple-element.78.refs_0_.fo_ref, bf16[128,64]{1,0:T(8,128)(2,1)} %get-tuple-element.77.refs_1_.fr_ref, bf16[48,128,128]{2,1,0:T(8,128)(2,1)} %bitcast.87, bf16[3,64,128,128]{3,2,1,0:T(8,128)(2,1)} %copy-done.2, ...), custom_call_target="tpu_custom_call" | custom-call | tf_op jit(solution)/shard_map/pallas_call | solution.py:223
  122.7 1.0 copy-done.4
  123.7 4.4 %shard_map.171 = bf16[48,128,128]{2,1,0:T(8,128)(2,1)} custom-call(bf16[128,64]{1,0:T(8,128)(2,1)} %get-tuple-element.78.refs_0_.fo_ref, bf16[128,64]{1,0:T(8,128)(2,1)} %get-tuple-element.77.refs_1_.fr_ref, bf16[48,64,128]{2,1,0:T(8,128)(2,1)} %bitcast.100, bf16[48,64,128]{2,1,0:T(8,128)(2,1)} %bitcast.101, bf16[48,128,128]{2,1,0:T(8,128)(2,1)} %shard_map.170.prod_ref, ...), custom_call_target="tpu_custom_call" | custom-call | tf_op jit(solution)/shard_map/pallas_call | solution.py:257
  (65 shorter events, 3.4 us)
Async XLA Ops:
  0.0 34.0 %copy-start = (bf16[3,48,16]{1,2,0:T(8,128)(2,1)S(1)}, bf16[3,48,16]{1,2,0:T(8,128)(2,1)}, u32[]{:S(2)}) copy-start(bf16[3,48,16]{1,2,0:T(8,128)(2,1)} %param.19) | copy-start | bytes 13828
  0.0 20.7 %collective-permute-start = (bf16[3,8,128,128]{3,2,1,0:T(8,128)(2,1)}, bf16[3,8,128,128]{3,2,1,0:T(8,128)(2,1)S(1)}, u32[]{:S(2)}, u32[]{:S(2)}) collective-permute-start(bf16[3,8,128,128]{3,2,1,0:T(8,128)(2,1)} %bitcast.102), channel_id=1, source_target_pairs={{0,4},{4,8},{8,12},{12,14},{14,10},{10,6},{6,2},{2,0},{1,5},{5,9},... | collective-permute-start | bytes 2359304 | tf_op jit(solution)/shard_map/ppermute | solution.py:313
  3.0 19.3 %collective-permute-start.1 = (bf16[3,8,128,128]{3,2,1,0:T(8,128)(2,1)}, bf16[3,8,128,128]{3,2,1,0:T(8,128)(2,1)}, u32[]{:S(2)}, u32[]{:S(2)}) collective-permute-start(bf16[3,8,128,128]{3,2,1,0:T(8,128)(2,1)} %bitcast.103), channel_id=1, source_target_pairs={{0,2},{4,0},{8,4},{12,8},{14,12},{10,14},{6,10},{2,6},{1,3},{5,1},... | collective-permute-start | bytes 2359304 | tf_op jit(solution)/shard_map/ppermute | solution.py:314
  3.0 9.3 %copy-start.12 = (s32[8]{0:T(128)}, s32[8]{0:T(128)S(1)}, u32[]{:S(2)}) copy-start(s32[8]{0:T(128)S(1)} %get-tuple-element.135) | copy-start | bytes 100
  7.2 17.2 %copy-start.9 = (bf16[256,256]{1,0:T(8,128)(2,1)S(1)}, bf16[256,256]{1,0:T(8,128)(2,1)}, u32[]{:S(2)}) copy-start(bf16[256,256]{1,0:T(8,128)(2,1)} %constant.255.clone) | copy-start | bytes 393220
  12.1 16.1 %collective-permute-start.4 = (bf16[48,64,128]{2,1,0:T(8,128)(2,1)}, bf16[48,64,128]{2,1,0:T(8,128)(2,1)S(1)}, u32[]{:S(2)}, u32[]{:S(2)}) collective-permute-start(bf16[48,64,128]{2,1,0:T(8,128)(2,1)} %get-tuple-element.43), channel_id=1, source_target_pairs={{0,1},{1,0},{2,3},{3,2},{4,5},{5,4},{6,7},{7,6},{8,9},{9,8},{10,11... | collective-permute-start | bytes 2359304 | tf_op jit(solution)/shard_map/ppermute | solution.py:345
  20.7 13.3 %copy-start.6 = (bf16[3,8,128,128]{3,2,1,0:T(8,128)(2,1)}, bf16[3,8,128,128]{3,2,1,0:T(8,128)(2,1)S(1)}, u32[]{:S(2)}) copy-start(bf16[3,8,128,128]{3,2,1,0:T(8,128)(2,1)S(1)} %collective-permute-done) | copy-start | bytes 2359300
  22.3 18.4 %collective-permute-start.2 = (bf16[3,8,128,128]{3,2,1,0:T(8,128)(2,1)S(1)}, bf16[3,8,128,128]{3,2,1,0:T(8,128)(2,1)}, u32[]{:S(2)}, u32[]{:S(2)}) collective-permute-start(bf16[3,8,128,128]{3,2,1,0:T(8,128)(2,1)S(1)} %collective-permute-done), channel_id=1, source_target_pairs={{0,4},{4,8},{8,12},{12,14},{14,10},{10,6},{6,2},{2,0},{1,5},{5,9},... | collective-permute-start | bytes 2359304 | tf_op jit(solution)/shard_map/ppermute | solution.py:313
  23.9 18.1 %collective-permute-start.3 = (bf16[3,8,128,128]{3,2,1,0:T(8,128)(2,1)}, bf16[3,8,128,128]{3,2,1,0:T(8,128)(2,1)}, u32[]{:S(2)}, u32[]{:S(2)}) collective-permute-start(bf16[3,8,128,128]{3,2,1,0:T(8,128)(2,1)} %collective-permute-done.1), channel_id=1, source_target_pairs={{0,2},{4,0},{8,4},{12,8},{14,12},{10,14},{6,10},{2,6},{1,3},{5,1},... | collective-permute-start | bytes 2359304 | tf_op jit(solution)/shard_map/ppermute | solution.py:314
  28.3 0.9 copy-start.3
  42.0 18.1 %collective-permute-start.5 = (bf16[3,8,128,128]{3,2,1,0:T(8,128)(2,1)}, bf16[3,8,128,128]{3,2,1,0:T(8,128)(2,1)S(1)}, u32[]{:S(2)}, u32[]{:S(2)}) collective-permute-start(bf16[3,8,128,128]{3,2,1,0:T(8,128)(2,1)} %collective-permute-done.2), channel_id=1, source_target_pairs={{0,4},{4,8},{8,12},{12,14},{14,10},{10,6},{6,2},{2,0},{1,5},{5,9},... | collective-permute-start | bytes 2359304 | tf_op jit(solution)/shard_map/ppermute | solution.py:313
  43.6 16.9 %collective-permute-start.6 = (bf16[3,8,128,128]{3,2,1,0:T(8,128)(2,1)}, bf16[3,8,128,128]{3,2,1,0:T(8,128)(2,1)}, u32[]{:S(2)}, u32[]{:S(2)}) collective-permute-start(bf16[3,8,128,128]{3,2,1,0:T(8,128)(2,1)} %collective-permute-done.3), channel_id=1, source_target_pairs={{0,2},{4,0},{8,4},{12,8},{14,12},{10,14},{6,10},{2,6},{1,3},{5,1},... | collective-permute-start | bytes 2359304 | tf_op jit(solution)/shard_map/ppermute | solution.py:314
  47.4 13.1 %copy-start.14 = (s32[8]{0:T(128)S(1)}, s32[8]{0:T(128)}, u32[]{:S(2)}) copy-start(s32[8]{0:T(128)} %constant.254.clone) | copy-start | bytes 100
  47.4 18.4 %copy-start.11 = (s32[8]{0:T(128)S(1)}, s32[8]{0:T(128)}, u32[]{:S(2)}) copy-start(s32[8]{0:T(128)} %constant.253.clone) | copy-start | bytes 100
  47.4 23.6 %copy-start.10 = (bf16[128,128]{1,0:T(8,128)(2,1)S(1)}, bf16[128,128]{1,0:T(8,128)(2,1)}, u32[]{:S(2)}) copy-start(bf16[128,128]{1,0:T(8,128)(2,1)} %constant.256.clone) | copy-start | bytes 98308
  60.6 28.5 %collective-permute-start.9 = (bf16[3,48,64,128]{3,2,1,0:T(8,128)(2,1)}, bf16[3,48,64,128]{3,2,1,0:T(8,128)(2,1)S(1)}, u32[]{:S(2)}, u32[]{:S(2)}) collective-permute-start(bf16[3,48,64,128]{3,2,1,0:T(8,128)(2,1)} %get-tuple-element.60), channel_id=1, source_target_pairs={{0,1},{1,0},{2,3},{3,2},{4,5},{5,4},{6,7},{7,6},{8,9},{9,8},{10,11... | collective-permute-start | bytes 7077896 | tf_op jit(solution)/shard_map/ppermute | solution.py:345
  71.0 2.3 %copy-start.5 = (bf16[1,3,8,128,128]{4,3,2,1,0:T(8,128)(2,1)S(1)}, bf16[1,3,8,128,128]{4,3,2,1,0:T(8,128)(2,1)}, u32[]{:S(2)}) copy-start(bf16[1,3,8,128,128]{4,3,2,1,0:T(8,128)(2,1)} %param.18) | copy-start | bytes 2359300
  71.0 2.4 %copy-start.7 = (bf16[3,8,128,128]{3,2,1,0:T(8,128)(2,1)S(1)}, bf16[3,8,128,128]{3,2,1,0:T(8,128)(2,1)}, u32[]{:S(2)}) copy-start(bf16[3,8,128,128]{3,2,1,0:T(8,128)(2,1)} %copy-done.6) | copy-start | bytes 2359300
  77.1 11.6 %collective-permute-start.8 = (bf16[3,8,64,128]{3,2,1,0:T(8,128)(2,1)S(1)}, bf16[3,8,64,128]{3,2,1,0:T(8,128)(2,1)S(1)}, u32[]{:S(2)}, u32[]{:S(2)}) collective-permute-start(bf16[3,8,64,128]{3,2,1,0:T(8,128)(2,1)S(1)} %slice.7), channel_id=1, source_target_pairs={{0,2},{4,0},{8,4},{12,8},{14,12},{10,14},{6,10},{2,6},{1,3},{5,1},... | collective-permute-start | bytes 1179656 | tf_op jit(solution)/shard_map/ppermute | solution.py:324
  77.7 11.3 %collective-permute-start.7 = (bf16[3,8,64,128]{3,2,1,0:T(8,128)(2,1)S(1)}, bf16[3,8,64,128]{3,2,1,0:T(8,128)(2,1)S(1)}, u32[]{:S(2)}, u32[]{:S(2)}) collective-permute-start(bf16[3,8,64,128]{3,2,1,0:T(8,128)(2,1)S(1)} %slice.6), channel_id=1, source_target_pairs={{0,4},{4,8},{8,12},{12,14},{14,10},{10,6},{6,2},{2,0},{1,5},{5,9},... | collective-permute-start | bytes 1179656 | tf_op jit(solution)/shard_map/ppermute | solution.py:323
  89.1 2.7 %copy-start.2 = (bf16[3,64,128,128]{3,2,1,0:T(8,128)(2,1)}, bf16[3,64,128,128]{3,2,1,0:T(8,128)(2,1)S(1)}, u32[]{:S(2)}) copy-start(bf16[3,64,128,128]{3,2,1,0:T(8,128)(2,1)S(1)} %maximum_dynamic-update-slice_fusion.refs_3_) | copy-start | bytes 18874372
  91.8 1.4 %copy-start.1 = (bf16[3,48,64,128]{3,2,1,0:T(8,128)(2,1)}, bf16[3,48,64,128]{3,2,1,0:T(8,128)(2,1)S(1)}, u32[]{:S(2)}) copy-start(bf16[3,48,64,128]{3,2,1,0:T(8,128)(2,1)S(1)} %collective-permute-done.9.refs_5_.refs_7_.refs_9_) | copy-start | bytes 7077892
  97.0 7.7 %copy-start.13 = (bf16[48,16]{0,1:T(8,128)(2,1)S(1)}, bf16[48,16]{0,1:T(8,128)(2,1)}, u32[]{:S(2)}) copy-start(bf16[48,16]{0,1:T(8,128)(2,1)} %param.20) | copy-start | bytes 4612
  99.6 1.7 %collective-permute-start.10 = (bf16[16,64,128]{2,1,0:T(8,128)(2,1)}, bf16[16,64,128]{2,1,0:T(8,128)(2,1)S(1)}, u32[]{:S(2)}, u32[]{:S(2)}) collective-permute-start(bf16[16,64,128]{2,1,0:T(8,128)(2,1)} %get-tuple-element.62), channel_id=1, source_target_pairs={{0,1},{1,0},{2,3},{3,2},{4,5},{5,4},{6,7},{7,6},{8,9},{9,8},{10,11... | collective-permute-start | bytes 786440 | tf_op jit(solution)/shard_map/ppermute | solution.py:345
  101.3 0.7 copy-start.8
  115.5 7.2 %collective-permute-start.11 = (bf16[1,48,64,128]{3,2,1,0:T(8,128)(2,1)}, bf16[1,48,64,128]{3,2,1,0:T(8,128)(2,1)S(1)}, u32[]{:S(2)}, u32[]{:S(2)}) collective-permute-start(bf16[1,48,64,128]{3,2,1,0:T(8,128)(2,1)} %get-tuple-element.64), channel_id=1, source_target_pairs={{0,1},{1,0},{2,3},{3,2},{4,5},{5,4},{6,7},{7,6},{8,9},{9,8},{10,11... | collective-permute-start | bytes 2359304 | tf_op jit(solution)/shard_map/ppermute | solution.py:345
  122.7 1.0 copy-start.4

commit v8 on v7

--- a/solution.py
+++ b/solution.py
@@ -143,7 +143,8 @@
     )(own, recv, v_row, f_own, f_oth)
 
 
-def _fwd_col_kernel(sj_ref, st_ref, se_ref, me_ref, x_ref, v_ref, w_ref, ft_ref, own_ref, send_ref):
+def _fwd_col_kernel(sj_ref, st_ref, se_ref, me_ref, x_ref, v_ref, w_ref, ft_ref, *rest):
+    own_ref, send_ref = rest[-2:]
     n, rows_l, cols = x_ref.shape
     g = (x_ref[...].astype(F32) * v_ref[...]).astype(BF16)
     h = jnp.dot(g.reshape(n * rows_l, cols), ft_ref[...], preferred_element_type=F32)
@@ -152,7 +153,7 @@
     _split_store(me_ref, h[:, :, :half], h[:, :, half:], own_ref, send_ref)
 
 
-def fwd_col(me_arr, x, v_row, w_row, ft, steps):
+def fwd_col(me_arr, x, v_row, w_row, ft, steps, into=None):
     groups, n, rows_l, cols = x.shape
     half = cols // 2
     sj, st, se = (jnp.array([step[k] for step in steps], I32) for k in range(3))
@@ -168,22 +169,28 @@
             ts,
             ts,
             pl.BlockSpec((cols, cols), lambda i, a, b, c: (0, 0)),
-        ],
+        ]
+        + ([pl.BlockSpec(memory_space=pl.ANY)] * 2 if into else []),
         out_specs=[os, os],
     )
     return pl.pallas_call(
         _fwd_col_kernel,
         grid_spec=grid_spec,
         out_shape=[jax.ShapeDtypeStruct((groups, n, rows_l, half), BF16)] * 2,
-    )(sj, st, se, me_arr, x, v_row, w_row, ft)
+        input_output_aliases={8: 0, 9: 1} if into else {},
+        cost_estimate=pl.CostEstimate(
+            flops=2 * len(steps) * BLK * rows_l * cols * cols,
+            transcendentals=0,
+            bytes_accessed=len(steps) * BLK * rows_l * cols * 12,
+        ),
+    )(sj, st, se, me_arr, x, v_row, w_row, ft, *(into or ()))
 
 
 def _product_kernel(eb0, fo_ref, fr_ref, cip_ref, key_ref, *rest):
     halves = rest[: 2 * DIGITS]
     out_ref, acc_ref = rest[2 * DIGITS :]
     eb = pl.program_id(0) + eb0
-    fo = fo_ref[...]
-    fr = fr_ref[...]
+    f = jnp.concatenate([fo_ref[...], fr_ref[...]], axis=1)
     acc_ref[...] = jnp.zeros_like(acc_ref)
     n = acc_ref.shape[0]
     for j in range(DIGITS):
@@ -196,8 +203,8 @@
         @pl.when(eb != j)
         def _():
             for l in range(n):
-                y = jnp.dot(fo, own_ref[l], preferred_element_type=F32)
-                y = (y + jnp.dot(fr, recv_ref[l], preferred_element_type=F32)).astype(BF16)
+                h = jnp.concatenate([own_ref[l], recv_ref[l]], axis=0)
+                y = jnp.dot(f, h, preferred_element_type=F32).astype(BF16)
                 acc_ref[l] += y.astype(F32) * key_ref[j, l].astype(F32)
 
     out_ref[...] = acc_ref[...].astype(BF16)
@@ -239,13 +246,12 @@
 
 
 def _final_kernel(fo_ref, fr_ref, own_ref, recv_ref, prod_ref, s_ref, out_ref):
-    fo = fo_ref[...]
-    fr = fr_ref[...]
+    f = jnp.concatenate([fo_ref[...], fr_ref[...]], axis=1)
     n = own_ref.shape[0]
     base = pl.program_id(0) * n
     for l in range(n):
-        y = jnp.dot(fo, own_ref[l], preferred_element_type=F32)
-        y = (y + jnp.dot(fr, recv_ref[l], preferred_element_type=F32)).astype(BF16)
+        h = jnp.concatenate([own_ref[l], recv_ref[l]], axis=0)
+        y = jnp.dot(f, h, preferred_element_type=F32).astype(BF16)
         diff = prod_ref[l].astype(F32) - y.astype(F32)
         out_ref[l] = (diff * s_ref[base + l]).astype(BF16)
 
@@ -319,9 +325,13 @@
             st["full"], st["b"], order[(p + s) % n] * width, axis=1
         )
     else:
-        h = st["a"].shape[2] // 2
-        a = lax.ppermute(st["a"][:, :, :h], "limb", st["cw"])
-        b = lax.ppermute(st["b"][:, :, h:], "limb", st["ccw"])
+        if st.get("halved"):
+            a = lax.ppermute(st["a"], "limb", st["cw"])
+            b = lax.ppermute(st["b"], "limb", st["ccw"])
+        else:
+            h = st["a"].shape[2] // 2
+            a = lax.ppermute(st["a"][:, :, :h], "limb", st["cw"])
+            b = lax.ppermute(st["b"][:, :, h:], "limb", st["ccw"])
         src = order[(p + s) % n] * width
         st["full"] = lax.dynamic_update_slice_in_dim(
             st["full"], jnp.concatenate([a, b], axis=2), src, axis=1
@@ -331,7 +341,11 @@
 def ring_hold(st, x):
     if st["s"] >= ring_steps(st):
         return x
-    st["a"], st["b"], x = lax.optimization_barrier((st["a"], st["b"], x))
+    if 2 * (st["s"] + 1) >= st["n"]:
+        h = st["a"].shape[2] // 2
+        st["a"], st["b"] = st["a"][:, :, :h], st["b"][:, :, h:]
+        st["halved"] = True
+    st["a"], st["b"], st["full"], x = lax.optimization_barrier((st["a"], st["b"], st["full"], x))
     ring_step(st)
     return x
 
@@ -384,8 +398,10 @@
         for j in range(DIGITS):
             if j != eb:
                 digit_steps.append((j, eb if eb < j else eb - 1, eb))
-    own2, send2 = fwd_col(me_arr, raised, v_row, w_row, ft_cols, digit_steps)
-    own2, send2 = ring_hold(ring, (own2, send2))
+    cut = len(digit_steps) // 2
+    first = fwd_col(me_arr, raised, v_row, w_row, ft_cols, digit_steps[:cut])
+    first = ring_hold(ring, first)
+    own2, send2 = fwd_col(me_arr, raised, v_row, w_row, ft_cols, digit_steps[cut:], first)
     recv2 = swap(send2)
     key = ring_finish(ring)
 

time: 129 us -> 153 us (1.19)
  local copies, waits for them, and re-layouts: 25.5 us -> 39.7 us
  other arithmetic: 13.4 us -> 18.1 us
  waiting for transfers between devices: 16.5 us -> 19.4 us
    mul x4, local copies, waits for them, and re-layouts: 0.83 us -> 4.77 us  [_twiddle(): return 1.0 + 0.5 * (cp * cq - sp * sq)]
    dynamic_update_slice x3, local copies, waits for them, and re-layouts: 1.48 us -> 4.4 us  [ring_step(): lax.dynamic_update_slice_in_dim(st['full'], st['a'], order[(p - s) % n] *...]
    broadcast_in_dim x1, local copies, waits for them, and re-layouts: 1.57 us -> 4.26 us  [ring_setup(): full = jnp.zeros((shard.shape[0], n * width) + shard.shape[2:], shard.dtype)]
    ppermute x3, starting transfers between devices: 0.9 us -> 3.57 us  [ring_step(): st['b'] = lax.ppermute(st['b'], 'limb', st['ccw'])]
    ppermute x3, starting transfers between devices: 6.18 us -> 3.56 us  [ring_step(): st['a'] = lax.ppermute(st['a'], 'limb', st['cw'])]
    unnamed x30 -> x32, local copies, waits for them, and re-layouts: 6.68 us -> 4.07 us
    ppermute x2, waiting for transfers between devices: 7.02 us -> 9.49 us  [the longest x1 8.21 us: ring_step(): a = lax.ppermute(st['a'], 'limb', st['cw'])]
    dynamic_update_slice x1, other arithmetic: 0.11 us -> 2.17 us  [ring_step(): lax.dynamic_update_slice_in_dim(st['full'], jnp.concatenate([a, b], axis=...]
  transfers between devices with their start and end apart: 12 -> 12, of which waited for: 7 -> 6; matrix products, arithmetic and copies ran while one was open for 25% -> 31% of each run, Pallas kernels for 23% -> 15%
where the time goes in v8:
time: 153 us; the launch traced here: 151 us
  Pallas kernels  50.5 us (33%)
  local copies, waits for them, and re-layouts  39.7 us (26%)
  waiting for transfers between devices  19.4 us (13%)
  other arithmetic  18.1 us (12%)
  between operations  9.65 us (6%)
  starting transfers between devices  9.29 us (6%)
  matrix products  4.53 us (3%)
    pallas_call x3, Pallas kernels, fwd_col(): pl.pallas_call(_fwd_col_kernel, grid_spec=grid_spec, out_shape=[jax.Shape...  20.8 us
    pallas_call x2, Pallas kernels, product(): pl.pallas_call(lambda *refs: _product_kernel(eb0, *refs), grid=(nblocks,)...  10.4 us
    add x3, other arithmetic, _twiddle(): return 1.0 + 0.5 * (cp * cq - sp * sq)  10 us
    ppermute x1, waiting for transfers between devices, ring_step(): a = lax.ppermute(st['a'], 'limb', st['cw'])  8.21 us
    pallas_call x2, Pallas kernels, inv_col(): pl.pallas_call(_inv_col_kernel, grid=(n // BLK,), in_specs=[blk, blk, pl....  7.47 us
    pallas_call x2, Pallas kernels, inv_row(): pl.pallas_call(_inv_row_kernel, grid=(n // BLK,), in_specs=[SMEM_SPEC, bl...  7.41 us
    dynamic_update_slice x3, local copies, waits for them, and re-layouts, ring_step(): lax.dynamic_update_slice_in_dim(st['full'], st['b'], order[(p + s) % n] *...  5.49 us
    ppermute x3, waiting for transfers between devices, ring_step(): st['a'] = lax.ppermute(st['a'], 'limb', st['cw'])  5.01 us
  transfers between devices with their start and end apart: 12, of which 6 were waited for; matrix products, arithmetic and copies ran while one was open for 31% of the time, Pallas kernels for 15%

profile of v8, /device:TPU:0, one launch (start us, length us, event | category | flops | bytes accessed | tf_op | source)
XLA Modules:
  0.0 151.2 jit_solution(4780287828302022929)
XLA Ops:
  0.0 3.0 %collective-permute-start.1 = (bf16[3,8,128,128]{3,2,1,0:T(8,128)(2,1)}, bf16[3,8,128,128]{3,2,1,0:T(8,128)(2,1)S(1)}, u32[]{:S(2)}, u32[]{:S(2)}) collective-permute-start(bf16[3,8,128,128]{3,2,1,0:T(8,128)(2,1)} %bitcast.103), channel_id=1, source_target_pairs={{0,2},{4,0},{8,4},{12,8},{14,12},{10,14},{6,10},{2,6},{1,3},{5,1},... | collective-permute-start | bytes 2359304 | tf_op jit(solution)/shard_map/ppermute | solution.py:320
  4.4 2.9 %add_bitcast_fusion.1.w_ref = f32[64,128,128]{2,1,0:T(8,128)} fusion(f32[64,8,128]{2,1,0:T(8,128)S(1)} %bitcast.99, f32[64,16,128]{2,1,0:T(8,128)S(1)} %bitcast.97, f32[64,8,128]{2,1,0:T(8,128)S(1)} %bitcast.100, f32[64,16,128]{2,1,0:T(8,128)S(1)} %bitcast.98), kind=kLoop, calls=%fused_computation.8 | loop fusion | flops 5242880 | bytes 5767168 | tf_op jit(solution)/shard_map/add | solution.py:53
  7.2 4.8 %shard_map.190 = (bf16[48,64,128]{2,1,0:T(8,128)(2,1)}, bf16[48,64,128]{2,1,0:T(8,128)(2,1)}) custom-call(s32[1]{0:T(128)} %bitcast.me_ref, bf16[48,128,128]{2,1,0:T(8,128)(2,1)} %bitcast.86, f32[64,128,128]{2,1,0:T(8,128)} %add_bitcast_fusion.1.w_ref, bf16[128,128]{1,0:T(8,128)(2,1)} %constant.263.clone.ft_ref), custom_call_target="tpu_custom_call" | custom-call | tf_op jit(solution)/shard_map/pallas_call | solution.py:101
  12.4 2.4 %fusion.50 = (f32[8,8,256]{2,1,0:T(8,128)S(1)}, f32[8,8,256]{2,1,0:T(8,128)S(1)}, f32[8,8,256]{2,1,0:T(8,128)S(1)}, f32[8,8,256]{2,1,0:T(8,128)S(1)}, f32[8,8,25...) fusion(s32[8,256]{1,0:T(8,128)S(1)} %add_select_fusion.12, ...), kind=kLoop, calls=%fused_computation.119 | loop fusion | flops 1376256 | bytes 811072 | tf_op jit(solution)/shard_map/cos | solution.py:35
  15.7 1.4 add.605
  17.1 1.4 sub.135
  18.5 1.3 broadcast_bitcast_fusion.1
  19.8 4.3 %broadcast_in_dim.6 = bf16[3,64,128,128]{3,2,1,0:T(8,128)(2,1)} broadcast(bf16[]{:T(256)} %constant.239.clone.1), dimensions={} | broadcast | bytes 6291458 | tf_op jit(solution)/shard_map/broadcast_in_dim | solution.py:294
  24.1 1.1 constant_dynamic-update-slice_fusion.6
  25.7 1.3 dynamic_slice.38
  34.0 2.3 %constant_dynamic-update-slice_fusion.5 = bf16[3,64,128,128]{3,2,1,0:T(8,128)(2,1)} fusion(bf16[3,64,128,128]{3,2,1,0:T(8,128)(2,1)} %constant_dynamic-update-slice_fusion.6, bf16[3,8,128,128]{3,2,1,0:T(8,128)(2,1)} %collective-permute-done, s32[]{:T(128)S(6)} %select_n.357), kind=kLoop, calls=%fused_computation.189 | loop fusion | bytes 1572868 | tf_op jit(solution)/shard_map/dynamic_update_slice | solution.py:321
  36.2 1.1 constant_dynamic-update-slice_fusion.4
  37.3 1.9 %collective-permute-start.2 = (bf16[3,8,128,128]{3,2,1,0:T(8,128)(2,1)}, bf16[3,8,128,128]{3,2,1,0:T(8,128)(2,1)S(1)}, u32[]{:S(2)}, u32[]{:S(2)}) collective-permute-start(bf16[3,8,128,128]{3,2,1,0:T(8,128)(2,1)} %collective-permute-done), channel_id=1, source_target_pairs={{0,4},{4,8},{8,12},{12,14},{14,10},{10,6},{6,2},{2,0},{1,5},{5,9},... | collective-permute-start | bytes 2359304 | tf_op jit(solution)/shard_map/ppermute | solution.py:319
  39.2 1.5 %constant_dynamic-slice_fusion = (bf16[128,256]{1,0:T(8,128)(2,1)}, bf16[128,256]{1,0:T(8,128)(2,1)}) fusion(bf16[256,256]{1,0:T(8,128)(2,1)} %constant.261.clone, s32[]{:T(128)S(6)} %select_n.380, s32[]{:T(128)S(6)} %select_n.379), kind=kLoop, calls=%fused_computation.184 | loop fusion | bytes 262152 | tf_op jit(solution)/shard_map/dynamic_slice | solution.py:380
  42.1 1.4 copy.27
  43.5 1.4 copy.28
  45.1 4.1 %fusion.3.v_ref = f32[64,64,256]{2,1,0:T(8,128)} fusion(f32[64,64]{1,0:T(8,128)} %copy.28, f32[64,8,256]{2,1,0:T(8,128)S(1)} %bitcast.95, f32[64,64]{1,0:T(8,128)} %copy.27, f32[64,8,256]{2,1,0:T(8,128)S(1)} %bitcast.96), kind=kLoop, calls=%fused_computation.5 | loop fusion | flops 5242880 | bytes 5275648 | tf_op jit(solution)/shard_map/add | solution.py:53
  49.1 0.9 copy-done.2
  50.1 4.8 %shard_map.191 = bf16[48,64,256]{2,1,0:T(8,128)(2,1)} custom-call(bf16[48,64,128]{2,1,0:T(8,128)(2,1)} %get-tuple-element.48.own_ref, bf16[48,64,128]{2,1,0:T(8,128)(2,1)} %copy-done.2, f32[64,64,256]{2,1,0:T(8,128)} %fusion.3.v_ref, bf16[128,256]{1,0:T(8,128)(2,1)} %get-tuple-element.84.fo_ref, bf16[128,256]{1,0:T(8,128)(2,1)} %get-tuple-element.83.fr_ref), custom_call_target="tpu_custom_call" | custom-call | tf_op jit(solution)/shard_map/pallas_call | solution.py:131
  54.9 2.9 %fusion.5 = bf16[3,64,256,48]{2,3,1,0:T(8,128)(2,1)S(1)} fusion(bf16[3,16,64,256]{3,2,1,0:T(8,128)(2,1)} %bitcast.89, bf16[3,48,16]{1,2,0:T(8,128)(2,1)S(1)} %copy-done), kind=kOutput, calls=%fused_computation.11 | convolution fusion | flops 75497472 | bytes 6296064 | tf_op jit(solution)/shard_map/dot_general | solution.py:391
  57.8 3.9 %copy.44 = bf16[3,64,256,48]{2,1,3,0:T(8,128)(2,1)} copy(bf16[3,64,256,48]{2,3,1,0:T(8,128)(2,1)S(1)} %fusion.5) | data formatting | bytes 9437184 | tf_op jit(solution)/shard_map/dot_general | solution.py:391
  61.7 1.1 constant_dynamic-update-slice_fusion.3
  62.9 1.9 %collective-permute-done.3 = bf16[3,8,128,128]{3,2,1,0:T(8,128)(2,1)} collective-permute-done((bf16[3,8,128,128]{3,2,1,0:T(8,128)(2,1)S(1)}, bf16[3,8,128,128]{3,2,1,0:T(8,128)(2,1)}, u32[]{:S(2)}, u32[]{:S(2)}) %collective-permute-start.3) | collective-permute-done | bytes 786464 | tf_op jit(solution)/shard_map/ppermute | solution.py:320
  64.7 2.2 %constant_dynamic-update-slice_fusion.2 = bf16[3,64,128,128]{3,2,1,0:T(8,128)(2,1)} fusion(bf16[3,64,128,128]{3,2,1,0:T(8,128)(2,1)} %constant_dynamic-update-slice_fusion.3, bf16[3,8,128,128]{3,2,1,0:T(8,128)(2,1)} %collective-permute-done.3, s32[]{:T(128)S(6)} %select_n.372), kind=kLoop, calls=%fused_computation.186 | loop fusion | bytes 1572868 | tf_op jit(solution)/shard_map/dynamic_update_slice | solution.py:324
  67.0 1.5 collective-permute-start.5
  70.4 1.0 multiply_add_fusion.1
  71.4 3.1 %add_bitcast_fusion.w_ref = f32[64,64,256]{2,1,0:T(8,128)} fusion(f32[64,8,256]{2,1,0:T(8,128)S(1)} %bitcast.91, f32[64,8,256]{2,1,0:T(8,128)S(1)} %bitcast.93, f32[64,8,256]{2,1,0:T(8,128)S(1)} %bitcast.92, f32[64,8,256]{2,1,0:T(8,128)S(1)} %bitcast.94), kind=kLoop, calls=%fused_computation.7 | loop fusion | flops 5242880 | bytes 6291456 | tf_op jit(solution)/shard_map/add | solution.py:53
  74.5 6.5 %shard_map.192 = (bf16[3,48,64,128]{3,2,1,0:T(8,128)(2,1)}, bf16[3,48,64,128]{3,2,1,0:T(8,128)(2,1)}) custom-call(s32[4]{0:T(128)} %constant.264.clone.sj_ref, s32[4]{0:T(128)} %constant.265.clone.st_ref, s32[4]{0:T(128)} %constant.266.clone.se_ref, s32[1]{0:T(128)} %bitcast.me_ref, bf16[3,48,64,256]{3,2,1,0:T(8,128)(2,1)} %bitcast.84, ...), custom_call_target="tpu_custom_call" | custom-call | flops 536870912 | bytes 12582912 | tf_op jit(solution)/shard_map/pallas_call | solution.py:176
  81.0 5.0 %collective-permute-done.5 = bf16[3,8,128,128]{3,2,1,0:T(8,128)(2,1)S(1)} collective-permute-done((bf16[3,8,128,128]{3,2,1,0:T(8,128)(2,1)}, bf16[3,8,128,128]{3,2,1,0:T(8,128)(2,1)S(1)}, u32[]{:S(2)}, u32[]{:S(2)}) %collective-permute-start.5) | collective-permute-done | bytes 786464 | tf_op jit(solution)/shard_map/ppermute | solution.py:319
  86.1 1.3 collective-permute-done.6
  87.4 1.8 %slice.9 = bf16[3,8,64,128]{3,2,1,0:T(8,128)(2,1)} slice(bf16[3,8,128,128]{3,2,1,0:T(8,128)(2,1)} %collective-permute-done.6), slice={[0:3], [0:8], [64:128], [0:128]} | slice | bytes 786432 | tf_op jit(solution)/shard_map/slice | solution.py:346
  89.1 1.0 constant_dynamic-update-slice_fusion.1
  90.1 2.2 %constant_dynamic-update-slice_fusion = bf16[3,64,128,128]{3,2,1,0:T(8,128)(2,1)} fusion(bf16[3,64,128,128]{3,2,1,0:T(8,128)(2,1)} %constant_dynamic-update-slice_fusion.1, bf16[3,8,128,128]{3,2,1,0:T(8,128)(2,1)} %collective-permute-done.6, s32[]{:T(128)S(6)} %select_n.386), kind=kLoop, calls=%fused_computation.182 | loop fusion | bytes 1572868 | tf_op jit(solution)/shard_map/dynamic_update_slice | solution.py:324
  92.4 7.8 %shard_map.193 = (bf16[3,48,64,128]{3,2,1,0:T(8,128)(2,1)}, bf16[3,48,64,128]{3,2,1,0:T(8,128)(2,1)}) custom-call(s32[5]{0:T(128)} %constant.268.clone.sj_ref, s32[5]{0:T(128)} %constant.269.clone.st_ref, s32[5]{0:T(128)} %constant.270.clone.se_ref, s32[1]{0:T(128)} %bitcast.me_ref, ...), custom_call_target="tpu_custom_call", output_to_operand_aliasing={{0}: (8, {}), {1}: (9, {})} | custom-call | flops 671088640 | bytes 15728640 | tf_op jit(solution)/shard_map/pallas_call | solution.py:176
  100.2 1.6 %collective-permute-start.7 = (bf16[3,8,64,128]{3,2,1,0:T(8,128)(2,1)S(1)}, bf16[3,8,64,128]{3,2,1,0:T(8,128)(2,1)}, u32[]{:S(2)}, u32[]{:S(2)}) collective-permute-start(bf16[3,8,64,128]{3,2,1,0:T(8,128)(2,1)S(1)} %slice.8), channel_id=1, source_target_pairs={{0,4},{4,8},{8,12},{12,14},{14,10},{10,6},{6,2},{2,0},{1,5},{5,9},... | collective-permute-start | bytes 1179656 | tf_op jit(solution)/shard_map/ppermute | solution.py:329
  103.6 8.2 %collective-permute-done.7 = bf16[3,8,64,128]{3,2,1,0:T(8,128)(2,1)} collective-permute-done((bf16[3,8,64,128]{3,2,1,0:T(8,128)(2,1)S(1)}, bf16[3,8,64,128]{3,2,1,0:T(8,128)(2,1)}, u32[]{:S(2)}, u32[]{:S(2)}) %collective-permute-start.7) | collective-permute-done | bytes 393248 | tf_op jit(solution)/shard_map/ppermute | solution.py:329
  111.8 1.3 collective-permute-done.8
  113.1 2.2 %maximum_dynamic-update-slice_fusion.refs_3_ = bf16[3,64,128,128]{3,2,1,0:T(8,128)(2,1)} fusion(bf16[3,64,128,128]{3,2,1,0:T(8,128)(2,1)} %constant_dynamic-update-slice_fusion, s32[]{:T(128)S(6)} %select_n.395, bf16[3,8,64,128]{3,2,1,0:T(8,128)(2,1)} %collective-permute-done.8, bf16[3,8,64,128]{3,2,1,0:T(8,128)(2,1)} %collective-permute-done.7), kind=kLoop, calls=%fused_computation.13 | loop fusion | flops 1572864 | bytes 1572868 | tf_op jit(solution)/shard_map/dynamic_update_slice | solution.py:336
  115.3 1.5 copy-done.1
  116.8 3.5 %shard_map.194.y_ref = bf16[16,128,128]{2,1,0:T(8,128)(2,1)} custom-call(bf16[128,64]{1,0:T(8,128)(2,1)} %get-tuple-element.88.refs_0_.fo_ref, bf16[128,64]{1,0:T(8,128)(2,1)} %get-tuple-element.87.refs_1_.fr_ref, bf16[48,128,128]{2,1,0:T(8,128)(2,1)} %bitcast.87, bf16[3,64,128,128]{3,2,1,0:T(8,128)(2,1)} %maximum_dynamic-update-slice_fusion.refs_3_, ...), custom_call_target="tpu_custom_call" | custom-call | tf_op jit(solution)/shard_map/pallas_call | solution.py:230
  120.3 2.6 %shard_map.195 = (bf16[16,64,128]{2,1,0:T(8,128)(2,1)}, bf16[16,64,128]{2,1,0:T(8,128)(2,1)}) custom-call(s32[1]{0:T(128)} %bitcast.me_ref, bf16[16,128,128]{2,1,0:T(8,128)(2,1)} %shard_map.194.y_ref, f32[64,128,128]{2,1,0:T(8,128)} %add_bitcast_fusion.1.w_ref, bf16[128,128]{1,0:T(8,128)(2,1)} %constant.263.clone.ft_ref), custom_call_target="tpu_custom_call" | custom-call | tf_op jit(solution)/shard_map/pallas_call | solution.py:101
  122.9 1.7 %collective-permute-done.10.recv_ref = bf16[16,64,128]{2,1,0:T(8,128)(2,1)S(1)} collective-permute-done((bf16[16,64,128]{2,1,0:T(8,128)(2,1)}, bf16[16,64,128]{2,1,0:T(8,128)(2,1)S(1)}, u32[]{:S(2)}, u32[]{:S(2)}) %collective-permute-start.10) | collective-permute-done | bytes 262176 | tf_op jit(solution)/shard_map/ppermute | solution.py:359
  125.3 2.6 %shard_map.196 = bf16[16,64,256]{2,1,0:T(8,128)(2,1)} custom-call(bf16[16,64,128]{2,1,0:T(8,128)(2,1)} %get-tuple-element.71.own_ref, bf16[16,64,128]{2,1,0:T(8,128)(2,1)} %copy-done.11, f32[64,64,256]{2,1,0:T(8,128)} %fusion.3.v_ref, bf16[128,256]{1,0:T(8,128)(2,1)} %get-tuple-element.84.fo_ref, bf16[128,256]{1,0:T(8,128)(2,1)} %get-tuple-element.83.fr_ref), custom_call_target="tpu_custom_call" | custom-call | tf_op jit(solution)/shard_map/pallas_call | solution.py:131
  128.0 1.7 %fusion.7 = bf16[64,256,48]{1,2,0:T(8,128)(2,1)S(1)} fusion(bf16[16,64,256]{2,1,0:T(8,128)(2,1)} %shard_map.196, bf16[48,16]{0,1:T(8,128)(2,1)S(1)} %copy-done.15), kind=kOutput, calls=%fused_computation.14 | convolution fusion | flops 25165824 | bytes 2098688 | tf_op jit(solution)/shard_map/dot_general | solution.py:413
  129.6 1.7 %copy.45 = bf16[64,256,48]{1,0,2:T(8,128)(2,1)} copy(bf16[64,256,48]{1,2,0:T(8,128)(2,1)S(1)} %fusion.7) | data formatting | bytes 3145728 | tf_op jit(solution)/shard_map/dot_general | solution.py:413
  132.5 6.4 %shard_map.197 = (bf16[1,48,64,128]{3,2,1,0:T(8,128)(2,1)}, bf16[1,48,64,128]{3,2,1,0:T(8,128)(2,1)}) custom-call(s32[3]{0:T(128)} %call_exported.0.sj_ref, s32[3]{0:T(128)} %call_exported.1.st_ref.se_ref, s32[3]{0:T(128)} %call_exported.1.st_ref.se_ref, s32[1]{0:T(128)} %bitcast.me_ref, bf16[1,48,64,256]{3,2,1,0:T(8,128)(2,1)} %bitcast.90, ...), custom_call_target="tpu_custom_call" | custom-call | flops 402653184 | bytes 9437184 | tf_op jit(solution)/shard_map/pallas_call | solution.py:176
  139.0 6.9 %shard_map.198.prod_ref = bf16[48,128,128]{2,1,0:T(8,128)(2,1)} custom-call(bf16[128,64]{1,0:T(8,128)(2,1)} %get-tuple-element.88.refs_0_.fo_ref, bf16[128,64]{1,0:T(8,128)(2,1)} %get-tuple-element.87.refs_1_.fr_ref, bf16[48,128,128]{2,1,0:T(8,128)(2,1)} %bitcast.88, bf16[3,64,128,128]{3,2,1,0:T(8,128)(2,1)} %maximum_dynamic-update-slice_fusion.refs_3_, ...), custom_call_target="tpu_custom_call" | custom-call | tf_op jit(solution)/shard_map/pallas_call | solution.py:230
  146.8 4.4 %shard_map.199 = bf16[48,128,128]{2,1,0:T(8,128)(2,1)} custom-call(bf16[128,64]{1,0:T(8,128)(2,1)} %get-tuple-element.88.refs_0_.fo_ref, bf16[128,64]{1,0:T(8,128)(2,1)} %get-tuple-element.87.refs_1_.fr_ref, bf16[48,64,128]{2,1,0:T(8,128)(2,1)} %bitcast.101, bf16[48,64,128]{2,1,0:T(8,128)(2,1)} %bitcast.102, bf16[48,128,128]{2,1,0:T(8,128)(2,1)} %shard_map.198.prod_ref, ...), custom_call_target="tpu_custom_call" | custom-call | tf_op jit(solution)/shard_map/pallas_call | solution.py:263
  (68 shorter events, 8.7 us)
Async XLA Ops:
  0.0 54.9 %copy-start = (bf16[3,48,16]{1,2,0:T(8,128)(2,1)S(1)}, bf16[3,48,16]{1,2,0:T(8,128)(2,1)}, u32[]{:S(2)}) copy-start(bf16[3,48,16]{1,2,0:T(8,128)(2,1)} %param.22) | copy-start | bytes 13828
  0.0 36.2 %collective-permute-start.1 = (bf16[3,8,128,128]{3,2,1,0:T(8,128)(2,1)}, bf16[3,8,128,128]{3,2,1,0:T(8,128)(2,1)S(1)}, u32[]{:S(2)}, u32[]{:S(2)}) collective-permute-start(bf16[3,8,128,128]{3,2,1,0:T(8,128)(2,1)} %bitcast.103), channel_id=1, source_target_pairs={{0,2},{4,0},{8,4},{12,8},{14,12},{10,14},{6,10},{2,6},{1,3},{5,1},... | collective-permute-start | bytes 2359304 | tf_op jit(solution)/shard_map/ppermute | solution.py:320
  3.0 31.0 %collective-permute-start = (bf16[3,8,128,128]{3,2,1,0:T(8,128)(2,1)}, bf16[3,8,128,128]{3,2,1,0:T(8,128)(2,1)}, u32[]{:S(2)}, u32[]{:S(2)}) collective-permute-start(bf16[3,8,128,128]{3,2,1,0:T(8,128)(2,1)} %bitcast.104), channel_id=1, source_target_pairs={{0,4},{4,8},{8,12},{12,14},{14,10},{10,6},{6,2},{2,0},{1,5},{5,9},... | collective-permute-start | bytes 2359304 | tf_op jit(solution)/shard_map/ppermute | solution.py:319
  12.1 37.1 %collective-permute-start.4 = (bf16[48,64,128]{2,1,0:T(8,128)(2,1)}, bf16[48,64,128]{2,1,0:T(8,128)(2,1)S(1)}, u32[]{:S(2)}, u32[]{:S(2)}) collective-permute-start(bf16[48,64,128]{2,1,0:T(8,128)(2,1)} %get-tuple-element.49), channel_id=1, source_target_pairs={{0,1},{1,0},{2,3},{3,2},{4,5},{5,4},{6,7},{7,6},{8,9},{9,8},{10,11... | collective-permute-start | bytes 2359304 | tf_op jit(solution)/shard_map/ppermute | solution.py:359
  12.4 11.7 %copy-start.4 = (bf16[1,3,8,128,128]{4,3,2,1,0:T(8,128)(2,1)S(1)}, bf16[1,3,8,128,128]{4,3,2,1,0:T(8,128)(2,1)}, u32[]{:S(2)}) copy-start(bf16[1,3,8,128,128]{4,3,2,1,0:T(8,128)(2,1)} %param.21) | copy-start | bytes 2359300
  14.9 17.0 %copy-start.13 = (s32[8]{0:T(128)S(1)}, s32[8]{0:T(128)}, u32[]{:S(2)}) copy-start(s32[8]{0:T(128)} %constant.259.clone) | copy-start | bytes 100
  18.5 6.6 %copy-start.14 = (f32[64,1,8,1]{0,2,3,1:T(8,128)S(1)}, f32[64,1,8,1]{0,2,3,1:T(8,128)}, u32[]{:S(2)}) copy-start(f32[64,1,8,1]{0,2,3,1:T(8,128)} %add.605) | copy-start | bytes 6148
  37.3 24.4 %collective-permute-start.2 = (bf16[3,8,128,128]{3,2,1,0:T(8,128)(2,1)}, bf16[3,8,128,128]{3,2,1,0:T(8,128)(2,1)S(1)}, u32[]{:S(2)}, u32[]{:S(2)}) collective-permute-start(bf16[3,8,128,128]{3,2,1,0:T(8,128)(2,1)} %collective-permute-done), channel_id=1, source_target_pairs={{0,4},{4,8},{8,12},{12,14},{14,10},{10,6},{6,2},{2,0},{1,5},{5,9},... | collective-permute-start | bytes 2359304 | tf_op jit(solution)/shard_map/ppermute | solution.py:319
  45.0 19.8 %collective-permute-start.3 = (bf16[3,8,128,128]{3,2,1,0:T(8,128)(2,1)S(1)}, bf16[3,8,128,128]{3,2,1,0:T(8,128)(2,1)}, u32[]{:S(2)}, u32[]{:S(2)}) collective-permute-start(bf16[3,8,128,128]{3,2,1,0:T(8,128)(2,1)S(1)} %collective-permute-done.1), channel_id=1, source_target_pairs={{0,2},{4,0},{8,4},{12,8},{14,12},{10,14},{6,10},{2,6},{1,3},{5,1},... | collective-permute-start | bytes 2359304 | tf_op jit(solution)/shard_map/ppermute | solution.py:320
  49.1 0.9 copy-start.2
  57.8 11.2 %copy-start.7 = (f32[8,8,256]{2,1,0:T(8,128)S(1)}, f32[8,8,256]{2,1,0:T(8,128)}, u32[]{:S(2)}) copy-start(f32[8,8,256]{2,1,0:T(8,128)} %get-tuple-element.121) | copy-start | bytes 196612
  57.8 11.2 %copy-start.8 = (f32[8,8,256]{2,1,0:T(8,128)S(1)}, f32[8,8,256]{2,1,0:T(8,128)}, u32[]{:S(2)}) copy-start(f32[8,8,256]{2,1,0:T(8,128)} %get-tuple-element.122) | copy-start | bytes 196612
  57.8 11.2 %copy-start.9 = (f32[8,8,256]{2,1,0:T(8,128)S(1)}, f32[8,8,256]{2,1,0:T(8,128)}, u32[]{:S(2)}) copy-start(f32[8,8,256]{2,1,0:T(8,128)} %get-tuple-element.123) | copy-start | bytes 196612
  57.8 11.2 %copy-start.10 = (f32[8,8,256]{2,1,0:T(8,128)S(1)}, f32[8,8,256]{2,1,0:T(8,128)}, u32[]{:S(2)}) copy-start(f32[8,8,256]{2,1,0:T(8,128)} %get-tuple-element.124) | copy-start | bytes 196612
  61.7 5.2 %copy-start.5 = (bf16[3,8,128,128]{3,2,1,0:T(8,128)(2,1)}, bf16[3,8,128,128]{3,2,1,0:T(8,128)(2,1)S(1)}, u32[]{:S(2)}) copy-start(bf16[3,8,128,128]{3,2,1,0:T(8,128)(2,1)S(1)} %collective-permute-done.2) | copy-start | bytes 2359300
  67.0 19.1 %collective-permute-start.5 = (bf16[3,8,128,128]{3,2,1,0:T(8,128)(2,1)}, bf16[3,8,128,128]{3,2,1,0:T(8,128)(2,1)S(1)}, u32[]{:S(2)}, u32[]{:S(2)}) collective-permute-start(bf16[3,8,128,128]{3,2,1,0:T(8,128)(2,1)} %copy-done.5), channel_id=1, source_target_pairs={{0,4},{4,8},{8,12},{12,14},{14,10},{10,6},{6,2},{2,0},{1,5},{5,9},... | collective-permute-start | bytes 2359304 | tf_op jit(solution)/shard_map/ppermute | solution.py:319
  68.5 18.9 %collective-permute-start.6 = (bf16[3,8,128,128]{3,2,1,0:T(8,128)(2,1)}, bf16[3,8,128,128]{3,2,1,0:T(8,128)(2,1)}, u32[]{:S(2)}, u32[]{:S(2)}) collective-permute-start(bf16[3,8,128,128]{3,2,1,0:T(8,128)(2,1)} %collective-permute-done.3), channel_id=1, source_target_pairs={{0,2},{4,0},{8,4},{12,8},{14,12},{10,14},{6,10},{2,6},{1,3},{5,1},... | collective-permute-start | bytes 2359304 | tf_op jit(solution)/shard_map/ppermute | solution.py:320
  92.4 9.4 %copy-start.6 = (bf16[3,8,64,128]{3,2,1,0:T(8,128)(2,1)S(1)}, bf16[3,8,64,128]{3,2,1,0:T(8,128)(2,1)}, u32[]{:S(2)}) copy-start(bf16[3,8,64,128]{3,2,1,0:T(8,128)(2,1)} %slice.9) | copy-start | bytes 1179652
  92.4 10.5 %copy-start.12 = (bf16[128,128]{1,0:T(8,128)(2,1)S(1)}, bf16[128,128]{1,0:T(8,128)(2,1)}, u32[]{:S(2)}) copy-start(bf16[128,128]{1,0:T(8,128)(2,1)} %constant.262.clone) | copy-start | bytes 98308
  100.2 15.1 %collective-permute-start.9 = (bf16[3,48,64,128]{3,2,1,0:T(8,128)(2,1)}, bf16[3,48,64,128]{3,2,1,0:T(8,128)(2,1)S(1)}, u32[]{:S(2)}, u32[]{:S(2)}) collective-permute-start(bf16[3,48,64,128]{3,2,1,0:T(8,128)(2,1)} %get-tuple-element.70), channel_id=1, source_target_pairs={{0,1},{1,0},{2,3},{3,2},{4,5},{5,4},{6,7},{7,6},{8,9},{9,8},{10,11... | collective-permute-start | bytes 7077896 | tf_op jit(solution)/shard_map/ppermute | solution.py:359
  100.2 11.6 %collective-permute-start.7 = (bf16[3,8,64,128]{3,2,1,0:T(8,128)(2,1)S(1)}, bf16[3,8,64,128]{3,2,1,0:T(8,128)(2,1)}, u32[]{:S(2)}, u32[]{:S(2)}) collective-permute-start(bf16[3,8,64,128]{3,2,1,0:T(8,128)(2,1)S(1)} %slice.8), channel_id=1, source_target_pairs={{0,4},{4,8},{8,12},{12,14},{14,10},{10,6},{6,2},{2,0},{1,5},{5,9},... | collective-permute-start | bytes 1179656 | tf_op jit(solution)/shard_map/ppermute | solution.py:329
  101.8 11.3 %collective-permute-start.8 = (bf16[3,8,64,128]{3,2,1,0:T(8,128)(2,1)S(1)}, bf16[3,8,64,128]{3,2,1,0:T(8,128)(2,1)}, u32[]{:S(2)}, u32[]{:S(2)}) collective-permute-start(bf16[3,8,64,128]{3,2,1,0:T(8,128)(2,1)S(1)} %copy-done.6), channel_id=1, source_target_pairs={{0,2},{4,0},{8,4},{12,8},{14,12},{10,14},{6,10},{2,6},{1,3},{5,1},... | collective-permute-start | bytes 1179656 | tf_op jit(solution)/shard_map/ppermute | solution.py:330
  115.3 1.5 copy-start.1
  120.3 7.7 %copy-start.15 = (bf16[48,16]{0,1:T(8,128)(2,1)S(1)}, bf16[48,16]{0,1:T(8,128)(2,1)}, u32[]{:S(2)}) copy-start(bf16[48,16]{0,1:T(8,128)(2,1)} %param.23) | copy-start | bytes 4612
  122.9 1.7 %collective-permute-start.10 = (bf16[16,64,128]{2,1,0:T(8,128)(2,1)}, bf16[16,64,128]{2,1,0:T(8,128)(2,1)S(1)}, u32[]{:S(2)}, u32[]{:S(2)}) collective-permute-start(bf16[16,64,128]{2,1,0:T(8,128)(2,1)} %get-tuple-element.72), channel_id=1, source_target_pairs={{0,1},{1,0},{2,3},{3,2},{4,5},{5,4},{6,7},{7,6},{8,9},{9,8},{10,11... | collective-permute-start | bytes 786440 | tf_op jit(solution)/shard_map/ppermute | solution.py:359
  124.6 0.7 copy-start.11
  138.9 7.0 %collective-permute-start.11 = (bf16[1,48,64,128]{3,2,1,0:T(8,128)(2,1)}, bf16[1,48,64,128]{3,2,1,0:T(8,128)(2,1)S(1)}, u32[]{:S(2)}, u32[]{:S(2)}) collective-permute-start(bf16[1,48,64,128]{3,2,1,0:T(8,128)(2,1)} %get-tuple-element.74), channel_id=1, source_target_pairs={{0,1},{1,0},{2,3},{3,2},{4,5},{5,4},{6,7},{7,6},{8,9},{9,8},{10,11... | collective-permute-start | bytes 2359304 | tf_op jit(solution)/shard_map/ppermute | solution.py:359
  145.8 0.9 copy-start.3

commit v9 on v2

--- a/solution.py
+++ b/solution.py
@@ -171,8 +171,7 @@
     halves = rest[: 2 * DIGITS]
     out_ref, acc_ref = rest[2 * DIGITS :]
     eb = pl.program_id(0) + eb0
-    fo = fo_ref[...]
-    fr = fr_ref[...]
+    f = jnp.concatenate([fo_ref[...], fr_ref[...]], axis=1)
     acc_ref[...] = jnp.zeros_like(acc_ref)
     n = acc_ref.shape[0]
     for j in range(DIGITS):
@@ -185,8 +184,8 @@
         @pl.when(eb != j)
         def _():
             for l in range(n):
-                y = jnp.dot(fo, own_ref[l], preferred_element_type=F32)
-                y = (y + jnp.dot(fr, recv_ref[l], preferred_element_type=F32)).astype(BF16)
+                h = jnp.concatenate([own_ref[l], recv_ref[l]], axis=0)
+                y = jnp.dot(f, h, preferred_element_type=F32).astype(BF16)
                 acc_ref[l] += y.astype(F32) * key_ref[j, l].astype(F32)
 
     out_ref[...] = acc_ref[...].astype(BF16)
@@ -228,11 +227,10 @@
 
 
 def _final_kernel(fo_ref, fr_ref, own_ref, recv_ref, prod_ref, s_ref, out_ref):
-    fo = fo_ref[...]
-    fr = fr_ref[...]
+    f = jnp.concatenate([fo_ref[...], fr_ref[...]], axis=1)
     for l in range(own_ref.shape[0]):
-        y = jnp.dot(fo, own_ref[l], preferred_element_type=F32)
-        y = (y + jnp.dot(fr, recv_ref[l], preferred_element_type=F32)).astype(BF16)
+        h = jnp.concatenate([own_ref[l], recv_ref[l]], axis=0)
+        y = jnp.dot(f, h, preferred_element_type=F32).astype(BF16)
         diff = prod_ref[l].astype(F32) - y.astype(F32)
         out_ref[l] = (diff * s_ref[l]).astype(BF16)
 

time: 128 us -> 127 us (level)
  no operation moved by 1% of the time
where the time goes in v9:
time: 127 us; the launch traced here: 126 us
  Pallas kernels  48.9 us (39%)
  local copies, waits for them, and re-layouts  24.5 us (19%)
  waiting for transfers between devices  16 us (13%)
  other arithmetic  13.4 us (11%)
  starting transfers between devices  9.4 us (7%)
  between operations  9.29 us (7%)
  matrix products  4.53 us (4%)
    pallas_call x2, Pallas kernels, fwd_col(): pl.pallas_call(_fwd_col_kernel, grid=(groups, n // BLK), in_specs=[SMEM_S...  19.2 us
    pallas_call x2, Pallas kernels, product(): pl.pallas_call(lambda *refs: _product_kernel(eb0, *refs), grid=(nblocks,)...  10.4 us
    add x3, other arithmetic, _twiddle(): return 1.0 + 0.5 * (cp * cq - sp * sq)  9.03 us
    pallas_call x2, Pallas kernels, inv_row(): pl.pallas_call(_inv_row_kernel, grid=(n // BLK,), in_specs=[SMEM_SPEC, bl...  7.51 us
    pallas_call x2, Pallas kernels, inv_col(): pl.pallas_call(_inv_col_kernel, grid=(n // BLK,), in_specs=[blk, blk, pl....  7.46 us
    ppermute x1, waiting for transfers between devices, ring_step(): b = lax.ppermute(st['b'][:, :, h:], 'limb', st['ccw'])  6.74 us
    ppermute x3, starting transfers between devices, ring_step(): st['a'] = lax.ppermute(st['a'], 'limb', st['cw'])  6.18 us
    unnamed x32, local copies, waits for them, and re-layouts  5.77 us
  transfers between devices with their start and end apart: 12, of which 6 were waited for; matrix products, arithmetic and copies ran while one was open for 26% of the time, Pallas kernels for 24%

profile of v9, /device:TPU:0, one launch (start us, length us, event | category | flops | bytes accessed | tf_op | source)
XLA Modules:
  0.0 126.0 jit_solution(18311781245212512150)
XLA Ops:
  0.0 3.0 %collective-permute-start = (bf16[3,8,128,128]{3,2,1,0:T(8,128)(2,1)}, bf16[3,8,128,128]{3,2,1,0:T(8,128)(2,1)S(1)}, u32[]{:S(2)}, u32[]{:S(2)}) collective-permute-start(bf16[3,8,128,128]{3,2,1,0:T(8,128)(2,1)} %bitcast.102), channel_id=1, source_target_pairs={{0,4},{4,8},{8,12},{12,14},{14,10},{10,6},{6,2},{2,0},{1,5},{5,9},... | collective-permute-start | bytes 2359304 | tf_op jit(solution)/shard_map/ppermute | solution.py:298
  3.2 0.6 fusion.54
  3.8 0.3 fusion.58
  4.3 2.9 %add_bitcast_fusion.1.w_ref = f32[64,128,128]{2,1,0:T(8,128)} fusion(f32[64,8,128]{2,1,0:T(8,128)S(1)} %bitcast.98, f32[64,16,128]{2,1,0:T(8,128)S(1)} %bitcast.96, f32[64,8,128]{2,1,0:T(8,128)S(1)} %bitcast.99, f32[64,16,128]{2,1,0:T(8,128)S(1)} %bitcast.97), kind=kLoop, calls=%fused_computation.8 | loop fusion | flops 5242880 | bytes 5767168 | tf_op jit(solution)/shard_map/add | solution.py:53
  7.2 4.9 %shard_map.109 = (bf16[48,64,128]{2,1,0:T(8,128)(2,1)}, bf16[48,64,128]{2,1,0:T(8,128)(2,1)}) custom-call(s32[1]{0:T(128)} %bitcast.me_ref, bf16[48,128,128]{2,1,0:T(8,128)(2,1)} %bitcast.85, f32[64,128,128]{2,1,0:T(8,128)} %add_bitcast_fusion.1.w_ref, bf16[128,128]{1,0:T(8,128)(2,1)} %constant.247.clone.ft_ref), custom_call_target="tpu_custom_call" | custom-call | tf_op jit(solution)/shard_map/pallas_call | solution.py:101
  12.5 2.3 %fusion.50 = (f32[8,8,256]{2,1,0:T(8,128)S(1)}, f32[8,8,256]{2,1,0:T(8,128)S(1)}, f32[8,8,256]{2,1,0:T(8,128)S(1)}, f32[8,8,256]{2,1,0:T(8,128)S(1)}, f32[8,8,25...) fusion(s32[8,256]{1,0:T(8,128)S(1)} %add_select_fusion.12, ...), kind=kLoop, calls=%fused_computation.119 | loop fusion | flops 1376256 | bytes 811072 | tf_op jit(solution)/shard_map/cos | solution.py:35
  14.9 0.7 add.605
  15.7 0.7 broadcast_bitcast_fusion
  16.4 4.3 %collective-permute-done = bf16[3,8,128,128]{3,2,1,0:T(8,128)(2,1)S(1)} collective-permute-done((bf16[3,8,128,128]{3,2,1,0:T(8,128)(2,1)}, bf16[3,8,128,128]{3,2,1,0:T(8,128)(2,1)S(1)}, u32[]{:S(2)}, u32[]{:S(2)}) %collective-permute-start) | collective-permute-done | bytes 786464 | tf_op jit(solution)/shard_map/ppermute | solution.py:298
  20.7 1.6 %collective-permute-done.1 = bf16[3,8,128,128]{3,2,1,0:T(8,128)(2,1)} collective-permute-done((bf16[3,8,128,128]{3,2,1,0:T(8,128)(2,1)}, bf16[3,8,128,128]{3,2,1,0:T(8,128)(2,1)}, u32[]{:S(2)}, u32[]{:S(2)}) %collective-permute-start.1) | collective-permute-done | bytes 786464 | tf_op jit(solution)/shard_map/ppermute | solution.py:299
  22.3 1.6 %collective-permute-start.2 = (bf16[3,8,128,128]{3,2,1,0:T(8,128)(2,1)S(1)}, bf16[3,8,128,128]{3,2,1,0:T(8,128)(2,1)}, u32[]{:S(2)}, u32[]{:S(2)}) collective-permute-start(bf16[3,8,128,128]{3,2,1,0:T(8,128)(2,1)S(1)} %collective-permute-done), channel_id=1, source_target_pairs={{0,4},{4,8},{8,12},{12,14},{14,10},{10,6},{6,2},{2,0},{1,5},{5,9},... | collective-permute-start | bytes 2359304 | tf_op jit(solution)/shard_map/ppermute | solution.py:298
  23.9 0.4 collective-permute-start.3
  24.4 0.7 constant_dynamic-slice_fusion
  25.2 3.1 %fusion.3.v_ref = f32[64,64,256]{2,1,0:T(8,128)} fusion(f32[64,64]{1,0:T(8,128)S(1)} %copy.17, f32[64,8,256]{2,1,0:T(8,128)S(1)} %bitcast.94, f32[64,64]{1,0:T(8,128)S(1)} %copy.16, f32[64,8,256]{2,1,0:T(8,128)S(1)} %bitcast.95), kind=kLoop, calls=%fused_computation.5 | loop fusion | flops 5242880 | bytes 5275648 | tf_op jit(solution)/shard_map/add | solution.py:53
  28.3 0.9 copy-done.3
  29.1 4.8 %shard_map.110 = bf16[48,64,256]{2,1,0:T(8,128)(2,1)} custom-call(bf16[48,64,128]{2,1,0:T(8,128)(2,1)} %get-tuple-element.42.own_ref, bf16[48,64,128]{2,1,0:T(8,128)(2,1)} %copy-done.3, f32[64,64,256]{2,1,0:T(8,128)} %fusion.3.v_ref, bf16[128,256]{1,0:T(8,128)(2,1)} %get-tuple-element.74.fo_ref, bf16[128,256]{1,0:T(8,128)(2,1)} %get-tuple-element.73.fr_ref), custom_call_target="tpu_custom_call" | custom-call | tf_op jit(solution)/shard_map/pallas_call | solution.py:131
  34.0 2.9 %fusion.5 = bf16[3,64,256,48]{2,3,1,0:T(8,128)(2,1)S(1)} fusion(bf16[3,16,64,256]{3,2,1,0:T(8,128)(2,1)} %bitcast.88, bf16[3,48,16]{1,2,0:T(8,128)(2,1)S(1)} %copy-done), kind=kOutput, calls=%fused_computation.11 | convolution fusion | flops 75497472 | bytes 6296064 | tf_op jit(solution)/shard_map/dot_general | solution.py:362
  36.9 3.9 %copy.33 = bf16[3,64,256,48]{2,1,3,0:T(8,128)(2,1)} copy(bf16[3,64,256,48]{2,3,1,0:T(8,128)(2,1)S(1)} %fusion.5) | data formatting | bytes 9437184 | tf_op jit(solution)/shard_map/dot_general | solution.py:362
  40.7 1.3 %collective-permute-done.3 = bf16[3,8,128,128]{3,2,1,0:T(8,128)(2,1)} collective-permute-done((bf16[3,8,128,128]{3,2,1,0:T(8,128)(2,1)}, bf16[3,8,128,128]{3,2,1,0:T(8,128)(2,1)}, u32[]{:S(2)}, u32[]{:S(2)}) %collective-permute-start.3) | collective-permute-done | bytes 786464 | tf_op jit(solution)/shard_map/ppermute | solution.py:299
  42.0 1.6 %collective-permute-start.5 = (bf16[3,8,128,128]{3,2,1,0:T(8,128)(2,1)}, bf16[3,8,128,128]{3,2,1,0:T(8,128)(2,1)S(1)}, u32[]{:S(2)}, u32[]{:S(2)}) collective-permute-start(bf16[3,8,128,128]{3,2,1,0:T(8,128)(2,1)} %collective-permute-done.2), channel_id=1, source_target_pairs={{0,4},{4,8},{8,12},{12,14},{14,10},{10,6},{6,2},{2,0},{1,5},{5,9},... | collective-permute-start | bytes 2359304 | tf_op jit(solution)/shard_map/ppermute | solution.py:298
  43.6 0.5 collective-permute-start.6
  44.4 3.0 %add_bitcast_fusion.w_ref = f32[64,64,256]{2,1,0:T(8,128)} fusion(f32[64,8,256]{2,1,0:T(8,128)S(1)} %bitcast.92, f32[64,8,256]{2,1,0:T(8,128)S(1)} %bitcast.90, f32[64,8,256]{2,1,0:T(8,128)S(1)} %bitcast.93, f32[64,8,256]{2,1,0:T(8,128)S(1)} %bitcast.91), kind=kLoop, calls=%fused_computation.7 | loop fusion | flops 5242880 | bytes 6291456 | tf_op jit(solution)/shard_map/add | solution.py:53
  47.4 13.4 %shard_map.111 = (bf16[3,48,64,128]{3,2,1,0:T(8,128)(2,1)}, bf16[3,48,64,128]{3,2,1,0:T(8,128)(2,1)}) custom-call(s32[1]{0:T(128)} %bitcast.me_ref, bf16[3,48,64,256]{3,2,1,0:T(8,128)(2,1)} %bitcast.84, f32[64,64,256]{2,1,0:T(8,128)} %fusion.3.v_ref, f32[64,64,256]{2,1,0:T(8,128)} %add_bitcast_fusion.w_ref, bf16[256,256]{1,0:T(8,128)(2,1)} %constant.248.clone.ft_ref), custom_call_target="tpu_custom_call" | custom-call | tf_op jit(solution)/shard_map/pallas_call | solution.py:161
  61.0 0.6 dynamic_slice.38
  66.2 0.7 fusion.89
  71.2 0.7 constant_dynamic-slice_fusion.2
  71.9 1.6 %broadcast_in_dim.8 = bf16[3,64,128,128]{3,2,1,0:T(8,128)(2,1)S(1)} broadcast(bf16[]{:T(256)} %constant.223.clone.1), dimensions={} | broadcast | bytes 6291458 | tf_op jit(solution)/shard_map/broadcast_in_dim | solution.py:273
  73.8 1.3 %constant_dynamic-update-slice_fusion.4 = bf16[3,64,128,128]{3,2,1,0:T(8,128)(2,1)S(1)} fusion(bf16[3,64,128,128]{3,2,1,0:T(8,128)(2,1)S(1)} %constant_dynamic-update-slice_fusion.5, bf16[3,8,128,128]{3,2,1,0:T(8,128)(2,1)} %collective-permute-done.1, s32[]{:T(128)S(6)} %select_n.360), kind=kLoop, calls=%fused_computation.188 | loop fusion | bytes 1572868 | tf_op jit(solution)/shard_map/dynamic_update_slice | solution.py:303
  75.0 1.3 %constant_dynamic-update-slice_fusion.3 = bf16[3,64,128,128]{3,2,1,0:T(8,128)(2,1)S(1)} fusion(bf16[3,64,128,128]{3,2,1,0:T(8,128)(2,1)S(1)} %constant_dynamic-update-slice_fusion.4, bf16[3,8,128,128]{3,2,1,0:T(8,128)(2,1)} %collective-permute-done.2, s32[]{:T(128)S(6)} %select_n.369), kind=kLoop, calls=%fused_computation.187 | loop fusion | bytes 1572868 | tf_op jit(solution)/shard_map/dynamic_update_slice | solution.py:300
  76.3 1.0 slice.7
  77.3 0.5 collective-permute-start.8
  77.9 1.6 %collective-permute-start.7 = (bf16[3,8,64,128]{3,2,1,0:T(8,128)(2,1)S(1)}, bf16[3,8,64,128]{3,2,1,0:T(8,128)(2,1)S(1)}, u32[]{:S(2)}, u32[]{:S(2)}) collective-permute-start(bf16[3,8,64,128]{3,2,1,0:T(8,128)(2,1)S(1)} %slice.6), channel_id=1, source_target_pairs={{0,4},{4,8},{8,12},{12,14},{14,10},{10,6},{6,2},{2,0},{1,5},{5,9},... | collective-permute-start | bytes 1179656 | tf_op jit(solution)/shard_map/ppermute | solution.py:308
  79.5 1.3 constant_dynamic-update-slice_fusion.2
  80.9 1.3 %constant_dynamic-update-slice_fusion = bf16[3,64,128,128]{3,2,1,0:T(8,128)(2,1)S(1)} fusion(bf16[3,64,128,128]{3,2,1,0:T(8,128)(2,1)S(1)} %constant_dynamic-update-slice_fusion.1, bf16[3,8,128,128]{3,2,1,0:T(8,128)(2,1)} %collective-permute-done.6, s32[]{:T(128)S(6)} %select_n.386), kind=kLoop, calls=%fused_computation.182 | loop fusion | bytes 1572868 | tf_op jit(solution)/shard_map/dynamic_update_slice | solution.py:303
  82.2 6.7 %collective-permute-done.8 = bf16[3,8,64,128]{3,2,1,0:T(8,128)(2,1)S(1)} collective-permute-done((bf16[3,8,64,128]{3,2,1,0:T(8,128)(2,1)S(1)}, bf16[3,8,64,128]{3,2,1,0:T(8,128)(2,1)S(1)}, u32[]{:S(2)}, u32[]{:S(2)}) %collective-permute-start.8) | collective-permute-done | bytes 393248 | tf_op jit(solution)/shard_map/ppermute | solution.py:309
  89.3 2.7 %copy-done.2 = bf16[3,64,128,128]{3,2,1,0:T(8,128)(2,1)} copy-done((bf16[3,64,128,128]{3,2,1,0:T(8,128)(2,1)}, bf16[3,64,128,128]{3,2,1,0:T(8,128)(2,1)S(1)}, u32[]{:S(2)}) %copy-start.2) | copy-done | bytes 6291480
  92.0 1.5 %copy-done.1 = bf16[3,48,64,128]{3,2,1,0:T(8,128)(2,1)} copy-done((bf16[3,48,64,128]{3,2,1,0:T(8,128)(2,1)}, bf16[3,48,64,128]{3,2,1,0:T(8,128)(2,1)S(1)}, u32[]{:S(2)}) %copy-start.1) | copy-done | bytes 2359320
  93.4 3.5 %shard_map.112.y_ref = bf16[16,128,128]{2,1,0:T(8,128)(2,1)} custom-call(bf16[128,64]{1,0:T(8,128)(2,1)} %get-tuple-element.78.refs_0_.fo_ref, bf16[128,64]{1,0:T(8,128)(2,1)} %get-tuple-element.77.refs_1_.fr_ref, bf16[48,128,128]{2,1,0:T(8,128)(2,1)} %bitcast.86, bf16[3,64,128,128]{3,2,1,0:T(8,128)(2,1)} %copy-done.2, ...), custom_call_target="tpu_custom_call" | custom-call | tf_op jit(solution)/shard_map/pallas_call | solution.py:211
  96.9 2.6 %shard_map.113 = (bf16[16,64,128]{2,1,0:T(8,128)(2,1)}, bf16[16,64,128]{2,1,0:T(8,128)(2,1)}) custom-call(s32[1]{0:T(128)} %bitcast.me_ref, bf16[16,128,128]{2,1,0:T(8,128)(2,1)} %shard_map.112.y_ref, f32[64,128,128]{2,1,0:T(8,128)} %add_bitcast_fusion.1.w_ref, bf16[128,128]{1,0:T(8,128)(2,1)} %constant.247.clone.ft_ref), custom_call_target="tpu_custom_call" | custom-call | tf_op jit(solution)/shard_map/pallas_call | solution.py:101
  99.5 1.7 %collective-permute-done.10.recv_ref = bf16[16,64,128]{2,1,0:T(8,128)(2,1)S(1)} collective-permute-done((bf16[16,64,128]{2,1,0:T(8,128)(2,1)}, bf16[16,64,128]{2,1,0:T(8,128)(2,1)S(1)}, u32[]{:S(2)}, u32[]{:S(2)}) %collective-permute-start.10) | collective-permute-done | bytes 262176 | tf_op jit(solution)/shard_map/ppermute | solution.py:330
  101.3 0.7 copy-done.8
  102.0 2.6 %shard_map.114 = bf16[16,64,256]{2,1,0:T(8,128)(2,1)} custom-call(bf16[16,64,128]{2,1,0:T(8,128)(2,1)} %get-tuple-element.61.own_ref, bf16[16,64,128]{2,1,0:T(8,128)(2,1)} %copy-done.8, f32[64,64,256]{2,1,0:T(8,128)} %fusion.3.v_ref, bf16[128,256]{1,0:T(8,128)(2,1)} %get-tuple-element.74.fo_ref, bf16[128,256]{1,0:T(8,128)(2,1)} %get-tuple-element.73.fr_ref), custom_call_target="tpu_custom_call" | custom-call | tf_op jit(solution)/shard_map/pallas_call | solution.py:131
  104.6 1.6 %fusion.7 = bf16[64,256,48]{1,2,0:T(8,128)(2,1)S(1)} fusion(bf16[16,64,256]{2,1,0:T(8,128)(2,1)} %shard_map.114, bf16[48,16]{0,1:T(8,128)(2,1)S(1)} %copy-done.13), kind=kOutput, calls=%fused_computation.14 | convolution fusion | flops 25165824 | bytes 2098688 | tf_op jit(solution)/shard_map/dot_general | solution.py:379
  106.3 1.7 %copy.34 = bf16[64,256,48]{1,0,2:T(8,128)(2,1)} copy(bf16[64,256,48]{1,2,0:T(8,128)(2,1)S(1)} %fusion.7) | data formatting | bytes 3145728 | tf_op jit(solution)/shard_map/dot_general | solution.py:379
  108.0 5.7 %shard_map.115 = (bf16[1,48,64,128]{3,2,1,0:T(8,128)(2,1)}, bf16[1,48,64,128]{3,2,1,0:T(8,128)(2,1)}) custom-call(s32[1]{0:T(128)} %bitcast.me_ref, bf16[1,48,64,256]{3,2,1,0:T(8,128)(2,1)} %bitcast.89, f32[64,64,256]{2,1,0:T(8,128)} %fusion.3.v_ref, f32[64,64,256]{2,1,0:T(8,128)} %add_bitcast_fusion.w_ref, bf16[256,256]{1,0:T(8,128)(2,1)} %constant.248.clone.ft_ref), custom_call_target="tpu_custom_call" | custom-call | tf_op jit(solution)/shard_map/pallas_call | solution.py:161
  113.8 6.9 %shard_map.116.prod_ref = bf16[48,128,128]{2,1,0:T(8,128)(2,1)} custom-call(bf16[128,64]{1,0:T(8,128)(2,1)} %get-tuple-element.78.refs_0_.fo_ref, bf16[128,64]{1,0:T(8,128)(2,1)} %get-tuple-element.77.refs_1_.fr_ref, bf16[48,128,128]{2,1,0:T(8,128)(2,1)} %bitcast.87, bf16[3,64,128,128]{3,2,1,0:T(8,128)(2,1)} %copy-done.2, ...), custom_call_target="tpu_custom_call" | custom-call | tf_op jit(solution)/shard_map/pallas_call | solution.py:211
  120.7 0.9 broadcast_in_dim.10.s_ref
  121.6 4.4 %shard_map.117 = bf16[48,128,128]{2,1,0:T(8,128)(2,1)} custom-call(bf16[128,64]{1,0:T(8,128)(2,1)} %get-tuple-element.78.refs_0_.fo_ref, bf16[128,64]{1,0:T(8,128)(2,1)} %get-tuple-element.77.refs_1_.fr_ref, bf16[48,64,128]{2,1,0:T(8,128)(2,1)} %bitcast.100, bf16[48,64,128]{2,1,0:T(8,128)(2,1)} %bitcast.101, bf16[48,128,128]{2,1,0:T(8,128)(2,1)} %shard_map.116.prod_ref, ...), custom_call_target="tpu_custom_call" | custom-call | tf_op jit(solution)/shard_map/pallas_call | solution.py:242
  (66 shorter events, 2.3 us)
Async XLA Ops:
  0.0 34.0 %copy-start = (bf16[3,48,16]{1,2,0:T(8,128)(2,1)S(1)}, bf16[3,48,16]{1,2,0:T(8,128)(2,1)}, u32[]{:S(2)}) copy-start(bf16[3,48,16]{1,2,0:T(8,128)(2,1)} %param.13) | copy-start | bytes 13828
  0.0 20.7 %collective-permute-start = (bf16[3,8,128,128]{3,2,1,0:T(8,128)(2,1)}, bf16[3,8,128,128]{3,2,1,0:T(8,128)(2,1)S(1)}, u32[]{:S(2)}, u32[]{:S(2)}) collective-permute-start(bf16[3,8,128,128]{3,2,1,0:T(8,128)(2,1)} %bitcast.102), channel_id=1, source_target_pairs={{0,4},{4,8},{8,12},{12,14},{14,10},{10,6},{6,2},{2,0},{1,5},{5,9},... | collective-permute-start | bytes 2359304 | tf_op jit(solution)/shard_map/ppermute | solution.py:298
  3.0 19.3 %collective-permute-start.1 = (bf16[3,8,128,128]{3,2,1,0:T(8,128)(2,1)}, bf16[3,8,128,128]{3,2,1,0:T(8,128)(2,1)}, u32[]{:S(2)}, u32[]{:S(2)}) collective-permute-start(bf16[3,8,128,128]{3,2,1,0:T(8,128)(2,1)} %bitcast.103), channel_id=1, source_target_pairs={{0,2},{4,0},{8,4},{12,8},{14,12},{10,14},{6,10},{2,6},{1,3},{5,1},... | collective-permute-start | bytes 2359304 | tf_op jit(solution)/shard_map/ppermute | solution.py:299
  3.0 9.3 %copy-start.12 = (s32[8]{0:T(128)}, s32[8]{0:T(128)S(1)}, u32[]{:S(2)}) copy-start(s32[8]{0:T(128)S(1)} %get-tuple-element.135) | copy-start | bytes 100
  7.2 17.1 %copy-start.9 = (bf16[256,256]{1,0:T(8,128)(2,1)S(1)}, bf16[256,256]{1,0:T(8,128)(2,1)}, u32[]{:S(2)}) copy-start(bf16[256,256]{1,0:T(8,128)(2,1)} %constant.245.clone) | copy-start | bytes 393220
  12.2 16.1 %collective-permute-start.4 = (bf16[48,64,128]{2,1,0:T(8,128)(2,1)}, bf16[48,64,128]{2,1,0:T(8,128)(2,1)S(1)}, u32[]{:S(2)}, u32[]{:S(2)}) collective-permute-start(bf16[48,64,128]{2,1,0:T(8,128)(2,1)} %get-tuple-element.43), channel_id=1, source_target_pairs={{0,1},{1,0},{2,3},{3,2},{4,5},{5,4},{6,7},{7,6},{8,9},{9,8},{10,11... | collective-permute-start | bytes 2359304 | tf_op jit(solution)/shard_map/ppermute | solution.py:330
  20.7 13.2 %copy-start.6 = (bf16[3,8,128,128]{3,2,1,0:T(8,128)(2,1)}, bf16[3,8,128,128]{3,2,1,0:T(8,128)(2,1)S(1)}, u32[]{:S(2)}) copy-start(bf16[3,8,128,128]{3,2,1,0:T(8,128)(2,1)S(1)} %collective-permute-done) | copy-start | bytes 2359300
  22.3 18.4 %collective-permute-start.2 = (bf16[3,8,128,128]{3,2,1,0:T(8,128)(2,1)S(1)}, bf16[3,8,128,128]{3,2,1,0:T(8,128)(2,1)}, u32[]{:S(2)}, u32[]{:S(2)}) collective-permute-start(bf16[3,8,128,128]{3,2,1,0:T(8,128)(2,1)S(1)} %collective-permute-done), channel_id=1, source_target_pairs={{0,4},{4,8},{8,12},{12,14},{14,10},{10,6},{6,2},{2,0},{1,5},{5,9},... | collective-permute-start | bytes 2359304 | tf_op jit(solution)/shard_map/ppermute | solution.py:298
  23.9 18.1 %collective-permute-start.3 = (bf16[3,8,128,128]{3,2,1,0:T(8,128)(2,1)}, bf16[3,8,128,128]{3,2,1,0:T(8,128)(2,1)}, u32[]{:S(2)}, u32[]{:S(2)}) collective-permute-start(bf16[3,8,128,128]{3,2,1,0:T(8,128)(2,1)} %collective-permute-done.1), channel_id=1, source_target_pairs={{0,2},{4,0},{8,4},{12,8},{14,12},{10,14},{6,10},{2,6},{1,3},{5,1},... | collective-permute-start | bytes 2359304 | tf_op jit(solution)/shard_map/ppermute | solution.py:299
  28.3 0.9 copy-start.3
  42.0 18.8 %collective-permute-start.5 = (bf16[3,8,128,128]{3,2,1,0:T(8,128)(2,1)}, bf16[3,8,128,128]{3,2,1,0:T(8,128)(2,1)S(1)}, u32[]{:S(2)}, u32[]{:S(2)}) collective-permute-start(bf16[3,8,128,128]{3,2,1,0:T(8,128)(2,1)} %collective-permute-done.2), channel_id=1, source_target_pairs={{0,4},{4,8},{8,12},{12,14},{14,10},{10,6},{6,2},{2,0},{1,5},{5,9},... | collective-permute-start | bytes 2359304 | tf_op jit(solution)/shard_map/ppermute | solution.py:298
  43.6 17.2 %collective-permute-start.6 = (bf16[3,8,128,128]{3,2,1,0:T(8,128)(2,1)}, bf16[3,8,128,128]{3,2,1,0:T(8,128)(2,1)}, u32[]{:S(2)}, u32[]{:S(2)}) collective-permute-start(bf16[3,8,128,128]{3,2,1,0:T(8,128)(2,1)} %collective-permute-done.3), channel_id=1, source_target_pairs={{0,2},{4,0},{8,4},{12,8},{14,12},{10,14},{6,10},{2,6},{1,3},{5,1},... | collective-permute-start | bytes 2359304 | tf_op jit(solution)/shard_map/ppermute | solution.py:299
  47.4 13.5 %copy-start.15 = (s32[8]{0:T(128)S(1)}, s32[8]{0:T(128)}, u32[]{:S(2)}) copy-start(s32[8]{0:T(128)} %constant.244.clone) | copy-start | bytes 100
  47.4 18.8 %copy-start.11 = (s32[8]{0:T(128)S(1)}, s32[8]{0:T(128)}, u32[]{:S(2)}) copy-start(s32[8]{0:T(128)} %constant.243.clone) | copy-start | bytes 100
  47.4 23.8 %copy-start.10 = (bf16[128,128]{1,0:T(8,128)(2,1)S(1)}, bf16[128,128]{1,0:T(8,128)(2,1)}, u32[]{:S(2)}) copy-start(bf16[128,128]{1,0:T(8,128)(2,1)} %constant.246.clone) | copy-start | bytes 98308
  60.9 28.4 %collective-permute-start.9 = (bf16[3,48,64,128]{3,2,1,0:T(8,128)(2,1)}, bf16[3,48,64,128]{3,2,1,0:T(8,128)(2,1)S(1)}, u32[]{:S(2)}, u32[]{:S(2)}) collective-permute-start(bf16[3,48,64,128]{3,2,1,0:T(8,128)(2,1)} %get-tuple-element.60), channel_id=1, source_target_pairs={{0,1},{1,0},{2,3},{3,2},{4,5},{5,4},{6,7},{7,6},{8,9},{9,8},{10,11... | collective-permute-start | bytes 7077896 | tf_op jit(solution)/shard_map/ppermute | solution.py:330
  71.2 2.3 %copy-start.5 = (bf16[1,3,8,128,128]{4,3,2,1,0:T(8,128)(2,1)S(1)}, bf16[1,3,8,128,128]{4,3,2,1,0:T(8,128)(2,1)}, u32[]{:S(2)}) copy-start(bf16[1,3,8,128,128]{4,3,2,1,0:T(8,128)(2,1)} %param.12) | copy-start | bytes 2359300
  71.2 2.4 %copy-start.7 = (bf16[3,8,128,128]{3,2,1,0:T(8,128)(2,1)S(1)}, bf16[3,8,128,128]{3,2,1,0:T(8,128)(2,1)}, u32[]{:S(2)}) copy-start(bf16[3,8,128,128]{3,2,1,0:T(8,128)(2,1)} %copy-done.6) | copy-start | bytes 2359300
  77.3 11.5 %collective-permute-start.8 = (bf16[3,8,64,128]{3,2,1,0:T(8,128)(2,1)S(1)}, bf16[3,8,64,128]{3,2,1,0:T(8,128)(2,1)S(1)}, u32[]{:S(2)}, u32[]{:S(2)}) collective-permute-start(bf16[3,8,64,128]{3,2,1,0:T(8,128)(2,1)S(1)} %slice.7), channel_id=1, source_target_pairs={{0,2},{4,0},{8,4},{12,8},{14,12},{10,14},{6,10},{2,6},{1,3},{5,1},... | collective-permute-start | bytes 1179656 | tf_op jit(solution)/shard_map/ppermute | solution.py:309
  77.9 11.3 %collective-permute-start.7 = (bf16[3,8,64,128]{3,2,1,0:T(8,128)(2,1)S(1)}, bf16[3,8,64,128]{3,2,1,0:T(8,128)(2,1)S(1)}, u32[]{:S(2)}, u32[]{:S(2)}) collective-permute-start(bf16[3,8,64,128]{3,2,1,0:T(8,128)(2,1)S(1)} %slice.6), channel_id=1, source_target_pairs={{0,4},{4,8},{8,12},{12,14},{14,10},{10,6},{6,2},{2,0},{1,5},{5,9},... | collective-permute-start | bytes 1179656 | tf_op jit(solution)/shard_map/ppermute | solution.py:308
  89.3 2.7 %copy-start.2 = (bf16[3,64,128,128]{3,2,1,0:T(8,128)(2,1)}, bf16[3,64,128,128]{3,2,1,0:T(8,128)(2,1)S(1)}, u32[]{:S(2)}) copy-start(bf16[3,64,128,128]{3,2,1,0:T(8,128)(2,1)S(1)} %maximum_dynamic-update-slice_fusion.refs_3_) | copy-start | bytes 18874372
  92.0 1.5 %copy-start.1 = (bf16[3,48,64,128]{3,2,1,0:T(8,128)(2,1)}, bf16[3,48,64,128]{3,2,1,0:T(8,128)(2,1)S(1)}, u32[]{:S(2)}) copy-start(bf16[3,48,64,128]{3,2,1,0:T(8,128)(2,1)S(1)} %collective-permute-done.9.refs_5_.refs_7_.refs_9_) | copy-start | bytes 7077892
  96.9 7.7 %copy-start.13 = (bf16[48,16]{0,1:T(8,128)(2,1)S(1)}, bf16[48,16]{0,1:T(8,128)(2,1)}, u32[]{:S(2)}) copy-start(bf16[48,16]{0,1:T(8,128)(2,1)} %param.14) | copy-start | bytes 4612
  99.5 1.7 %collective-permute-start.10 = (bf16[16,64,128]{2,1,0:T(8,128)(2,1)}, bf16[16,64,128]{2,1,0:T(8,128)(2,1)S(1)}, u32[]{:S(2)}, u32[]{:S(2)}) collective-permute-start(bf16[16,64,128]{2,1,0:T(8,128)(2,1)} %get-tuple-element.62), channel_id=1, source_target_pairs={{0,1},{1,0},{2,3},{3,2},{4,5},{5,4},{6,7},{7,6},{8,9},{9,8},{10,11... | collective-permute-start | bytes 786440 | tf_op jit(solution)/shard_map/ppermute | solution.py:330
  101.3 0.7 copy-start.8
  113.7 7.0 %copy-start.14 = (f32[48]{0:T(128)S(1)}, f32[48]{0:T(128)}, u32[]{:S(2)}) copy-start(f32[48]{0:T(128)} %param.15) | copy-start | bytes 580
  113.7 7.0 %collective-permute-start.11 = (bf16[1,48,64,128]{3,2,1,0:T(8,128)(2,1)}, bf16[1,48,64,128]{3,2,1,0:T(8,128)(2,1)S(1)}, u32[]{:S(2)}, u32[]{:S(2)}) collective-permute-start(bf16[1,48,64,128]{3,2,1,0:T(8,128)(2,1)} %get-tuple-element.64), channel_id=1, source_target_pairs={{0,1},{1,0},{2,3},{3,2},{4,5},{5,4},{6,7},{7,6},{8,9},{9,8},{10,11... | collective-permute-start | bytes 2359304 | tf_op jit(solution)/shard_map/ppermute | solution.py:330
  120.7 0.9 copy-start.4

commit v10 on v9

--- a/solution.py
+++ b/solution.py
@@ -117,8 +117,8 @@
     n, rows_l, half = own_ref.shape
     a = own_ref[...].reshape(n * rows_l, half)
     b = recv_ref[...].reshape(n * rows_l, half)
-    x = jnp.dot(a, fo_ref[...], preferred_element_type=F32)
-    x = x + jnp.dot(b, fr_ref[...], preferred_element_type=F32)
+    f = jnp.concatenate([fo_ref[...], fr_ref[...]], axis=0)
+    x = jnp.dot(jnp.concatenate([a, b], axis=1), f, preferred_element_type=F32)
     x = x.reshape(n, rows_l, -1)
     out_ref[...] = (x / v_ref[...]).astype(BF16)
 

time: 127 us -> 127 us (level)
  no operation moved by 1% of the time
where the time goes in v10:
time: 127 us; the launch traced here: 126 us
  Pallas kernels  48.6 us (38%)
  local copies, waits for them, and re-layouts  24.5 us (19%)
  waiting for transfers between devices  16.2 us (13%)
  other arithmetic  13.4 us (11%)
  starting transfers between devices  9.42 us (7%)
  between operations  9.29 us (7%)
  matrix products  4.51 us (4%)
    pallas_call x2, Pallas kernels, fwd_col(): pl.pallas_call(_fwd_col_kernel, grid=(groups, n // BLK), in_specs=[SMEM_S...  19.1 us
    pallas_call x2, Pallas kernels, product(): pl.pallas_call(lambda *refs: _product_kernel(eb0, *refs), grid=(nblocks,)...  10.4 us
    add x3, other arithmetic, _twiddle(): return 1.0 + 0.5 * (cp * cq - sp * sq)  9.03 us
    pallas_call x2, Pallas kernels, inv_row(): pl.pallas_call(_inv_row_kernel, grid=(n // BLK,), in_specs=[SMEM_SPEC, bl...  7.51 us
    pallas_call x2, Pallas kernels, inv_col(): pl.pallas_call(_inv_col_kernel, grid=(n // BLK,), in_specs=[blk, blk, pl....  7.14 us
    ppermute x1, waiting for transfers between devices, ring_step(): b = lax.ppermute(st['b'][:, :, h:], 'limb', st['ccw'])  6.74 us
    ppermute x3, starting transfers between devices, ring_step(): st['a'] = lax.ppermute(st['a'], 'limb', st['cw'])  6.18 us
    unnamed x32, local copies, waits for them, and re-layouts  5.77 us
  transfers between devices with their start and end apart: 12, of which 6 were waited for; matrix products, arithmetic and copies ran while one was open for 26% of the time, Pallas kernels for 24%

profile of v10, /device:TPU:0, one launch (start us, length us, event | category | flops | bytes accessed | tf_op | source)
XLA Modules:
  0.0 125.9 jit_solution(1420514109423629997)
XLA Ops:
  0.0 3.0 %collective-permute-start = (bf16[3,8,128,128]{3,2,1,0:T(8,128)(2,1)}, bf16[3,8,128,128]{3,2,1,0:T(8,128)(2,1)S(1)}, u32[]{:S(2)}, u32[]{:S(2)}) collective-permute-start(bf16[3,8,128,128]{3,2,1,0:T(8,128)(2,1)} %bitcast.102), channel_id=1, source_target_pairs={{0,4},{4,8},{8,12},{12,14},{14,10},{10,6},{6,2},{2,0},{1,5},{5,9},... | collective-permute-start | bytes 2359304 | tf_op jit(solution)/shard_map/ppermute | solution.py:298
  3.2 0.6 fusion.54
  3.8 0.3 fusion.58
  4.3 2.9 %add_bitcast_fusion.1.w_ref = f32[64,128,128]{2,1,0:T(8,128)} fusion(f32[64,8,128]{2,1,0:T(8,128)S(1)} %bitcast.98, f32[64,16,128]{2,1,0:T(8,128)S(1)} %bitcast.96, f32[64,8,128]{2,1,0:T(8,128)S(1)} %bitcast.99, f32[64,16,128]{2,1,0:T(8,128)S(1)} %bitcast.97), kind=kLoop, calls=%fused_computation.8 | loop fusion | flops 5242880 | bytes 5767168 | tf_op jit(solution)/shard_map/add | solution.py:53
  7.2 4.9 %shard_map.109 = (bf16[48,64,128]{2,1,0:T(8,128)(2,1)}, bf16[48,64,128]{2,1,0:T(8,128)(2,1)}) custom-call(s32[1]{0:T(128)} %bitcast.me_ref, bf16[48,128,128]{2,1,0:T(8,128)(2,1)} %bitcast.85, f32[64,128,128]{2,1,0:T(8,128)} %add_bitcast_fusion.1.w_ref, bf16[128,128]{1,0:T(8,128)(2,1)} %constant.247.clone.ft_ref), custom_call_target="tpu_custom_call" | custom-call | tf_op jit(solution)/shard_map/pallas_call | solution.py:101
  12.5 2.3 %fusion.50 = (f32[8,8,256]{2,1,0:T(8,128)S(1)}, f32[8,8,256]{2,1,0:T(8,128)S(1)}, f32[8,8,256]{2,1,0:T(8,128)S(1)}, f32[8,8,256]{2,1,0:T(8,128)S(1)}, f32[8,8,25...) fusion(s32[8,256]{1,0:T(8,128)S(1)} %add_select_fusion.12, ...), kind=kLoop, calls=%fused_computation.119 | loop fusion | flops 1376256 | bytes 811072 | tf_op jit(solution)/shard_map/cos | solution.py:35
  14.9 0.7 add.605
  15.7 0.7 broadcast_bitcast_fusion
  16.4 4.3 %collective-permute-done = bf16[3,8,128,128]{3,2,1,0:T(8,128)(2,1)S(1)} collective-permute-done((bf16[3,8,128,128]{3,2,1,0:T(8,128)(2,1)}, bf16[3,8,128,128]{3,2,1,0:T(8,128)(2,1)S(1)}, u32[]{:S(2)}, u32[]{:S(2)}) %collective-permute-start) | collective-permute-done | bytes 786464 | tf_op jit(solution)/shard_map/ppermute | solution.py:298
  20.7 1.6 %collective-permute-done.1 = bf16[3,8,128,128]{3,2,1,0:T(8,128)(2,1)} collective-permute-done((bf16[3,8,128,128]{3,2,1,0:T(8,128)(2,1)}, bf16[3,8,128,128]{3,2,1,0:T(8,128)(2,1)}, u32[]{:S(2)}, u32[]{:S(2)}) %collective-permute-start.1) | collective-permute-done | bytes 786464 | tf_op jit(solution)/shard_map/ppermute | solution.py:299
  22.3 1.6 %collective-permute-start.2 = (bf16[3,8,128,128]{3,2,1,0:T(8,128)(2,1)S(1)}, bf16[3,8,128,128]{3,2,1,0:T(8,128)(2,1)}, u32[]{:S(2)}, u32[]{:S(2)}) collective-permute-start(bf16[3,8,128,128]{3,2,1,0:T(8,128)(2,1)S(1)} %collective-permute-done), channel_id=1, source_target_pairs={{0,4},{4,8},{8,12},{12,14},{14,10},{10,6},{6,2},{2,0},{1,5},{5,9},... | collective-permute-start | bytes 2359304 | tf_op jit(solution)/shard_map/ppermute | solution.py:298
  23.9 0.4 collective-permute-start.3
  24.4 0.7 constant_dynamic-slice_fusion
  25.2 3.1 %fusion.3.v_ref = f32[64,64,256]{2,1,0:T(8,128)} fusion(f32[64,64]{1,0:T(8,128)S(1)} %copy.17, f32[64,8,256]{2,1,0:T(8,128)S(1)} %bitcast.94, f32[64,64]{1,0:T(8,128)S(1)} %copy.16, f32[64,8,256]{2,1,0:T(8,128)S(1)} %bitcast.95), kind=kLoop, calls=%fused_computation.5 | loop fusion | flops 5242880 | bytes 5275648 | tf_op jit(solution)/shard_map/add | solution.py:53
  28.3 0.9 copy-done.3
  29.1 4.6 %shard_map.110 = bf16[48,64,256]{2,1,0:T(8,128)(2,1)} custom-call(bf16[48,64,128]{2,1,0:T(8,128)(2,1)} %get-tuple-element.42.own_ref, bf16[48,64,128]{2,1,0:T(8,128)(2,1)} %copy-done.3, f32[64,64,256]{2,1,0:T(8,128)} %fusion.3.v_ref, bf16[128,256]{1,0:T(8,128)(2,1)} %get-tuple-element.74.fo_ref, bf16[128,256]{1,0:T(8,128)(2,1)} %get-tuple-element.73.fr_ref), custom_call_target="tpu_custom_call" | custom-call | tf_op jit(solution)/shard_map/pallas_call | solution.py:131
  33.8 2.9 %fusion.5 = bf16[3,64,256,48]{2,3,1,0:T(8,128)(2,1)S(1)} fusion(bf16[3,16,64,256]{3,2,1,0:T(8,128)(2,1)} %bitcast.88, bf16[3,48,16]{1,2,0:T(8,128)(2,1)S(1)} %copy-done), kind=kOutput, calls=%fused_computation.11 | convolution fusion | flops 75497472 | bytes 6296064 | tf_op jit(solution)/shard_map/dot_general | solution.py:362
  36.6 3.9 %copy.33 = bf16[3,64,256,48]{2,1,3,0:T(8,128)(2,1)} copy(bf16[3,64,256,48]{2,3,1,0:T(8,128)(2,1)S(1)} %fusion.5) | data formatting | bytes 9437184 | tf_op jit(solution)/shard_map/dot_general | solution.py:362
  40.5 1.5 %collective-permute-done.3 = bf16[3,8,128,128]{3,2,1,0:T(8,128)(2,1)} collective-permute-done((bf16[3,8,128,128]{3,2,1,0:T(8,128)(2,1)}, bf16[3,8,128,128]{3,2,1,0:T(8,128)(2,1)}, u32[]{:S(2)}, u32[]{:S(2)}) %collective-permute-start.3) | collective-permute-done | bytes 786464 | tf_op jit(solution)/shard_map/ppermute | solution.py:299
  42.0 1.6 %collective-permute-start.5 = (bf16[3,8,128,128]{3,2,1,0:T(8,128)(2,1)}, bf16[3,8,128,128]{3,2,1,0:T(8,128)(2,1)S(1)}, u32[]{:S(2)}, u32[]{:S(2)}) collective-permute-start(bf16[3,8,128,128]{3,2,1,0:T(8,128)(2,1)} %collective-permute-done.2), channel_id=1, source_target_pairs={{0,4},{4,8},{8,12},{12,14},{14,10},{10,6},{6,2},{2,0},{1,5},{5,9},... | collective-permute-start | bytes 2359304 | tf_op jit(solution)/shard_map/ppermute | solution.py:298
  43.6 0.5 collective-permute-start.6
  44.4 3.0 %add_bitcast_fusion.w_ref = f32[64,64,256]{2,1,0:T(8,128)} fusion(f32[64,8,256]{2,1,0:T(8,128)S(1)} %bitcast.92, f32[64,8,256]{2,1,0:T(8,128)S(1)} %bitcast.90, f32[64,8,256]{2,1,0:T(8,128)S(1)} %bitcast.93, f32[64,8,256]{2,1,0:T(8,128)S(1)} %bitcast.91), kind=kLoop, calls=%fused_computation.7 | loop fusion | flops 5242880 | bytes 6291456 | tf_op jit(solution)/shard_map/add | solution.py:53
  47.4 13.4 %shard_map.111 = (bf16[3,48,64,128]{3,2,1,0:T(8,128)(2,1)}, bf16[3,48,64,128]{3,2,1,0:T(8,128)(2,1)}) custom-call(s32[1]{0:T(128)} %bitcast.me_ref, bf16[3,48,64,256]{3,2,1,0:T(8,128)(2,1)} %bitcast.84, f32[64,64,256]{2,1,0:T(8,128)} %fusion.3.v_ref, f32[64,64,256]{2,1,0:T(8,128)} %add_bitcast_fusion.w_ref, bf16[256,256]{1,0:T(8,128)(2,1)} %constant.248.clone.ft_ref), custom_call_target="tpu_custom_call" | custom-call | tf_op jit(solution)/shard_map/pallas_call | solution.py:161
  61.0 0.6 dynamic_slice.38
  66.2 0.7 fusion.89
  71.2 0.7 constant_dynamic-slice_fusion.2
  71.9 1.6 %broadcast_in_dim.8 = bf16[3,64,128,128]{3,2,1,0:T(8,128)(2,1)S(1)} broadcast(bf16[]{:T(256)} %constant.223.clone.1), dimensions={} | broadcast | bytes 6291458 | tf_op jit(solution)/shard_map/broadcast_in_dim | solution.py:273
  73.8 1.3 %constant_dynamic-update-slice_fusion.4 = bf16[3,64,128,128]{3,2,1,0:T(8,128)(2,1)S(1)} fusion(bf16[3,64,128,128]{3,2,1,0:T(8,128)(2,1)S(1)} %constant_dynamic-update-slice_fusion.5, bf16[3,8,128,128]{3,2,1,0:T(8,128)(2,1)} %collective-permute-done.1, s32[]{:T(128)S(6)} %select_n.360), kind=kLoop, calls=%fused_computation.188 | loop fusion | bytes 1572868 | tf_op jit(solution)/shard_map/dynamic_update_slice | solution.py:303
  75.0 1.3 %constant_dynamic-update-slice_fusion.3 = bf16[3,64,128,128]{3,2,1,0:T(8,128)(2,1)S(1)} fusion(bf16[3,64,128,128]{3,2,1,0:T(8,128)(2,1)S(1)} %constant_dynamic-update-slice_fusion.4, bf16[3,8,128,128]{3,2,1,0:T(8,128)(2,1)} %collective-permute-done.2, s32[]{:T(128)S(6)} %select_n.369), kind=kLoop, calls=%fused_computation.187 | loop fusion | bytes 1572868 | tf_op jit(solution)/shard_map/dynamic_update_slice | solution.py:300
  76.3 1.0 slice.7
  77.3 0.5 collective-permute-start.8
  77.9 1.6 %collective-permute-start.7 = (bf16[3,8,64,128]{3,2,1,0:T(8,128)(2,1)S(1)}, bf16[3,8,64,128]{3,2,1,0:T(8,128)(2,1)S(1)}, u32[]{:S(2)}, u32[]{:S(2)}) collective-permute-start(bf16[3,8,64,128]{3,2,1,0:T(8,128)(2,1)S(1)} %slice.6), channel_id=1, source_target_pairs={{0,4},{4,8},{8,12},{12,14},{14,10},{10,6},{6,2},{2,0},{1,5},{5,9},... | collective-permute-start | bytes 1179656 | tf_op jit(solution)/shard_map/ppermute | solution.py:308
  79.5 1.3 constant_dynamic-update-slice_fusion.2
  80.9 1.3 %constant_dynamic-update-slice_fusion = bf16[3,64,128,128]{3,2,1,0:T(8,128)(2,1)S(1)} fusion(bf16[3,64,128,128]{3,2,1,0:T(8,128)(2,1)S(1)} %constant_dynamic-update-slice_fusion.1, bf16[3,8,128,128]{3,2,1,0:T(8,128)(2,1)} %collective-permute-done.6, s32[]{:T(128)S(6)} %select_n.386), kind=kLoop, calls=%fused_computation.182 | loop fusion | bytes 1572868 | tf_op jit(solution)/shard_map/dynamic_update_slice | solution.py:303
  82.2 6.7 %collective-permute-done.8 = bf16[3,8,64,128]{3,2,1,0:T(8,128)(2,1)S(1)} collective-permute-done((bf16[3,8,64,128]{3,2,1,0:T(8,128)(2,1)S(1)}, bf16[3,8,64,128]{3,2,1,0:T(8,128)(2,1)S(1)}, u32[]{:S(2)}, u32[]{:S(2)}) %collective-permute-start.8) | collective-permute-done | bytes 393248 | tf_op jit(solution)/shard_map/ppermute | solution.py:309
  89.3 2.7 %copy-done.2 = bf16[3,64,128,128]{3,2,1,0:T(8,128)(2,1)} copy-done((bf16[3,64,128,128]{3,2,1,0:T(8,128)(2,1)}, bf16[3,64,128,128]{3,2,1,0:T(8,128)(2,1)S(1)}, u32[]{:S(2)}) %copy-start.2) | copy-done | bytes 6291480
  92.0 1.5 %copy-done.1 = bf16[3,48,64,128]{3,2,1,0:T(8,128)(2,1)} copy-done((bf16[3,48,64,128]{3,2,1,0:T(8,128)(2,1)}, bf16[3,48,64,128]{3,2,1,0:T(8,128)(2,1)S(1)}, u32[]{:S(2)}) %copy-start.1) | copy-done | bytes 2359320
  93.4 3.5 %shard_map.112.y_ref = bf16[16,128,128]{2,1,0:T(8,128)(2,1)} custom-call(bf16[128,64]{1,0:T(8,128)(2,1)} %get-tuple-element.78.refs_0_.fo_ref, bf16[128,64]{1,0:T(8,128)(2,1)} %get-tuple-element.77.refs_1_.fr_ref, bf16[48,128,128]{2,1,0:T(8,128)(2,1)} %bitcast.86, bf16[3,64,128,128]{3,2,1,0:T(8,128)(2,1)} %copy-done.2, ...), custom_call_target="tpu_custom_call" | custom-call | tf_op jit(solution)/shard_map/pallas_call | solution.py:211
  96.9 2.6 %shard_map.113 = (bf16[16,64,128]{2,1,0:T(8,128)(2,1)}, bf16[16,64,128]{2,1,0:T(8,128)(2,1)}) custom-call(s32[1]{0:T(128)} %bitcast.me_ref, bf16[16,128,128]{2,1,0:T(8,128)(2,1)} %shard_map.112.y_ref, f32[64,128,128]{2,1,0:T(8,128)} %add_bitcast_fusion.1.w_ref, bf16[128,128]{1,0:T(8,128)(2,1)} %constant.247.clone.ft_ref), custom_call_target="tpu_custom_call" | custom-call | tf_op jit(solution)/shard_map/pallas_call | solution.py:101
  99.5 1.7 %collective-permute-done.10.recv_ref = bf16[16,64,128]{2,1,0:T(8,128)(2,1)S(1)} collective-permute-done((bf16[16,64,128]{2,1,0:T(8,128)(2,1)}, bf16[16,64,128]{2,1,0:T(8,128)(2,1)S(1)}, u32[]{:S(2)}, u32[]{:S(2)}) %collective-permute-start.10) | collective-permute-done | bytes 262176 | tf_op jit(solution)/shard_map/ppermute | solution.py:330
  101.3 0.7 copy-done.8
  102.0 2.5 %shard_map.114 = bf16[16,64,256]{2,1,0:T(8,128)(2,1)} custom-call(bf16[16,64,128]{2,1,0:T(8,128)(2,1)} %get-tuple-element.61.own_ref, bf16[16,64,128]{2,1,0:T(8,128)(2,1)} %copy-done.8, f32[64,64,256]{2,1,0:T(8,128)} %fusion.3.v_ref, bf16[128,256]{1,0:T(8,128)(2,1)} %get-tuple-element.74.fo_ref, bf16[128,256]{1,0:T(8,128)(2,1)} %get-tuple-element.73.fr_ref), custom_call_target="tpu_custom_call" | custom-call | tf_op jit(solution)/shard_map/pallas_call | solution.py:131
  104.5 1.6 %fusion.7 = bf16[64,256,48]{1,2,0:T(8,128)(2,1)S(1)} fusion(bf16[16,64,256]{2,1,0:T(8,128)(2,1)} %shard_map.114, bf16[48,16]{0,1:T(8,128)(2,1)S(1)} %copy-done.13), kind=kOutput, calls=%fused_computation.14 | convolution fusion | flops 25165824 | bytes 2098688 | tf_op jit(solution)/shard_map/dot_general | solution.py:379
  106.2 1.7 %copy.34 = bf16[64,256,48]{1,0,2:T(8,128)(2,1)} copy(bf16[64,256,48]{1,2,0:T(8,128)(2,1)S(1)} %fusion.7) | data formatting | bytes 3145728 | tf_op jit(solution)/shard_map/dot_general | solution.py:379
  107.9 5.7 %shard_map.115 = (bf16[1,48,64,128]{3,2,1,0:T(8,128)(2,1)}, bf16[1,48,64,128]{3,2,1,0:T(8,128)(2,1)}) custom-call(s32[1]{0:T(128)} %bitcast.me_ref, bf16[1,48,64,256]{3,2,1,0:T(8,128)(2,1)} %bitcast.89, f32[64,64,256]{2,1,0:T(8,128)} %fusion.3.v_ref, f32[64,64,256]{2,1,0:T(8,128)} %add_bitcast_fusion.w_ref, bf16[256,256]{1,0:T(8,128)(2,1)} %constant.248.clone.ft_ref), custom_call_target="tpu_custom_call" | custom-call | tf_op jit(solution)/shard_map/pallas_call | solution.py:161
  113.7 6.9 %shard_map.116.prod_ref = bf16[48,128,128]{2,1,0:T(8,128)(2,1)} custom-call(bf16[128,64]{1,0:T(8,128)(2,1)} %get-tuple-element.78.refs_0_.fo_ref, bf16[128,64]{1,0:T(8,128)(2,1)} %get-tuple-element.77.refs_1_.fr_ref, bf16[48,128,128]{2,1,0:T(8,128)(2,1)} %bitcast.87, bf16[3,64,128,128]{3,2,1,0:T(8,128)(2,1)} %copy-done.2, ...), custom_call_target="tpu_custom_call" | custom-call | tf_op jit(solution)/shard_map/pallas_call | solution.py:211
  120.6 0.9 broadcast_in_dim.10.s_ref
  121.5 4.4 %shard_map.117 = bf16[48,128,128]{2,1,0:T(8,128)(2,1)} custom-call(bf16[128,64]{1,0:T(8,128)(2,1)} %get-tuple-element.78.refs_0_.fo_ref, bf16[128,64]{1,0:T(8,128)(2,1)} %get-tuple-element.77.refs_1_.fr_ref, bf16[48,64,128]{2,1,0:T(8,128)(2,1)} %bitcast.100, bf16[48,64,128]{2,1,0:T(8,128)(2,1)} %bitcast.101, bf16[48,128,128]{2,1,0:T(8,128)(2,1)} %shard_map.116.prod_ref, ...), custom_call_target="tpu_custom_call" | custom-call | tf_op jit(solution)/shard_map/pallas_call | solution.py:242
  (66 shorter events, 2.4 us)
Async XLA Ops:
  0.0 33.8 %copy-start = (bf16[3,48,16]{1,2,0:T(8,128)(2,1)S(1)}, bf16[3,48,16]{1,2,0:T(8,128)(2,1)}, u32[]{:S(2)}) copy-start(bf16[3,48,16]{1,2,0:T(8,128)(2,1)} %param.13) | copy-start | bytes 13828
  0.0 20.7 %collective-permute-start = (bf16[3,8,128,128]{3,2,1,0:T(8,128)(2,1)}, bf16[3,8,128,128]{3,2,1,0:T(8,128)(2,1)S(1)}, u32[]{:S(2)}, u32[]{:S(2)}) collective-permute-start(bf16[3,8,128,128]{3,2,1,0:T(8,128)(2,1)} %bitcast.102), channel_id=1, source_target_pairs={{0,4},{4,8},{8,12},{12,14},{14,10},{10,6},{6,2},{2,0},{1,5},{5,9},... | collective-permute-start | bytes 2359304 | tf_op jit(solution)/shard_map/ppermute | solution.py:298
  3.0 19.3 %collective-permute-start.1 = (bf16[3,8,128,128]{3,2,1,0:T(8,128)(2,1)}, bf16[3,8,128,128]{3,2,1,0:T(8,128)(2,1)}, u32[]{:S(2)}, u32[]{:S(2)}) collective-permute-start(bf16[3,8,128,128]{3,2,1,0:T(8,128)(2,1)} %bitcast.103), channel_id=1, source_target_pairs={{0,2},{4,0},{8,4},{12,8},{14,12},{10,14},{6,10},{2,6},{1,3},{5,1},... | collective-permute-start | bytes 2359304 | tf_op jit(solution)/shard_map/ppermute | solution.py:299
  3.0 9.3 %copy-start.12 = (s32[8]{0:T(128)}, s32[8]{0:T(128)S(1)}, u32[]{:S(2)}) copy-start(s32[8]{0:T(128)S(1)} %get-tuple-element.135) | copy-start | bytes 100
  7.2 17.1 %copy-start.9 = (bf16[256,256]{1,0:T(8,128)(2,1)S(1)}, bf16[256,256]{1,0:T(8,128)(2,1)}, u32[]{:S(2)}) copy-start(bf16[256,256]{1,0:T(8,128)(2,1)} %constant.245.clone) | copy-start | bytes 393220
  12.2 16.1 %collective-permute-start.4 = (bf16[48,64,128]{2,1,0:T(8,128)(2,1)}, bf16[48,64,128]{2,1,0:T(8,128)(2,1)S(1)}, u32[]{:S(2)}, u32[]{:S(2)}) collective-permute-start(bf16[48,64,128]{2,1,0:T(8,128)(2,1)} %get-tuple-element.43), channel_id=1, source_target_pairs={{0,1},{1,0},{2,3},{3,2},{4,5},{5,4},{6,7},{7,6},{8,9},{9,8},{10,11... | collective-permute-start | bytes 2359304 | tf_op jit(solution)/shard_map/ppermute | solution.py:330
  20.7 13.0 %copy-start.6 = (bf16[3,8,128,128]{3,2,1,0:T(8,128)(2,1)}, bf16[3,8,128,128]{3,2,1,0:T(8,128)(2,1)S(1)}, u32[]{:S(2)}) copy-start(bf16[3,8,128,128]{3,2,1,0:T(8,128)(2,1)S(1)} %collective-permute-done) | copy-start | bytes 2359300
  22.3 18.2 %collective-permute-start.2 = (bf16[3,8,128,128]{3,2,1,0:T(8,128)(2,1)S(1)}, bf16[3,8,128,128]{3,2,1,0:T(8,128)(2,1)}, u32[]{:S(2)}, u32[]{:S(2)}) collective-permute-start(bf16[3,8,128,128]{3,2,1,0:T(8,128)(2,1)S(1)} %collective-permute-done), channel_id=1, source_target_pairs={{0,4},{4,8},{8,12},{12,14},{14,10},{10,6},{6,2},{2,0},{1,5},{5,9},... | collective-permute-start | bytes 2359304 | tf_op jit(solution)/shard_map/ppermute | solution.py:298
  23.9 18.1 %collective-permute-start.3 = (bf16[3,8,128,128]{3,2,1,0:T(8,128)(2,1)}, bf16[3,8,128,128]{3,2,1,0:T(8,128)(2,1)}, u32[]{:S(2)}, u32[]{:S(2)}) collective-permute-start(bf16[3,8,128,128]{3,2,1,0:T(8,128)(2,1)} %collective-permute-done.1), channel_id=1, source_target_pairs={{0,2},{4,0},{8,4},{12,8},{14,12},{10,14},{6,10},{2,6},{1,3},{5,1},... | collective-permute-start | bytes 2359304 | tf_op jit(solution)/shard_map/ppermute | solution.py:299
  28.3 0.9 copy-start.3
  42.0 18.8 %collective-permute-start.5 = (bf16[3,8,128,128]{3,2,1,0:T(8,128)(2,1)}, bf16[3,8,128,128]{3,2,1,0:T(8,128)(2,1)S(1)}, u32[]{:S(2)}, u32[]{:S(2)}) collective-permute-start(bf16[3,8,128,128]{3,2,1,0:T(8,128)(2,1)} %collective-permute-done.2), channel_id=1, source_target_pairs={{0,4},{4,8},{8,12},{12,14},{14,10},{10,6},{6,2},{2,0},{1,5},{5,9},... | collective-permute-start | bytes 2359304 | tf_op jit(solution)/shard_map/ppermute | solution.py:298
  43.6 17.2 %collective-permute-start.6 = (bf16[3,8,128,128]{3,2,1,0:T(8,128)(2,1)}, bf16[3,8,128,128]{3,2,1,0:T(8,128)(2,1)}, u32[]{:S(2)}, u32[]{:S(2)}) collective-permute-start(bf16[3,8,128,128]{3,2,1,0:T(8,128)(2,1)} %collective-permute-done.3), channel_id=1, source_target_pairs={{0,2},{4,0},{8,4},{12,8},{14,12},{10,14},{6,10},{2,6},{1,3},{5,1},... | collective-permute-start | bytes 2359304 | tf_op jit(solution)/shard_map/ppermute | solution.py:299
  47.4 13.5 %copy-start.15 = (s32[8]{0:T(128)S(1)}, s32[8]{0:T(128)}, u32[]{:S(2)}) copy-start(s32[8]{0:T(128)} %constant.244.clone) | copy-start | bytes 100
  47.4 18.8 %copy-start.11 = (s32[8]{0:T(128)S(1)}, s32[8]{0:T(128)}, u32[]{:S(2)}) copy-start(s32[8]{0:T(128)} %constant.243.clone) | copy-start | bytes 100
  47.4 23.8 %copy-start.10 = (bf16[128,128]{1,0:T(8,128)(2,1)S(1)}, bf16[128,128]{1,0:T(8,128)(2,1)}, u32[]{:S(2)}) copy-start(bf16[128,128]{1,0:T(8,128)(2,1)} %constant.246.clone) | copy-start | bytes 98308
  60.9 28.4 %collective-permute-start.9 = (bf16[3,48,64,128]{3,2,1,0:T(8,128)(2,1)}, bf16[3,48,64,128]{3,2,1,0:T(8,128)(2,1)S(1)}, u32[]{:S(2)}, u32[]{:S(2)}) collective-permute-start(bf16[3,48,64,128]{3,2,1,0:T(8,128)(2,1)} %get-tuple-element.60), channel_id=1, source_target_pairs={{0,1},{1,0},{2,3},{3,2},{4,5},{5,4},{6,7},{7,6},{8,9},{9,8},{10,11... | collective-permute-start | bytes 7077896 | tf_op jit(solution)/shard_map/ppermute | solution.py:330
  71.2 2.3 %copy-start.5 = (bf16[1,3,8,128,128]{4,3,2,1,0:T(8,128)(2,1)S(1)}, bf16[1,3,8,128,128]{4,3,2,1,0:T(8,128)(2,1)}, u32[]{:S(2)}) copy-start(bf16[1,3,8,128,128]{4,3,2,1,0:T(8,128)(2,1)} %param.12) | copy-start | bytes 2359300
  71.2 2.4 %copy-start.7 = (bf16[3,8,128,128]{3,2,1,0:T(8,128)(2,1)S(1)}, bf16[3,8,128,128]{3,2,1,0:T(8,128)(2,1)}, u32[]{:S(2)}) copy-start(bf16[3,8,128,128]{3,2,1,0:T(8,128)(2,1)} %copy-done.6) | copy-start | bytes 2359300
  77.3 11.5 %collective-permute-start.8 = (bf16[3,8,64,128]{3,2,1,0:T(8,128)(2,1)S(1)}, bf16[3,8,64,128]{3,2,1,0:T(8,128)(2,1)S(1)}, u32[]{:S(2)}, u32[]{:S(2)}) collective-permute-start(bf16[3,8,64,128]{3,2,1,0:T(8,128)(2,1)S(1)} %slice.7), channel_id=1, source_target_pairs={{0,2},{4,0},{8,4},{12,8},{14,12},{10,14},{6,10},{2,6},{1,3},{5,1},... | collective-permute-start | bytes 1179656 | tf_op jit(solution)/shard_map/ppermute | solution.py:309
  77.9 11.3 %collective-permute-start.7 = (bf16[3,8,64,128]{3,2,1,0:T(8,128)(2,1)S(1)}, bf16[3,8,64,128]{3,2,1,0:T(8,128)(2,1)S(1)}, u32[]{:S(2)}, u32[]{:S(2)}) collective-permute-start(bf16[3,8,64,128]{3,2,1,0:T(8,128)(2,1)S(1)} %slice.6), channel_id=1, source_target_pairs={{0,4},{4,8},{8,12},{12,14},{14,10},{10,6},{6,2},{2,0},{1,5},{5,9},... | collective-permute-start | bytes 1179656 | tf_op jit(solution)/shard_map/ppermute | solution.py:308
  89.3 2.7 %copy-start.2 = (bf16[3,64,128,128]{3,2,1,0:T(8,128)(2,1)}, bf16[3,64,128,128]{3,2,1,0:T(8,128)(2,1)S(1)}, u32[]{:S(2)}) copy-start(bf16[3,64,128,128]{3,2,1,0:T(8,128)(2,1)S(1)} %maximum_dynamic-update-slice_fusion.refs_3_) | copy-start | bytes 18874372
  92.0 1.5 %copy-start.1 = (bf16[3,48,64,128]{3,2,1,0:T(8,128)(2,1)}, bf16[3,48,64,128]{3,2,1,0:T(8,128)(2,1)S(1)}, u32[]{:S(2)}) copy-start(bf16[3,48,64,128]{3,2,1,0:T(8,128)(2,1)S(1)} %collective-permute-done.9.refs_5_.refs_7_.refs_9_) | copy-start | bytes 7077892
  96.9 7.6 %copy-start.13 = (bf16[48,16]{0,1:T(8,128)(2,1)S(1)}, bf16[48,16]{0,1:T(8,128)(2,1)}, u32[]{:S(2)}) copy-start(bf16[48,16]{0,1:T(8,128)(2,1)} %param.14) | copy-start | bytes 4612
  99.5 1.7 %collective-permute-start.10 = (bf16[16,64,128]{2,1,0:T(8,128)(2,1)}, bf16[16,64,128]{2,1,0:T(8,128)(2,1)S(1)}, u32[]{:S(2)}, u32[]{:S(2)}) collective-permute-start(bf16[16,64,128]{2,1,0:T(8,128)(2,1)} %get-tuple-element.62), channel_id=1, source_target_pairs={{0,1},{1,0},{2,3},{3,2},{4,5},{5,4},{6,7},{7,6},{8,9},{9,8},{10,11... | collective-permute-start | bytes 786440 | tf_op jit(solution)/shard_map/ppermute | solution.py:330
  101.3 0.7 copy-start.8
  113.6 7.0 %copy-start.14 = (f32[48]{0:T(128)S(1)}, f32[48]{0:T(128)}, u32[]{:S(2)}) copy-start(f32[48]{0:T(128)} %param.15) | copy-start | bytes 580
  113.6 7.0 %collective-permute-start.11 = (bf16[1,48,64,128]{3,2,1,0:T(8,128)(2,1)}, bf16[1,48,64,128]{3,2,1,0:T(8,128)(2,1)S(1)}, u32[]{:S(2)}, u32[]{:S(2)}) collective-permute-start(bf16[1,48,64,128]{3,2,1,0:T(8,128)(2,1)} %get-tuple-element.64), channel_id=1, source_target_pairs={{0,1},{1,0},{2,3},{3,2},{4,5},{5,4},{6,7},{7,6},{8,9},{9,8},{10,11... | collective-permute-start | bytes 2359304 | tf_op jit(solution)/shard_map/ppermute | solution.py:330
  120.6 0.9 copy-start.4

commit v11 on v10

--- a/solution.py
+++ b/solution.py
@@ -304,13 +304,9 @@
             st["full"], st["b"], order[(p + s) % n] * width, axis=1
         )
     else:
-        h = st["a"].shape[2] // 2
-        a = lax.ppermute(st["a"][:, :, :h], "limb", st["cw"])
-        b = lax.ppermute(st["b"][:, :, h:], "limb", st["ccw"])
+        a = lax.ppermute(st["a"], "limb", st["cw"])
         src = order[(p + s) % n] * width
-        st["full"] = lax.dynamic_update_slice_in_dim(
-            st["full"], jnp.concatenate([a, b], axis=2), src, axis=1
-        )
+        st["full"] = lax.dynamic_update_slice_in_dim(st["full"], a, src, axis=1)
 
 
 def ring_hold(st, x):
@@ -321,10 +317,11 @@
     return x
 
 
-def ring_finish(st):
+def ring_finish(st, x):
     while st["s"] < ring_steps(st):
         ring_step(st)
-    return st["full"]
+    st["full"], x = lax.optimization_barrier((st["full"], x))
+    return st["full"], x
 
 def swap(x):
     return lax.ppermute(x, "coef", perm=[(0, 1), (1, 0)])
@@ -358,6 +355,7 @@
     own1 = ring_hold(ring, own1)
     coeffs = inv_col(own1, swap(send1), v_row, fc_own, fc_oth, 0)
 
+    coeffs = ring_hold(ring, coeffs)
     blocks = coeffs.reshape(DIGITS, DIGIT_LIMBS, rows_l, cols)
     raised = lax.dot_general(
         raise_table, blocks, (((2,), (1,)), ((0,), (0,))), preferred_element_type=F32
@@ -367,9 +365,8 @@
     own2, send2 = fwd_col(
         me_arr, raised, v_row, w_row, ft_cols, lambda j, t: jnp.where(t >= j, t + 1, t)
     )
-    own2, send2 = ring_hold(ring, (own2, send2))
+    key, (own2, send2) = ring_finish(ring, (own2, send2))
     recv2 = swap(send2)
-    key = ring_finish(ring)
 
     prod_special = product(ct, key, own2, recv2, fr_own, fr_oth, DIGITS, 1)
     prod_cipher = product(ct, key, own2, recv2, fr_own, fr_oth, 0, DIGITS)

time: 127 us -> 134 us (1.055)
  local copies, waits for them, and re-layouts: 24.5 us -> 33.6 us
  other arithmetic: 13.4 us -> 14.9 us
    ppermute x2 -> x1, waiting for transfers between devices: 6.99 us -> 0.01 us  [ring_step(): a = lax.ppermute(st['a'], 'limb', st['cw'])]
    dynamic_update_slice x3, local copies, waits for them, and re-layouts: 1.48 us -> 6.68 us  [ring_step(): lax.dynamic_update_slice_in_dim(st['full'], st['a'], order[(p - s) % n] *...]
    ppermute x4, waiting for transfers between devices: 1.75 us -> 5.63 us  [swap(): return lax.ppermute(x, 'coef', perm=[(0, 1), (1, 0)])]
    dynamic_update_slice x3, local copies, waits for them, and re-layouts: 3.78 us -> 6.66 us  [ring_step(): lax.dynamic_update_slice_in_dim(st['full'], st['b'], order[(p + s) % n] *...]
    unnamed x32 -> x26, local copies, waits for them, and re-layouts: 5.77 us -> 3.08 us
    broadcast_in_dim x1, local copies, waits for them, and re-layouts: 1.57 us -> 4.23 us  [ring_setup(): full = jnp.zeros((shard.shape[0], n * width) + shard.shape[2:], shard.dtype)]
    ppermute x3, waiting for transfers between devices: 4.34 us -> 6.4 us  [ring_step(): st['a'] = lax.ppermute(st['a'], 'limb', st['cw'])]
    add x3, other arithmetic: 9.03 us -> 10.5 us  [_twiddle(): return 1.0 + 0.5 * (cp * cq - sp * sq)]
  transfers between devices with their start and end apart: 12 -> 11, of which waited for: 6 -> 6; matrix products, arithmetic and copies ran while one was open for 26% -> 33% of each run, Pallas kernels for 24% -> 22%
where the time goes in v11:
time: 134 us; the launch traced here: 133 us
  Pallas kernels  48.5 us (36%)
  local copies, waits for them, and re-layouts  33.6 us (25%)
  other arithmetic  14.9 us (11%)
  waiting for transfers between devices  14.9 us (11%)
  starting transfers between devices  8.96 us (7%)
  between operations  8.64 us (6%)
  matrix products  3.2 us (2%)
    pallas_call x2, Pallas kernels, fwd_col(): pl.pallas_call(_fwd_col_kernel, grid=(groups, n // BLK), in_specs=[SMEM_S...  19.1 us
    add x3, other arithmetic, _twiddle(): return 1.0 + 0.5 * (cp * cq - sp * sq)  10.5 us
    pallas_call x2, Pallas kernels, product(): pl.pallas_call(lambda *refs: _product_kernel(eb0, *refs), grid=(nblocks,)...  10.4 us
    pallas_call x2, Pallas kernels, inv_row(): pl.pallas_call(_inv_row_kernel, grid=(n // BLK,), in_specs=[SMEM_SPEC, bl...  7.45 us
    pallas_call x2, Pallas kernels, inv_col(): pl.pallas_call(_inv_col_kernel, grid=(n // BLK,), in_specs=[blk, blk, pl....  7.16 us
    dynamic_update_slice x3, local copies, waits for them, and re-layouts, ring_step(): lax.dynamic_update_slice_in_dim(st['full'], st['a'], order[(p - s) % n] *...  6.68 us
    dynamic_update_slice x3, local copies, waits for them, and re-layouts, ring_step(): lax.dynamic_update_slice_in_dim(st['full'], st['b'], order[(p + s) % n] *...  6.66 us
    ppermute x3, waiting for transfers between devices, ring_step(): st['a'] = lax.ppermute(st['a'], 'limb', st['cw'])  6.4 us
  transfers between devices with their start and end apart: 11, of which 6 were waited for; matrix products, arithmetic and copies ran while one was open for 33% of the time, Pallas kernels for 22%

profile of v11, /device:TPU:0, one launch (start us, length us, event | category | flops | bytes accessed | tf_op | source)
XLA Modules:
  0.0 132.7 jit_solution(16313287544167980381)
XLA Ops:
  0.0 3.0 %collective-permute-start = (bf16[3,8,128,128]{3,2,1,0:T(8,128)(2,1)}, bf16[3,8,128,128]{3,2,1,0:T(8,128)(2,1)}, u32[]{:S(2)}, u32[]{:S(2)}) collective-permute-start(bf16[3,8,128,128]{3,2,1,0:T(8,128)(2,1)} %bitcast.102), channel_id=1, source_target_pairs={{0,4},{4,8},{8,12},{12,14},{14,10},{10,6},{6,2},{2,0},{1,5},{5,9},... | collective-permute-start | bytes 2359304 | tf_op jit(solution)/shard_map/ppermute | solution.py:298
  3.1 0.6 fusion.54
  4.3 3.1 %add_bitcast_fusion.1.w_ref = f32[64,128,128]{2,1,0:T(8,128)} fusion(f32[64,8,128]{2,1,0:T(8,128)S(1)} %bitcast.98, f32[64,16,128]{2,1,0:T(8,128)S(1)} %bitcast.96, f32[64,8,128]{2,1,0:T(8,128)S(1)} %bitcast.99, f32[64,16,128]{2,1,0:T(8,128)S(1)} %bitcast.97), kind=kLoop, calls=%fused_computation.8 | loop fusion | flops 5242880 | bytes 5767168 | tf_op jit(solution)/shard_map/add | solution.py:53
  7.4 4.9 %shard_map.109 = (bf16[48,64,128]{2,1,0:T(8,128)(2,1)}, bf16[48,64,128]{2,1,0:T(8,128)(2,1)}) custom-call(s32[1]{0:T(128)} %bitcast.me_ref, bf16[48,128,128]{2,1,0:T(8,128)(2,1)} %bitcast.85, f32[64,128,128]{2,1,0:T(8,128)} %add_bitcast_fusion.1.w_ref, bf16[128,128]{1,0:T(8,128)(2,1)} %constant.247.clone.ft_ref), custom_call_target="tpu_custom_call" | custom-call | tf_op jit(solution)/shard_map/pallas_call | solution.py:101
  12.6 1.6 %fusion.50 = (f32[8,8,256]{2,1,0:T(8,128)S(1)}, f32[8,8,256]{2,1,0:T(8,128)S(1)}, f32[8,8,256]{2,1,0:T(8,128)S(1)}, f32[8,8,256]{2,1,0:T(8,128)S(1)}, f32[8,8,25...) fusion(s32[8,256]{1,0:T(8,128)S(1)} %add_select_fusion.12, ...), kind=kLoop, calls=%fused_computation.118 | loop fusion | flops 1376256 | bytes 811072 | tf_op jit(solution)/shard_map/cos | solution.py:35
  14.6 0.6 broadcast_bitcast_fusion
  15.4 5.5 %collective-permute-done = bf16[3,8,128,128]{3,2,1,0:T(8,128)(2,1)} collective-permute-done((bf16[3,8,128,128]{3,2,1,0:T(8,128)(2,1)}, bf16[3,8,128,128]{3,2,1,0:T(8,128)(2,1)}, u32[]{:S(2)}, u32[]{:S(2)}) %collective-permute-start) | collective-permute-done | bytes 786464 | tf_op jit(solution)/shard_map/ppermute | solution.py:298
  20.8 1.5 %collective-permute-done.1 = bf16[3,8,128,128]{3,2,1,0:T(8,128)(2,1)} collective-permute-done((bf16[3,8,128,128]{3,2,1,0:T(8,128)(2,1)}, bf16[3,8,128,128]{3,2,1,0:T(8,128)(2,1)}, u32[]{:S(2)}, u32[]{:S(2)}) %collective-permute-start.1) | collective-permute-done | bytes 786464 | tf_op jit(solution)/shard_map/ppermute | solution.py:299
  22.3 1.6 %collective-permute-start.2 = (bf16[3,8,128,128]{3,2,1,0:T(8,128)(2,1)}, bf16[3,8,128,128]{3,2,1,0:T(8,128)(2,1)}, u32[]{:S(2)}, u32[]{:S(2)}) collective-permute-start(bf16[3,8,128,128]{3,2,1,0:T(8,128)(2,1)} %collective-permute-done), channel_id=1, source_target_pairs={{0,4},{4,8},{8,12},{12,14},{14,10},{10,6},{6,2},{2,0},{1,5},{5,9},... | collective-permute-start | bytes 2359304 | tf_op jit(solution)/shard_map/ppermute | solution.py:298
  24.4 0.8 copy.17
  25.3 0.7 constant_dynamic-slice_fusion
  26.0 4.2 %broadcast_in_dim.8 = bf16[3,64,128,128]{3,2,1,0:T(8,128)(2,1)} broadcast(bf16[]{:T(256)} %constant.223.clone.1), dimensions={} | broadcast | bytes 6291458 | tf_op jit(solution)/shard_map/broadcast_in_dim | solution.py:273
  30.2 1.0 constant_dynamic-update-slice_fusion.7
  31.3 3.0 %fusion.3.v_ref = f32[64,64,256]{2,1,0:T(8,128)} fusion(f32[64,64]{1,0:T(8,128)S(1)} %copy.17, f32[64,8,256]{2,1,0:T(8,128)S(1)} %bitcast.94, f32[64,64]{1,0:T(8,128)S(1)} %copy.16, f32[64,8,256]{2,1,0:T(8,128)S(1)} %bitcast.95), kind=kLoop, calls=%fused_computation.5 | loop fusion | flops 5242880 | bytes 5275648 | tf_op jit(solution)/shard_map/add | solution.py:53
  34.3 0.9 copy-done.3
  35.2 4.6 %shard_map.110 = bf16[48,64,256]{2,1,0:T(8,128)(2,1)} custom-call(bf16[48,64,128]{2,1,0:T(8,128)(2,1)} %get-tuple-element.43.own_ref, bf16[48,64,128]{2,1,0:T(8,128)(2,1)} %copy-done.3, f32[64,64,256]{2,1,0:T(8,128)} %fusion.3.v_ref, bf16[128,256]{1,0:T(8,128)(2,1)} %get-tuple-element.76.fo_ref, bf16[128,256]{1,0:T(8,128)(2,1)} %get-tuple-element.75.fr_ref), custom_call_target="tpu_custom_call" | custom-call | tf_op jit(solution)/shard_map/pallas_call | solution.py:131
  39.8 0.9 collective-permute-done.2
  40.8 1.3 collective-permute-done.3
  42.0 1.6 %collective-permute-start.5 = (bf16[3,8,128,128]{3,2,1,0:T(8,128)(2,1)}, bf16[3,8,128,128]{3,2,1,0:T(8,128)(2,1)}, u32[]{:S(2)}, u32[]{:S(2)}) collective-permute-start(bf16[3,8,128,128]{3,2,1,0:T(8,128)(2,1)} %collective-permute-done.2), channel_id=1, source_target_pairs={{0,4},{4,8},{8,12},{12,14},{14,10},{10,6},{6,2},{2,0},{1,5},{5,9},... | collective-permute-start | bytes 2359304 | tf_op jit(solution)/shard_map/ppermute | solution.py:298
  44.1 1.0 multiply_add_fusion
  45.0 0.6 dynamic_slice.38
  49.8 0.7 fusion.89
  54.8 4.4 %add_bitcast_fusion.w_ref = f32[64,64,256]{2,1,0:T(8,128)} fusion(f32[64,8,256]{2,1,0:T(8,128)S(1)} %bitcast.92, f32[64,8,256]{2,1,0:T(8,128)S(1)} %bitcast.90, f32[64,8,256]{2,1,0:T(8,128)} %bitcast.93, f32[64,8,256]{2,1,0:T(8,128)S(1)} %bitcast.91), kind=kLoop, calls=%fused_computation.7 | loop fusion | flops 5242880 | bytes 6291456 | tf_op jit(solution)/shard_map/add | solution.py:53
  59.1 1.5 %fusion.5 = bf16[3,64,256,48]{2,3,1,0:T(8,128)(2,1)S(1)} fusion(bf16[3,16,64,256]{3,2,1,0:T(8,128)(2,1)S(1)} %bitcast.88, bf16[3,48,16]{1,2,0:T(8,128)(2,1)S(1)} %copy-done), kind=kOutput, calls=%fused_computation.11 | convolution fusion | flops 75497472 | bytes 6296064 | tf_op jit(solution)/shard_map/dot_general | solution.py:360
  60.7 3.9 %copy.33 = bf16[3,64,256,48]{2,1,3,0:T(8,128)(2,1)} copy(bf16[3,64,256,48]{2,3,1,0:T(8,128)(2,1)S(1)} %fusion.5) | data formatting | bytes 9437184 | tf_op jit(solution)/shard_map/dot_general | solution.py:360
  64.6 1.6 %collective-permute-start.7 = (bf16[3,8,128,128]{3,2,1,0:T(8,128)(2,1)}, bf16[3,8,128,128]{3,2,1,0:T(8,128)(2,1)S(1)}, u32[]{:S(2)}, u32[]{:S(2)}) collective-permute-start(bf16[3,8,128,128]{3,2,1,0:T(8,128)(2,1)} %collective-permute-done.5), channel_id=1, source_target_pairs={{0,4},{4,8},{8,12},{12,14},{14,10},{10,6},{6,2},{2,0},{1,5},{5,9},... | collective-permute-start | bytes 2359304 | tf_op jit(solution)/shard_map/ppermute | solution.py:307
  66.2 2.2 %constant_dynamic-update-slice_fusion.6 = bf16[3,64,128,128]{3,2,1,0:T(8,128)(2,1)} fusion(bf16[3,64,128,128]{3,2,1,0:T(8,128)(2,1)} %constant_dynamic-update-slice_fusion.7, bf16[3,8,128,128]{3,2,1,0:T(8,128)(2,1)} %collective-permute-done, s32[]{:T(128)S(6)} %select_n.357), kind=kLoop, calls=%fused_computation.189 | loop fusion | bytes 1572868 | tf_op jit(solution)/shard_map/dynamic_update_slice | solution.py:300
  68.4 2.2 %constant_dynamic-update-slice_fusion.5 = bf16[3,64,128,128]{3,2,1,0:T(8,128)(2,1)} fusion(bf16[3,64,128,128]{3,2,1,0:T(8,128)(2,1)} %constant_dynamic-update-slice_fusion.6, bf16[3,8,128,128]{3,2,1,0:T(8,128)(2,1)} %collective-permute-done.1, s32[]{:T(128)S(6)} %select_n.360), kind=kLoop, calls=%fused_computation.188 | loop fusion | bytes 1572868 | tf_op jit(solution)/shard_map/dynamic_update_slice | solution.py:303
  70.7 2.2 %constant_dynamic-update-slice_fusion.4 = bf16[3,64,128,128]{3,2,1,0:T(8,128)(2,1)} fusion(bf16[3,64,128,128]{3,2,1,0:T(8,128)(2,1)} %constant_dynamic-update-slice_fusion.5, bf16[3,8,128,128]{3,2,1,0:T(8,128)(2,1)} %collective-permute-done.2, s32[]{:T(128)S(6)} %select_n.369), kind=kLoop, calls=%fused_computation.187 | loop fusion | bytes 1572868 | tf_op jit(solution)/shard_map/dynamic_update_slice | solution.py:300
  72.9 2.2 %constant_dynamic-update-slice_fusion.3 = bf16[3,64,128,128]{3,2,1,0:T(8,128)(2,1)} fusion(bf16[3,64,128,128]{3,2,1,0:T(8,128)(2,1)} %constant_dynamic-update-slice_fusion.4, bf16[3,8,128,128]{3,2,1,0:T(8,128)(2,1)} %collective-permute-done.3, s32[]{:T(128)S(6)} %select_n.372), kind=kLoop, calls=%fused_computation.186 | loop fusion | bytes 1572868 | tf_op jit(solution)/shard_map/dynamic_update_slice | solution.py:303
  75.1 13.4 %shard_map.111 = (bf16[3,48,64,128]{3,2,1,0:T(8,128)(2,1)}, bf16[3,48,64,128]{3,2,1,0:T(8,128)(2,1)}) custom-call(s32[1]{0:T(128)} %bitcast.me_ref, bf16[3,48,64,256]{3,2,1,0:T(8,128)(2,1)} %bitcast.84, f32[64,64,256]{2,1,0:T(8,128)} %fusion.3.v_ref, f32[64,64,256]{2,1,0:T(8,128)} %add_bitcast_fusion.w_ref, bf16[256,256]{1,0:T(8,128)(2,1)} %constant.248.clone.ft_ref), custom_call_target="tpu_custom_call" | custom-call | tf_op jit(solution)/shard_map/pallas_call | solution.py:161
  88.5 2.2 %constant_dynamic-update-slice_fusion.2 = bf16[3,64,128,128]{3,2,1,0:T(8,128)(2,1)} fusion(bf16[3,64,128,128]{3,2,1,0:T(8,128)(2,1)} %constant_dynamic-update-slice_fusion.3, bf16[3,8,128,128]{3,2,1,0:T(8,128)(2,1)} %collective-permute-done.5, s32[]{:T(128)S(6)} %select_n.383), kind=kLoop, calls=%fused_computation.183 | loop fusion | bytes 1572868 | tf_op jit(solution)/shard_map/dynamic_update_slice | solution.py:300
  90.7 2.2 %constant_dynamic-update-slice_fusion.1 = bf16[3,64,128,128]{3,2,1,0:T(8,128)(2,1)} fusion(bf16[3,64,128,128]{3,2,1,0:T(8,128)(2,1)} %constant_dynamic-update-slice_fusion.2, bf16[3,8,128,128]{3,2,1,0:T(8,128)(2,1)} %collective-permute-done.6, s32[]{:T(128)S(6)} %select_n.386), kind=kLoop, calls=%fused_computation.182 | loop fusion | bytes 1572868 | tf_op jit(solution)/shard_map/dynamic_update_slice | solution.py:303
  92.9 1.1 constant_dynamic-update-slice_fusion.refs_3_
  94.0 0.7 constant_dynamic-slice_fusion.2
  94.7 4.0 %collective-permute-done.8.refs_5_.refs_7_.refs_9_ = bf16[3,48,64,128]{3,2,1,0:T(8,128)(2,1)S(1)} collective-permute-done((bf16[3,48,64,128]{3,2,1,0:T(8,128)(2,1)}, bf16[3,48,64,128]{3,2,1,0:T(8,128)(2,1)S(1)}, u32[]{:S(2)}, u32[]{:S(2)}) %collective-permute-start.8) | collective-permute-done | bytes 2359328 | tf_op jit(solution)/shard_map/ppermute | solution.py:327
  98.7 1.4 %copy-done.1 = bf16[3,48,64,128]{3,2,1,0:T(8,128)(2,1)} copy-done((bf16[3,48,64,128]{3,2,1,0:T(8,128)(2,1)}, bf16[3,48,64,128]{3,2,1,0:T(8,128)(2,1)S(1)}, u32[]{:S(2)}) %copy-start.1) | copy-done | bytes 2359320
  100.2 3.5 %shard_map.112.y_ref = bf16[16,128,128]{2,1,0:T(8,128)(2,1)} custom-call(bf16[128,64]{1,0:T(8,128)(2,1)} %get-tuple-element.80.refs_0_.fo_ref, bf16[128,64]{1,0:T(8,128)(2,1)} %get-tuple-element.79.refs_1_.fr_ref, bf16[48,128,128]{2,1,0:T(8,128)(2,1)} %bitcast.86, bf16[3,64,128,128]{3,2,1,0:T(8,128)(2,1)} %constant_dynamic-update-slice_fusion.refs_3_, ...), custom_call_target="tpu_custom_call" | custom-call | tf_op jit(solution)/shard_map/pallas_call | solution.py:211
  103.7 2.6 %shard_map.113 = (bf16[16,64,128]{2,1,0:T(8,128)(2,1)}, bf16[16,64,128]{2,1,0:T(8,128)(2,1)}) custom-call(s32[1]{0:T(128)} %bitcast.me_ref, bf16[16,128,128]{2,1,0:T(8,128)(2,1)} %shard_map.112.y_ref, f32[64,128,128]{2,1,0:T(8,128)} %add_bitcast_fusion.1.w_ref, bf16[128,128]{1,0:T(8,128)(2,1)} %constant.247.clone.ft_ref), custom_call_target="tpu_custom_call" | custom-call | tf_op jit(solution)/shard_map/pallas_call | solution.py:101
  106.5 1.6 %collective-permute-done.9.recv_ref = bf16[16,64,128]{2,1,0:T(8,128)(2,1)S(1)} collective-permute-done((bf16[16,64,128]{2,1,0:T(8,128)(2,1)}, bf16[16,64,128]{2,1,0:T(8,128)(2,1)S(1)}, u32[]{:S(2)}, u32[]{:S(2)}) %collective-permute-start.9) | collective-permute-done | bytes 262176 | tf_op jit(solution)/shard_map/ppermute | solution.py:327
  108.1 0.7 copy-done.6
  108.8 2.5 %shard_map.114 = bf16[16,64,256]{2,1,0:T(8,128)(2,1)} custom-call(bf16[16,64,128]{2,1,0:T(8,128)(2,1)} %get-tuple-element.63.own_ref, bf16[16,64,128]{2,1,0:T(8,128)(2,1)} %copy-done.6, f32[64,64,256]{2,1,0:T(8,128)} %fusion.3.v_ref, bf16[128,256]{1,0:T(8,128)(2,1)} %get-tuple-element.76.fo_ref, bf16[128,256]{1,0:T(8,128)(2,1)} %get-tuple-element.75.fr_ref), custom_call_target="tpu_custom_call" | custom-call | tf_op jit(solution)/shard_map/pallas_call | solution.py:131
  111.3 1.7 %fusion.7 = bf16[64,256,48]{1,2,0:T(8,128)(2,1)S(1)} fusion(bf16[16,64,256]{2,1,0:T(8,128)(2,1)} %shard_map.114, bf16[48,16]{0,1:T(8,128)(2,1)S(1)} %copy-done.10), kind=kOutput, calls=%fused_computation.13 | convolution fusion | flops 25165824 | bytes 2098688 | tf_op jit(solution)/shard_map/dot_general | solution.py:376
  112.9 1.7 %copy.34 = bf16[64,256,48]{1,0,2:T(8,128)(2,1)} copy(bf16[64,256,48]{1,2,0:T(8,128)(2,1)S(1)} %fusion.7) | data formatting | bytes 3145728 | tf_op jit(solution)/shard_map/dot_general | solution.py:376
  114.6 5.7 %shard_map.115 = (bf16[1,48,64,128]{3,2,1,0:T(8,128)(2,1)}, bf16[1,48,64,128]{3,2,1,0:T(8,128)(2,1)}) custom-call(s32[1]{0:T(128)} %bitcast.me_ref, bf16[1,48,64,256]{3,2,1,0:T(8,128)(2,1)} %bitcast.89, f32[64,64,256]{2,1,0:T(8,128)} %fusion.3.v_ref, f32[64,64,256]{2,1,0:T(8,128)} %add_bitcast_fusion.w_ref, bf16[256,256]{1,0:T(8,128)(2,1)} %constant.248.clone.ft_ref), custom_call_target="tpu_custom_call" | custom-call | tf_op jit(solution)/shard_map/pallas_call | solution.py:161
  120.5 6.9 %shard_map.116.prod_ref = bf16[48,128,128]{2,1,0:T(8,128)(2,1)} custom-call(bf16[128,64]{1,0:T(8,128)(2,1)} %get-tuple-element.80.refs_0_.fo_ref, bf16[128,64]{1,0:T(8,128)(2,1)} %get-tuple-element.79.refs_1_.fr_ref, bf16[48,128,128]{2,1,0:T(8,128)(2,1)} %bitcast.87, bf16[3,64,128,128]{3,2,1,0:T(8,128)(2,1)} %constant_dynamic-update-slice_fusion.refs_3_, ...), custom_call_target="tpu_custom_call" | custom-call | tf_op jit(solution)/shard_map/pallas_call | solution.py:211
  127.3 0.9 broadcast_in_dim.10.s_ref
  128.2 4.4 %shard_map.117 = bf16[48,128,128]{2,1,0:T(8,128)(2,1)} custom-call(bf16[128,64]{1,0:T(8,128)(2,1)} %get-tuple-element.80.refs_0_.fo_ref, bf16[128,64]{1,0:T(8,128)(2,1)} %get-tuple-element.79.refs_1_.fr_ref, bf16[48,64,128]{2,1,0:T(8,128)(2,1)} %bitcast.100, bf16[48,64,128]{2,1,0:T(8,128)(2,1)} %bitcast.101, bf16[48,128,128]{2,1,0:T(8,128)(2,1)} %shard_map.116.prod_ref, ...), custom_call_target="tpu_custom_call" | custom-call | tf_op jit(solution)/shard_map/pallas_call | solution.py:242
  (56 shorter events, 2.8 us)
Async XLA Ops:
  0.0 59.1 %copy-start = (bf16[3,48,16]{1,2,0:T(8,128)(2,1)S(1)}, bf16[3,48,16]{1,2,0:T(8,128)(2,1)}, u32[]{:S(2)}) copy-start(bf16[3,48,16]{1,2,0:T(8,128)(2,1)} %param.13) | copy-start | bytes 13828
  0.0 20.8 %collective-permute-start = (bf16[3,8,128,128]{3,2,1,0:T(8,128)(2,1)}, bf16[3,8,128,128]{3,2,1,0:T(8,128)(2,1)}, u32[]{:S(2)}, u32[]{:S(2)}) collective-permute-start(bf16[3,8,128,128]{3,2,1,0:T(8,128)(2,1)} %bitcast.102), channel_id=1, source_target_pairs={{0,4},{4,8},{8,12},{12,14},{14,10},{10,6},{6,2},{2,0},{1,5},{5,9},... | collective-permute-start | bytes 2359304 | tf_op jit(solution)/shard_map/ppermute | solution.py:298
  3.0 19.3 %collective-permute-start.1 = (bf16[3,8,128,128]{3,2,1,0:T(8,128)(2,1)}, bf16[3,8,128,128]{3,2,1,0:T(8,128)(2,1)}, u32[]{:S(2)}, u32[]{:S(2)}) collective-permute-start(bf16[3,8,128,128]{3,2,1,0:T(8,128)(2,1)} %bitcast.103), channel_id=1, source_target_pairs={{0,2},{4,0},{8,4},{12,8},{14,12},{10,14},{6,10},{2,6},{1,3},{5,1},... | collective-permute-start | bytes 2359304 | tf_op jit(solution)/shard_map/ppermute | solution.py:299
  7.4 17.9 %copy-start.7 = (bf16[256,256]{1,0:T(8,128)(2,1)S(1)}, bf16[256,256]{1,0:T(8,128)(2,1)}, u32[]{:S(2)}) copy-start(bf16[256,256]{1,0:T(8,128)(2,1)} %constant.245.clone) | copy-start | bytes 393220
  12.3 22.0 %collective-permute-start.4 = (bf16[48,64,128]{2,1,0:T(8,128)(2,1)}, bf16[48,64,128]{2,1,0:T(8,128)(2,1)S(1)}, u32[]{:S(2)}, u32[]{:S(2)}) collective-permute-start(bf16[48,64,128]{2,1,0:T(8,128)(2,1)} %get-tuple-element.44), channel_id=1, source_target_pairs={{0,1},{1,0},{2,3},{3,2},{4,5},{5,4},{6,7},{7,6},{8,9},{9,8},{10,11... | collective-permute-start | bytes 2359304 | tf_op jit(solution)/shard_map/ppermute | solution.py:327
  22.3 18.4 %collective-permute-start.2 = (bf16[3,8,128,128]{3,2,1,0:T(8,128)(2,1)}, bf16[3,8,128,128]{3,2,1,0:T(8,128)(2,1)}, u32[]{:S(2)}, u32[]{:S(2)}) collective-permute-start(bf16[3,8,128,128]{3,2,1,0:T(8,128)(2,1)} %collective-permute-done), channel_id=1, source_target_pairs={{0,4},{4,8},{8,12},{12,14},{14,10},{10,6},{6,2},{2,0},{1,5},{5,9},... | collective-permute-start | bytes 2359304 | tf_op jit(solution)/shard_map/ppermute | solution.py:298
  23.9 18.1 %collective-permute-start.3 = (bf16[3,8,128,128]{3,2,1,0:T(8,128)(2,1)}, bf16[3,8,128,128]{3,2,1,0:T(8,128)(2,1)}, u32[]{:S(2)}, u32[]{:S(2)}) collective-permute-start(bf16[3,8,128,128]{3,2,1,0:T(8,128)(2,1)} %collective-permute-done.1), channel_id=1, source_target_pairs={{0,2},{4,0},{8,4},{12,8},{14,12},{10,14},{6,10},{2,6},{1,3},{5,1},... | collective-permute-start | bytes 2359304 | tf_op jit(solution)/shard_map/ppermute | solution.py:299
  25.3 4.9 %copy-start.5 = (bf16[1,3,8,128,128]{4,3,2,1,0:T(8,128)(2,1)S(1)}, bf16[1,3,8,128,128]{4,3,2,1,0:T(8,128)(2,1)}, u32[]{:S(2)}) copy-start(bf16[1,3,8,128,128]{4,3,2,1,0:T(8,128)(2,1)} %param.12) | copy-start | bytes 2359300
  34.3 0.9 copy-start.3
  35.2 9.9 %copy-start.12 = (s32[8]{0:T(128)S(1)}, s32[8]{0:T(128)}, u32[]{:S(2)}) copy-start(s32[8]{0:T(128)} %constant.244.clone) | copy-start | bytes 100
  35.2 14.6 %copy-start.9 = (s32[8]{0:T(128)S(1)}, s32[8]{0:T(128)}, u32[]{:S(2)}) copy-start(s32[8]{0:T(128)} %constant.243.clone) | copy-start | bytes 100
  39.8 19.3 %copy-start.2 = (bf16[48,64,256]{2,1,0:T(8,128)(2,1)S(1)}, bf16[48,64,256]{2,1,0:T(8,128)(2,1)}, u32[]{:S(2)}) copy-start(bf16[48,64,256]{2,1,0:T(8,128)(2,1)} %shard_map.110) | copy-start | bytes 4718596
  42.0 22.6 %collective-permute-start.5 = (bf16[3,8,128,128]{3,2,1,0:T(8,128)(2,1)}, bf16[3,8,128,128]{3,2,1,0:T(8,128)(2,1)}, u32[]{:S(2)}, u32[]{:S(2)}) collective-permute-start(bf16[3,8,128,128]{3,2,1,0:T(8,128)(2,1)} %collective-permute-done.2), channel_id=1, source_target_pairs={{0,4},{4,8},{8,12},{12,14},{14,10},{10,6},{6,2},{2,0},{1,5},{5,9},... | collective-permute-start | bytes 2359304 | tf_op jit(solution)/shard_map/ppermute | solution.py:298
  43.6 21.0 %collective-permute-start.6 = (bf16[3,8,128,128]{3,2,1,0:T(8,128)(2,1)}, bf16[3,8,128,128]{3,2,1,0:T(8,128)(2,1)}, u32[]{:S(2)}, u32[]{:S(2)}) collective-permute-start(bf16[3,8,128,128]{3,2,1,0:T(8,128)(2,1)} %collective-permute-done.3), channel_id=1, source_target_pairs={{0,2},{4,0},{8,4},{12,8},{14,12},{10,14},{6,10},{2,6},{1,3},{5,1},... | collective-permute-start | bytes 2359304 | tf_op jit(solution)/shard_map/ppermute | solution.py:299
  64.6 28.3 %collective-permute-start.7 = (bf16[3,8,128,128]{3,2,1,0:T(8,128)(2,1)}, bf16[3,8,128,128]{3,2,1,0:T(8,128)(2,1)S(1)}, u32[]{:S(2)}, u32[]{:S(2)}) collective-permute-start(bf16[3,8,128,128]{3,2,1,0:T(8,128)(2,1)} %collective-permute-done.5), channel_id=1, source_target_pairs={{0,4},{4,8},{8,12},{12,14},{14,10},{10,6},{6,2},{2,0},{1,5},{5,9},... | collective-permute-start | bytes 2359304 | tf_op jit(solution)/shard_map/ppermute | solution.py:307
  88.5 5.5 %copy-start.8 = (bf16[128,128]{1,0:T(8,128)(2,1)S(1)}, bf16[128,128]{1,0:T(8,128)(2,1)}, u32[]{:S(2)}) copy-start(bf16[128,128]{1,0:T(8,128)(2,1)} %constant.246.clone) | copy-start | bytes 98308
  94.0 4.7 %collective-permute-start.8 = (bf16[3,48,64,128]{3,2,1,0:T(8,128)(2,1)}, bf16[3,48,64,128]{3,2,1,0:T(8,128)(2,1)S(1)}, u32[]{:S(2)}, u32[]{:S(2)}) collective-permute-start(bf16[3,48,64,128]{3,2,1,0:T(8,128)(2,1)} %get-tuple-element.62), channel_id=1, source_target_pairs={{0,1},{1,0},{2,3},{3,2},{4,5},{5,4},{6,7},{7,6},{8,9},{9,8},{10,11... | collective-permute-start | bytes 7077896 | tf_op jit(solution)/shard_map/ppermute | solution.py:327
  98.7 1.4 %copy-start.1 = (bf16[3,48,64,128]{3,2,1,0:T(8,128)(2,1)}, bf16[3,48,64,128]{3,2,1,0:T(8,128)(2,1)S(1)}, u32[]{:S(2)}) copy-start(bf16[3,48,64,128]{3,2,1,0:T(8,128)(2,1)S(1)} %collective-permute-done.8.refs_5_.refs_7_.refs_9_) | copy-start | bytes 7077892
  103.7 7.6 %copy-start.10 = (bf16[48,16]{0,1:T(8,128)(2,1)S(1)}, bf16[48,16]{0,1:T(8,128)(2,1)}, u32[]{:S(2)}) copy-start(bf16[48,16]{0,1:T(8,128)(2,1)} %param.14) | copy-start | bytes 4612
  106.3 1.7 %collective-permute-start.9 = (bf16[16,64,128]{2,1,0:T(8,128)(2,1)}, bf16[16,64,128]{2,1,0:T(8,128)(2,1)S(1)}, u32[]{:S(2)}, u32[]{:S(2)}) collective-permute-start(bf16[16,64,128]{2,1,0:T(8,128)(2,1)} %get-tuple-element.64), channel_id=1, source_target_pairs={{0,1},{1,0},{2,3},{3,2},{4,5},{5,4},{6,7},{7,6},{8,9},{9,8},{10,11... | collective-permute-start | bytes 786440 | tf_op jit(solution)/shard_map/ppermute | solution.py:327
  108.1 0.7 copy-start.6
  120.3 7.0 %copy-start.11 = (f32[48]{0:T(128)S(1)}, f32[48]{0:T(128)}, u32[]{:S(2)}) copy-start(f32[48]{0:T(128)} %param.15) | copy-start | bytes 580
  120.3 7.0 %collective-permute-start.10 = (bf16[1,48,64,128]{3,2,1,0:T(8,128)(2,1)}, bf16[1,48,64,128]{3,2,1,0:T(8,128)(2,1)S(1)}, u32[]{:S(2)}, u32[]{:S(2)}) collective-permute-start(bf16[1,48,64,128]{3,2,1,0:T(8,128)(2,1)} %get-tuple-element.66), channel_id=1, source_target_pairs={{0,1},{1,0},{2,3},{3,2},{4,5},{5,4},{6,7},{7,6},{8,9},{9,8},{10,11... | collective-permute-start | bytes 2359304 | tf_op jit(solution)/shard_map/ppermute | solution.py:327
  127.3 0.9 copy-start.4

commit v12 on v11

--- a/solution.py
+++ b/solution.py
@@ -304,9 +304,13 @@
             st["full"], st["b"], order[(p + s) % n] * width, axis=1
         )
     else:
-        a = lax.ppermute(st["a"], "limb", st["cw"])
+        h = st["a"].shape[2] // 2
+        a = lax.ppermute(st["a"][:, :, :h], "limb", st["cw"])
+        b = lax.ppermute(st["b"][:, :, h:], "limb", st["ccw"])
         src = order[(p + s) % n] * width
-        st["full"] = lax.dynamic_update_slice_in_dim(st["full"], a, src, axis=1)
+        st["full"] = lax.dynamic_update_slice_in_dim(
+            st["full"], jnp.concatenate([a, b], axis=2), src, axis=1
+        )
 
 
 def ring_hold(st, x):

time: 134 us -> 124 us (0.925)
  local copies, waits for them, and re-layouts: 33.6 us -> 28 us
  waiting for transfers between devices: 14.9 us -> 11.9 us
    ppermute x3, waiting for transfers between devices: 6.4 us -> 3.39 us  [ring_step(): st['a'] = lax.ppermute(st['a'], 'limb', st['cw'])]
    add x3, other arithmetic: 10.5 us -> 8.96 us  [_twiddle(): return 1.0 + 0.5 * (cp * cq - sp * sq)]
    mul x4, local copies, waits for them, and re-layouts: 1.52 us -> 0.16 us  [_twiddle(): return 1.0 + 0.5 * (cp * cq - sp * sq)]
    unnamed x26 -> x24, local copies, waits for them, and re-layouts: 3.08 us -> 2.2 us
  transfers between devices with their start and end apart: 11 -> 12, of which waited for: 6 -> 6; matrix products, arithmetic and copies ran while one was open for 33% -> 30% of each run, Pallas kernels for 22% -> 24%
where the time goes in v12:
time: 124 us; the launch traced here: 123 us
  Pallas kernels  48.4 us (39%)
  local copies, waits for them, and re-layouts  28 us (23%)
  other arithmetic  13.6 us (11%)
  waiting for transfers between devices  11.9 us (10%)
  starting transfers between devices  9.52 us (8%)
  between operations  8.63 us (7%)
  matrix products  3.18 us (3%)
    pallas_call x2, Pallas kernels, fwd_col(): pl.pallas_call(_fwd_col_kernel, grid=(groups, n // BLK), in_specs=[SMEM_S...  19.1 us
    pallas_call x2, Pallas kernels, product(): pl.pallas_call(lambda *refs: _product_kernel(eb0, *refs), grid=(nblocks,)...  10.4 us
    add x3, other arithmetic, _twiddle(): return 1.0 + 0.5 * (cp * cq - sp * sq)  8.96 us
    pallas_call x2, Pallas kernels, inv_row(): pl.pallas_call(_inv_row_kernel, grid=(n // BLK,), in_specs=[SMEM_SPEC, bl...  7.41 us
    pallas_call x2, Pallas kernels, inv_col(): pl.pallas_call(_inv_col_kernel, grid=(n // BLK,), in_specs=[blk, blk, pl....  7.17 us
    ppermute x3, starting transfers between devices, ring_step(): st['a'] = lax.ppermute(st['a'], 'limb', st['cw'])  6.18 us
    ppermute x4, waiting for transfers between devices, swap(): return lax.ppermute(x, 'coef', perm=[(0, 1), (1, 0)])  5.64 us
    dynamic_update_slice x3, local copies, waits for them, and re-layouts, ring_step(): lax.dynamic_update_slice_in_dim(st['full'], st['a'], order[(p - s) % n] *...  5.47 us
  transfers between devices with their start and end apart: 12, of which 6 were waited for; matrix products, arithmetic and copies ran while one was open for 30% of the time, Pallas kernels for 24%

profile of v12, /device:TPU:0, one launch (start us, length us, event | category | flops | bytes accessed | tf_op | source)
XLA Modules:
  0.0 123.3 jit_solution(8868422787560469575)
XLA Ops:
  0.0 3.0 %collective-permute-start = (bf16[3,8,128,128]{3,2,1,0:T(8,128)(2,1)}, bf16[3,8,128,128]{3,2,1,0:T(8,128)(2,1)}, u32[]{:S(2)}, u32[]{:S(2)}) collective-permute-start(bf16[3,8,128,128]{3,2,1,0:T(8,128)(2,1)} %bitcast.102), channel_id=1, source_target_pairs={{0,4},{4,8},{8,12},{12,14},{14,10},{10,6},{6,2},{2,0},{1,5},{5,9},... | collective-permute-start | bytes 2359304 | tf_op jit(solution)/shard_map/ppermute | solution.py:298
  3.1 0.6 fusion.54
  3.7 0.3 fusion.58
  4.3 2.9 %add_bitcast_fusion.1.w_ref = f32[64,128,128]{2,1,0:T(8,128)} fusion(f32[64,8,128]{2,1,0:T(8,128)S(1)} %bitcast.98, f32[64,16,128]{2,1,0:T(8,128)S(1)} %bitcast.96, f32[64,8,128]{2,1,0:T(8,128)S(1)} %bitcast.99, f32[64,16,128]{2,1,0:T(8,128)S(1)} %bitcast.97), kind=kLoop, calls=%fused_computation.8 | loop fusion | flops 5242880 | bytes 5767168 | tf_op jit(solution)/shard_map/add | solution.py:53
  7.2 4.8 %shard_map.109 = (bf16[48,64,128]{2,1,0:T(8,128)(2,1)}, bf16[48,64,128]{2,1,0:T(8,128)(2,1)}) custom-call(s32[1]{0:T(128)} %bitcast.me_ref, bf16[48,128,128]{2,1,0:T(8,128)(2,1)} %bitcast.85, f32[64,128,128]{2,1,0:T(8,128)} %add_bitcast_fusion.1.w_ref, bf16[128,128]{1,0:T(8,128)(2,1)} %constant.247.clone.ft_ref), custom_call_target="tpu_custom_call" | custom-call | tf_op jit(solution)/shard_map/pallas_call | solution.py:101
  12.6 1.6 %fusion.50 = (f32[8,8,256]{2,1,0:T(8,128)S(1)}, f32[8,8,256]{2,1,0:T(8,128)S(1)}, f32[8,8,256]{2,1,0:T(8,128)S(1)}, f32[8,8,256]{2,1,0:T(8,128)S(1)}, f32[8,8,25...) fusion(s32[8,256]{1,0:T(8,128)S(1)} %add_select_fusion.12, ...), kind=kLoop, calls=%fused_computation.119 | loop fusion | flops 1376256 | bytes 811072 | tf_op jit(solution)/shard_map/cos | solution.py:35
  14.7 4.2 %broadcast_in_dim.8 = bf16[3,64,128,128]{3,2,1,0:T(8,128)(2,1)} broadcast(bf16[]{:T(256)} %constant.223.clone.1), dimensions={} | broadcast | bytes 6291458 | tf_op jit(solution)/shard_map/broadcast_in_dim | solution.py:273
  18.9 1.0 constant_dynamic-update-slice_fusion.6
  20.0 0.8 collective-permute-done
  20.8 1.5 %collective-permute-done.1 = bf16[3,8,128,128]{3,2,1,0:T(8,128)(2,1)} collective-permute-done((bf16[3,8,128,128]{3,2,1,0:T(8,128)(2,1)}, bf16[3,8,128,128]{3,2,1,0:T(8,128)(2,1)}, u32[]{:S(2)}, u32[]{:S(2)}) %collective-permute-start.1) | collective-permute-done | bytes 786464 | tf_op jit(solution)/shard_map/ppermute | solution.py:299
  22.3 1.6 %collective-permute-start.2 = (bf16[3,8,128,128]{3,2,1,0:T(8,128)(2,1)}, bf16[3,8,128,128]{3,2,1,0:T(8,128)(2,1)}, u32[]{:S(2)}, u32[]{:S(2)}) collective-permute-start(bf16[3,8,128,128]{3,2,1,0:T(8,128)(2,1)} %collective-permute-done), channel_id=1, source_target_pairs={{0,4},{4,8},{8,12},{12,14},{14,10},{10,6},{6,2},{2,0},{1,5},{5,9},... | collective-permute-start | bytes 2359304 | tf_op jit(solution)/shard_map/ppermute | solution.py:298
  23.9 0.4 collective-permute-start.3
  24.4 0.7 constant_dynamic-slice_fusion
  25.0 0.6 dynamic_slice.38
  27.5 3.0 %fusion.3.v_ref = f32[64,64,256]{2,1,0:T(8,128)} fusion(f32[64,64]{1,0:T(8,128)S(1)} %copy.17, f32[64,8,256]{2,1,0:T(8,128)S(1)} %bitcast.94, f32[64,64]{1,0:T(8,128)S(1)} %copy.16, f32[64,8,256]{2,1,0:T(8,128)S(1)} %bitcast.95), kind=kLoop, calls=%fused_computation.5 | loop fusion | flops 5242880 | bytes 5275648 | tf_op jit(solution)/shard_map/add | solution.py:53
  30.5 3.0 %add_bitcast_fusion.w_ref = f32[64,64,256]{2,1,0:T(8,128)} fusion(f32[64,8,256]{2,1,0:T(8,128)S(1)} %bitcast.92, f32[64,8,256]{2,1,0:T(8,128)S(1)} %bitcast.90, f32[64,8,256]{2,1,0:T(8,128)S(1)} %bitcast.93, f32[64,8,256]{2,1,0:T(8,128)S(1)} %bitcast.91), kind=kLoop, calls=%fused_computation.7 | loop fusion | flops 5242880 | bytes 6291456 | tf_op jit(solution)/shard_map/add | solution.py:53
  33.6 4.6 %shard_map.110 = bf16[48,64,256]{2,1,0:T(8,128)(2,1)} custom-call(bf16[48,64,128]{2,1,0:T(8,128)(2,1)} %get-tuple-element.44.own_ref, bf16[48,64,128]{2,1,0:T(8,128)(2,1)} %collective-permute-done.4.recv_ref, f32[64,64,256]{2,1,0:T(8,128)} %fusion.3.v_ref, bf16[128,256]{1,0:T(8,128)(2,1)} %get-tuple-element.78.fo_ref, bf16[128,256]{1,0:T(8,128)(2,1)} %get-tuple-element.77.fr_ref), custom_call_target="tpu_custom_call" | custom-call | tf_op jit(solution)/shard_map/pallas_call | solution.py:131
  38.2 2.5 %collective-permute-done.2 = bf16[3,8,128,128]{3,2,1,0:T(8,128)(2,1)} collective-permute-done((bf16[3,8,128,128]{3,2,1,0:T(8,128)(2,1)}, bf16[3,8,128,128]{3,2,1,0:T(8,128)(2,1)}, u32[]{:S(2)}, u32[]{:S(2)}) %collective-permute-start.2) | collective-permute-done | bytes 786464 | tf_op jit(solution)/shard_map/ppermute | solution.py:298
  40.8 1.3 %collective-permute-done.3 = bf16[3,8,128,128]{3,2,1,0:T(8,128)(2,1)} collective-permute-done((bf16[3,8,128,128]{3,2,1,0:T(8,128)(2,1)}, bf16[3,8,128,128]{3,2,1,0:T(8,128)(2,1)}, u32[]{:S(2)}, u32[]{:S(2)}) %collective-permute-start.3) | collective-permute-done | bytes 786464 | tf_op jit(solution)/shard_map/ppermute | solution.py:299
  42.0 1.6 %collective-permute-start.5 = (bf16[3,8,128,128]{3,2,1,0:T(8,128)(2,1)}, bf16[3,8,128,128]{3,2,1,0:T(8,128)(2,1)S(1)}, u32[]{:S(2)}, u32[]{:S(2)}) collective-permute-start(bf16[3,8,128,128]{3,2,1,0:T(8,128)(2,1)} %collective-permute-done.2), channel_id=1, source_target_pairs={{0,4},{4,8},{8,12},{12,14},{14,10},{10,6},{6,2},{2,0},{1,5},{5,9},... | collective-permute-start | bytes 2359304 | tf_op jit(solution)/shard_map/ppermute | solution.py:298
  43.6 0.5 collective-permute-start.6
  46.5 0.7 fusion.89
  51.4 2.2 %constant_dynamic-update-slice_fusion.5 = bf16[3,64,128,128]{3,2,1,0:T(8,128)(2,1)} fusion(bf16[3,64,128,128]{3,2,1,0:T(8,128)(2,1)} %constant_dynamic-update-slice_fusion.6, bf16[3,8,128,128]{3,2,1,0:T(8,128)(2,1)} %collective-permute-done, s32[]{:T(128)S(6)} %select_n.357), kind=kLoop, calls=%fused_computation.189 | loop fusion | bytes 1572868 | tf_op jit(solution)/shard_map/dynamic_update_slice | solution.py:300
  53.7 2.2 %constant_dynamic-update-slice_fusion.4 = bf16[3,64,128,128]{3,2,1,0:T(8,128)(2,1)} fusion(bf16[3,64,128,128]{3,2,1,0:T(8,128)(2,1)} %constant_dynamic-update-slice_fusion.5, bf16[3,8,128,128]{3,2,1,0:T(8,128)(2,1)} %collective-permute-done.1, s32[]{:T(128)S(6)} %select_n.360), kind=kLoop, calls=%fused_computation.188 | loop fusion | bytes 1572868 | tf_op jit(solution)/shard_map/dynamic_update_slice | solution.py:303
  55.9 1.5 %fusion.5 = bf16[3,64,256,48]{2,3,1,0:T(8,128)(2,1)S(1)} fusion(bf16[3,16,64,256]{3,2,1,0:T(8,128)(2,1)S(1)} %bitcast.88, bf16[3,48,16]{1,2,0:T(8,128)(2,1)S(1)} %copy-done), kind=kOutput, calls=%fused_computation.11 | convolution fusion | flops 75497472 | bytes 6296064 | tf_op jit(solution)/shard_map/dot_general | solution.py:364
  57.4 4.1 %copy.33 = bf16[3,64,256,48]{2,1,3,0:T(8,128)(2,1)} copy(bf16[3,64,256,48]{2,3,1,0:T(8,128)(2,1)S(1)} %fusion.5) | data formatting | bytes 9437184 | tf_op jit(solution)/shard_map/dot_general | solution.py:364
  61.5 2.2 %constant_dynamic-update-slice_fusion.3 = bf16[3,64,128,128]{3,2,1,0:T(8,128)(2,1)} fusion(bf16[3,64,128,128]{3,2,1,0:T(8,128)(2,1)} %constant_dynamic-update-slice_fusion.4, bf16[3,8,128,128]{3,2,1,0:T(8,128)(2,1)} %collective-permute-done.2, s32[]{:T(128)S(6)} %select_n.369), kind=kLoop, calls=%fused_computation.187 | loop fusion | bytes 1572868 | tf_op jit(solution)/shard_map/dynamic_update_slice | solution.py:300
  63.8 0.5 collective-permute-start.8
  64.3 1.7 %collective-permute-start.7 = (bf16[3,8,64,128]{3,2,1,0:T(8,128)(2,1)S(1)}, bf16[3,8,64,128]{3,2,1,0:T(8,128)(2,1)S(1)}, u32[]{:S(2)}, u32[]{:S(2)}) collective-permute-start(bf16[3,8,64,128]{3,2,1,0:T(8,128)(2,1)S(1)} %slice.6), channel_id=1, source_target_pairs={{0,4},{4,8},{8,12},{12,14},{14,10},{10,6},{6,2},{2,0},{1,5},{5,9},... | collective-permute-start | bytes 1179656 | tf_op jit(solution)/shard_map/ppermute | solution.py:308
  65.9 2.2 %constant_dynamic-update-slice_fusion.2 = bf16[3,64,128,128]{3,2,1,0:T(8,128)(2,1)} fusion(bf16[3,64,128,128]{3,2,1,0:T(8,128)(2,1)} %constant_dynamic-update-slice_fusion.3, bf16[3,8,128,128]{3,2,1,0:T(8,128)(2,1)} %collective-permute-done.3, s32[]{:T(128)S(6)} %select_n.372), kind=kLoop, calls=%fused_computation.186 | loop fusion | bytes 1572868 | tf_op jit(solution)/shard_map/dynamic_update_slice | solution.py:303
  68.2 13.4 %shard_map.111 = (bf16[3,48,64,128]{3,2,1,0:T(8,128)(2,1)}, bf16[3,48,64,128]{3,2,1,0:T(8,128)(2,1)}) custom-call(s32[1]{0:T(128)} %bitcast.me_ref, bf16[3,48,64,256]{3,2,1,0:T(8,128)(2,1)} %bitcast.84, f32[64,64,256]{2,1,0:T(8,128)} %fusion.3.v_ref, f32[64,64,256]{2,1,0:T(8,128)} %add_bitcast_fusion.w_ref, bf16[256,256]{1,0:T(8,128)(2,1)} %constant.248.clone.ft_ref), custom_call_target="tpu_custom_call" | custom-call | tf_op jit(solution)/shard_map/pallas_call | solution.py:161
  81.5 1.0 constant_dynamic-update-slice_fusion.1
  82.5 1.0 constant_dynamic-update-slice_fusion
  83.5 1.0 maximum_dynamic-update-slice_fusion.refs_3_
  84.6 0.7 constant_dynamic-slice_fusion.2
  85.3 4.0 %collective-permute-done.9.refs_5_.refs_7_.refs_9_ = bf16[3,48,64,128]{3,2,1,0:T(8,128)(2,1)S(1)} collective-permute-done((bf16[3,48,64,128]{3,2,1,0:T(8,128)(2,1)}, bf16[3,48,64,128]{3,2,1,0:T(8,128)(2,1)S(1)}, u32[]{:S(2)}, u32[]{:S(2)}) %collective-permute-start.9) | collective-permute-done | bytes 2359328 | tf_op jit(solution)/shard_map/ppermute | solution.py:331
  89.3 1.4 %copy-done.1 = bf16[3,48,64,128]{3,2,1,0:T(8,128)(2,1)} copy-done((bf16[3,48,64,128]{3,2,1,0:T(8,128)(2,1)}, bf16[3,48,64,128]{3,2,1,0:T(8,128)(2,1)S(1)}, u32[]{:S(2)}) %copy-start.1) | copy-done | bytes 2359320
  90.8 3.5 %shard_map.112.y_ref = bf16[16,128,128]{2,1,0:T(8,128)(2,1)} custom-call(bf16[128,64]{1,0:T(8,128)(2,1)} %get-tuple-element.82.refs_0_.fo_ref, bf16[128,64]{1,0:T(8,128)(2,1)} %get-tuple-element.81.refs_1_.fr_ref, bf16[48,128,128]{2,1,0:T(8,128)(2,1)} %bitcast.86, bf16[3,64,128,128]{3,2,1,0:T(8,128)(2,1)} %maximum_dynamic-update-slice_fusion.refs_3_, ...), custom_call_target="tpu_custom_call" | custom-call | tf_op jit(solution)/shard_map/pallas_call | solution.py:211
  94.3 2.6 %shard_map.113 = (bf16[16,64,128]{2,1,0:T(8,128)(2,1)}, bf16[16,64,128]{2,1,0:T(8,128)(2,1)}) custom-call(s32[1]{0:T(128)} %bitcast.me_ref, bf16[16,128,128]{2,1,0:T(8,128)(2,1)} %shard_map.112.y_ref, f32[64,128,128]{2,1,0:T(8,128)} %add_bitcast_fusion.1.w_ref, bf16[128,128]{1,0:T(8,128)(2,1)} %constant.247.clone.ft_ref), custom_call_target="tpu_custom_call" | custom-call | tf_op jit(solution)/shard_map/pallas_call | solution.py:101
  97.0 1.6 %collective-permute-done.10.recv_ref = bf16[16,64,128]{2,1,0:T(8,128)(2,1)S(1)} collective-permute-done((bf16[16,64,128]{2,1,0:T(8,128)(2,1)}, bf16[16,64,128]{2,1,0:T(8,128)(2,1)S(1)}, u32[]{:S(2)}, u32[]{:S(2)}) %collective-permute-start.10) | collective-permute-done | bytes 262176 | tf_op jit(solution)/shard_map/ppermute | solution.py:331
  98.6 0.7 copy-done.5
  99.3 2.5 %shard_map.114 = bf16[16,64,256]{2,1,0:T(8,128)(2,1)} custom-call(bf16[16,64,128]{2,1,0:T(8,128)(2,1)} %get-tuple-element.65.own_ref, bf16[16,64,128]{2,1,0:T(8,128)(2,1)} %copy-done.5, f32[64,64,256]{2,1,0:T(8,128)} %fusion.3.v_ref, bf16[128,256]{1,0:T(8,128)(2,1)} %get-tuple-element.78.fo_ref, bf16[128,256]{1,0:T(8,128)(2,1)} %get-tuple-element.77.fr_ref), custom_call_target="tpu_custom_call" | custom-call | tf_op jit(solution)/shard_map/pallas_call | solution.py:131
  101.9 1.6 %fusion.7 = bf16[64,256,48]{1,2,0:T(8,128)(2,1)S(1)} fusion(bf16[16,64,256]{2,1,0:T(8,128)(2,1)} %shard_map.114, bf16[48,16]{0,1:T(8,128)(2,1)S(1)} %copy-done.9), kind=kOutput, calls=%fused_computation.14 | convolution fusion | flops 25165824 | bytes 2098688 | tf_op jit(solution)/shard_map/dot_general | solution.py:380
  103.5 1.7 %copy.34 = bf16[64,256,48]{1,0,2:T(8,128)(2,1)} copy(bf16[64,256,48]{1,2,0:T(8,128)(2,1)S(1)} %fusion.7) | data formatting | bytes 3145728 | tf_op jit(solution)/shard_map/dot_general | solution.py:380
  105.2 5.7 %shard_map.115 = (bf16[1,48,64,128]{3,2,1,0:T(8,128)(2,1)}, bf16[1,48,64,128]{3,2,1,0:T(8,128)(2,1)}) custom-call(s32[1]{0:T(128)} %bitcast.me_ref, bf16[1,48,64,256]{3,2,1,0:T(8,128)(2,1)} %bitcast.89, f32[64,64,256]{2,1,0:T(8,128)} %fusion.3.v_ref, f32[64,64,256]{2,1,0:T(8,128)} %add_bitcast_fusion.w_ref, bf16[256,256]{1,0:T(8,128)(2,1)} %constant.248.clone.ft_ref), custom_call_target="tpu_custom_call" | custom-call | tf_op jit(solution)/shard_map/pallas_call | solution.py:161
  111.1 6.9 %shard_map.116.prod_ref = bf16[48,128,128]{2,1,0:T(8,128)(2,1)} custom-call(bf16[128,64]{1,0:T(8,128)(2,1)} %get-tuple-element.82.refs_0_.fo_ref, bf16[128,64]{1,0:T(8,128)(2,1)} %get-tuple-element.81.refs_1_.fr_ref, bf16[48,128,128]{2,1,0:T(8,128)(2,1)} %bitcast.87, bf16[3,64,128,128]{3,2,1,0:T(8,128)(2,1)} %maximum_dynamic-update-slice_fusion.refs_3_, ...), custom_call_target="tpu_custom_call" | custom-call | tf_op jit(solution)/shard_map/pallas_call | solution.py:211
  118.0 0.9 broadcast_in_dim.10.s_ref
  118.9 4.4 %shard_map.117 = bf16[48,128,128]{2,1,0:T(8,128)(2,1)} custom-call(bf16[128,64]{1,0:T(8,128)(2,1)} %get-tuple-element.82.refs_0_.fo_ref, bf16[128,64]{1,0:T(8,128)(2,1)} %get-tuple-element.81.refs_1_.fr_ref, bf16[48,64,128]{2,1,0:T(8,128)(2,1)} %bitcast.100, bf16[48,64,128]{2,1,0:T(8,128)(2,1)} %bitcast.101, bf16[48,128,128]{2,1,0:T(8,128)(2,1)} %shard_map.116.prod_ref, ...), custom_call_target="tpu_custom_call" | custom-call | tf_op jit(solution)/shard_map/pallas_call | solution.py:242
  (58 shorter events, 1.9 us)
Async XLA Ops:
  0.0 55.9 %copy-start = (bf16[3,48,16]{1,2,0:T(8,128)(2,1)S(1)}, bf16[3,48,16]{1,2,0:T(8,128)(2,1)}, u32[]{:S(2)}) copy-start(bf16[3,48,16]{1,2,0:T(8,128)(2,1)} %param.13) | copy-start | bytes 13828
  0.0 20.8 %collective-permute-start = (bf16[3,8,128,128]{3,2,1,0:T(8,128)(2,1)}, bf16[3,8,128,128]{3,2,1,0:T(8,128)(2,1)}, u32[]{:S(2)}, u32[]{:S(2)}) collective-permute-start(bf16[3,8,128,128]{3,2,1,0:T(8,128)(2,1)} %bitcast.102), channel_id=1, source_target_pairs={{0,4},{4,8},{8,12},{12,14},{14,10},{10,6},{6,2},{2,0},{1,5},{5,9},... | collective-permute-start | bytes 2359304 | tf_op jit(solution)/shard_map/ppermute | solution.py:298
  3.0 19.3 %collective-permute-start.1 = (bf16[3,8,128,128]{3,2,1,0:T(8,128)(2,1)}, bf16[3,8,128,128]{3,2,1,0:T(8,128)(2,1)}, u32[]{:S(2)}, u32[]{:S(2)}) collective-permute-start(bf16[3,8,128,128]{3,2,1,0:T(8,128)(2,1)} %bitcast.103), channel_id=1, source_target_pairs={{0,2},{4,0},{8,4},{12,8},{14,12},{10,14},{6,10},{2,6},{1,3},{5,1},... | collective-permute-start | bytes 2359304 | tf_op jit(solution)/shard_map/ppermute | solution.py:299
  12.0 21.5 %collective-permute-start.4 = (bf16[48,64,128]{2,1,0:T(8,128)(2,1)}, bf16[48,64,128]{2,1,0:T(8,128)(2,1)}, u32[]{:S(2)}, u32[]{:S(2)}) collective-permute-start(bf16[48,64,128]{2,1,0:T(8,128)(2,1)} %get-tuple-element.45), channel_id=1, source_target_pairs={{0,1},{1,0},{2,3},{3,2},{4,5},{5,4},{6,7},{7,6},{8,9},{9,8},{10,11... | collective-permute-start | bytes 2359304 | tf_op jit(solution)/shard_map/ppermute | solution.py:331
  14.4 4.6 %copy-start.4 = (bf16[1,3,8,128,128]{4,3,2,1,0:T(8,128)(2,1)S(1)}, bf16[1,3,8,128,128]{4,3,2,1,0:T(8,128)(2,1)}, u32[]{:S(2)}) copy-start(bf16[1,3,8,128,128]{4,3,2,1,0:T(8,128)(2,1)} %param.12) | copy-start | bytes 2359300
  14.7 9.7 %copy-start.6 = (bf16[256,256]{1,0:T(8,128)(2,1)S(1)}, bf16[256,256]{1,0:T(8,128)(2,1)}, u32[]{:S(2)}) copy-start(bf16[256,256]{1,0:T(8,128)(2,1)} %constant.245.clone) | copy-start | bytes 393220
  14.7 10.3 %copy-start.11 = (s32[8]{0:T(128)S(1)}, s32[8]{0:T(128)}, u32[]{:S(2)}) copy-start(s32[8]{0:T(128)} %constant.244.clone) | copy-start | bytes 100
  22.3 18.4 %collective-permute-start.2 = (bf16[3,8,128,128]{3,2,1,0:T(8,128)(2,1)}, bf16[3,8,128,128]{3,2,1,0:T(8,128)(2,1)}, u32[]{:S(2)}, u32[]{:S(2)}) collective-permute-start(bf16[3,8,128,128]{3,2,1,0:T(8,128)(2,1)} %collective-permute-done), channel_id=1, source_target_pairs={{0,4},{4,8},{8,12},{12,14},{14,10},{10,6},{6,2},{2,0},{1,5},{5,9},... | collective-permute-start | bytes 2359304 | tf_op jit(solution)/shard_map/ppermute | solution.py:298
  23.9 18.1 %collective-permute-start.3 = (bf16[3,8,128,128]{3,2,1,0:T(8,128)(2,1)}, bf16[3,8,128,128]{3,2,1,0:T(8,128)(2,1)}, u32[]{:S(2)}, u32[]{:S(2)}) collective-permute-start(bf16[3,8,128,128]{3,2,1,0:T(8,128)(2,1)} %collective-permute-done.1), channel_id=1, source_target_pairs={{0,2},{4,0},{8,4},{12,8},{14,12},{10,14},{6,10},{2,6},{1,3},{5,1},... | collective-permute-start | bytes 2359304 | tf_op jit(solution)/shard_map/ppermute | solution.py:299
  33.6 12.9 %copy-start.8 = (s32[8]{0:T(128)S(1)}, s32[8]{0:T(128)}, u32[]{:S(2)}) copy-start(s32[8]{0:T(128)} %constant.243.clone) | copy-start | bytes 100
  38.2 17.7 %copy-start.2 = (bf16[48,64,256]{2,1,0:T(8,128)(2,1)S(1)}, bf16[48,64,256]{2,1,0:T(8,128)(2,1)}, u32[]{:S(2)}) copy-start(bf16[48,64,256]{2,1,0:T(8,128)(2,1)} %shard_map.110) | copy-start | bytes 4718596
  42.0 21.7 %collective-permute-start.5 = (bf16[3,8,128,128]{3,2,1,0:T(8,128)(2,1)}, bf16[3,8,128,128]{3,2,1,0:T(8,128)(2,1)S(1)}, u32[]{:S(2)}, u32[]{:S(2)}) collective-permute-start(bf16[3,8,128,128]{3,2,1,0:T(8,128)(2,1)} %collective-permute-done.2), channel_id=1, source_target_pairs={{0,4},{4,8},{8,12},{12,14},{14,10},{10,6},{6,2},{2,0},{1,5},{5,9},... | collective-permute-start | bytes 2359304 | tf_op jit(solution)/shard_map/ppermute | solution.py:298
  43.6 20.1 %collective-permute-start.6 = (bf16[3,8,128,128]{3,2,1,0:T(8,128)(2,1)}, bf16[3,8,128,128]{3,2,1,0:T(8,128)(2,1)S(1)}, u32[]{:S(2)}, u32[]{:S(2)}) collective-permute-start(bf16[3,8,128,128]{3,2,1,0:T(8,128)(2,1)} %collective-permute-done.3), channel_id=1, source_target_pairs={{0,2},{4,0},{8,4},{12,8},{14,12},{10,14},{6,10},{2,6},{1,3},{5,1},... | collective-permute-start | bytes 2359304 | tf_op jit(solution)/shard_map/ppermute | solution.py:299
  63.8 19.8 %collective-permute-start.8 = (bf16[3,8,64,128]{3,2,1,0:T(8,128)(2,1)S(1)}, bf16[3,8,64,128]{3,2,1,0:T(8,128)(2,1)S(1)}, u32[]{:S(2)}, u32[]{:S(2)}) collective-permute-start(bf16[3,8,64,128]{3,2,1,0:T(8,128)(2,1)S(1)} %slice.7), channel_id=1, source_target_pairs={{0,2},{4,0},{8,4},{12,8},{14,12},{10,14},{6,10},{2,6},{1,3},{5,1},... | collective-permute-start | bytes 1179656 | tf_op jit(solution)/shard_map/ppermute | solution.py:309
  64.3 19.3 %collective-permute-start.7 = (bf16[3,8,64,128]{3,2,1,0:T(8,128)(2,1)S(1)}, bf16[3,8,64,128]{3,2,1,0:T(8,128)(2,1)S(1)}, u32[]{:S(2)}, u32[]{:S(2)}) collective-permute-start(bf16[3,8,64,128]{3,2,1,0:T(8,128)(2,1)S(1)} %slice.6), channel_id=1, source_target_pairs={{0,4},{4,8},{8,12},{12,14},{14,10},{10,6},{6,2},{2,0},{1,5},{5,9},... | collective-permute-start | bytes 1179656 | tf_op jit(solution)/shard_map/ppermute | solution.py:308
  81.5 3.1 %copy-start.7 = (bf16[128,128]{1,0:T(8,128)(2,1)S(1)}, bf16[128,128]{1,0:T(8,128)(2,1)}, u32[]{:S(2)}) copy-start(bf16[128,128]{1,0:T(8,128)(2,1)} %constant.246.clone) | copy-start | bytes 98308
  84.6 4.7 %collective-permute-start.9 = (bf16[3,48,64,128]{3,2,1,0:T(8,128)(2,1)}, bf16[3,48,64,128]{3,2,1,0:T(8,128)(2,1)S(1)}, u32[]{:S(2)}, u32[]{:S(2)}) collective-permute-start(bf16[3,48,64,128]{3,2,1,0:T(8,128)(2,1)} %get-tuple-element.64), channel_id=1, source_target_pairs={{0,1},{1,0},{2,3},{3,2},{4,5},{5,4},{6,7},{7,6},{8,9},{9,8},{10,11... | collective-permute-start | bytes 7077896 | tf_op jit(solution)/shard_map/ppermute | solution.py:331
  89.3 1.4 %copy-start.1 = (bf16[3,48,64,128]{3,2,1,0:T(8,128)(2,1)}, bf16[3,48,64,128]{3,2,1,0:T(8,128)(2,1)S(1)}, u32[]{:S(2)}) copy-start(bf16[3,48,64,128]{3,2,1,0:T(8,128)(2,1)S(1)} %collective-permute-done.9.refs_5_.refs_7_.refs_9_) | copy-start | bytes 7077892
  94.3 7.6 %copy-start.9 = (bf16[48,16]{0,1:T(8,128)(2,1)S(1)}, bf16[48,16]{0,1:T(8,128)(2,1)}, u32[]{:S(2)}) copy-start(bf16[48,16]{0,1:T(8,128)(2,1)} %param.14) | copy-start | bytes 4612
  96.9 1.7 %collective-permute-start.10 = (bf16[16,64,128]{2,1,0:T(8,128)(2,1)}, bf16[16,64,128]{2,1,0:T(8,128)(2,1)S(1)}, u32[]{:S(2)}, u32[]{:S(2)}) collective-permute-start(bf16[16,64,128]{2,1,0:T(8,128)(2,1)} %get-tuple-element.66), channel_id=1, source_target_pairs={{0,1},{1,0},{2,3},{3,2},{4,5},{5,4},{6,7},{7,6},{8,9},{9,8},{10,11... | collective-permute-start | bytes 786440 | tf_op jit(solution)/shard_map/ppermute | solution.py:331
  98.6 0.7 copy-start.5
  110.9 7.0 %copy-start.10 = (f32[48]{0:T(128)S(1)}, f32[48]{0:T(128)}, u32[]{:S(2)}) copy-start(f32[48]{0:T(128)} %param.15) | copy-start | bytes 580
  110.9 7.0 %collective-permute-start.11 = (bf16[1,48,64,128]{3,2,1,0:T(8,128)(2,1)}, bf16[1,48,64,128]{3,2,1,0:T(8,128)(2,1)S(1)}, u32[]{:S(2)}, u32[]{:S(2)}) collective-permute-start(bf16[1,48,64,128]{3,2,1,0:T(8,128)(2,1)} %get-tuple-element.68), channel_id=1, source_target_pairs={{0,1},{1,0},{2,3},{3,2},{4,5},{5,4},{6,7},{7,6},{8,9},{9,8},{10,11... | collective-permute-start | bytes 2359304 | tf_op jit(solution)/shard_map/ppermute | solution.py:331
  117.9 0.9 copy-start.3

commit v13 on v12

--- a/solution.py
+++ b/solution.py
@@ -165,6 +165,41 @@
         out_specs=[os, os],
         out_shape=[jax.ShapeDtypeStruct((groups, n, rows_l, half), BF16)] * 2,
     )(me_arr, x, v_row, w_row, ft)
+
+
+def _fwd_col_steps_kernel(sj_ref, st_ref, se_ref, me_ref, x_ref, v_ref, w_ref, ft_ref, own_ref, send_ref):
+    n, rows_l, cols = x_ref.shape
+    g = (x_ref[...].astype(F32) * v_ref[...]).astype(BF16)
+    h = jnp.dot(g.reshape(n * rows_l, cols), ft_ref[...], preferred_element_type=F32)
+    h = (h.reshape(n, rows_l, cols) * w_ref[...]).astype(BF16)
+    half = cols // 2
+    _split_store(me_ref, h[:, :, :half], h[:, :, half:], own_ref, send_ref)
+
+
+def fwd_col_steps(me_arr, x, v_row, w_row, ft, steps):
+    groups, n, rows_l, cols = x.shape
+    half = cols // 2
+    sj, st, se = (jnp.array([step[k] for step in steps], I32) for k in range(3))
+    xs = pl.BlockSpec((None, BLK, rows_l, cols), lambda i, a, b, c: (a[i], b[i], 0, 0))
+    ts = pl.BlockSpec((BLK, rows_l, cols), lambda i, a, b, c: (c[i], 0, 0))
+    os = pl.BlockSpec((None, BLK, rows_l, half), lambda i, a, b, c: (a[i], b[i], 0, 0))
+    grid_spec = pltpu.PrefetchScalarGridSpec(
+        num_scalar_prefetch=3,
+        grid=(len(steps),),
+        in_specs=[
+            SMEM_SPEC,
+            xs,
+            ts,
+            ts,
+            pl.BlockSpec((cols, cols), lambda i, a, b, c: (0, 0)),
+        ],
+        out_specs=[os, os],
+    )
+    return pl.pallas_call(
+        _fwd_col_steps_kernel,
+        grid_spec=grid_spec,
+        out_shape=[jax.ShapeDtypeStruct((groups, n, rows_l, half), BF16)] * 2,
+    )(sj, st, se, me_arr, x, v_row, w_row, ft)
 
 
 def _product_kernel(eb0, fo_ref, fr_ref, cip_ref, key_ref, *rest):
@@ -366,9 +401,12 @@
     ).astype(BF16)
 
     raised = ring_hold(ring, raised)
-    own2, send2 = fwd_col(
-        me_arr, raised, v_row, w_row, ft_cols, lambda j, t: jnp.where(t >= j, t + 1, t)
-    )
+    digit_steps = []
+    for eb in range(EXTENDED // BLK):
+        for j in range(DIGITS):
+            if j != eb:
+                digit_steps.append((j, eb if eb < j else eb - 1, eb))
+    own2, send2 = fwd_col_steps(me_arr, raised, v_row, w_row, ft_cols, digit_steps)
     key, (own2, send2) = ring_finish(ring, (own2, send2))
     recv2 = swap(send2)
 

time: 124 us -> 123 us (level)
    pallas_call x2 -> x1, Pallas kernels: 19.1 us -> 5.7 us  [fwd_col(): pl.pallas_call(_fwd_col_kernel, grid=(groups, n // BLK), in_specs=[SMEM_S...]
    pallas_call x0 -> x1, Pallas kernels: none -> 12.6 us  [fwd_col_steps(): pl.pallas_call(_fwd_col_steps_kernel, grid_spec=grid_spec, out_shape=[jax...]
where the time goes in v13:
time: 123 us; the launch traced here: 122 us
  Pallas kernels  47.7 us (39%)
  local copies, waits for them, and re-layouts  27.9 us (23%)
  other arithmetic  13.7 us (11%)
  waiting for transfers between devices  11.9 us (10%)
  starting transfers between devices  9.48 us (8%)
  between operations  8.63 us (7%)
  matrix products  3.2 us (3%)
    pallas_call x1, Pallas kernels, fwd_col_steps(): pl.pallas_call(_fwd_col_steps_kernel, grid_spec=grid_spec, out_shape=[jax...  12.6 us
    pallas_call x2, Pallas kernels, product(): pl.pallas_call(lambda *refs: _product_kernel(eb0, *refs), grid=(nblocks,)...  10.4 us
    add x3, other arithmetic, _twiddle(): return 1.0 + 0.5 * (cp * cq - sp * sq)  8.96 us
    pallas_call x2, Pallas kernels, inv_row(): pl.pallas_call(_inv_row_kernel, grid=(n // BLK,), in_specs=[SMEM_SPEC, bl...  7.41 us
    pallas_call x2, Pallas kernels, inv_col(): pl.pallas_call(_inv_col_kernel, grid=(n // BLK,), in_specs=[blk, blk, pl....  7.17 us
    ppermute x3, starting transfers between devices, ring_step(): st['a'] = lax.ppermute(st['a'], 'limb', st['cw'])  6.18 us
    pallas_call x1, Pallas kernels, fwd_col(): pl.pallas_call(_fwd_col_kernel, grid=(groups, n // BLK), in_specs=[SMEM_S...  5.7 us
    ppermute x4, waiting for transfers between devices, swap(): return lax.ppermute(x, 'coef', perm=[(0, 1), (1, 0)])  5.65 us
  transfers between devices with their start and end apart: 12, of which 6 were waited for; matrix products, arithmetic and copies ran while one was open for 30% of the time, Pallas kernels for 24%

profile of v13, /device:TPU:0, one launch (start us, length us, event | category | flops | bytes accessed | tf_op | source)
XLA Modules:
  0.0 122.4 jit_solution(2818541740587687291)
XLA Ops:
  0.0 3.0 %collective-permute-start = (bf16[3,8,128,128]{3,2,1,0:T(8,128)(2,1)}, bf16[3,8,128,128]{3,2,1,0:T(8,128)(2,1)}, u32[]{:S(2)}, u32[]{:S(2)}) collective-permute-start(bf16[3,8,128,128]{3,2,1,0:T(8,128)(2,1)} %bitcast.102), channel_id=1, source_target_pairs={{0,4},{4,8},{8,12},{12,14},{14,10},{10,6},{6,2},{2,0},{1,5},{5,9},... | collective-permute-start | bytes 2359304 | tf_op jit(solution)/shard_map/ppermute | solution.py:333
  3.1 0.6 fusion.54
  3.7 0.3 fusion.58
  4.3 2.9 %add_bitcast_fusion.1.w_ref = f32[64,128,128]{2,1,0:T(8,128)} fusion(f32[64,8,128]{2,1,0:T(8,128)S(1)} %bitcast.98, f32[64,16,128]{2,1,0:T(8,128)S(1)} %bitcast.96, f32[64,8,128]{2,1,0:T(8,128)S(1)} %bitcast.99, f32[64,16,128]{2,1,0:T(8,128)S(1)} %bitcast.97), kind=kLoop, calls=%fused_computation.8 | loop fusion | flops 5242880 | bytes 5767168 | tf_op jit(solution)/shard_map/add | solution.py:53
  7.2 4.8 %shard_map.136 = (bf16[48,64,128]{2,1,0:T(8,128)(2,1)}, bf16[48,64,128]{2,1,0:T(8,128)(2,1)}) custom-call(s32[1]{0:T(128)} %bitcast.me_ref, bf16[48,128,128]{2,1,0:T(8,128)(2,1)} %bitcast.85, f32[64,128,128]{2,1,0:T(8,128)} %add_bitcast_fusion.1.w_ref, bf16[128,128]{1,0:T(8,128)(2,1)} %constant.253.clone.ft_ref), custom_call_target="tpu_custom_call" | custom-call | tf_op jit(solution)/shard_map/pallas_call | solution.py:101
  12.6 1.6 %fusion.50 = (f32[8,8,256]{2,1,0:T(8,128)S(1)}, f32[8,8,256]{2,1,0:T(8,128)S(1)}, f32[8,8,256]{2,1,0:T(8,128)S(1)}, f32[8,8,256]{2,1,0:T(8,128)S(1)}, f32[8,8,25...) fusion(s32[8,256]{1,0:T(8,128)S(1)} %add_select_fusion.12, ...), kind=kLoop, calls=%fused_computation.119 | loop fusion | flops 1376256 | bytes 811072 | tf_op jit(solution)/shard_map/cos | solution.py:35
  14.7 4.2 %broadcast_in_dim.8 = bf16[3,64,128,128]{3,2,1,0:T(8,128)(2,1)} broadcast(bf16[]{:T(256)} %constant.229.clone.1), dimensions={} | broadcast | bytes 6291458 | tf_op jit(solution)/shard_map/broadcast_in_dim | solution.py:308
  18.9 1.0 constant_dynamic-update-slice_fusion.6
  20.0 0.8 collective-permute-done
  20.8 1.5 %collective-permute-done.1 = bf16[3,8,128,128]{3,2,1,0:T(8,128)(2,1)} collective-permute-done((bf16[3,8,128,128]{3,2,1,0:T(8,128)(2,1)}, bf16[3,8,128,128]{3,2,1,0:T(8,128)(2,1)}, u32[]{:S(2)}, u32[]{:S(2)}) %collective-permute-start.1) | collective-permute-done | bytes 786464 | tf_op jit(solution)/shard_map/ppermute | solution.py:334
  22.3 1.6 %collective-permute-start.2 = (bf16[3,8,128,128]{3,2,1,0:T(8,128)(2,1)}, bf16[3,8,128,128]{3,2,1,0:T(8,128)(2,1)}, u32[]{:S(2)}, u32[]{:S(2)}) collective-permute-start(bf16[3,8,128,128]{3,2,1,0:T(8,128)(2,1)} %collective-permute-done), channel_id=1, source_target_pairs={{0,4},{4,8},{8,12},{12,14},{14,10},{10,6},{6,2},{2,0},{1,5},{5,9},... | collective-permute-start | bytes 2359304 | tf_op jit(solution)/shard_map/ppermute | solution.py:333
  23.9 0.4 collective-permute-start.3
  24.4 0.7 constant_dynamic-slice_fusion
  25.0 0.6 dynamic_slice.38
  27.5 3.0 %fusion.3.v_ref = f32[64,64,256]{2,1,0:T(8,128)} fusion(f32[64,64]{1,0:T(8,128)S(1)} %copy.20, f32[64,8,256]{2,1,0:T(8,128)S(1)} %bitcast.94, f32[64,64]{1,0:T(8,128)S(1)} %copy.19, f32[64,8,256]{2,1,0:T(8,128)S(1)} %bitcast.95), kind=kLoop, calls=%fused_computation.5 | loop fusion | flops 5242880 | bytes 5275648 | tf_op jit(solution)/shard_map/add | solution.py:53
  30.5 3.0 %add_bitcast_fusion.w_ref = f32[64,64,256]{2,1,0:T(8,128)} fusion(f32[64,8,256]{2,1,0:T(8,128)S(1)} %bitcast.92, f32[64,8,256]{2,1,0:T(8,128)S(1)} %bitcast.90, f32[64,8,256]{2,1,0:T(8,128)S(1)} %bitcast.93, f32[64,8,256]{2,1,0:T(8,128)S(1)} %bitcast.91), kind=kLoop, calls=%fused_computation.7 | loop fusion | flops 5242880 | bytes 6291456 | tf_op jit(solution)/shard_map/add | solution.py:53
  33.6 4.6 %shard_map.137 = bf16[48,64,256]{2,1,0:T(8,128)(2,1)} custom-call(bf16[48,64,128]{2,1,0:T(8,128)(2,1)} %get-tuple-element.44.own_ref, bf16[48,64,128]{2,1,0:T(8,128)(2,1)} %collective-permute-done.4.recv_ref, f32[64,64,256]{2,1,0:T(8,128)} %fusion.3.v_ref, bf16[128,256]{1,0:T(8,128)(2,1)} %get-tuple-element.78.fo_ref, bf16[128,256]{1,0:T(8,128)(2,1)} %get-tuple-element.77.fr_ref), custom_call_target="tpu_custom_call" | custom-call | tf_op jit(solution)/shard_map/pallas_call | solution.py:131
  38.2 2.5 %collective-permute-done.2 = bf16[3,8,128,128]{3,2,1,0:T(8,128)(2,1)} collective-permute-done((bf16[3,8,128,128]{3,2,1,0:T(8,128)(2,1)}, bf16[3,8,128,128]{3,2,1,0:T(8,128)(2,1)}, u32[]{:S(2)}, u32[]{:S(2)}) %collective-permute-start.2) | collective-permute-done | bytes 786464 | tf_op jit(solution)/shard_map/ppermute | solution.py:333
  40.8 1.3 %collective-permute-done.3 = bf16[3,8,128,128]{3,2,1,0:T(8,128)(2,1)} collective-permute-done((bf16[3,8,128,128]{3,2,1,0:T(8,128)(2,1)}, bf16[3,8,128,128]{3,2,1,0:T(8,128)(2,1)}, u32[]{:S(2)}, u32[]{:S(2)}) %collective-permute-start.3) | collective-permute-done | bytes 786464 | tf_op jit(solution)/shard_map/ppermute | solution.py:334
  42.0 1.6 %collective-permute-start.5 = (bf16[3,8,128,128]{3,2,1,0:T(8,128)(2,1)}, bf16[3,8,128,128]{3,2,1,0:T(8,128)(2,1)S(1)}, u32[]{:S(2)}, u32[]{:S(2)}) collective-permute-start(bf16[3,8,128,128]{3,2,1,0:T(8,128)(2,1)} %collective-permute-done.2), channel_id=1, source_target_pairs={{0,4},{4,8},{8,12},{12,14},{14,10},{10,6},{6,2},{2,0},{1,5},{5,9},... | collective-permute-start | bytes 2359304 | tf_op jit(solution)/shard_map/ppermute | solution.py:333
  43.6 0.5 collective-permute-start.6
  46.5 0.7 fusion.89
  51.4 2.2 %constant_dynamic-update-slice_fusion.5 = bf16[3,64,128,128]{3,2,1,0:T(8,128)(2,1)} fusion(bf16[3,64,128,128]{3,2,1,0:T(8,128)(2,1)} %constant_dynamic-update-slice_fusion.6, bf16[3,8,128,128]{3,2,1,0:T(8,128)(2,1)} %collective-permute-done, s32[]{:T(128)S(6)} %select_n.357), kind=kLoop, calls=%fused_computation.189 | loop fusion | bytes 1572868 | tf_op jit(solution)/shard_map/dynamic_update_slice | solution.py:335
  53.7 2.2 %constant_dynamic-update-slice_fusion.4 = bf16[3,64,128,128]{3,2,1,0:T(8,128)(2,1)} fusion(bf16[3,64,128,128]{3,2,1,0:T(8,128)(2,1)} %constant_dynamic-update-slice_fusion.5, bf16[3,8,128,128]{3,2,1,0:T(8,128)(2,1)} %collective-permute-done.1, s32[]{:T(128)S(6)} %select_n.360), kind=kLoop, calls=%fused_computation.188 | loop fusion | bytes 1572868 | tf_op jit(solution)/shard_map/dynamic_update_slice | solution.py:338
  55.9 1.5 %fusion.5 = bf16[3,64,256,48]{2,3,1,0:T(8,128)(2,1)S(1)} fusion(bf16[3,16,64,256]{3,2,1,0:T(8,128)(2,1)S(1)} %bitcast.88, bf16[3,48,16]{1,2,0:T(8,128)(2,1)S(1)} %copy-done), kind=kOutput, calls=%fused_computation.11 | convolution fusion | flops 75497472 | bytes 6296064 | tf_op jit(solution)/shard_map/dot_general | solution.py:399
  57.4 3.9 %copy.36 = bf16[3,64,256,48]{2,1,3,0:T(8,128)(2,1)} copy(bf16[3,64,256,48]{2,3,1,0:T(8,128)(2,1)S(1)} %fusion.5) | data formatting | bytes 9437184 | tf_op jit(solution)/shard_map/dot_general | solution.py:399
  61.4 2.2 %constant_dynamic-update-slice_fusion.3 = bf16[3,64,128,128]{3,2,1,0:T(8,128)(2,1)} fusion(bf16[3,64,128,128]{3,2,1,0:T(8,128)(2,1)} %constant_dynamic-update-slice_fusion.4, bf16[3,8,128,128]{3,2,1,0:T(8,128)(2,1)} %collective-permute-done.2, s32[]{:T(128)S(6)} %select_n.369), kind=kLoop, calls=%fused_computation.187 | loop fusion | bytes 1572868 | tf_op jit(solution)/shard_map/dynamic_update_slice | solution.py:335
  63.7 0.5 collective-permute-start.8
  64.2 1.7 %collective-permute-start.7 = (bf16[3,8,64,128]{3,2,1,0:T(8,128)(2,1)S(1)}, bf16[3,8,64,128]{3,2,1,0:T(8,128)(2,1)S(1)}, u32[]{:S(2)}, u32[]{:S(2)}) collective-permute-start(bf16[3,8,64,128]{3,2,1,0:T(8,128)(2,1)S(1)} %slice.6), channel_id=1, source_target_pairs={{0,4},{4,8},{8,12},{12,14},{14,10},{10,6},{6,2},{2,0},{1,5},{5,9},... | collective-permute-start | bytes 1179656 | tf_op jit(solution)/shard_map/ppermute | solution.py:343
  65.8 2.2 %constant_dynamic-update-slice_fusion.2 = bf16[3,64,128,128]{3,2,1,0:T(8,128)(2,1)} fusion(bf16[3,64,128,128]{3,2,1,0:T(8,128)(2,1)} %constant_dynamic-update-slice_fusion.3, bf16[3,8,128,128]{3,2,1,0:T(8,128)(2,1)} %collective-permute-done.3, s32[]{:T(128)S(6)} %select_n.372), kind=kLoop, calls=%fused_computation.186 | loop fusion | bytes 1572868 | tf_op jit(solution)/shard_map/dynamic_update_slice | solution.py:338
  68.0 12.6 %shard_map.138 = (bf16[3,48,64,128]{3,2,1,0:T(8,128)(2,1)}, bf16[3,48,64,128]{3,2,1,0:T(8,128)(2,1)}) custom-call(s32[9]{0:T(128)} %constant.254.clone.sj_ref, s32[9]{0:T(128)} %constant.255.clone.st_ref, s32[9]{0:T(128)} %constant.256.clone.se_ref, s32[1]{0:T(128)} %bitcast.me_ref, bf16[3,48,64,256]{3,2,1,0:T(8,128)(2,1)} %bitcast.84, ...), custom_call_target="tpu_custom_call" | custom-call | tf_op jit(solution)/shard_map/pallas_call | solution.py:198
  80.7 1.0 constant_dynamic-update-slice_fusion.1
  81.7 1.0 constant_dynamic-update-slice_fusion
  82.7 1.0 maximum_dynamic-update-slice_fusion.refs_3_
  83.7 0.7 constant_dynamic-slice_fusion.2
  84.4 4.0 %collective-permute-done.9.refs_5_.refs_7_.refs_9_ = bf16[3,48,64,128]{3,2,1,0:T(8,128)(2,1)S(1)} collective-permute-done((bf16[3,48,64,128]{3,2,1,0:T(8,128)(2,1)}, bf16[3,48,64,128]{3,2,1,0:T(8,128)(2,1)S(1)}, u32[]{:S(2)}, u32[]{:S(2)}) %collective-permute-start.9) | collective-permute-done | bytes 2359328 | tf_op jit(solution)/shard_map/ppermute | solution.py:366
  88.5 1.4 %copy-done.1 = bf16[3,48,64,128]{3,2,1,0:T(8,128)(2,1)} copy-done((bf16[3,48,64,128]{3,2,1,0:T(8,128)(2,1)}, bf16[3,48,64,128]{3,2,1,0:T(8,128)(2,1)S(1)}, u32[]{:S(2)}) %copy-start.1) | copy-done | bytes 2359320
  89.9 3.5 %shard_map.139.y_ref = bf16[16,128,128]{2,1,0:T(8,128)(2,1)} custom-call(bf16[128,64]{1,0:T(8,128)(2,1)} %get-tuple-element.82.refs_0_.fo_ref, bf16[128,64]{1,0:T(8,128)(2,1)} %get-tuple-element.81.refs_1_.fr_ref, bf16[48,128,128]{2,1,0:T(8,128)(2,1)} %bitcast.86, bf16[3,64,128,128]{3,2,1,0:T(8,128)(2,1)} %maximum_dynamic-update-slice_fusion.refs_3_, ...), custom_call_target="tpu_custom_call" | custom-call | tf_op jit(solution)/shard_map/pallas_call | solution.py:246
  93.5 2.6 %shard_map.140 = (bf16[16,64,128]{2,1,0:T(8,128)(2,1)}, bf16[16,64,128]{2,1,0:T(8,128)(2,1)}) custom-call(s32[1]{0:T(128)} %bitcast.me_ref, bf16[16,128,128]{2,1,0:T(8,128)(2,1)} %shard_map.139.y_ref, f32[64,128,128]{2,1,0:T(8,128)} %add_bitcast_fusion.1.w_ref, bf16[128,128]{1,0:T(8,128)(2,1)} %constant.253.clone.ft_ref), custom_call_target="tpu_custom_call" | custom-call | tf_op jit(solution)/shard_map/pallas_call | solution.py:101
  96.2 1.6 %collective-permute-done.10.recv_ref = bf16[16,64,128]{2,1,0:T(8,128)(2,1)S(1)} collective-permute-done((bf16[16,64,128]{2,1,0:T(8,128)(2,1)}, bf16[16,64,128]{2,1,0:T(8,128)(2,1)S(1)}, u32[]{:S(2)}, u32[]{:S(2)}) %collective-permute-start.10) | collective-permute-done | bytes 262176 | tf_op jit(solution)/shard_map/ppermute | solution.py:366
  97.8 0.7 copy-done.5
  98.5 2.5 %shard_map.141 = bf16[16,64,256]{2,1,0:T(8,128)(2,1)} custom-call(bf16[16,64,128]{2,1,0:T(8,128)(2,1)} %get-tuple-element.65.own_ref, bf16[16,64,128]{2,1,0:T(8,128)(2,1)} %copy-done.5, f32[64,64,256]{2,1,0:T(8,128)} %fusion.3.v_ref, bf16[128,256]{1,0:T(8,128)(2,1)} %get-tuple-element.78.fo_ref, bf16[128,256]{1,0:T(8,128)(2,1)} %get-tuple-element.77.fr_ref), custom_call_target="tpu_custom_call" | custom-call | tf_op jit(solution)/shard_map/pallas_call | solution.py:131
  101.0 1.7 %fusion.7 = bf16[64,256,48]{1,2,0:T(8,128)(2,1)S(1)} fusion(bf16[16,64,256]{2,1,0:T(8,128)(2,1)} %shard_map.141, bf16[48,16]{0,1:T(8,128)(2,1)S(1)} %copy-done.9), kind=kOutput, calls=%fused_computation.14 | convolution fusion | flops 25165824 | bytes 2098688 | tf_op jit(solution)/shard_map/dot_general | solution.py:418
  102.7 1.7 %copy.37 = bf16[64,256,48]{1,0,2:T(8,128)(2,1)} copy(bf16[64,256,48]{1,2,0:T(8,128)(2,1)S(1)} %fusion.7) | data formatting | bytes 3145728 | tf_op jit(solution)/shard_map/dot_general | solution.py:418
  104.4 5.7 %shard_map.142 = (bf16[1,48,64,128]{3,2,1,0:T(8,128)(2,1)}, bf16[1,48,64,128]{3,2,1,0:T(8,128)(2,1)}) custom-call(s32[1]{0:T(128)} %bitcast.me_ref, bf16[1,48,64,256]{3,2,1,0:T(8,128)(2,1)} %bitcast.89, f32[64,64,256]{2,1,0:T(8,128)} %fusion.3.v_ref, f32[64,64,256]{2,1,0:T(8,128)} %add_bitcast_fusion.w_ref, bf16[256,256]{1,0:T(8,128)(2,1)} %constant.257.clone.ft_ref), custom_call_target="tpu_custom_call" | custom-call | tf_op jit(solution)/shard_map/pallas_call | solution.py:161
  110.2 6.9 %shard_map.143.prod_ref = bf16[48,128,128]{2,1,0:T(8,128)(2,1)} custom-call(bf16[128,64]{1,0:T(8,128)(2,1)} %get-tuple-element.82.refs_0_.fo_ref, bf16[128,64]{1,0:T(8,128)(2,1)} %get-tuple-element.81.refs_1_.fr_ref, bf16[48,128,128]{2,1,0:T(8,128)(2,1)} %bitcast.87, bf16[3,64,128,128]{3,2,1,0:T(8,128)(2,1)} %maximum_dynamic-update-slice_fusion.refs_3_, ...), custom_call_target="tpu_custom_call" | custom-call | tf_op jit(solution)/shard_map/pallas_call | solution.py:246
  117.1 0.9 broadcast_in_dim.10.s_ref
  118.0 4.4 %shard_map.144 = bf16[48,128,128]{2,1,0:T(8,128)(2,1)} custom-call(bf16[128,64]{1,0:T(8,128)(2,1)} %get-tuple-element.82.refs_0_.fo_ref, bf16[128,64]{1,0:T(8,128)(2,1)} %get-tuple-element.81.refs_1_.fr_ref, bf16[48,64,128]{2,1,0:T(8,128)(2,1)} %bitcast.100, bf16[48,64,128]{2,1,0:T(8,128)(2,1)} %bitcast.101, bf16[48,128,128]{2,1,0:T(8,128)(2,1)} %shard_map.143.prod_ref, ...), custom_call_target="tpu_custom_call" | custom-call | tf_op jit(solution)/shard_map/pallas_call | solution.py:277
  (58 shorter events, 1.8 us)
Async XLA Ops:
  0.0 55.9 %copy-start = (bf16[3,48,16]{1,2,0:T(8,128)(2,1)S(1)}, bf16[3,48,16]{1,2,0:T(8,128)(2,1)}, u32[]{:S(2)}) copy-start(bf16[3,48,16]{1,2,0:T(8,128)(2,1)} %param.16) | copy-start | bytes 13828
  0.0 20.8 %collective-permute-start = (bf16[3,8,128,128]{3,2,1,0:T(8,128)(2,1)}, bf16[3,8,128,128]{3,2,1,0:T(8,128)(2,1)}, u32[]{:S(2)}, u32[]{:S(2)}) collective-permute-start(bf16[3,8,128,128]{3,2,1,0:T(8,128)(2,1)} %bitcast.102), channel_id=1, source_target_pairs={{0,4},{4,8},{8,12},{12,14},{14,10},{10,6},{6,2},{2,0},{1,5},{5,9},... | collective-permute-start | bytes 2359304 | tf_op jit(solution)/shard_map/ppermute | solution.py:333
  3.0 19.3 %collective-permute-start.1 = (bf16[3,8,128,128]{3,2,1,0:T(8,128)(2,1)}, bf16[3,8,128,128]{3,2,1,0:T(8,128)(2,1)}, u32[]{:S(2)}, u32[]{:S(2)}) collective-permute-start(bf16[3,8,128,128]{3,2,1,0:T(8,128)(2,1)} %bitcast.103), channel_id=1, source_target_pairs={{0,2},{4,0},{8,4},{12,8},{14,12},{10,14},{6,10},{2,6},{1,3},{5,1},... | collective-permute-start | bytes 2359304 | tf_op jit(solution)/shard_map/ppermute | solution.py:334
  12.0 21.5 %collective-permute-start.4 = (bf16[48,64,128]{2,1,0:T(8,128)(2,1)}, bf16[48,64,128]{2,1,0:T(8,128)(2,1)}, u32[]{:S(2)}, u32[]{:S(2)}) collective-permute-start(bf16[48,64,128]{2,1,0:T(8,128)(2,1)} %get-tuple-element.45), channel_id=1, source_target_pairs={{0,1},{1,0},{2,3},{3,2},{4,5},{5,4},{6,7},{7,6},{8,9},{9,8},{10,11... | collective-permute-start | bytes 2359304 | tf_op jit(solution)/shard_map/ppermute | solution.py:366
  14.4 4.6 %copy-start.4 = (bf16[1,3,8,128,128]{4,3,2,1,0:T(8,128)(2,1)S(1)}, bf16[1,3,8,128,128]{4,3,2,1,0:T(8,128)(2,1)}, u32[]{:S(2)}) copy-start(bf16[1,3,8,128,128]{4,3,2,1,0:T(8,128)(2,1)} %param.15) | copy-start | bytes 2359300
  14.7 9.7 %copy-start.6 = (bf16[256,256]{1,0:T(8,128)(2,1)S(1)}, bf16[256,256]{1,0:T(8,128)(2,1)}, u32[]{:S(2)}) copy-start(bf16[256,256]{1,0:T(8,128)(2,1)} %constant.251.clone) | copy-start | bytes 393220
  14.7 10.3 %copy-start.11 = (s32[8]{0:T(128)S(1)}, s32[8]{0:T(128)}, u32[]{:S(2)}) copy-start(s32[8]{0:T(128)} %constant.250.clone) | copy-start | bytes 100
  22.3 18.4 %collective-permute-start.2 = (bf16[3,8,128,128]{3,2,1,0:T(8,128)(2,1)}, bf16[3,8,128,128]{3,2,1,0:T(8,128)(2,1)}, u32[]{:S(2)}, u32[]{:S(2)}) collective-permute-start(bf16[3,8,128,128]{3,2,1,0:T(8,128)(2,1)} %collective-permute-done), channel_id=1, source_target_pairs={{0,4},{4,8},{8,12},{12,14},{14,10},{10,6},{6,2},{2,0},{1,5},{5,9},... | collective-permute-start | bytes 2359304 | tf_op jit(solution)/shard_map/ppermute | solution.py:333
  23.9 18.1 %collective-permute-start.3 = (bf16[3,8,128,128]{3,2,1,0:T(8,128)(2,1)}, bf16[3,8,128,128]{3,2,1,0:T(8,128)(2,1)}, u32[]{:S(2)}, u32[]{:S(2)}) collective-permute-start(bf16[3,8,128,128]{3,2,1,0:T(8,128)(2,1)} %collective-permute-done.1), channel_id=1, source_target_pairs={{0,2},{4,0},{8,4},{12,8},{14,12},{10,14},{6,10},{2,6},{1,3},{5,1},... | collective-permute-start | bytes 2359304 | tf_op jit(solution)/shard_map/ppermute | solution.py:334
  33.6 12.9 %copy-start.8 = (s32[8]{0:T(128)S(1)}, s32[8]{0:T(128)}, u32[]{:S(2)}) copy-start(s32[8]{0:T(128)} %constant.249.clone) | copy-start | bytes 100
  38.2 17.7 %copy-start.2 = (bf16[48,64,256]{2,1,0:T(8,128)(2,1)S(1)}, bf16[48,64,256]{2,1,0:T(8,128)(2,1)}, u32[]{:S(2)}) copy-start(bf16[48,64,256]{2,1,0:T(8,128)(2,1)} %shard_map.137) | copy-start | bytes 4718596
  42.0 21.6 %collective-permute-start.5 = (bf16[3,8,128,128]{3,2,1,0:T(8,128)(2,1)}, bf16[3,8,128,128]{3,2,1,0:T(8,128)(2,1)S(1)}, u32[]{:S(2)}, u32[]{:S(2)}) collective-permute-start(bf16[3,8,128,128]{3,2,1,0:T(8,128)(2,1)} %collective-permute-done.2), channel_id=1, source_target_pairs={{0,4},{4,8},{8,12},{12,14},{14,10},{10,6},{6,2},{2,0},{1,5},{5,9},... | collective-permute-start | bytes 2359304 | tf_op jit(solution)/shard_map/ppermute | solution.py:333
  43.6 20.0 %collective-permute-start.6 = (bf16[3,8,128,128]{3,2,1,0:T(8,128)(2,1)}, bf16[3,8,128,128]{3,2,1,0:T(8,128)(2,1)S(1)}, u32[]{:S(2)}, u32[]{:S(2)}) collective-permute-start(bf16[3,8,128,128]{3,2,1,0:T(8,128)(2,1)} %collective-permute-done.3), channel_id=1, source_target_pairs={{0,2},{4,0},{8,4},{12,8},{14,12},{10,14},{6,10},{2,6},{1,3},{5,1},... | collective-permute-start | bytes 2359304 | tf_op jit(solution)/shard_map/ppermute | solution.py:334
  63.7 19.0 %collective-permute-start.8 = (bf16[3,8,64,128]{3,2,1,0:T(8,128)(2,1)S(1)}, bf16[3,8,64,128]{3,2,1,0:T(8,128)(2,1)S(1)}, u32[]{:S(2)}, u32[]{:S(2)}) collective-permute-start(bf16[3,8,64,128]{3,2,1,0:T(8,128)(2,1)S(1)} %slice.7), channel_id=1, source_target_pairs={{0,2},{4,0},{8,4},{12,8},{14,12},{10,14},{6,10},{2,6},{1,3},{5,1},... | collective-permute-start | bytes 1179656 | tf_op jit(solution)/shard_map/ppermute | solution.py:344
  64.2 18.5 %collective-permute-start.7 = (bf16[3,8,64,128]{3,2,1,0:T(8,128)(2,1)S(1)}, bf16[3,8,64,128]{3,2,1,0:T(8,128)(2,1)S(1)}, u32[]{:S(2)}, u32[]{:S(2)}) collective-permute-start(bf16[3,8,64,128]{3,2,1,0:T(8,128)(2,1)S(1)} %slice.6), channel_id=1, source_target_pairs={{0,4},{4,8},{8,12},{12,14},{14,10},{10,6},{6,2},{2,0},{1,5},{5,9},... | collective-permute-start | bytes 1179656 | tf_op jit(solution)/shard_map/ppermute | solution.py:343
  80.7 3.1 %copy-start.7 = (bf16[128,128]{1,0:T(8,128)(2,1)S(1)}, bf16[128,128]{1,0:T(8,128)(2,1)}, u32[]{:S(2)}) copy-start(bf16[128,128]{1,0:T(8,128)(2,1)} %constant.252.clone) | copy-start | bytes 98308
  83.7 4.7 %collective-permute-start.9 = (bf16[3,48,64,128]{3,2,1,0:T(8,128)(2,1)}, bf16[3,48,64,128]{3,2,1,0:T(8,128)(2,1)S(1)}, u32[]{:S(2)}, u32[]{:S(2)}) collective-permute-start(bf16[3,48,64,128]{3,2,1,0:T(8,128)(2,1)} %get-tuple-element.64), channel_id=1, source_target_pairs={{0,1},{1,0},{2,3},{3,2},{4,5},{5,4},{6,7},{7,6},{8,9},{9,8},{10,11... | collective-permute-start | bytes 7077896 | tf_op jit(solution)/shard_map/ppermute | solution.py:366
  88.5 1.4 %copy-start.1 = (bf16[3,48,64,128]{3,2,1,0:T(8,128)(2,1)}, bf16[3,48,64,128]{3,2,1,0:T(8,128)(2,1)S(1)}, u32[]{:S(2)}) copy-start(bf16[3,48,64,128]{3,2,1,0:T(8,128)(2,1)S(1)} %collective-permute-done.9.refs_5_.refs_7_.refs_9_) | copy-start | bytes 7077892
  93.4 7.6 %copy-start.9 = (bf16[48,16]{0,1:T(8,128)(2,1)S(1)}, bf16[48,16]{0,1:T(8,128)(2,1)}, u32[]{:S(2)}) copy-start(bf16[48,16]{0,1:T(8,128)(2,1)} %param.17) | copy-start | bytes 4612
  96.0 1.7 %collective-permute-start.10 = (bf16[16,64,128]{2,1,0:T(8,128)(2,1)}, bf16[16,64,128]{2,1,0:T(8,128)(2,1)S(1)}, u32[]{:S(2)}, u32[]{:S(2)}) collective-permute-start(bf16[16,64,128]{2,1,0:T(8,128)(2,1)} %get-tuple-element.66), channel_id=1, source_target_pairs={{0,1},{1,0},{2,3},{3,2},{4,5},{5,4},{6,7},{7,6},{8,9},{9,8},{10,11... | collective-permute-start | bytes 786440 | tf_op jit(solution)/shard_map/ppermute | solution.py:366
  97.8 0.7 copy-start.5
  110.1 7.0 %copy-start.10 = (f32[48]{0:T(128)S(1)}, f32[48]{0:T(128)}, u32[]{:S(2)}) copy-start(f32[48]{0:T(128)} %param.18) | copy-start | bytes 580
  110.1 7.0 %collective-permute-start.11 = (bf16[1,48,64,128]{3,2,1,0:T(8,128)(2,1)}, bf16[1,48,64,128]{3,2,1,0:T(8,128)(2,1)S(1)}, u32[]{:S(2)}, u32[]{:S(2)}) collective-permute-start(bf16[1,48,64,128]{3,2,1,0:T(8,128)(2,1)} %get-tuple-element.68), channel_id=1, source_target_pairs={{0,1},{1,0},{2,3},{3,2},{4,5},{5,4},{6,7},{7,6},{8,9},{9,8},{10,11... | collective-permute-start | bytes 2359304 | tf_op jit(solution)/shard_map/ppermute | solution.py:366
  117.1 0.9 copy-start.3

commit v14 on v13

--- a/solution.py
+++ b/solution.py
@@ -343,9 +343,8 @@
         a = lax.ppermute(st["a"][:, :, :h], "limb", st["cw"])
         b = lax.ppermute(st["b"][:, :, h:], "limb", st["ccw"])
         src = order[(p + s) % n] * width
-        st["full"] = lax.dynamic_update_slice_in_dim(
-            st["full"], jnp.concatenate([a, b], axis=2), src, axis=1
-        )
+        st["full"] = lax.dynamic_update_slice(st["full"], a, (0, src, 0, 0))
+        st["full"] = lax.dynamic_update_slice(st["full"], b, (0, src, h, 0))
 
 
 def ring_hold(st, x):

time: 123 us -> 124 us (level)
  local copies, waits for them, and re-layouts: 27.9 us -> 29.7 us
    dynamic_update_slice x0 -> x2, local copies, waits for them, and re-layouts: none -> 1.65 us  [the longest x1 0.84 us: ring_step(): st['full'] = lax.dynamic_update_slice(st['full'], b, (0, src, h, 0))]
  transfers between devices with their start and end apart: 12 -> 12, of which waited for: 6 -> 6; matrix products, arithmetic and copies ran while one was open for 30% -> 31% of each run, Pallas kernels for 24% -> 24%
where the time goes in v14:
time: 124 us; the launch traced here: 123 us
  Pallas kernels  47.7 us (38%)
  local copies, waits for them, and re-layouts  29.7 us (24%)
  other arithmetic  12.6 us (10%)
  waiting for transfers between devices  11.9 us (10%)
  starting transfers between devices  9.46 us (8%)
  between operations  8.63 us (7%)
  matrix products  3.19 us (3%)
    pallas_call x1, Pallas kernels, fwd_col_steps(): pl.pallas_call(_fwd_col_steps_kernel, grid_spec=grid_spec, out_shape=[jax...  12.6 us
    pallas_call x2, Pallas kernels, product(): pl.pallas_call(lambda *refs: _product_kernel(eb0, *refs), grid=(nblocks,)...  10.4 us
    add x3, other arithmetic, _twiddle(): return 1.0 + 0.5 * (cp * cq - sp * sq)  8.96 us
    pallas_call x2, Pallas kernels, inv_row(): pl.pallas_call(_inv_row_kernel, grid=(n // BLK,), in_specs=[SMEM_SPEC, bl...  7.41 us
    pallas_call x2, Pallas kernels, inv_col(): pl.pallas_call(_inv_col_kernel, grid=(n // BLK,), in_specs=[blk, blk, pl....  7.17 us
    ppermute x3, starting transfers between devices, ring_step(): st['a'] = lax.ppermute(st['a'], 'limb', st['cw'])  6.18 us
    pallas_call x1, Pallas kernels, fwd_col(): pl.pallas_call(_fwd_col_kernel, grid=(groups, n // BLK), in_specs=[SMEM_S...  5.7 us
    ppermute x4, waiting for transfers between devices, swap(): return lax.ppermute(x, 'coef', perm=[(0, 1), (1, 0)])  5.64 us
  transfers between devices with their start and end apart: 12, of which 6 were waited for; matrix products, arithmetic and copies ran while one was open for 31% of the time, Pallas kernels for 24%

profile of v14, /device:TPU:0, one launch (start us, length us, event | category | flops | bytes accessed | tf_op | source)
XLA Modules:
  0.0 123.2 jit_solution(5077968264704006059)
XLA Ops:
  0.0 3.0 %collective-permute-start = (bf16[3,8,128,128]{3,2,1,0:T(8,128)(2,1)}, bf16[3,8,128,128]{3,2,1,0:T(8,128)(2,1)}, u32[]{:S(2)}, u32[]{:S(2)}) collective-permute-start(bf16[3,8,128,128]{3,2,1,0:T(8,128)(2,1)} %bitcast.102), channel_id=1, source_target_pairs={{0,4},{4,8},{8,12},{12,14},{14,10},{10,6},{6,2},{2,0},{1,5},{5,9},... | collective-permute-start | bytes 2359304 | tf_op jit(solution)/shard_map/ppermute | solution.py:333
  3.1 0.6 fusion.54
  4.3 2.9 %add_bitcast_fusion.1.w_ref = f32[64,128,128]{2,1,0:T(8,128)} fusion(f32[64,8,128]{2,1,0:T(8,128)S(1)} %bitcast.98, f32[64,16,128]{2,1,0:T(8,128)S(1)} %bitcast.96, f32[64,8,128]{2,1,0:T(8,128)S(1)} %bitcast.99, f32[64,16,128]{2,1,0:T(8,128)S(1)} %bitcast.97), kind=kLoop, calls=%fused_computation.8 | loop fusion | flops 5242880 | bytes 5767168 | tf_op jit(solution)/shard_map/add | solution.py:53
  7.2 4.8 %shard_map.136 = (bf16[48,64,128]{2,1,0:T(8,128)(2,1)}, bf16[48,64,128]{2,1,0:T(8,128)(2,1)}) custom-call(s32[1]{0:T(128)} %bitcast.me_ref, bf16[48,128,128]{2,1,0:T(8,128)(2,1)} %bitcast.85, f32[64,128,128]{2,1,0:T(8,128)} %add_bitcast_fusion.1.w_ref, bf16[128,128]{1,0:T(8,128)(2,1)} %constant.253.clone.ft_ref), custom_call_target="tpu_custom_call" | custom-call | tf_op jit(solution)/shard_map/pallas_call | solution.py:101
  12.6 1.6 %fusion.50 = (f32[8,8,256]{2,1,0:T(8,128)S(1)}, f32[8,8,256]{2,1,0:T(8,128)S(1)}, f32[8,8,256]{2,1,0:T(8,128)S(1)}, f32[8,8,256]{2,1,0:T(8,128)S(1)}, f32[8,8,25...) fusion(s32[8,256]{1,0:T(8,128)S(1)} %add_select_fusion.12, ...), kind=kLoop, calls=%fused_computation.118 | loop fusion | flops 1376256 | bytes 811072 | tf_op jit(solution)/shard_map/cos | solution.py:35
  14.7 4.2 %broadcast_in_dim.8 = bf16[3,64,128,128]{3,2,1,0:T(8,128)(2,1)} broadcast(bf16[]{:T(256)} %constant.229.clone.1), dimensions={} | broadcast | bytes 6291458 | tf_op jit(solution)/shard_map/broadcast_in_dim | solution.py:308
  18.9 1.0 constant_dynamic-update-slice_fusion.8
  20.0 0.8 collective-permute-done
  20.8 1.5 %collective-permute-done.1 = bf16[3,8,128,128]{3,2,1,0:T(8,128)(2,1)} collective-permute-done((bf16[3,8,128,128]{3,2,1,0:T(8,128)(2,1)}, bf16[3,8,128,128]{3,2,1,0:T(8,128)(2,1)}, u32[]{:S(2)}, u32[]{:S(2)}) %collective-permute-start.1) | collective-permute-done | bytes 786464 | tf_op jit(solution)/shard_map/ppermute | solution.py:334
  22.3 1.6 %collective-permute-start.2 = (bf16[3,8,128,128]{3,2,1,0:T(8,128)(2,1)}, bf16[3,8,128,128]{3,2,1,0:T(8,128)(2,1)}, u32[]{:S(2)}, u32[]{:S(2)}) collective-permute-start(bf16[3,8,128,128]{3,2,1,0:T(8,128)(2,1)} %collective-permute-done), channel_id=1, source_target_pairs={{0,4},{4,8},{8,12},{12,14},{14,10},{10,6},{6,2},{2,0},{1,5},{5,9},... | collective-permute-start | bytes 2359304 | tf_op jit(solution)/shard_map/ppermute | solution.py:333
  23.9 0.4 collective-permute-start.3
  24.4 0.7 constant_dynamic-slice_fusion
  25.0 0.6 dynamic_slice.38
  27.5 3.0 %fusion.3.v_ref = f32[64,64,256]{2,1,0:T(8,128)} fusion(f32[64,64]{1,0:T(8,128)S(1)} %copy.20, f32[64,8,256]{2,1,0:T(8,128)S(1)} %bitcast.94, f32[64,64]{1,0:T(8,128)S(1)} %copy.19, f32[64,8,256]{2,1,0:T(8,128)S(1)} %bitcast.95), kind=kLoop, calls=%fused_computation.5 | loop fusion | flops 5242880 | bytes 5275648 | tf_op jit(solution)/shard_map/add | solution.py:53
  30.5 3.0 %add_bitcast_fusion.w_ref = f32[64,64,256]{2,1,0:T(8,128)} fusion(f32[64,8,256]{2,1,0:T(8,128)S(1)} %bitcast.92, f32[64,8,256]{2,1,0:T(8,128)S(1)} %bitcast.90, f32[64,8,256]{2,1,0:T(8,128)S(1)} %bitcast.93, f32[64,8,256]{2,1,0:T(8,128)S(1)} %bitcast.91), kind=kLoop, calls=%fused_computation.7 | loop fusion | flops 5242880 | bytes 6291456 | tf_op jit(solution)/shard_map/add | solution.py:53
  33.6 4.6 %shard_map.137 = bf16[48,64,256]{2,1,0:T(8,128)(2,1)} custom-call(bf16[48,64,128]{2,1,0:T(8,128)(2,1)} %get-tuple-element.44.own_ref, bf16[48,64,128]{2,1,0:T(8,128)(2,1)} %collective-permute-done.4.recv_ref, f32[64,64,256]{2,1,0:T(8,128)} %fusion.3.v_ref, bf16[128,256]{1,0:T(8,128)(2,1)} %get-tuple-element.78.fo_ref, bf16[128,256]{1,0:T(8,128)(2,1)} %get-tuple-element.77.fr_ref), custom_call_target="tpu_custom_call" | custom-call | tf_op jit(solution)/shard_map/pallas_call | solution.py:131
  38.2 2.5 %collective-permute-done.2 = bf16[3,8,128,128]{3,2,1,0:T(8,128)(2,1)} collective-permute-done((bf16[3,8,128,128]{3,2,1,0:T(8,128)(2,1)}, bf16[3,8,128,128]{3,2,1,0:T(8,128)(2,1)}, u32[]{:S(2)}, u32[]{:S(2)}) %collective-permute-start.2) | collective-permute-done | bytes 786464 | tf_op jit(solution)/shard_map/ppermute | solution.py:333
  40.8 1.3 %collective-permute-done.3 = bf16[3,8,128,128]{3,2,1,0:T(8,128)(2,1)} collective-permute-done((bf16[3,8,128,128]{3,2,1,0:T(8,128)(2,1)}, bf16[3,8,128,128]{3,2,1,0:T(8,128)(2,1)}, u32[]{:S(2)}, u32[]{:S(2)}) %collective-permute-start.3) | collective-permute-done | bytes 786464 | tf_op jit(solution)/shard_map/ppermute | solution.py:334
  42.0 1.6 %collective-permute-start.5 = (bf16[3,8,128,128]{3,2,1,0:T(8,128)(2,1)}, bf16[3,8,128,128]{3,2,1,0:T(8,128)(2,1)S(1)}, u32[]{:S(2)}, u32[]{:S(2)}) collective-permute-start(bf16[3,8,128,128]{3,2,1,0:T(8,128)(2,1)} %collective-permute-done.2), channel_id=1, source_target_pairs={{0,4},{4,8},{8,12},{12,14},{14,10},{10,6},{6,2},{2,0},{1,5},{5,9},... | collective-permute-start | bytes 2359304 | tf_op jit(solution)/shard_map/ppermute | solution.py:333
  43.6 0.5 collective-permute-start.6
  46.5 0.7 fusion.89
  51.4 2.2 %constant_dynamic-update-slice_fusion.7 = bf16[3,64,128,128]{3,2,1,0:T(8,128)(2,1)} fusion(bf16[3,64,128,128]{3,2,1,0:T(8,128)(2,1)} %constant_dynamic-update-slice_fusion.8, bf16[3,8,128,128]{3,2,1,0:T(8,128)(2,1)} %collective-permute-done, s32[]{:T(128)S(6)} %select_n.358), kind=kLoop, calls=%fused_computation.190 | loop fusion | bytes 1572868 | tf_op jit(solution)/shard_map/dynamic_update_slice | solution.py:335
  53.7 2.2 %constant_dynamic-update-slice_fusion.6 = bf16[3,64,128,128]{3,2,1,0:T(8,128)(2,1)} fusion(bf16[3,64,128,128]{3,2,1,0:T(8,128)(2,1)} %constant_dynamic-update-slice_fusion.7, bf16[3,8,128,128]{3,2,1,0:T(8,128)(2,1)} %collective-permute-done.1, s32[]{:T(128)S(6)} %select_n.361), kind=kLoop, calls=%fused_computation.189 | loop fusion | bytes 1572868 | tf_op jit(solution)/shard_map/dynamic_update_slice | solution.py:338
  55.9 1.5 %fusion.5 = bf16[3,64,256,48]{2,3,1,0:T(8,128)(2,1)S(1)} fusion(bf16[3,16,64,256]{3,2,1,0:T(8,128)(2,1)S(1)} %bitcast.88, bf16[3,48,16]{1,2,0:T(8,128)(2,1)S(1)} %copy-done), kind=kOutput, calls=%fused_computation.11 | convolution fusion | flops 75497472 | bytes 6296064 | tf_op jit(solution)/shard_map/dot_general | solution.py:398
  57.4 4.1 %copy.36 = bf16[3,64,256,48]{2,1,3,0:T(8,128)(2,1)} copy(bf16[3,64,256,48]{2,3,1,0:T(8,128)(2,1)S(1)} %fusion.5) | data formatting | bytes 9437184 | tf_op jit(solution)/shard_map/dot_general | solution.py:398
  61.5 2.2 %constant_dynamic-update-slice_fusion.5 = bf16[3,64,128,128]{3,2,1,0:T(8,128)(2,1)} fusion(bf16[3,64,128,128]{3,2,1,0:T(8,128)(2,1)} %constant_dynamic-update-slice_fusion.6, bf16[3,8,128,128]{3,2,1,0:T(8,128)(2,1)} %collective-permute-done.2, s32[]{:T(128)S(6)} %select_n.370), kind=kLoop, calls=%fused_computation.188 | loop fusion | bytes 1572868 | tf_op jit(solution)/shard_map/dynamic_update_slice | solution.py:335
  63.8 1.6 %collective-permute-start.7 = (bf16[3,8,64,128]{3,2,1,0:T(8,128)(2,1)S(1)}, bf16[3,8,64,128]{3,2,1,0:T(8,128)(2,1)S(1)}, u32[]{:S(2)}, u32[]{:S(2)}) collective-permute-start(bf16[3,8,64,128]{3,2,1,0:T(8,128)(2,1)S(1)} %slice.6), channel_id=1, source_target_pairs={{0,4},{4,8},{8,12},{12,14},{14,10},{10,6},{6,2},{2,0},{1,5},{5,9},... | collective-permute-start | bytes 1179656 | tf_op jit(solution)/shard_map/ppermute | solution.py:343
  65.4 0.6 collective-permute-start.8
  65.9 2.2 %constant_dynamic-update-slice_fusion.4 = bf16[3,64,128,128]{3,2,1,0:T(8,128)(2,1)} fusion(bf16[3,64,128,128]{3,2,1,0:T(8,128)(2,1)} %constant_dynamic-update-slice_fusion.5, bf16[3,8,128,128]{3,2,1,0:T(8,128)(2,1)} %collective-permute-done.3, s32[]{:T(128)S(6)} %select_n.373), kind=kLoop, calls=%fused_computation.187 | loop fusion | bytes 1572868 | tf_op jit(solution)/shard_map/dynamic_update_slice | solution.py:338
  68.2 12.6 %shard_map.138 = (bf16[3,48,64,128]{3,2,1,0:T(8,128)(2,1)}, bf16[3,48,64,128]{3,2,1,0:T(8,128)(2,1)}) custom-call(s32[9]{0:T(128)} %constant.254.clone.sj_ref, s32[9]{0:T(128)} %constant.255.clone.st_ref, s32[9]{0:T(128)} %constant.256.clone.se_ref, s32[1]{0:T(128)} %bitcast.me_ref, bf16[3,48,64,256]{3,2,1,0:T(8,128)(2,1)} %bitcast.84, ...), custom_call_target="tpu_custom_call" | custom-call | tf_op jit(solution)/shard_map/pallas_call | solution.py:198
  80.8 1.0 constant_dynamic-update-slice_fusion.3
  81.8 1.0 constant_dynamic-update-slice_fusion.2
  82.8 0.8 constant_dynamic-update-slice_fusion.1
  83.6 0.8 constant_dynamic-update-slice_fusion.refs_3_
  84.5 0.7 constant_dynamic-slice_fusion.2
  85.2 4.0 %collective-permute-done.9.refs_5_.refs_7_.refs_9_ = bf16[3,48,64,128]{3,2,1,0:T(8,128)(2,1)S(1)} collective-permute-done((bf16[3,48,64,128]{3,2,1,0:T(8,128)(2,1)}, bf16[3,48,64,128]{3,2,1,0:T(8,128)(2,1)S(1)}, u32[]{:S(2)}, u32[]{:S(2)}) %collective-permute-start.9) | collective-permute-done | bytes 2359328 | tf_op jit(solution)/shard_map/ppermute | solution.py:365
  89.2 1.4 %copy-done.1 = bf16[3,48,64,128]{3,2,1,0:T(8,128)(2,1)} copy-done((bf16[3,48,64,128]{3,2,1,0:T(8,128)(2,1)}, bf16[3,48,64,128]{3,2,1,0:T(8,128)(2,1)S(1)}, u32[]{:S(2)}) %copy-start.1) | copy-done | bytes 2359320
  90.7 3.5 %shard_map.139.y_ref = bf16[16,128,128]{2,1,0:T(8,128)(2,1)} custom-call(bf16[128,64]{1,0:T(8,128)(2,1)} %get-tuple-element.82.refs_0_.fo_ref, bf16[128,64]{1,0:T(8,128)(2,1)} %get-tuple-element.81.refs_1_.fr_ref, bf16[48,128,128]{2,1,0:T(8,128)(2,1)} %bitcast.86, bf16[3,64,128,128]{3,2,1,0:T(8,128)(2,1)} %constant_dynamic-update-slice_fusion.refs_3_, ...), custom_call_target="tpu_custom_call" | custom-call | tf_op jit(solution)/shard_map/pallas_call | solution.py:246
  94.2 2.6 %shard_map.140 = (bf16[16,64,128]{2,1,0:T(8,128)(2,1)}, bf16[16,64,128]{2,1,0:T(8,128)(2,1)}) custom-call(s32[1]{0:T(128)} %bitcast.me_ref, bf16[16,128,128]{2,1,0:T(8,128)(2,1)} %shard_map.139.y_ref, f32[64,128,128]{2,1,0:T(8,128)} %add_bitcast_fusion.1.w_ref, bf16[128,128]{1,0:T(8,128)(2,1)} %constant.253.clone.ft_ref), custom_call_target="tpu_custom_call" | custom-call | tf_op jit(solution)/shard_map/pallas_call | solution.py:101
  96.9 1.6 %collective-permute-done.10.recv_ref = bf16[16,64,128]{2,1,0:T(8,128)(2,1)S(1)} collective-permute-done((bf16[16,64,128]{2,1,0:T(8,128)(2,1)}, bf16[16,64,128]{2,1,0:T(8,128)(2,1)S(1)}, u32[]{:S(2)}, u32[]{:S(2)}) %collective-permute-start.10) | collective-permute-done | bytes 262176 | tf_op jit(solution)/shard_map/ppermute | solution.py:365
  98.5 0.7 copy-done.5
  99.2 2.5 %shard_map.141 = bf16[16,64,256]{2,1,0:T(8,128)(2,1)} custom-call(bf16[16,64,128]{2,1,0:T(8,128)(2,1)} %get-tuple-element.65.own_ref, bf16[16,64,128]{2,1,0:T(8,128)(2,1)} %copy-done.5, f32[64,64,256]{2,1,0:T(8,128)} %fusion.3.v_ref, bf16[128,256]{1,0:T(8,128)(2,1)} %get-tuple-element.78.fo_ref, bf16[128,256]{1,0:T(8,128)(2,1)} %get-tuple-element.77.fr_ref), custom_call_target="tpu_custom_call" | custom-call | tf_op jit(solution)/shard_map/pallas_call | solution.py:131
  101.8 1.7 %fusion.7 = bf16[64,256,48]{1,2,0:T(8,128)(2,1)S(1)} fusion(bf16[16,64,256]{2,1,0:T(8,128)(2,1)} %shard_map.141, bf16[48,16]{0,1:T(8,128)(2,1)S(1)} %copy-done.9), kind=kOutput, calls=%fused_computation.13 | convolution fusion | flops 25165824 | bytes 2098688 | tf_op jit(solution)/shard_map/dot_general | solution.py:417
  103.4 1.7 %copy.37 = bf16[64,256,48]{1,0,2:T(8,128)(2,1)} copy(bf16[64,256,48]{1,2,0:T(8,128)(2,1)S(1)} %fusion.7) | data formatting | bytes 3145728 | tf_op jit(solution)/shard_map/dot_general | solution.py:417
  105.1 5.7 %shard_map.142 = (bf16[1,48,64,128]{3,2,1,0:T(8,128)(2,1)}, bf16[1,48,64,128]{3,2,1,0:T(8,128)(2,1)}) custom-call(s32[1]{0:T(128)} %bitcast.me_ref, bf16[1,48,64,256]{3,2,1,0:T(8,128)(2,1)} %bitcast.89, f32[64,64,256]{2,1,0:T(8,128)} %fusion.3.v_ref, f32[64,64,256]{2,1,0:T(8,128)} %add_bitcast_fusion.w_ref, bf16[256,256]{1,0:T(8,128)(2,1)} %constant.257.clone.ft_ref), custom_call_target="tpu_custom_call" | custom-call | tf_op jit(solution)/shard_map/pallas_call | solution.py:161
  110.9 6.9 %shard_map.143.prod_ref = bf16[48,128,128]{2,1,0:T(8,128)(2,1)} custom-call(bf16[128,64]{1,0:T(8,128)(2,1)} %get-tuple-element.82.refs_0_.fo_ref, bf16[128,64]{1,0:T(8,128)(2,1)} %get-tuple-element.81.refs_1_.fr_ref, bf16[48,128,128]{2,1,0:T(8,128)(2,1)} %bitcast.87, bf16[3,64,128,128]{3,2,1,0:T(8,128)(2,1)} %constant_dynamic-update-slice_fusion.refs_3_, ...), custom_call_target="tpu_custom_call" | custom-call | tf_op jit(solution)/shard_map/pallas_call | solution.py:246
  117.8 0.9 broadcast_in_dim.10.s_ref
  118.7 4.4 %shard_map.144 = bf16[48,128,128]{2,1,0:T(8,128)(2,1)} custom-call(bf16[128,64]{1,0:T(8,128)(2,1)} %get-tuple-element.82.refs_0_.fo_ref, bf16[128,64]{1,0:T(8,128)(2,1)} %get-tuple-element.81.refs_1_.fr_ref, bf16[48,64,128]{2,1,0:T(8,128)(2,1)} %bitcast.100, bf16[48,64,128]{2,1,0:T(8,128)(2,1)} %bitcast.101, bf16[48,128,128]{2,1,0:T(8,128)(2,1)} %shard_map.143.prod_ref, ...), custom_call_target="tpu_custom_call" | custom-call | tf_op jit(solution)/shard_map/pallas_call | solution.py:277
  (59 shorter events, 2.1 us)
Async XLA Ops:
  0.0 55.9 %copy-start = (bf16[3,48,16]{1,2,0:T(8,128)(2,1)S(1)}, bf16[3,48,16]{1,2,0:T(8,128)(2,1)}, u32[]{:S(2)}) copy-start(bf16[3,48,16]{1,2,0:T(8,128)(2,1)} %param.16) | copy-start | bytes 13828
  0.0 20.8 %collective-permute-start = (bf16[3,8,128,128]{3,2,1,0:T(8,128)(2,1)}, bf16[3,8,128,128]{3,2,1,0:T(8,128)(2,1)}, u32[]{:S(2)}, u32[]{:S(2)}) collective-permute-start(bf16[3,8,128,128]{3,2,1,0:T(8,128)(2,1)} %bitcast.102), channel_id=1, source_target_pairs={{0,4},{4,8},{8,12},{12,14},{14,10},{10,6},{6,2},{2,0},{1,5},{5,9},... | collective-permute-start | bytes 2359304 | tf_op jit(solution)/shard_map/ppermute | solution.py:333
  3.0 19.3 %collective-permute-start.1 = (bf16[3,8,128,128]{3,2,1,0:T(8,128)(2,1)}, bf16[3,8,128,128]{3,2,1,0:T(8,128)(2,1)}, u32[]{:S(2)}, u32[]{:S(2)}) collective-permute-start(bf16[3,8,128,128]{3,2,1,0:T(8,128)(2,1)} %bitcast.103), channel_id=1, source_target_pairs={{0,2},{4,0},{8,4},{12,8},{14,12},{10,14},{6,10},{2,6},{1,3},{5,1},... | collective-permute-start | bytes 2359304 | tf_op jit(solution)/shard_map/ppermute | solution.py:334
  12.0 21.5 %collective-permute-start.4 = (bf16[48,64,128]{2,1,0:T(8,128)(2,1)}, bf16[48,64,128]{2,1,0:T(8,128)(2,1)}, u32[]{:S(2)}, u32[]{:S(2)}) collective-permute-start(bf16[48,64,128]{2,1,0:T(8,128)(2,1)} %get-tuple-element.45), channel_id=1, source_target_pairs={{0,1},{1,0},{2,3},{3,2},{4,5},{5,4},{6,7},{7,6},{8,9},{9,8},{10,11... | collective-permute-start | bytes 2359304 | tf_op jit(solution)/shard_map/ppermute | solution.py:365
  14.4 4.6 %copy-start.4 = (bf16[1,3,8,128,128]{4,3,2,1,0:T(8,128)(2,1)S(1)}, bf16[1,3,8,128,128]{4,3,2,1,0:T(8,128)(2,1)}, u32[]{:S(2)}) copy-start(bf16[1,3,8,128,128]{4,3,2,1,0:T(8,128)(2,1)} %param.15) | copy-start | bytes 2359300
  14.7 9.7 %copy-start.6 = (bf16[256,256]{1,0:T(8,128)(2,1)S(1)}, bf16[256,256]{1,0:T(8,128)(2,1)}, u32[]{:S(2)}) copy-start(bf16[256,256]{1,0:T(8,128)(2,1)} %constant.251.clone) | copy-start | bytes 393220
  14.7 10.3 %copy-start.11 = (s32[8]{0:T(128)S(1)}, s32[8]{0:T(128)}, u32[]{:S(2)}) copy-start(s32[8]{0:T(128)} %constant.250.clone) | copy-start | bytes 100
  22.3 18.4 %collective-permute-start.2 = (bf16[3,8,128,128]{3,2,1,0:T(8,128)(2,1)}, bf16[3,8,128,128]{3,2,1,0:T(8,128)(2,1)}, u32[]{:S(2)}, u32[]{:S(2)}) collective-permute-start(bf16[3,8,128,128]{3,2,1,0:T(8,128)(2,1)} %collective-permute-done), channel_id=1, source_target_pairs={{0,4},{4,8},{8,12},{12,14},{14,10},{10,6},{6,2},{2,0},{1,5},{5,9},... | collective-permute-start | bytes 2359304 | tf_op jit(solution)/shard_map/ppermute | solution.py:333
  23.9 18.1 %collective-permute-start.3 = (bf16[3,8,128,128]{3,2,1,0:T(8,128)(2,1)}, bf16[3,8,128,128]{3,2,1,0:T(8,128)(2,1)}, u32[]{:S(2)}, u32[]{:S(2)}) collective-permute-start(bf16[3,8,128,128]{3,2,1,0:T(8,128)(2,1)} %collective-permute-done.1), channel_id=1, source_target_pairs={{0,2},{4,0},{8,4},{12,8},{14,12},{10,14},{6,10},{2,6},{1,3},{5,1},... | collective-permute-start | bytes 2359304 | tf_op jit(solution)/shard_map/ppermute | solution.py:334
  33.6 12.9 %copy-start.8 = (s32[8]{0:T(128)S(1)}, s32[8]{0:T(128)}, u32[]{:S(2)}) copy-start(s32[8]{0:T(128)} %constant.249.clone) | copy-start | bytes 100
  38.2 17.7 %copy-start.2 = (bf16[48,64,256]{2,1,0:T(8,128)(2,1)S(1)}, bf16[48,64,256]{2,1,0:T(8,128)(2,1)}, u32[]{:S(2)}) copy-start(bf16[48,64,256]{2,1,0:T(8,128)(2,1)} %shard_map.137) | copy-start | bytes 4718596
  42.0 21.7 %collective-permute-start.5 = (bf16[3,8,128,128]{3,2,1,0:T(8,128)(2,1)}, bf16[3,8,128,128]{3,2,1,0:T(8,128)(2,1)S(1)}, u32[]{:S(2)}, u32[]{:S(2)}) collective-permute-start(bf16[3,8,128,128]{3,2,1,0:T(8,128)(2,1)} %collective-permute-done.2), channel_id=1, source_target_pairs={{0,4},{4,8},{8,12},{12,14},{14,10},{10,6},{6,2},{2,0},{1,5},{5,9},... | collective-permute-start | bytes 2359304 | tf_op jit(solution)/shard_map/ppermute | solution.py:333
  43.6 20.1 %collective-permute-start.6 = (bf16[3,8,128,128]{3,2,1,0:T(8,128)(2,1)}, bf16[3,8,128,128]{3,2,1,0:T(8,128)(2,1)S(1)}, u32[]{:S(2)}, u32[]{:S(2)}) collective-permute-start(bf16[3,8,128,128]{3,2,1,0:T(8,128)(2,1)} %collective-permute-done.3), channel_id=1, source_target_pairs={{0,2},{4,0},{8,4},{12,8},{14,12},{10,14},{6,10},{2,6},{1,3},{5,1},... | collective-permute-start | bytes 2359304 | tf_op jit(solution)/shard_map/ppermute | solution.py:334
  63.8 19.0 %collective-permute-start.7 = (bf16[3,8,64,128]{3,2,1,0:T(8,128)(2,1)S(1)}, bf16[3,8,64,128]{3,2,1,0:T(8,128)(2,1)S(1)}, u32[]{:S(2)}, u32[]{:S(2)}) collective-permute-start(bf16[3,8,64,128]{3,2,1,0:T(8,128)(2,1)S(1)} %slice.6), channel_id=1, source_target_pairs={{0,4},{4,8},{8,12},{12,14},{14,10},{10,6},{6,2},{2,0},{1,5},{5,9},... | collective-permute-start | bytes 1179656 | tf_op jit(solution)/shard_map/ppermute | solution.py:343
  65.4 18.2 %collective-permute-start.8 = (bf16[3,8,64,128]{3,2,1,0:T(8,128)(2,1)S(1)}, bf16[3,8,64,128]{3,2,1,0:T(8,128)(2,1)S(1)}, u32[]{:S(2)}, u32[]{:S(2)}) collective-permute-start(bf16[3,8,64,128]{3,2,1,0:T(8,128)(2,1)S(1)} %slice.7), channel_id=1, source_target_pairs={{0,2},{4,0},{8,4},{12,8},{14,12},{10,14},{6,10},{2,6},{1,3},{5,1},... | collective-permute-start | bytes 1179656 | tf_op jit(solution)/shard_map/ppermute | solution.py:344
  80.8 3.7 %copy-start.7 = (bf16[128,128]{1,0:T(8,128)(2,1)S(1)}, bf16[128,128]{1,0:T(8,128)(2,1)}, u32[]{:S(2)}) copy-start(bf16[128,128]{1,0:T(8,128)(2,1)} %constant.252.clone) | copy-start | bytes 98308
  84.5 4.7 %collective-permute-start.9 = (bf16[3,48,64,128]{3,2,1,0:T(8,128)(2,1)}, bf16[3,48,64,128]{3,2,1,0:T(8,128)(2,1)S(1)}, u32[]{:S(2)}, u32[]{:S(2)}) collective-permute-start(bf16[3,48,64,128]{3,2,1,0:T(8,128)(2,1)} %get-tuple-element.64), channel_id=1, source_target_pairs={{0,1},{1,0},{2,3},{3,2},{4,5},{5,4},{6,7},{7,6},{8,9},{9,8},{10,11... | collective-permute-start | bytes 7077896 | tf_op jit(solution)/shard_map/ppermute | solution.py:365
  89.2 1.4 %copy-start.1 = (bf16[3,48,64,128]{3,2,1,0:T(8,128)(2,1)}, bf16[3,48,64,128]{3,2,1,0:T(8,128)(2,1)S(1)}, u32[]{:S(2)}) copy-start(bf16[3,48,64,128]{3,2,1,0:T(8,128)(2,1)S(1)} %collective-permute-done.9.refs_5_.refs_7_.refs_9_) | copy-start | bytes 7077892
  94.2 7.6 %copy-start.9 = (bf16[48,16]{0,1:T(8,128)(2,1)S(1)}, bf16[48,16]{0,1:T(8,128)(2,1)}, u32[]{:S(2)}) copy-start(bf16[48,16]{0,1:T(8,128)(2,1)} %param.17) | copy-start | bytes 4612
  96.8 1.7 %collective-permute-start.10 = (bf16[16,64,128]{2,1,0:T(8,128)(2,1)}, bf16[16,64,128]{2,1,0:T(8,128)(2,1)S(1)}, u32[]{:S(2)}, u32[]{:S(2)}) collective-permute-start(bf16[16,64,128]{2,1,0:T(8,128)(2,1)} %get-tuple-element.66), channel_id=1, source_target_pairs={{0,1},{1,0},{2,3},{3,2},{4,5},{5,4},{6,7},{7,6},{8,9},{9,8},{10,11... | collective-permute-start | bytes 786440 | tf_op jit(solution)/shard_map/ppermute | solution.py:365
  98.5 0.7 copy-start.5
  110.8 7.0 %copy-start.10 = (f32[48]{0:T(128)S(1)}, f32[48]{0:T(128)}, u32[]{:S(2)}) copy-start(f32[48]{0:T(128)} %param.18) | copy-start | bytes 580
  110.8 7.0 %collective-permute-start.11 = (bf16[1,48,64,128]{3,2,1,0:T(8,128)(2,1)}, bf16[1,48,64,128]{3,2,1,0:T(8,128)(2,1)S(1)}, u32[]{:S(2)}, u32[]{:S(2)}) collective-permute-start(bf16[1,48,64,128]{3,2,1,0:T(8,128)(2,1)} %get-tuple-element.68), channel_id=1, source_target_pairs={{0,1},{1,0},{2,3},{3,2},{4,5},{5,4},{6,7},{7,6},{8,9},{9,8},{10,11... | collective-permute-start | bytes 2359304 | tf_op jit(solution)/shard_map/ppermute | solution.py:365
  117.8 0.9 copy-start.3
